TPU v7x, 32 devices: a whole 2x2x4 slice. The times are simulated.
32 devices in a mesh: node: 8 (over z, x), feat: 4 (over y, core).
Axes of the slice: x: 2, y: 2, z: 4, core: 2. Of those that a mesh axis runs over, the one named last changes fastest.
Arguments:
- features: bfloat16 [128, 128, 128], P('node', 'feat'), may hold values from -6 to 6
- tile_values: bfloat16 [2048, 128, 128], P('node'), may hold values from -0.125 to 0.125
- tile_row: int32 [2048], P('node'), may hold values from 0 to 127, as said below
- tile_col: int32 [2048], P('node'), may hold values from 0 to 127, as said below
- tile_count: int32 [8], P('node'), may hold values from 32 to 256, as said below
- weight: float32 [128, 128], P('feat'), may hold values from -0.5 to 0.5
- first_moment: float32 [128, 128], P('feat'), may hold values from -3 to 3
- second_moment: float32 [128, 128], P('feat'), may hold values from 0.1 to 2
- cotangent: bfloat16 [128, 128, 128], P('node', 'feat'), may hold values from -6 to 6
Outputs:
- activated: bfloat16 [128, 128, 128], P('node', 'feat')
- feature_grad: float32 [128, 128, 128], P('node', 'feat')
- new_weight: float32 [128, 128], P('feat')
- new_first: float32 [128, 128], P('feat')
- new_second: float32 [128, 128], P('feat')
Inputs may be any that keep to these rules, and one draw needn't show every extreme that they name: `tile_row`: the slots of index d of node (slots d * 256 to (d + 1) * 256 - 1) name target blocks of that index only: d * 16 to (d + 1) * 16 - 1. `tile_col`: A slot's source block lies on an index of node at most 2 away from the slot's own index around the closed loop of node indices; both distances 2 occur on every index. `tile_count`: some index of node has all 256 slots live, some has 32.
All inputs are finite; a program needn't handle non-finite values.
Results may differ from a plain program's by a relative error of at most 0.0058.
Values may be sent and summed in bfloat16 or wider, within the bound.
No kernel may reach another device: no remote copies, remote signals or barrier semaphores. Data moves between devices by JAX's collectives and lax.ppermute only.
A program may use at most 64 MiB of HBM per device.

v0:
```python
import math

import jax
import jax.numpy as jnp
from jax import lax
from jax.sharding import PartitionSpec as P

REACH = 2


first_decay = 0.9
second_decay = 0.999
learn_rate = 0.05
first_fix = 1.0 - 0.9**10
second_fix = 1.0 - 0.999**10
adam_eps = 1e-08


def passed_along(block, axis, distance):
    devices = range(lax.axis_size(axis))
    route = [((i - distance) % len(devices), i) for i in devices]
    return lax.ppermute(block, axis, route)


def elu_slope(preact):
    return jnp.where(preact > 0, 1.0, jnp.exp(jnp.minimum(preact, 0.0)))


def one_hot_table(indices, count, dtype):
    return (indices[:, None] == jnp.arange(count)[None, :]).astype(dtype)


def per_device(
    features,
    tile_values,
    tile_row,
    tile_col,
    tile_count,
    weight,
    first_moment,
    second_moment,
    cotangent,
):
    cycle_size = lax.axis_size("node")
    own_node = lax.axis_index("node")
    blocks = features.shape[0]
    width_local = features.shape[1]
    tile_size = features.shape[2]
    slots = tile_values.shape[0]
    live = (jnp.arange(slots) < tile_count[0]).astype(jnp.float32)
    local_row = tile_row - own_node * blocks
    col_owner = tile_col // blocks
    col_block = tile_col % blocks
    offset = (col_owner - own_node) % cycle_size
    offset = jnp.where(offset > cycle_size // 2, offset - cycle_size, offset)
    source_slot = (offset + REACH) * blocks + col_block
    targets = (2 * REACH + 1) * blocks
    pick_source = one_hot_table(source_slot, targets, jnp.bfloat16)
    pick_row = one_hot_table(local_row, blocks, jnp.bfloat16)
    add_row = one_hot_table(local_row, blocks, jnp.float32) * live[:, None]
    add_source = one_hot_table(source_slot, targets, jnp.float32) * live[:, None]
    pieces = []
    for distance in range(-REACH, REACH + 1):
        if distance == 0:
            pieces.append(features)
        else:
            pieces.append(passed_along(features, "node", -distance))
    nearby = jnp.concatenate(pieces, axis=0)
    sources = jnp.einsum(
        "ts,sfk->tfk", pick_source, nearby, preferred_element_type=jnp.float32
    ).astype(jnp.bfloat16)
    forward_terms = jnp.einsum(
        "tfk,tjk->tfj", sources, tile_values, preferred_element_type=jnp.float32
    )
    aggregate = jnp.einsum("tb,tfj->bfj", add_row, forward_terms, precision=lax.Precision.HIGHEST)
    aggregate = aggregate.astype(jnp.bfloat16)
    weight_half = weight.astype(jnp.bfloat16)
    aggregate_all, weight_all = (
        lax.all_gather(aggregate, "feat", axis=1, tiled=True),
        lax.all_gather(weight_half, "feat", axis=0, tiled=True),
    )
    column_start = lax.axis_index("feat") * width_local
    weight_cols = lax.dynamic_slice_in_dim(weight_all, column_start, width_local, 1)
    preact = jnp.einsum(
        "bij,io->boj", aggregate_all, weight_cols, preferred_element_type=jnp.float32
    )
    activated = jax.nn.elu(preact).astype(jnp.bfloat16)
    slope_grad = (cotangent.astype(jnp.float32) * elu_slope(preact)).astype(jnp.bfloat16)
    slope_all = lax.all_gather(slope_grad, "feat", axis=1, tiled=True)
    node_total = cycle_size * blocks * tile_size
    grad_local = jnp.einsum("bij,boj->io", aggregate, slope_all, preferred_element_type=jnp.float32)
    grad = lax.psum(grad_local, "node") * (1.0 / math.sqrt(node_total))
    back_rows = jnp.einsum(
        "io,boj->bij", weight_half, slope_all, preferred_element_type=jnp.float32
    ).astype(jnp.bfloat16)
    back_sources = jnp.einsum(
        "tb,bfj->tfj", pick_row, back_rows, preferred_element_type=jnp.float32
    ).astype(jnp.bfloat16)
    back_terms = jnp.einsum(
        "tfj,tjk->tfk", back_sources, tile_values, preferred_element_type=jnp.float32
    )
    outgoing = jnp.einsum("ts,tfk->sfk", add_source, back_terms, precision=lax.Precision.HIGHEST)
    outgoing = outgoing.reshape(2 * REACH + 1, blocks, width_local, tile_size)
    feature_grad = outgoing[REACH]
    for distance in range(-REACH, REACH + 1):
        if distance != 0:
            feature_grad = feature_grad + passed_along(outgoing[distance + REACH], "node", distance)
    new_first = first_decay * first_moment + (1.0 - first_decay) * grad
    new_second = second_decay * second_moment + (1.0 - second_decay) * grad * grad
    new_weight = weight - learn_rate * (new_first / first_fix) / (
        jnp.sqrt(new_second / second_fix) + adam_eps
    )
    return (activated, feature_grad, new_weight, new_first, new_second)


def solution(mesh):
    return jax.shard_map(
        per_device,
        mesh=mesh,
        in_specs=(
            P("node", "feat", None),
            P("node", None, None),
            P("node"),
            P("node"),
            P("node"),
            P("feat", None),
            P("feat", None),
            P("feat", None),
            P("node", "feat", None),
        ),
        out_specs=(
            P("node", "feat", None),
            P("node", "feat", None),
            P("feat", None),
            P("feat", None),
            P("feat", None),
        ),
        check_vma=False,
    )
```

profile of v0, /device:TPU:0, one launch (start us, length us, event | category | flops | bytes accessed | tf_op | source)
XLA Modules:
  0.0 112.7 jit_solution(17020929460422994571)
XLA Ops:
  0.6 6.0 %collective-permute-start.2 = (bf16[16,32,128]{2,1,0:T(8,128)(2,1)}, bf16[16,32,128]{2,1,0:T(8,128)(2,1)S(1)}, u32[]{:S(2)}, u32[]{:S(2)}) collective-permute-start(bf16[16,32,128]{2,1,0:T(8,128)(2,1)} %param.9), channel_id=1, source_target_pairs={{4,0},{8,4},{12,8},{16,12},{20,16},{24,20},{28,24},{0,28},{5,1},{9... | collective-permute-start | bytes 393224 | tf_op jit(solution)/shard_map/ppermute | solution.py:22
  6.7 0.0 collective-permute-start.1
  6.7 0.0 collective-permute-start
  6.7 3.8 %collective-permute-start.3 = (bf16[16,32,128]{2,1,0:T(8,128)(2,1)}, bf16[16,32,128]{2,1,0:T(8,128)(2,1)S(1)}, u32[]{:S(2)}, u32[]{:S(2)}) collective-permute-start(bf16[16,32,128]{2,1,0:T(8,128)(2,1)} %param.9), channel_id=1, source_target_pairs={{8,0},{12,4},{16,8},{20,12},{24,16},{28,20},{0,24},{4,28},{9,1},{1... | collective-permute-start | bytes 393224 | tf_op jit(solution)/shard_map/ppermute | solution.py:22
  10.5 0.7 fusion.41
  11.2 0.7 broadcast_subtract_fusion
  12.5 0.7 convert_element_type.38
  13.3 5.2 %all_gather.9 = bf16[128,128]{1,0:T(8,128)(2,1)S(1)} all-gather(bf16[32,128]{1,0:T(8,128)(2,1)S(1)} %convert_element_type.38), channel_id=1, replica_groups=mesh['node'=8,'feat'=4] {'feat'}, dimensions={0}, use_global_device_ids=true | all-gather | bytes 40960 | tf_op jit(solution)/shard_map/all_gather | solution.py:80
  18.4 0.0 collective-permute-done
  18.5 0.0 collective-permute-done.1
  18.5 0.9 constant_dynamic-update-slice_fusion.2
  19.4 0.0 collective-permute-done.2
  19.5 0.0 collective-permute-done.3
  19.5 0.8 fusion.10
  20.3 7.2 %fusion.4 = f32[256,32,128]{2,1,0:T(8,128)S(1)} fusion(bf16[256,128,128]{2,1,0:T(8,128)(2,1)} %param.10, bf16[256,32,128]{2,0,1:T(8,128)(2,1)S(1)} %fusion.10), kind=kOutput, calls=%fused_computation.6 | convolution fusion | flops 268435456 | bytes 14680064 | tf_op jit(solution)/shard_map/tfk,tjk->tfj/dot_general | solution.py:72
  27.5 0.0 copy-start.1
  27.5 4.4 %fusion.7 = bf16[16,32,128]{2,0,1:T(8,128)(2,1)S(1)} fusion(f32[256,32,128]{2,1,0:T(8,128)S(1)} %fusion.4, f32[256]{0:T(256)S(1)} %compare_convert_fusion, s32[256]{0:T(256)S(1)} %broadcast_subtract_fusion), kind=kOutput, calls=%fused_computation.11 | convolution fusion | flops 201400320 | bytes 4327424 | tf_op jit(solution)/shard_map/tb,tfj->bfj/dot_general | solution.py:75
  31.9 7.3 %all_gather.10 = bf16[16,128,128]{2,0,1:T(8,128)(2,1)S(1)} all-gather(bf16[16,32,128]{2,0,1:T(8,128)(2,1)S(1)} %fusion.7), channel_id=1, replica_groups=mesh['node'=8,'feat'=4] {'feat'}, dimensions={1}, use_global_device_ids=true | all-gather | bytes 655360 | tf_op jit(solution)/shard_map/all_gather | solution.py:79
  39.1 0.0 copy-done.1
  39.1 1.1 fusion.16
  40.2 7.5 %all_gather.11 = bf16[16,128,128]{2,1,0:T(8,128)(2,1)S(1)} all-gather(bf16[16,32,128]{2,1,0:T(8,128)(2,1)S(1)} %get-tuple-element.22), channel_id=1, replica_groups=mesh['node'=8,'feat'=4] {'feat'}, dimensions={1}, use_global_device_ids=true | all-gather | bytes 655360 | tf_op jit(solution)/shard_map/all_gather | solution.py:89
  47.7 0.3 fusion.6
  48.0 0.2 copy.25
  48.3 0.7 fusion.34
  49.0 7.2 %fusion.5 = f32[256,32,128]{2,1,0:T(8,128)S(1)} fusion(bf16[256,128,128]{2,1,0:T(8,128)(2,1)} %param.10, bf16[256,32,128]{2,0,1:T(8,128)(2,1)S(1)} %fusion.34), kind=kOutput, calls=%fused_computation.7 | convolution fusion | flops 268435456 | bytes 14680064 | tf_op jit(solution)/shard_map/tfj,tjk->tfk/dot_general | solution.py:99
  56.2 0.0 copy-start
  56.2 4.9 %fusion = f32[80,32,128]{2,0,1:T(8,128)S(1)} fusion(f32[256,32,128]{2,1,0:T(8,128)S(1)} %fusion.5, f32[256]{0:T(256)S(1)} %compare_convert_fusion, s32[256]{0:T(256)S(1)} %fusion.41), kind=kOutput, calls=%fused_computation | convolution fusion | flops 1006673920 | bytes 5507072 | tf_op jit(solution)/shard_map/ts,tfk->sfk/dot_general | solution.py:102
  61.1 0.9 fusion.48
  62.0 0.0 collective-permute-start.4
  62.0 2.0 %collective-permute-start.7 = (f32[16,32,128]{2,0,1:T(8,128)}, f32[16,32,128]{2,0,1:T(8,128)S(1)}, u32[]{:S(2)}, u32[]{:S(2)}) collective-permute-start(f32[16,32,128]{2,0,1:T(8,128)} %get-tuple-element.19), channel_id=1, source_target_pairs={{24,0},{28,4},{0,8},{4,12},{8,16},{12,20},{16,24},{20,28},{25,1},{... | collective-permute-start | bytes 786440 | tf_op jit(solution)/shard_map/ppermute | solution.py:22
  64.0 1.5 %collective-permute-start.6 = (f32[16,32,128]{2,0,1:T(8,128)S(1)}, f32[16,32,128]{2,0,1:T(8,128)S(1)}, u32[]{:S(2)}, u32[]{:S(2)}) collective-permute-start(f32[16,32,128]{2,0,1:T(8,128)S(1)} %get-tuple-element.20), channel_id=1, source_target_pairs={{28,0},{0,4},{4,8},{8,12},{12,16},{16,20},{20,24},{24,28},{29,1},{... | collective-permute-start | bytes 786440 | tf_op jit(solution)/shard_map/ppermute | solution.py:22
  65.5 3.3 %collective-permute-start.5 = (f32[16,32,128]{2,0,1:T(8,128)S(1)}, f32[16,32,128]{2,0,1:T(8,128)S(1)}, u32[]{:S(2)}, u32[]{:S(2)}) collective-permute-start(f32[16,32,128]{2,0,1:T(8,128)S(1)} %get-tuple-element.21), channel_id=1, source_target_pairs={{4,0},{8,4},{12,8},{16,12},{20,16},{24,20},{28,24},{0,28},{5,1},{9... | collective-permute-start | bytes 786440 | tf_op jit(solution)/shard_map/ppermute | solution.py:22
  68.8 0.9 convolution_bitcast_fusion.1
  69.7 40.8 %psum.7 = f32[32,128]{1,0:T(8,128)S(1)} all-reduce(f32[32,128]{1,0:T(8,128)} %convolution_bitcast_fusion.1), channel_id=1, replica_groups=mesh['node'=8,'feat'=4] {'node'}, use_global_device_ids=true, to_apply=%region_0.1 | all-reduce | flops 4096 | bytes 32768 | tf_op jit(solution)/shard_map/psum | solution.py:92
  110.4 0.0 copy-done
  110.4 1.4 %divide_subtract_fusion = (f32[32,128]{1,0:T(8,128)}, f32[32,128]{1,0:T(8,128)}, f32[32,128]{1,0:T(8,128)}) fusion(f32[32,128]{1,0:T(8,128)S(1)} %copy-done, f32[32,128]{1,0:T(8,128)S(1)} %psum.7, f32[32,128]{1,0:T(8,128)} %param.15, f32[32,128]{1,0:T(8,128)} %param.16), kind=kLoop, calls=%fused_computation.39 | loop fusion | flops 53248 | bytes 114688 | tf_op jit(solution)/shard_map/sub | solution.py:110
  111.8 0.0 collective-permute-done.4
  111.8 0.0 collective-permute-done.7
  111.8 0.0 collective-permute-done.6
  111.8 0.0 collective-permute-done.5
  111.8 0.1 fusion.19
  111.9 0.8 copy.21
  (5 shorter events, 0.1 us)
Async XLA Ops:
  0.6 18.8 %collective-permute-start.2 = (bf16[16,32,128]{2,1,0:T(8,128)(2,1)}, bf16[16,32,128]{2,1,0:T(8,128)(2,1)S(1)}, u32[]{:S(2)}, u32[]{:S(2)}) collective-permute-start(bf16[16,32,128]{2,1,0:T(8,128)(2,1)} %param.9), channel_id=1, source_target_pairs={{4,0},{8,4},{12,8},{16,12},{20,16},{24,20},{28,24},{0,28},{5,1},{9... | collective-permute-start | bytes 393224 | tf_op jit(solution)/shard_map/ppermute | solution.py:22
  6.7 11.8 %collective-permute-start.1 = (bf16[16,32,128]{2,1,0:T(8,128)(2,1)}, bf16[16,32,128]{2,1,0:T(8,128)(2,1)S(1)}, u32[]{:S(2)}, u32[]{:S(2)}) collective-permute-start(bf16[16,32,128]{2,1,0:T(8,128)(2,1)} %param.9), channel_id=1, source_target_pairs={{28,0},{0,4},{4,8},{8,12},{12,16},{16,20},{20,24},{24,28},{29,1},{... | collective-permute-start | bytes 393224 | tf_op jit(solution)/shard_map/ppermute | solution.py:22
  6.7 11.8 %collective-permute-start = (bf16[16,32,128]{2,1,0:T(8,128)(2,1)}, bf16[16,32,128]{2,1,0:T(8,128)(2,1)S(1)}, u32[]{:S(2)}, u32[]{:S(2)}) collective-permute-start(bf16[16,32,128]{2,1,0:T(8,128)(2,1)} %param.9), channel_id=1, source_target_pairs={{24,0},{28,4},{0,8},{4,12},{8,16},{12,20},{16,24},{20,28},{25,1},{... | collective-permute-start | bytes 393224 | tf_op jit(solution)/shard_map/ppermute | solution.py:22
  6.7 12.8 %collective-permute-start.3 = (bf16[16,32,128]{2,1,0:T(8,128)(2,1)}, bf16[16,32,128]{2,1,0:T(8,128)(2,1)S(1)}, u32[]{:S(2)}, u32[]{:S(2)}) collective-permute-start(bf16[16,32,128]{2,1,0:T(8,128)(2,1)} %param.9), channel_id=1, source_target_pairs={{8,0},{12,4},{16,8},{20,12},{24,16},{28,20},{0,24},{4,28},{9,1},{1... | collective-permute-start | bytes 393224 | tf_op jit(solution)/shard_map/ppermute | solution.py:22
  27.5 11.6 %copy-start.1 = (bf16[16,32,128]{2,1,0:T(8,128)(2,1)S(1)}, bf16[16,32,128]{2,1,0:T(8,128)(2,1)}, u32[]{:S(2)}) copy-start(bf16[16,32,128]{2,1,0:T(8,128)(2,1)} %param.17) | copy-start | bytes 393220
  56.2 54.2 %copy-start = (f32[32,128]{1,0:T(8,128)S(1)}, f32[32,128]{1,0:T(8,128)}, u32[]{:S(2)}) copy-start(f32[32,128]{1,0:T(8,128)} %param.14) | copy-start | bytes 49156
  62.0 49.8 %collective-permute-start.4 = (f32[16,32,128]{2,0,1:T(8,128)}, f32[16,32,128]{2,0,1:T(8,128)S(1)}, u32[]{:S(2)}, u32[]{:S(2)}) collective-permute-start(f32[16,32,128]{2,0,1:T(8,128)} %get-tuple-element.18), channel_id=1, source_target_pairs={{8,0},{12,4},{16,8},{20,12},{24,16},{28,20},{0,24},{4,28},{9,1},{1... | collective-permute-start | bytes 786440 | tf_op jit(solution)/shard_map/ppermute | solution.py:22
  62.0 49.8 %collective-permute-start.7 = (f32[16,32,128]{2,0,1:T(8,128)}, f32[16,32,128]{2,0,1:T(8,128)S(1)}, u32[]{:S(2)}, u32[]{:S(2)}) collective-permute-start(f32[16,32,128]{2,0,1:T(8,128)} %get-tuple-element.19), channel_id=1, source_target_pairs={{24,0},{28,4},{0,8},{4,12},{8,16},{12,20},{16,24},{20,28},{25,1},{... | collective-permute-start | bytes 786440 | tf_op jit(solution)/shard_map/ppermute | solution.py:22
  64.0 47.7 %collective-permute-start.6 = (f32[16,32,128]{2,0,1:T(8,128)S(1)}, f32[16,32,128]{2,0,1:T(8,128)S(1)}, u32[]{:S(2)}, u32[]{:S(2)}) collective-permute-start(f32[16,32,128]{2,0,1:T(8,128)S(1)} %get-tuple-element.20), channel_id=1, source_target_pairs={{28,0},{0,4},{4,8},{8,12},{12,16},{16,20},{20,24},{24,28},{29,1},{... | collective-permute-start | bytes 786440 | tf_op jit(solution)/shard_map/ppermute | solution.py:22
  65.5 46.3 %collective-permute-start.5 = (f32[16,32,128]{2,0,1:T(8,128)S(1)}, f32[16,32,128]{2,0,1:T(8,128)S(1)}, u32[]{:S(2)}, u32[]{:S(2)}) collective-permute-start(f32[16,32,128]{2,0,1:T(8,128)S(1)} %get-tuple-element.21), channel_id=1, source_target_pairs={{4,0},{8,4},{12,8},{16,12},{20,16},{24,20},{28,24},{0,28},{5,1},{9... | collective-permute-start | bytes 786440 | tf_op jit(solution)/shard_map/ppermute | solution.py:22
where the time goes:
time: 113 us
  blocking collectives  60.6 us (54%)
  matrix products  27.5 us (24%)
  starting transfers between devices  16.6 us (15%)
  other arithmetic  3.56 us (3%)
  local copies, waits for them, and re-layouts  2.92 us (3%)
  between operations  1.42 us (1%)
    psum x1, blocking collectives, per_device(): grad = lax.psum(grad_local, 'node') * (1.0 / math.sqrt(node_total))  40.8 us
    ppermute x8, starting transfers between devices, passed_along(): return lax.ppermute(block, axis, route)  16.6 us
    all_gather x1, blocking collectives, per_device(): slope_all = lax.all_gather(slope_grad, 'feat', axis=1, tiled=True)  7.46 us
    all_gather x1, blocking collectives, per_device(): lax.all_gather(aggregate, 'feat', axis=1, tiled=True)  7.25 us
    dot_general x1, matrix products, per_device(): jnp.einsum('tfk,tjk->tfj', sources, tile_values, preferred_element_type=j...  7.25 us
    dot_general x1, matrix products, per_device(): jnp.einsum('tfj,tjk->tfk', back_sources, tile_values, preferred_element_t...  7.21 us
    all_gather x1, blocking collectives, per_device(): lax.all_gather(weight_half, 'feat', axis=0, tiled=True)  5.18 us
    dot_general x1, matrix products, per_device(): jnp.einsum('ts,tfk->sfk', add_source, back_terms, precision=lax.Precision...  4.89 us
  transfers between devices with their start and end apart: 8, of which 0 were waited for; matrix products, arithmetic and copies ran while one was open for 5% of the time, Pallas kernels for 0%

commit v1 on v0

--- a/solution.py
+++ b/solution.py
@@ -20,6 +20,30 @@
     devices = range(lax.axis_size(axis))
     route = [((i - distance) % len(devices), i) for i in devices]
     return lax.ppermute(block, axis, route)
+
+
+def gathered_along(block, axis, dim):
+    size = lax.axis_size(axis)
+    own = lax.axis_index(axis)
+    width = block.shape[dim]
+    shape = list(block.shape)
+    shape[dim] = size * width
+    whole = jnp.zeros(shape, block.dtype)
+    for step in range(size):
+        piece = block if step == 0 else passed_along(block, axis, -step)
+        whole = lax.dynamic_update_slice_in_dim(whole, piece, ((own + step) % size) * width, dim)
+    return whole
+
+
+def summed_over(block, axis):
+    size = lax.axis_size(axis)
+    if size & (size - 1):
+        return lax.psum(block, axis)
+    mask = 1
+    while mask < size:
+        block = block + lax.ppermute(block, axis, [(i, i ^ mask) for i in range(size)])
+        mask *= 2
+    return block
 
 
 def elu_slope(preact):
@@ -75,21 +99,19 @@
     aggregate = jnp.einsum("tb,tfj->bfj", add_row, forward_terms, precision=lax.Precision.HIGHEST)
     aggregate = aggregate.astype(jnp.bfloat16)
     weight_half = weight.astype(jnp.bfloat16)
-    aggregate_all, weight_all = (
-        lax.all_gather(aggregate, "feat", axis=1, tiled=True),
-        lax.all_gather(weight_half, "feat", axis=0, tiled=True),
+    aggregate_all = gathered_along(aggregate, "feat", 1)
+    weight_all = gathered_along(weight_half, "feat", 0)
+    cotangent_all = gathered_along(cotangent, "feat", 1)
+    column_start = lax.axis_index("feat") * width_local
+    preact = jnp.einsum(
+        "bij,io->boj", aggregate_all, weight_all, preferred_element_type=jnp.float32
     )
-    column_start = lax.axis_index("feat") * width_local
-    weight_cols = lax.dynamic_slice_in_dim(weight_all, column_start, width_local, 1)
-    preact = jnp.einsum(
-        "bij,io->boj", aggregate_all, weight_cols, preferred_element_type=jnp.float32
-    )
-    activated = jax.nn.elu(preact).astype(jnp.bfloat16)
-    slope_grad = (cotangent.astype(jnp.float32) * elu_slope(preact)).astype(jnp.bfloat16)
-    slope_all = lax.all_gather(slope_grad, "feat", axis=1, tiled=True)
+    activated = lax.dynamic_slice_in_dim(jax.nn.elu(preact), column_start, width_local, 1)
+    activated = activated.astype(jnp.bfloat16)
+    slope_all = (cotangent_all.astype(jnp.float32) * elu_slope(preact)).astype(jnp.bfloat16)
     node_total = cycle_size * blocks * tile_size
     grad_local = jnp.einsum("bij,boj->io", aggregate, slope_all, preferred_element_type=jnp.float32)
-    grad = lax.psum(grad_local, "node") * (1.0 / math.sqrt(node_total))
+    grad = summed_over(grad_local, "node") * (1.0 / math.sqrt(node_total))
     back_rows = jnp.einsum(
         "io,boj->bij", weight_half, slope_all, preferred_element_type=jnp.float32
     ).astype(jnp.bfloat16)

time: 113 us -> 86.6 us (0.77)
  blocking collectives: 60.6 us -> 0 us
  waiting for transfers between devices: 0.02 us -> 24.8 us
  starting transfers between devices: 16.6 us -> 24.5 us
  local copies, waits for them, and re-layouts: 2.92 us -> 5.39 us
    psum x1 -> x0, blocking collectives: 40.8 us -> none  [per_device(): grad = lax.psum(grad_local, 'node') * (1.0 / math.sqrt(node_total))]
    all_gather x3 -> x0, blocking collectives: 19.9 us -> none  [the longest x1 7.46 us: per_device(): slope_all = lax.all_gather(slope_grad, 'feat', axis=1, tiled=True)]
    ppermute x0 -> x3, waiting for transfers between devices: none -> 12.7 us  [summed_over(): lax.ppermute(block, axis, [(i, i ^ mask) for i in range(size)])]
    ppermute x8 -> x17, waiting for transfers between devices: 0.02 us -> 12.1 us  [passed_along(): return lax.ppermute(block, axis, route)]
    ppermute x8 -> x17, starting transfers between devices: 16.6 us -> 22.5 us  [passed_along(): return lax.ppermute(block, axis, route)]
    dynamic_update_slice x0 -> x12, local copies, waits for them, and re-layouts: none -> 2.59 us  [gathered_along(): lax.dynamic_update_slice_in_dim(whole, piece, (own + step) % size * width...]
    ppermute x0 -> x3, starting transfers between devices: none -> 2 us  [summed_over(): lax.ppermute(block, axis, [(i, i ^ mask) for i in range(size)])]
  transfers between devices with their start and end apart: 8 -> 20, of which waited for: 0 -> 5; matrix products, arithmetic and copies ran while one was open for 5% -> 37% of each run, Pallas kernels for 0% -> 0%
where the time goes in v1:
time: 86.6 us; the launch traced here: 86.4 us
  matrix products  26.4 us (30%)
  waiting for transfers between devices  24.8 us (29%)
  starting transfers between devices  24.5 us (28%)
  local copies, waits for them, and re-layouts  5.39 us (6%)
  other arithmetic  3.62 us (4%)
  between operations  1.65 us (2%)
    ppermute x17, starting transfers between devices, passed_along(): return lax.ppermute(block, axis, route)  22.5 us
    ppermute x3, waiting for transfers between devices, summed_over(): lax.ppermute(block, axis, [(i, i ^ mask) for i in range(size)])  12.7 us
    ppermute x17, waiting for transfers between devices, passed_along(): return lax.ppermute(block, axis, route)  12.1 us
    dot_general x1, matrix products, per_device(): jnp.einsum('tfk,tjk->tfj', sources, tile_values, preferred_element_type=j...  7.25 us
    dot_general x1, matrix products, per_device(): jnp.einsum('tfj,tjk->tfk', back_sources, tile_values, preferred_element_t...  7.21 us
    dot_general x1, matrix products, per_device(): jnp.einsum('ts,tfk->sfk', add_source, back_terms, precision=lax.Precision...  4.9 us
    dot_general x1, matrix products, per_device(): jnp.einsum('tb,tfj->bfj', add_row, forward_terms, precision=lax.Precision...  4.36 us
    dynamic_update_slice x12, local copies, waits for them, and re-layouts, gathered_along(): lax.dynamic_update_slice_in_dim(whole, piece, (own + step) % size * width...  2.59 us
  transfers between devices with their start and end apart: 20, of which 5 were waited for; matrix products, arithmetic and copies ran while one was open for 37% of the time, Pallas kernels for 0%

profile of v1, /device:TPU:0, one launch (start us, length us, event | category | flops | bytes accessed | tf_op | source)
XLA Modules:
  0.0 86.4 jit_solution(513082964107178995)
XLA Ops:
  0.6 0.7 convert_element_type.38
  1.4 0.5 collective-permute-start.2
  1.8 2.5 %collective-permute-start.1 = (bf16[32,128]{1,0:T(8,128)(2,1)S(1)}, bf16[32,128]{1,0:T(8,128)(2,1)S(1)}, u32[]{:S(2)}, u32[]{:S(2)}) collective-permute-start(bf16[32,128]{1,0:T(8,128)(2,1)S(1)} %convert_element_type.38), channel_id=1, source_target_pairs={{2,0},{3,1},{0,2},{1,3},{6,4},{7,5},{4,6},{5,7},{10,8},{11,9},{8,1... | collective-permute-start | bytes 24584 | tf_op jit(solution)/shard_map/ppermute | solution.py:22
  4.4 1.4 %collective-permute-start = (bf16[32,128]{1,0:T(8,128)(2,1)S(1)}, bf16[32,128]{1,0:T(8,128)(2,1)S(1)}, u32[]{:S(2)}, u32[]{:S(2)}) collective-permute-start(bf16[32,128]{1,0:T(8,128)(2,1)S(1)} %convert_element_type.38), channel_id=1, source_target_pairs={{1,0},{2,1},{3,2},{0,3},{5,4},{6,5},{7,6},{4,7},{9,8},{10,9},{11,1... | collective-permute-start | bytes 24584 | tf_op jit(solution)/shard_map/ppermute | solution.py:22
  5.8 1.5 %collective-permute-start.4 = (bf16[16,32,128]{2,1,0:T(8,128)(2,1)}, bf16[16,32,128]{2,1,0:T(8,128)(2,1)S(1)}, u32[]{:S(2)}, u32[]{:S(2)}) collective-permute-start(bf16[16,32,128]{2,1,0:T(8,128)(2,1)} %param.9), channel_id=1, source_target_pairs={{28,0},{0,4},{4,8},{8,12},{12,16},{16,20},{20,24},{24,28},{29,1},{... | collective-permute-start | bytes 393224 | tf_op jit(solution)/shard_map/ppermute | solution.py:22
  7.3 1.6 %collective-permute-start.3 = (bf16[16,32,128]{2,1,0:T(8,128)(2,1)}, bf16[16,32,128]{2,1,0:T(8,128)(2,1)S(1)}, u32[]{:S(2)}, u32[]{:S(2)}) collective-permute-start(bf16[16,32,128]{2,1,0:T(8,128)(2,1)} %param.9), channel_id=1, source_target_pairs={{24,0},{28,4},{0,8},{4,12},{8,16},{12,20},{16,24},{20,28},{25,1},{... | collective-permute-start | bytes 393224 | tf_op jit(solution)/shard_map/ppermute | solution.py:22
  8.9 0.7 fusion.35
  9.6 0.7 broadcast_subtract_fusion
  10.2 0.1 broadcast.46.clone.1
  10.3 0.9 %constant_dynamic-update-slice_fusion.8 = bf16[16,128,128]{2,1,0:T(8,128)(2,1)S(1)} fusion(bf16[16,128,128]{2,1,0:T(8,128)(2,1)S(1)} %broadcast.46.clone.1, bf16[16,32,128]{2,1,0:T(8,128)(2,1)} %param.17, s32[]{:T(128)S(6)} %select_n.90), kind=kLoop, calls=%fused_computation.58 | loop fusion | bytes 262148 | tf_op jit(solution)/shard_map/dynamic_update_slice | solution.py:34
  12.0 0.1 copy.14
  12.1 0.2 dynamic_update_slice.36
  12.3 0.1 collective-permute-start.10
  12.4 0.1 copy.15
  12.5 0.4 dynamic_update_slice.37
  12.9 0.0 collective-permute-done.1
  12.9 0.5 collective-permute-start.12
  13.5 0.1 copy.16
  13.6 0.4 dynamic_update_slice.38
  14.0 0.0 collective-permute-done.2
  14.0 0.4 collective-permute-start.11
  14.4 0.1 copy.17
  14.5 0.4 dynamic_update_slice.39
  14.9 0.0 collective-permute-done.3
  14.9 3.3 %collective-permute-start.5 = (bf16[16,32,128]{2,1,0:T(8,128)(2,1)}, bf16[16,32,128]{2,1,0:T(8,128)(2,1)S(1)}, u32[]{:S(2)}, u32[]{:S(2)}) collective-permute-start(bf16[16,32,128]{2,1,0:T(8,128)(2,1)} %param.9), channel_id=1, source_target_pairs={{4,0},{8,4},{12,8},{16,12},{20,16},{24,20},{28,24},{0,28},{5,1},{9... | collective-permute-start | bytes 393224 | tf_op jit(solution)/shard_map/ppermute | solution.py:22
  18.2 0.3 collective-permute-start.6
  18.6 0.9 %constant_dynamic-update-slice_fusion.2 = bf16[80,32,128]{2,1,0:T(8,128)(2,1)S(1)} fusion(bf16[80,32,128]{2,1,0:T(8,128)(2,1)S(1)} %constant_dynamic-update-slice_fusion.3, bf16[16,32,128]{2,1,0:T(8,128)(2,1)} %param.9), kind=kLoop, calls=%fused_computation.46 | loop fusion | bytes 262144
  19.5 2.9 %collective-permute-done.5 = bf16[16,32,128]{2,1,0:T(8,128)(2,1)S(1)} collective-permute-done((bf16[16,32,128]{2,1,0:T(8,128)(2,1)}, bf16[16,32,128]{2,1,0:T(8,128)(2,1)S(1)}, u32[]{:S(2)}, u32[]{:S(2)}) %collective-permute-start.5) | collective-permute-done | bytes 131104 | tf_op jit(solution)/shard_map/ppermute | solution.py:22
  22.4 2.8 %collective-permute-done.6 = bf16[16,32,128]{2,1,0:T(8,128)(2,1)S(1)} collective-permute-done((bf16[16,32,128]{2,1,0:T(8,128)(2,1)}, bf16[16,32,128]{2,1,0:T(8,128)(2,1)S(1)}, u32[]{:S(2)}, u32[]{:S(2)}) %collective-permute-start.6) | collective-permute-done | bytes 131104 | tf_op jit(solution)/shard_map/ppermute | solution.py:22
  25.3 0.8 fusion.10
  26.0 7.2 %fusion.4 = f32[256,32,128]{2,1,0:T(8,128)S(1)} fusion(bf16[256,128,128]{2,1,0:T(8,128)(2,1)} %param.10, bf16[256,32,128]{2,0,1:T(8,128)(2,1)S(1)} %fusion.10), kind=kOutput, calls=%fused_computation.6 | convolution fusion | flops 268435456 | bytes 14680064 | tf_op jit(solution)/shard_map/tfk,tjk->tfj/dot_general | solution.py:96
  33.3 4.4 %fusion.7 = bf16[16,32,128]{2,0,1:T(8,128)(2,1)S(1)} fusion(f32[256,32,128]{2,1,0:T(8,128)S(1)} %fusion.4, f32[256]{0:T(256)S(1)} %compare_convert_fusion, s32[256]{0:T(256)S(1)} %broadcast_subtract_fusion), kind=kOutput, calls=%fused_computation.11 | convolution fusion | flops 201400320 | bytes 4327424 | tf_op jit(solution)/shard_map/tb,tfj->bfj/dot_general | solution.py:99
  37.6 0.0 collective-permute-start.9
  37.7 1.0 %collective-permute-start.8 = (bf16[16,32,128]{2,0,1:T(8,128)(2,1)S(1)}, bf16[16,32,128]{2,0,1:T(8,128)(2,1)S(1)}, u32[]{:S(2)}, u32[]{:S(2)}) collective-permute-start(bf16[16,32,128]{2,0,1:T(8,128)(2,1)S(1)} %fusion.7), channel_id=1, source_target_pairs={{2,0},{3,1},{0,2},{1,3},{6,4},{7,5},{4,6},{5,7},{10,8},{11,9},{8,1... | collective-permute-start | bytes 393224 | tf_op jit(solution)/shard_map/ppermute | solution.py:22
  38.7 0.1 broadcast.46.clone
  38.8 0.1 copy_dynamic-update-slice_fusion.3
  38.9 1.6 %collective-permute-start.7 = (bf16[16,32,128]{2,0,1:T(8,128)(2,1)S(1)}, bf16[16,32,128]{2,0,1:T(8,128)(2,1)S(1)}, u32[]{:S(2)}, u32[]{:S(2)}) collective-permute-start(bf16[16,32,128]{2,0,1:T(8,128)(2,1)S(1)} %fusion.7), channel_id=1, source_target_pairs={{1,0},{2,1},{3,2},{0,3},{5,4},{6,5},{7,6},{4,7},{9,8},{10,9},{11,1... | collective-permute-start | bytes 393224 | tf_op jit(solution)/shard_map/ppermute | solution.py:22
  40.5 0.0 collective-permute-done.11
  40.6 4.1 %collective-permute-done.7 = bf16[16,32,128]{2,0,1:T(8,128)(2,1)S(1)} collective-permute-done((bf16[16,32,128]{2,0,1:T(8,128)(2,1)S(1)}, bf16[16,32,128]{2,0,1:T(8,128)(2,1)S(1)}, u32[]{:S(2)}, u32[]{:S(2)}) %collective-permute-start.7) | collective-permute-done | bytes 131104 | tf_op jit(solution)/shard_map/ppermute | solution.py:22
  44.8 0.1 copy_dynamic-update-slice_fusion.1
  44.8 0.0 collective-permute-done.9
  44.9 0.1 copy_dynamic-update-slice_fusion
  44.9 0.3 broadcast_compare_fusion
  45.2 0.4 convolution_bitcast_fusion.1
  45.6 0.5 fusion.6
  46.1 0.2 copy.27
  46.4 0.1 collective-permute-start.17
  46.5 0.7 fusion.28
  47.2 7.2 %fusion.5 = f32[256,32,128]{2,1,0:T(8,128)S(1)} fusion(bf16[256,128,128]{2,1,0:T(8,128)(2,1)} %param.10, bf16[256,32,128]{2,0,1:T(8,128)(2,1)S(1)} %fusion.28), kind=kOutput, calls=%fused_computation.7 | convolution fusion | flops 268435456 | bytes 14680064 | tf_op jit(solution)/shard_map/tfj,tjk->tfk/dot_general | solution.py:121
  54.4 0.0 copy-start.1
  54.4 0.0 copy-start.2
  54.4 4.9 %fusion = f32[80,32,128]{2,0,1:T(8,128)S(1)} fusion(f32[256,32,128]{2,1,0:T(8,128)S(1)} %fusion.5, f32[256]{0:T(256)S(1)} %compare_convert_fusion, s32[256]{0:T(256)S(1)} %fusion.35), kind=kOutput, calls=%fused_computation | convolution fusion | flops 1006673920 | bytes 5507072 | tf_op jit(solution)/shard_map/ts,tfk->sfk/dot_general | solution.py:124
  59.4 1.6 %collective-permute-start.18 = (f32[32,128]{1,0:T(8,128)S(1)}, f32[32,128]{1,0:T(8,128)S(1)}, u32[]{:S(2)}, u32[]{:S(2)}) collective-permute-start(f32[32,128]{1,0:T(8,128)S(1)} %add.134), channel_id=1, source_target_pairs={{0,8},{4,12},{8,0},{12,4},{16,24},{20,28},{24,16},{28,20},{1,9},{5... | collective-permute-start | bytes 49160 | tf_op jit(solution)/shard_map/ppermute | solution.py:44
  61.0 0.1 fusion.41
  61.1 2.5 %collective-permute-start.13 = (f32[16,32,128]{2,0,1:T(8,128)S(1)}, f32[16,32,128]{2,0,1:T(8,128)S(1)}, u32[]{:S(2)}, u32[]{:S(2)}) collective-permute-start(f32[16,32,128]{2,0,1:T(8,128)S(1)} %get-tuple-element.13), channel_id=1, source_target_pairs={{8,0},{12,4},{16,8},{20,12},{24,16},{28,20},{0,24},{4,28},{9,1},{1... | collective-permute-start | bytes 786440 | tf_op jit(solution)/shard_map/ppermute | solution.py:22
  63.7 2.0 %collective-permute-start.15 = (f32[16,32,128]{2,0,1:T(8,128)S(1)}, f32[16,32,128]{2,0,1:T(8,128)S(1)}, u32[]{:S(2)}, u32[]{:S(2)}) collective-permute-start(f32[16,32,128]{2,0,1:T(8,128)S(1)} %get-tuple-element.15), channel_id=1, source_target_pairs={{28,0},{0,4},{4,8},{8,12},{12,16},{16,20},{20,24},{24,28},{29,1},{... | collective-permute-start | bytes 786440 | tf_op jit(solution)/shard_map/ppermute | solution.py:22
  65.7 3.3 %collective-permute-start.14 = (f32[16,32,128]{2,0,1:T(8,128)S(1)}, f32[16,32,128]{2,0,1:T(8,128)S(1)}, u32[]{:S(2)}, u32[]{:S(2)}) collective-permute-start(f32[16,32,128]{2,0,1:T(8,128)S(1)} %get-tuple-element.16), channel_id=1, source_target_pairs={{4,0},{8,4},{12,8},{16,12},{20,16},{24,20},{28,24},{0,28},{5,1},{9... | collective-permute-start | bytes 786440 | tf_op jit(solution)/shard_map/ppermute | solution.py:22
  68.9 0.3 collective-permute-start.19
  69.2 0.8 select_convert_fusion
  70.0 12.7 %collective-permute-done.19 = f32[32,128]{1,0:T(8,128)S(1)} collective-permute-done((f32[32,128]{1,0:T(8,128)S(1)}, f32[32,128]{1,0:T(8,128)S(1)}, u32[]{:S(2)}, u32[]{:S(2)}) %collective-permute-start.19) | collective-permute-done | bytes 16416 | tf_op jit(solution)/shard_map/ppermute | solution.py:44
  82.7 0.6 divide_subtract_fusion
  83.3 2.2 %collective-permute-done.15 = f32[16,32,128]{2,0,1:T(8,128)S(1)} collective-permute-done((f32[16,32,128]{2,0,1:T(8,128)S(1)}, f32[16,32,128]{2,0,1:T(8,128)S(1)}, u32[]{:S(2)}, u32[]{:S(2)}) %collective-permute-start.15) | collective-permute-done | bytes 262176 | tf_op jit(solution)/shard_map/ppermute | solution.py:22
  85.5 0.1 fusion.14
  85.6 0.8 copy.23
  (27 shorter events, 0.2 us)
Async XLA Ops:
  1.4 12.7 %collective-permute-start.2 = (bf16[32,128]{1,0:T(8,128)(2,1)S(1)}, bf16[32,128]{1,0:T(8,128)(2,1)S(1)}, u32[]{:S(2)}, u32[]{:S(2)}) collective-permute-start(bf16[32,128]{1,0:T(8,128)(2,1)S(1)} %convert_element_type.38), channel_id=1, source_target_pairs={{3,0},{0,1},{1,2},{2,3},{7,4},{4,5},{5,6},{6,7},{11,8},{8,9},{9,10... | collective-permute-start | bytes 24584 | tf_op jit(solution)/shard_map/ppermute | solution.py:22
  1.8 11.1 %collective-permute-start.1 = (bf16[32,128]{1,0:T(8,128)(2,1)S(1)}, bf16[32,128]{1,0:T(8,128)(2,1)S(1)}, u32[]{:S(2)}, u32[]{:S(2)}) collective-permute-start(bf16[32,128]{1,0:T(8,128)(2,1)S(1)} %convert_element_type.38), channel_id=1, source_target_pairs={{2,0},{3,1},{0,2},{1,3},{6,4},{7,5},{4,6},{5,7},{10,8},{11,9},{8,1... | collective-permute-start | bytes 24584 | tf_op jit(solution)/shard_map/ppermute | solution.py:22
  4.4 8.0 %collective-permute-start = (bf16[32,128]{1,0:T(8,128)(2,1)S(1)}, bf16[32,128]{1,0:T(8,128)(2,1)S(1)}, u32[]{:S(2)}, u32[]{:S(2)}) collective-permute-start(bf16[32,128]{1,0:T(8,128)(2,1)S(1)} %convert_element_type.38), channel_id=1, source_target_pairs={{1,0},{2,1},{3,2},{0,3},{5,4},{6,5},{7,6},{4,7},{9,8},{10,9},{11,1... | collective-permute-start | bytes 24584 | tf_op jit(solution)/shard_map/ppermute | solution.py:22
  5.8 12.4 %collective-permute-start.4 = (bf16[16,32,128]{2,1,0:T(8,128)(2,1)}, bf16[16,32,128]{2,1,0:T(8,128)(2,1)S(1)}, u32[]{:S(2)}, u32[]{:S(2)}) collective-permute-start(bf16[16,32,128]{2,1,0:T(8,128)(2,1)} %param.9), channel_id=1, source_target_pairs={{28,0},{0,4},{4,8},{8,12},{12,16},{16,20},{20,24},{24,28},{29,1},{... | collective-permute-start | bytes 393224 | tf_op jit(solution)/shard_map/ppermute | solution.py:22
  7.3 7.6 %collective-permute-start.3 = (bf16[16,32,128]{2,1,0:T(8,128)(2,1)}, bf16[16,32,128]{2,1,0:T(8,128)(2,1)S(1)}, u32[]{:S(2)}, u32[]{:S(2)}) collective-permute-start(bf16[16,32,128]{2,1,0:T(8,128)(2,1)} %param.9), channel_id=1, source_target_pairs={{24,0},{28,4},{0,8},{4,12},{8,16},{12,20},{16,24},{20,28},{25,1},{... | collective-permute-start | bytes 393224 | tf_op jit(solution)/shard_map/ppermute | solution.py:22
  12.3 26.5 %collective-permute-start.10 = (bf16[16,32,128]{2,1,0:T(8,128)(2,1)}, bf16[16,32,128]{2,1,0:T(8,128)(2,1)S(1)}, u32[]{:S(2)}, u32[]{:S(2)}) collective-permute-start(bf16[16,32,128]{2,1,0:T(8,128)(2,1)} %param.17), channel_id=1, source_target_pairs={{1,0},{2,1},{3,2},{0,3},{5,4},{6,5},{7,6},{4,7},{9,8},{10,9},{11,1... | collective-permute-start | bytes 393224 | tf_op jit(solution)/shard_map/ppermute | solution.py:22
  12.9 27.6 %collective-permute-start.12 = (bf16[16,32,128]{2,1,0:T(8,128)(2,1)}, bf16[16,32,128]{2,1,0:T(8,128)(2,1)S(1)}, u32[]{:S(2)}, u32[]{:S(2)}) collective-permute-start(bf16[16,32,128]{2,1,0:T(8,128)(2,1)} %param.17), channel_id=1, source_target_pairs={{3,0},{0,1},{1,2},{2,3},{7,4},{4,5},{5,6},{6,7},{11,8},{8,9},{9,10... | collective-permute-start | bytes 393224 | tf_op jit(solution)/shard_map/ppermute | solution.py:22
  14.0 26.5 %collective-permute-start.11 = (bf16[16,32,128]{2,1,0:T(8,128)(2,1)}, bf16[16,32,128]{2,1,0:T(8,128)(2,1)S(1)}, u32[]{:S(2)}, u32[]{:S(2)}) collective-permute-start(bf16[16,32,128]{2,1,0:T(8,128)(2,1)} %param.17), channel_id=1, source_target_pairs={{2,0},{3,1},{0,2},{1,3},{6,4},{7,5},{4,6},{5,7},{10,8},{11,9},{8,1... | collective-permute-start | bytes 393224 | tf_op jit(solution)/shard_map/ppermute | solution.py:22
  14.9 7.5 %collective-permute-start.5 = (bf16[16,32,128]{2,1,0:T(8,128)(2,1)}, bf16[16,32,128]{2,1,0:T(8,128)(2,1)S(1)}, u32[]{:S(2)}, u32[]{:S(2)}) collective-permute-start(bf16[16,32,128]{2,1,0:T(8,128)(2,1)} %param.9), channel_id=1, source_target_pairs={{4,0},{8,4},{12,8},{16,12},{20,16},{24,20},{28,24},{0,28},{5,1},{9... | collective-permute-start | bytes 393224 | tf_op jit(solution)/shard_map/ppermute | solution.py:22
  18.2 7.0 %collective-permute-start.6 = (bf16[16,32,128]{2,1,0:T(8,128)(2,1)}, bf16[16,32,128]{2,1,0:T(8,128)(2,1)S(1)}, u32[]{:S(2)}, u32[]{:S(2)}) collective-permute-start(bf16[16,32,128]{2,1,0:T(8,128)(2,1)} %param.9), channel_id=1, source_target_pairs={{8,0},{12,4},{16,8},{20,12},{24,16},{28,20},{0,24},{4,28},{9,1},{1... | collective-permute-start | bytes 393224 | tf_op jit(solution)/shard_map/ppermute | solution.py:22
  37.6 7.2 %collective-permute-start.9 = (bf16[16,32,128]{2,0,1:T(8,128)(2,1)S(1)}, bf16[16,32,128]{2,0,1:T(8,128)(2,1)S(1)}, u32[]{:S(2)}, u32[]{:S(2)}) collective-permute-start(bf16[16,32,128]{2,0,1:T(8,128)(2,1)S(1)} %fusion.7), channel_id=1, source_target_pairs={{3,0},{0,1},{1,2},{2,3},{7,4},{4,5},{5,6},{6,7},{11,8},{8,9},{9,10... | collective-permute-start | bytes 393224 | tf_op jit(solution)/shard_map/ppermute | solution.py:22
  37.7 7.1 %collective-permute-start.8 = (bf16[16,32,128]{2,0,1:T(8,128)(2,1)S(1)}, bf16[16,32,128]{2,0,1:T(8,128)(2,1)S(1)}, u32[]{:S(2)}, u32[]{:S(2)}) collective-permute-start(bf16[16,32,128]{2,0,1:T(8,128)(2,1)S(1)} %fusion.7), channel_id=1, source_target_pairs={{2,0},{3,1},{0,2},{1,3},{6,4},{7,5},{4,6},{5,7},{10,8},{11,9},{8,1... | collective-permute-start | bytes 393224 | tf_op jit(solution)/shard_map/ppermute | solution.py:22
  38.9 5.9 %collective-permute-start.7 = (bf16[16,32,128]{2,0,1:T(8,128)(2,1)S(1)}, bf16[16,32,128]{2,0,1:T(8,128)(2,1)S(1)}, u32[]{:S(2)}, u32[]{:S(2)}) collective-permute-start(bf16[16,32,128]{2,0,1:T(8,128)(2,1)S(1)} %fusion.7), channel_id=1, source_target_pairs={{1,0},{2,1},{3,2},{0,3},{5,4},{6,5},{7,6},{4,7},{9,8},{10,9},{11,1... | collective-permute-start | bytes 393224 | tf_op jit(solution)/shard_map/ppermute | solution.py:22
  46.4 13.0 %collective-permute-start.17 = (f32[32,128]{1,0:T(8,128)S(1)}, f32[32,128]{1,0:T(8,128)S(1)}, u32[]{:S(2)}, u32[]{:S(2)}) collective-permute-start(f32[32,128]{1,0:T(8,128)S(1)} %convolution_bitcast_fusion.1), channel_id=1, source_target_pairs={{0,4},{4,0},{8,12},{12,8},{16,20},{20,16},{24,28},{28,24},{1,5},{5... | collective-permute-start | bytes 49160 | tf_op jit(solution)/shard_map/ppermute | solution.py:44
  54.4 28.3 %copy-start = (f32[32,128]{1,0:T(8,128)S(1)}, f32[32,128]{1,0:T(8,128)}, u32[]{:S(2)}) copy-start(f32[32,128]{1,0:T(8,128)} %param.14) | copy-start | bytes 49156
  54.4 28.3 %copy-start.1 = (f32[32,128]{1,0:T(8,128)S(1)}, f32[32,128]{1,0:T(8,128)}, u32[]{:S(2)}) copy-start(f32[32,128]{1,0:T(8,128)} %param.15) | copy-start | bytes 49156
  54.4 28.2 %copy-start.2 = (f32[32,128]{1,0:T(8,128)S(1)}, f32[32,128]{1,0:T(8,128)}, u32[]{:S(2)}) copy-start(f32[32,128]{1,0:T(8,128)} %param.16) | copy-start | bytes 49156
  59.4 9.6 %collective-permute-start.18 = (f32[32,128]{1,0:T(8,128)S(1)}, f32[32,128]{1,0:T(8,128)S(1)}, u32[]{:S(2)}, u32[]{:S(2)}) collective-permute-start(f32[32,128]{1,0:T(8,128)S(1)} %add.134), channel_id=1, source_target_pairs={{0,8},{4,12},{8,0},{12,4},{16,24},{20,28},{24,16},{28,20},{1,9},{5... | collective-permute-start | bytes 49160 | tf_op jit(solution)/shard_map/ppermute | solution.py:44
  61.1 22.2 %collective-permute-start.13 = (f32[16,32,128]{2,0,1:T(8,128)S(1)}, f32[16,32,128]{2,0,1:T(8,128)S(1)}, u32[]{:S(2)}, u32[]{:S(2)}) collective-permute-start(f32[16,32,128]{2,0,1:T(8,128)S(1)} %get-tuple-element.13), channel_id=1, source_target_pairs={{8,0},{12,4},{16,8},{20,12},{24,16},{28,20},{0,24},{4,28},{9,1},{1... | collective-permute-start | bytes 786440 | tf_op jit(solution)/shard_map/ppermute | solution.py:22
  63.7 19.7 %collective-permute-start.16 = (f32[16,32,128]{2,0,1:T(8,128)S(1)}, f32[16,32,128]{2,0,1:T(8,128)S(1)}, u32[]{:S(2)}, u32[]{:S(2)}) collective-permute-start(f32[16,32,128]{2,0,1:T(8,128)S(1)} %get-tuple-element.14), channel_id=1, source_target_pairs={{24,0},{28,4},{0,8},{4,12},{8,16},{12,20},{16,24},{20,28},{25,1},{... | collective-permute-start | bytes 786440 | tf_op jit(solution)/shard_map/ppermute | solution.py:22
  63.7 21.8 %collective-permute-start.15 = (f32[16,32,128]{2,0,1:T(8,128)S(1)}, f32[16,32,128]{2,0,1:T(8,128)S(1)}, u32[]{:S(2)}, u32[]{:S(2)}) collective-permute-start(f32[16,32,128]{2,0,1:T(8,128)S(1)} %get-tuple-element.15), channel_id=1, source_target_pairs={{28,0},{0,4},{4,8},{8,12},{12,16},{16,20},{20,24},{24,28},{29,1},{... | collective-permute-start | bytes 786440 | tf_op jit(solution)/shard_map/ppermute | solution.py:22
  65.7 19.8 %collective-permute-start.14 = (f32[16,32,128]{2,0,1:T(8,128)S(1)}, f32[16,32,128]{2,0,1:T(8,128)S(1)}, u32[]{:S(2)}, u32[]{:S(2)}) collective-permute-start(f32[16,32,128]{2,0,1:T(8,128)S(1)} %get-tuple-element.16), channel_id=1, source_target_pairs={{4,0},{8,4},{12,8},{16,12},{20,16},{24,20},{28,24},{0,28},{5,1},{9... | collective-permute-start | bytes 786440 | tf_op jit(solution)/shard_map/ppermute | solution.py:22
  68.9 13.7 %collective-permute-start.19 = (f32[32,128]{1,0:T(8,128)S(1)}, f32[32,128]{1,0:T(8,128)S(1)}, u32[]{:S(2)}, u32[]{:S(2)}) collective-permute-start(f32[32,128]{1,0:T(8,128)S(1)} %add.135), channel_id=1, source_target_pairs={{0,16},{4,20},{8,24},{12,28},{16,0},{20,4},{24,8},{28,12},{1,17},{... | collective-permute-start | bytes 49160 | tf_op jit(solution)/shard_map/ppermute | solution.py:44

commit v2 on v1

--- a/solution.py
+++ b/solution.py
@@ -99,9 +99,11 @@
     aggregate = jnp.einsum("tb,tfj->bfj", add_row, forward_terms, precision=lax.Precision.HIGHEST)
     aggregate = aggregate.astype(jnp.bfloat16)
     weight_half = weight.astype(jnp.bfloat16)
-    aggregate_all = gathered_along(aggregate, "feat", 1)
-    weight_all = gathered_along(weight_half, "feat", 0)
-    cotangent_all = gathered_along(cotangent, "feat", 1)
+    packed = jnp.concatenate([aggregate, cotangent, weight_half[None]], axis=0)
+    packed_all = gathered_along(packed, "feat", 1)
+    aggregate_all = packed_all[:blocks]
+    cotangent_all = packed_all[blocks : 2 * blocks]
+    weight_all = packed_all[2 * blocks]
     column_start = lax.axis_index("feat") * width_local
     preact = jnp.einsum(
         "bij,io->boj", aggregate_all, weight_all, preferred_element_type=jnp.float32
@@ -123,6 +125,7 @@
     )
     outgoing = jnp.einsum("ts,tfk->sfk", add_source, back_terms, precision=lax.Precision.HIGHEST)
     outgoing = outgoing.reshape(2 * REACH + 1, blocks, width_local, tile_size)
+    outgoing, grad = lax.optimization_barrier((outgoing, grad))
     feature_grad = outgoing[REACH]
     for distance in range(-REACH, REACH + 1):
         if distance != 0:

time: 86.6 us -> 85.5 us (0.987)
  waiting for transfers between devices: 24.8 us -> 27.3 us
  starting transfers between devices: 24.5 us -> 22.2 us
  local copies, waits for them, and re-layouts: 5.39 us -> 3.31 us
  other arithmetic: 3.62 us -> 4.67 us
    ppermute x17 -> x11, waiting for transfers between devices: 12.1 us -> 25.6 us  [passed_along(): return lax.ppermute(block, axis, route)]
    ppermute x3, waiting for transfers between devices: 12.7 us -> 1.66 us  [summed_over(): lax.ppermute(block, axis, [(i, i ^ mask) for i in range(size)])]
    ppermute x17 -> x11, starting transfers between devices: 22.5 us -> 16.7 us  [passed_along(): return lax.ppermute(block, axis, route)]
    ppermute x3, starting transfers between devices: 2 us -> 5.46 us  [summed_over(): lax.ppermute(block, axis, [(i, i ^ mask) for i in range(size)])]
    dynamic_update_slice x12 -> x4, local copies, waits for them, and re-layouts: 2.59 us -> 0.27 us  [gathered_along(): lax.dynamic_update_slice_in_dim(whole, piece, (own + step) % size * width...]
  transfers between devices with their start and end apart: 20 -> 14, of which waited for: 5 -> 7; matrix products, arithmetic and copies ran while one was open for 37% -> 22% of each run, Pallas kernels for 0% -> 0%
where the time goes in v2:
time: 85.5 us; the launch traced here: 85.1 us
  waiting for transfers between devices  27.3 us (32%)
  matrix products  26.1 us (31%)
  starting transfers between devices  22.2 us (26%)
  other arithmetic  4.67 us (5%)
  local copies, waits for them, and re-layouts  3.31 us (4%)
  between operations  1.53 us (2%)
    ppermute x11, waiting for transfers between devices, passed_along(): return lax.ppermute(block, axis, route)  25.6 us
    ppermute x11, starting transfers between devices, passed_along(): return lax.ppermute(block, axis, route)  16.7 us
    dot_general x1, matrix products, per_device(): jnp.einsum('tfk,tjk->tfj', sources, tile_values, preferred_element_type=j...  7.25 us
    dot_general x1, matrix products, per_device(): jnp.einsum('tfj,tjk->tfk', back_sources, tile_values, preferred_element_t...  7.19 us
    ppermute x3, starting transfers between devices, summed_over(): lax.ppermute(block, axis, [(i, i ^ mask) for i in range(size)])  5.46 us
    dot_general x1, matrix products, per_device(): jnp.einsum('ts,tfk->sfk', add_source, back_terms, precision=lax.Precision...  4.9 us
    dot_general x1, matrix products, per_device(): jnp.einsum('tb,tfj->bfj', add_row, forward_terms, precision=lax.Precision...  4.36 us
    unnamed x11, local copies, waits for them, and re-layouts  2.03 us
  transfers between devices with their start and end apart: 14, of which 7 were waited for; matrix products, arithmetic and copies ran while one was open for 22% of the time, Pallas kernels for 0%

profile of v2, /device:TPU:0, one launch (start us, length us, event | category | flops | bytes accessed | tf_op | source)
XLA Modules:
  0.0 85.1 jit_solution(299173077940368967)
XLA Ops:
  0.6 3.1 %collective-permute-start = (bf16[16,32,128]{2,1,0:T(8,128)(2,1)}, bf16[16,32,128]{2,1,0:T(8,128)(2,1)S(1)}, u32[]{:S(2)}, u32[]{:S(2)}) collective-permute-start(bf16[16,32,128]{2,1,0:T(8,128)(2,1)} %param.9), channel_id=1, source_target_pairs={{24,0},{28,4},{0,8},{4,12},{8,16},{12,20},{16,24},{20,28},{25,1},{... | collective-permute-start | bytes 393224 | tf_op jit(solution)/shard_map/ppermute | solution.py:22
  3.7 1.5 %collective-permute-start.1 = (bf16[16,32,128]{2,1,0:T(8,128)(2,1)}, bf16[16,32,128]{2,1,0:T(8,128)(2,1)S(1)}, u32[]{:S(2)}, u32[]{:S(2)}) collective-permute-start(bf16[16,32,128]{2,1,0:T(8,128)(2,1)} %param.9), channel_id=1, source_target_pairs={{28,0},{0,4},{4,8},{8,12},{12,16},{16,20},{20,24},{24,28},{29,1},{... | collective-permute-start | bytes 393224 | tf_op jit(solution)/shard_map/ppermute | solution.py:22
  5.2 3.2 %collective-permute-start.2 = (bf16[16,32,128]{2,1,0:T(8,128)(2,1)}, bf16[16,32,128]{2,1,0:T(8,128)(2,1)S(1)}, u32[]{:S(2)}, u32[]{:S(2)}) collective-permute-start(bf16[16,32,128]{2,1,0:T(8,128)(2,1)} %param.9), channel_id=1, source_target_pairs={{4,0},{8,4},{12,8},{16,12},{20,16},{24,20},{28,24},{0,28},{5,1},{9... | collective-permute-start | bytes 393224 | tf_op jit(solution)/shard_map/ppermute | solution.py:22
  8.4 0.3 collective-permute-start.3
  8.7 0.7 convert_bitcast_fusion
  9.4 0.7 fusion.38
  10.1 0.7 broadcast_subtract_fusion
  11.5 1.0 %copy.26 = bf16[16,32,128]{2,0,1:T(8,128)(2,1)S(1)} copy(bf16[16,32,128]{2,1,0:T(8,128)(2,1)} %param.17) | data formatting | bytes 262144 | tf_op args[8]
  12.5 0.0 collective-permute-done
  12.5 1.8 %collective-permute-done.1 = bf16[16,32,128]{2,1,0:T(8,128)(2,1)S(1)} collective-permute-done((bf16[16,32,128]{2,1,0:T(8,128)(2,1)}, bf16[16,32,128]{2,1,0:T(8,128)(2,1)S(1)}, u32[]{:S(2)}, u32[]{:S(2)}) %collective-permute-start.1) | collective-permute-done | bytes 131104 | tf_op jit(solution)/shard_map/ppermute | solution.py:22
  14.3 0.9 %constant_dynamic-update-slice_fusion.2 = bf16[80,32,128]{2,1,0:T(8,128)(2,1)S(1)} fusion(bf16[80,32,128]{2,1,0:T(8,128)(2,1)S(1)} %constant_dynamic-update-slice_fusion.3, bf16[16,32,128]{2,1,0:T(8,128)(2,1)} %param.9), kind=kLoop, calls=%fused_computation.55 | loop fusion | bytes 262144
  15.2 0.0 collective-permute-done.2
  15.3 0.0 collective-permute-done.3
  15.3 0.8 fusion.10
  16.1 7.2 %fusion.4 = f32[256,32,128]{2,1,0:T(8,128)S(1)} fusion(bf16[256,128,128]{2,1,0:T(8,128)(2,1)} %param.10, bf16[256,32,128]{2,0,1:T(8,128)(2,1)S(1)} %fusion.10), kind=kOutput, calls=%fused_computation.6 | convolution fusion | flops 268435456 | bytes 14680064 | tf_op jit(solution)/shard_map/tfk,tjk->tfj/dot_general | solution.py:96
  23.3 4.4 %fusion.7 = bf16[16,32,128]{2,0,1:T(8,128)(2,1)S(1)} fusion(f32[256,32,128]{2,1,0:T(8,128)S(1)} %fusion.4, f32[256]{0:T(256)S(1)} %compare_convert_fusion, s32[256]{0:T(256)S(1)} %broadcast_subtract_fusion), kind=kOutput, calls=%fused_computation.11 | convolution fusion | flops 201400320 | bytes 4327424 | tf_op jit(solution)/shard_map/tb,tfj->bfj/dot_general | solution.py:99
  27.7 0.5 collective-permute-start.4
  28.2 1.2 %collective-permute-start.5 = (bf16[33,32,128]{2,0,1:T(8,128)(2,1)S(1)}, bf16[33,32,128]{2,0,1:T(8,128)(2,1)S(1)}, u32[]{:S(2)}, u32[]{:S(2)}) collective-permute-start(bf16[33,32,128]{2,0,1:T(8,128)(2,1)S(1)} %pad_maximum_fusion), channel_id=1, source_target_pairs={{2,0},{3,1},{0,2},{1,3},{6,4},{7,5},{4,6},{5,7},{10,8},{11,9},{8,1... | collective-permute-start | bytes 811016 | tf_op jit(solution)/shard_map/ppermute | solution.py:22
  29.5 0.1 collective-permute-start.6
  29.6 0.2 broadcast_in_dim.9
  29.8 0.1 copy_dynamic-update-slice_fusion.3
  29.9 5.9 %collective-permute-done.4 = bf16[33,32,128]{2,0,1:T(8,128)(2,1)S(1)} collective-permute-done((bf16[33,32,128]{2,0,1:T(8,128)(2,1)S(1)}, bf16[33,32,128]{2,0,1:T(8,128)(2,1)S(1)}, u32[]{:S(2)}, u32[]{:S(2)}) %collective-permute-start.4) | collective-permute-done | bytes 270368 | tf_op jit(solution)/shard_map/ppermute | solution.py:22
  35.7 0.1 copy_dynamic-update-slice_fusion.2
  35.8 9.1 %collective-permute-done.5 = bf16[33,32,128]{2,0,1:T(8,128)(2,1)S(1)} collective-permute-done((bf16[33,32,128]{2,0,1:T(8,128)(2,1)S(1)}, bf16[33,32,128]{2,0,1:T(8,128)(2,1)S(1)}, u32[]{:S(2)}, u32[]{:S(2)}) %collective-permute-start.5) | collective-permute-done | bytes 270368 | tf_op jit(solution)/shard_map/ppermute | solution.py:22
  44.9 0.1 copy_dynamic-update-slice_fusion.1
  44.9 0.0 collective-permute-done.6
  44.9 0.1 copy_dynamic-update-slice_fusion
  45.0 0.0 copy-start
  45.0 0.3 broadcast_compare_fusion
  45.4 0.3 multiply_convert_fusion
  45.7 0.1 copy-done
  45.7 0.3 fusion.6
  46.1 0.3 convolution_bitcast_fusion.1
  46.3 0.3 copy.43
  46.6 1.4 %collective-permute-start.7 = (f32[32,128]{1,0:T(8,128)S(1)}, f32[32,128]{1,0:T(8,128)S(1)}, u32[]{:S(2)}, u32[]{:S(2)}) collective-permute-start(f32[32,128]{1,0:T(8,128)S(1)} %convolution_bitcast_fusion.1), channel_id=1, source_target_pairs={{0,4},{4,0},{8,12},{12,8},{16,20},{20,16},{24,28},{28,24},{1,5},{5... | collective-permute-start | bytes 49160 | tf_op jit(solution)/shard_map/ppermute | solution.py:44
  48.0 0.7 fusion.30
  48.8 1.7 %collective-permute-done.7 = f32[32,128]{1,0:T(8,128)S(1)} collective-permute-done((f32[32,128]{1,0:T(8,128)S(1)}, f32[32,128]{1,0:T(8,128)S(1)}, u32[]{:S(2)}, u32[]{:S(2)}) %collective-permute-start.7) | collective-permute-done | bytes 16416 | tf_op jit(solution)/shard_map/ppermute | solution.py:44
  50.4 0.5 collective-permute-start.8
  50.9 7.2 %fusion.5 = f32[256,32,128]{2,1,0:T(8,128)S(1)} fusion(bf16[256,128,128]{2,1,0:T(8,128)(2,1)} %param.10, bf16[256,32,128]{2,0,1:T(8,128)(2,1)S(1)} %fusion.30), kind=kOutput, calls=%fused_computation.7 | convolution fusion | flops 268435456 | bytes 14680064 | tf_op jit(solution)/shard_map/tfj,tjk->tfk/dot_general | solution.py:123
  58.1 0.0 collective-permute-done.8
  58.1 3.6 %collective-permute-start.9 = (f32[32,128]{1,0:T(8,128)S(1)}, f32[32,128]{1,0:T(8,128)S(1)}, u32[]{:S(2)}, u32[]{:S(2)}) collective-permute-start(f32[32,128]{1,0:T(8,128)S(1)} %add.109), channel_id=1, source_target_pairs={{0,16},{4,20},{8,24},{12,28},{16,0},{20,4},{24,8},{28,12},{1,17},{... | collective-permute-start | bytes 49160 | tf_op jit(solution)/shard_map/ppermute | solution.py:44
  61.7 4.9 %fusion = f32[80,32,128]{2,0,1:T(8,128)S(1)} fusion(f32[256,32,128]{2,1,0:T(8,128)S(1)} %fusion.5, f32[256]{0:T(256)S(1)} %compare_convert_fusion, s32[256]{0:T(256)S(1)} %fusion.38), kind=kOutput, calls=%fused_computation | convolution fusion | flops 1006673920 | bytes 5507072 | tf_op jit(solution)/shard_map/ts,tfk->sfk/dot_general | solution.py:126
  66.6 0.0 collective-permute-done.9
  66.6 0.0 copy-start.1
  66.6 0.0 copy-start.2
  66.6 0.4 copy.34
  67.1 0.1 slice_bitcast_fusion.3
  67.1 0.5 collective-permute-start.13
  67.6 0.0 collective-permute-start.12
  67.6 4.7 %collective-permute-start.11 = (f32[16,32,128]{2,1,0:T(8,128)S(1)}, f32[16,32,128]{2,1,0:T(8,128)S(1)}, u32[]{:S(2)}, u32[]{:S(2)}) collective-permute-start(f32[16,32,128]{2,1,0:T(8,128)S(1)} %get-tuple-element.15), channel_id=1, source_target_pairs={{4,0},{8,4},{12,8},{16,12},{20,16},{24,20},{28,24},{0,28},{5,1},{9... | collective-permute-start | bytes 786440 | tf_op jit(solution)/shard_map/ppermute | solution.py:22
  72.4 1.6 %collective-permute-start.10 = (f32[16,32,128]{2,1,0:T(8,128)S(1)}, f32[16,32,128]{2,1,0:T(8,128)S(1)}, u32[]{:S(2)}, u32[]{:S(2)}) collective-permute-start(f32[16,32,128]{2,1,0:T(8,128)S(1)} %get-tuple-element.12), channel_id=1, source_target_pairs={{8,0},{12,4},{16,8},{20,12},{24,16},{28,20},{0,24},{4,28},{9,1},{1... | collective-permute-start | bytes 786440 | tf_op jit(solution)/shard_map/ppermute | solution.py:22
  73.9 0.8 select_convert_fusion
  74.7 0.0 copy-done.1
  74.7 0.0 copy-done.2
  74.7 0.6 divide_subtract_fusion
  75.3 2.9 %collective-permute-done.13 = f32[16,32,128]{2,1,0:T(8,128)S(1)} collective-permute-done((f32[16,32,128]{2,1,0:T(8,128)S(1)}, f32[16,32,128]{2,1,0:T(8,128)S(1)}, u32[]{:S(2)}, u32[]{:S(2)}) %collective-permute-start.13) | collective-permute-done | bytes 262176 | tf_op jit(solution)/shard_map/ppermute | solution.py:22
  78.2 3.7 %collective-permute-done.12 = f32[16,32,128]{2,1,0:T(8,128)S(1)} collective-permute-done((f32[16,32,128]{2,1,0:T(8,128)S(1)}, f32[16,32,128]{2,1,0:T(8,128)S(1)}, u32[]{:S(2)}, u32[]{:S(2)}) %collective-permute-start.12) | collective-permute-done | bytes 262176 | tf_op jit(solution)/shard_map/ppermute | solution.py:22
  81.9 0.0 collective-permute-done.11
  81.9 2.3 %collective-permute-done.10 = f32[16,32,128]{2,1,0:T(8,128)S(1)} collective-permute-done((f32[16,32,128]{2,1,0:T(8,128)S(1)}, f32[16,32,128]{2,1,0:T(8,128)S(1)}, u32[]{:S(2)}, u32[]{:S(2)}) %collective-permute-start.10) | collective-permute-done | bytes 262176 | tf_op jit(solution)/shard_map/ppermute | solution.py:22
  84.3 0.8 fusion.16
  (10 shorter events, 0.1 us)
Async XLA Ops:
  0.6 11.9 %collective-permute-start = (bf16[16,32,128]{2,1,0:T(8,128)(2,1)}, bf16[16,32,128]{2,1,0:T(8,128)(2,1)S(1)}, u32[]{:S(2)}, u32[]{:S(2)}) collective-permute-start(bf16[16,32,128]{2,1,0:T(8,128)(2,1)} %param.9), channel_id=1, source_target_pairs={{24,0},{28,4},{0,8},{4,12},{8,16},{12,20},{16,24},{20,28},{25,1},{... | collective-permute-start | bytes 393224 | tf_op jit(solution)/shard_map/ppermute | solution.py:22
  3.7 10.6 %collective-permute-start.1 = (bf16[16,32,128]{2,1,0:T(8,128)(2,1)}, bf16[16,32,128]{2,1,0:T(8,128)(2,1)S(1)}, u32[]{:S(2)}, u32[]{:S(2)}) collective-permute-start(bf16[16,32,128]{2,1,0:T(8,128)(2,1)} %param.9), channel_id=1, source_target_pairs={{28,0},{0,4},{4,8},{8,12},{12,16},{16,20},{20,24},{24,28},{29,1},{... | collective-permute-start | bytes 393224 | tf_op jit(solution)/shard_map/ppermute | solution.py:22
  5.2 10.0 %collective-permute-start.2 = (bf16[16,32,128]{2,1,0:T(8,128)(2,1)}, bf16[16,32,128]{2,1,0:T(8,128)(2,1)S(1)}, u32[]{:S(2)}, u32[]{:S(2)}) collective-permute-start(bf16[16,32,128]{2,1,0:T(8,128)(2,1)} %param.9), channel_id=1, source_target_pairs={{4,0},{8,4},{12,8},{16,12},{20,16},{24,20},{28,24},{0,28},{5,1},{9... | collective-permute-start | bytes 393224 | tf_op jit(solution)/shard_map/ppermute | solution.py:22
  8.4 6.9 %collective-permute-start.3 = (bf16[16,32,128]{2,1,0:T(8,128)(2,1)}, bf16[16,32,128]{2,1,0:T(8,128)(2,1)S(1)}, u32[]{:S(2)}, u32[]{:S(2)}) collective-permute-start(bf16[16,32,128]{2,1,0:T(8,128)(2,1)} %param.9), channel_id=1, source_target_pairs={{8,0},{12,4},{16,8},{20,12},{24,16},{28,20},{0,24},{4,28},{9,1},{1... | collective-permute-start | bytes 393224 | tf_op jit(solution)/shard_map/ppermute | solution.py:22
  27.7 8.0 %collective-permute-start.4 = (bf16[33,32,128]{2,0,1:T(8,128)(2,1)S(1)}, bf16[33,32,128]{2,0,1:T(8,128)(2,1)S(1)}, u32[]{:S(2)}, u32[]{:S(2)}) collective-permute-start(bf16[33,32,128]{2,0,1:T(8,128)(2,1)S(1)} %pad_maximum_fusion), channel_id=1, source_target_pairs={{1,0},{2,1},{3,2},{0,3},{5,4},{6,5},{7,6},{4,7},{9,8},{10,9},{11,1... | collective-permute-start | bytes 811016 | tf_op jit(solution)/shard_map/ppermute | solution.py:22
  28.2 16.6 %collective-permute-start.5 = (bf16[33,32,128]{2,0,1:T(8,128)(2,1)S(1)}, bf16[33,32,128]{2,0,1:T(8,128)(2,1)S(1)}, u32[]{:S(2)}, u32[]{:S(2)}) collective-permute-start(bf16[33,32,128]{2,0,1:T(8,128)(2,1)S(1)} %pad_maximum_fusion), channel_id=1, source_target_pairs={{2,0},{3,1},{0,2},{1,3},{6,4},{7,5},{4,6},{5,7},{10,8},{11,9},{8,1... | collective-permute-start | bytes 811016 | tf_op jit(solution)/shard_map/ppermute | solution.py:22
  29.5 15.5 %collective-permute-start.6 = (bf16[33,32,128]{2,0,1:T(8,128)(2,1)S(1)}, bf16[33,32,128]{2,0,1:T(8,128)(2,1)S(1)}, u32[]{:S(2)}, u32[]{:S(2)}) collective-permute-start(bf16[33,32,128]{2,0,1:T(8,128)(2,1)S(1)} %pad_maximum_fusion), channel_id=1, source_target_pairs={{3,0},{0,1},{1,2},{2,3},{7,4},{4,5},{5,6},{6,7},{11,8},{8,9},{9,10... | collective-permute-start | bytes 811016 | tf_op jit(solution)/shard_map/ppermute | solution.py:22
  45.0 0.7 copy-start
  46.6 3.8 %collective-permute-start.7 = (f32[32,128]{1,0:T(8,128)S(1)}, f32[32,128]{1,0:T(8,128)S(1)}, u32[]{:S(2)}, u32[]{:S(2)}) collective-permute-start(f32[32,128]{1,0:T(8,128)S(1)} %convolution_bitcast_fusion.1), channel_id=1, source_target_pairs={{0,4},{4,0},{8,12},{12,8},{16,20},{20,16},{24,28},{28,24},{1,5},{5... | collective-permute-start | bytes 49160 | tf_op jit(solution)/shard_map/ppermute | solution.py:44
  50.4 7.7 %collective-permute-start.8 = (f32[32,128]{1,0:T(8,128)S(1)}, f32[32,128]{1,0:T(8,128)S(1)}, u32[]{:S(2)}, u32[]{:S(2)}) collective-permute-start(f32[32,128]{1,0:T(8,128)S(1)} %add.108), channel_id=1, source_target_pairs={{0,8},{4,12},{8,0},{12,4},{16,24},{20,28},{24,16},{28,20},{1,9},{5... | collective-permute-start | bytes 49160 | tf_op jit(solution)/shard_map/ppermute | solution.py:44
  58.1 8.5 %collective-permute-start.9 = (f32[32,128]{1,0:T(8,128)S(1)}, f32[32,128]{1,0:T(8,128)S(1)}, u32[]{:S(2)}, u32[]{:S(2)}) collective-permute-start(f32[32,128]{1,0:T(8,128)S(1)} %add.109), channel_id=1, source_target_pairs={{0,16},{4,20},{8,24},{12,28},{16,0},{20,4},{24,8},{28,12},{1,17},{... | collective-permute-start | bytes 49160 | tf_op jit(solution)/shard_map/ppermute | solution.py:44
  66.6 8.1 %copy-start.1 = (f32[32,128]{1,0:T(8,128)S(1)}, f32[32,128]{1,0:T(8,128)}, u32[]{:S(2)}) copy-start(f32[32,128]{1,0:T(8,128)} %param.15) | copy-start | bytes 49156
  66.6 8.1 %copy-start.2 = (f32[32,128]{1,0:T(8,128)S(1)}, f32[32,128]{1,0:T(8,128)}, u32[]{:S(2)}) copy-start(f32[32,128]{1,0:T(8,128)} %param.16) | copy-start | bytes 49156
  67.1 11.1 %collective-permute-start.13 = (f32[16,32,128]{2,1,0:T(8,128)S(1)}, f32[16,32,128]{2,1,0:T(8,128)S(1)}, u32[]{:S(2)}, u32[]{:S(2)}) collective-permute-start(f32[16,32,128]{2,1,0:T(8,128)S(1)} %get-tuple-element.13), channel_id=1, source_target_pairs={{24,0},{28,4},{0,8},{4,12},{8,16},{12,20},{16,24},{20,28},{25,1},{... | collective-permute-start | bytes 786440 | tf_op jit(solution)/shard_map/ppermute | solution.py:22
  67.6 14.3 %collective-permute-start.12 = (f32[16,32,128]{2,1,0:T(8,128)S(1)}, f32[16,32,128]{2,1,0:T(8,128)S(1)}, u32[]{:S(2)}, u32[]{:S(2)}) collective-permute-start(f32[16,32,128]{2,1,0:T(8,128)S(1)} %get-tuple-element.14), channel_id=1, source_target_pairs={{28,0},{0,4},{4,8},{8,12},{12,16},{16,20},{20,24},{24,28},{29,1},{... | collective-permute-start | bytes 786440 | tf_op jit(solution)/shard_map/ppermute | solution.py:22
  67.6 14.3 %collective-permute-start.11 = (f32[16,32,128]{2,1,0:T(8,128)S(1)}, f32[16,32,128]{2,1,0:T(8,128)S(1)}, u32[]{:S(2)}, u32[]{:S(2)}) collective-permute-start(f32[16,32,128]{2,1,0:T(8,128)S(1)} %get-tuple-element.15), channel_id=1, source_target_pairs={{4,0},{8,4},{12,8},{16,12},{20,16},{24,20},{28,24},{0,28},{5,1},{9... | collective-permute-start | bytes 786440 | tf_op jit(solution)/shard_map/ppermute | solution.py:22
  72.4 11.9 %collective-permute-start.10 = (f32[16,32,128]{2,1,0:T(8,128)S(1)}, f32[16,32,128]{2,1,0:T(8,128)S(1)}, u32[]{:S(2)}, u32[]{:S(2)}) collective-permute-start(f32[16,32,128]{2,1,0:T(8,128)S(1)} %get-tuple-element.12), channel_id=1, source_target_pairs={{8,0},{12,4},{16,8},{20,12},{24,16},{28,20},{0,24},{4,28},{9,1},{1... | collective-permute-start | bytes 786440 | tf_op jit(solution)/shard_map/ppermute | solution.py:22

commit v3 on v1

--- a/solution.py
+++ b/solution.py
@@ -26,12 +26,23 @@
     size = lax.axis_size(axis)
     own = lax.axis_index(axis)
     width = block.shape[dim]
+    if size & (size - 1):
+        pieces = [(block, own)]
+        for step in range(1, size):
+            pieces.append((passed_along(block, axis, -step), (own + step) % size))
+    else:
+        pieces = [(block, own)]
+        mask = size // 2
+        while mask >= 1:
+            held = jnp.stack([piece for piece, _ in pieces])
+            got = lax.ppermute(held, axis, [(i, i ^ mask) for i in range(size)])
+            pieces = pieces + [(got[k], index ^ mask) for k, (_, index) in enumerate(pieces)]
+            mask //= 2
     shape = list(block.shape)
     shape[dim] = size * width
     whole = jnp.zeros(shape, block.dtype)
-    for step in range(size):
-        piece = block if step == 0 else passed_along(block, axis, -step)
-        whole = lax.dynamic_update_slice_in_dim(whole, piece, ((own + step) % size) * width, dim)
+    for piece, index in pieces:
+        whole = lax.dynamic_update_slice_in_dim(whole, piece, index * width, dim)
     return whole
 
 
@@ -90,6 +101,12 @@
         else:
             pieces.append(passed_along(features, "node", -distance))
     nearby = jnp.concatenate(pieces, axis=0)
+    weight_half = weight.astype(jnp.bfloat16)
+    packed = jnp.concatenate([cotangent, weight_half[None]], axis=0)
+    packed_all = gathered_along(packed, "feat", 1)
+    cotangent_all = packed_all[:blocks]
+    weight_all = packed_all[blocks]
+    nearby, cotangent_all, weight_all = lax.optimization_barrier((nearby, cotangent_all, weight_all))
     sources = jnp.einsum(
         "ts,sfk->tfk", pick_source, nearby, preferred_element_type=jnp.float32
     ).astype(jnp.bfloat16)
@@ -98,10 +115,7 @@
     )
     aggregate = jnp.einsum("tb,tfj->bfj", add_row, forward_terms, precision=lax.Precision.HIGHEST)
     aggregate = aggregate.astype(jnp.bfloat16)
-    weight_half = weight.astype(jnp.bfloat16)
     aggregate_all = gathered_along(aggregate, "feat", 1)
-    weight_all = gathered_along(weight_half, "feat", 0)
-    cotangent_all = gathered_along(cotangent, "feat", 1)
     column_start = lax.axis_index("feat") * width_local
     preact = jnp.einsum(
         "bij,io->boj", aggregate_all, weight_all, preferred_element_type=jnp.float32
@@ -123,6 +137,7 @@
     )
     outgoing = jnp.einsum("ts,tfk->sfk", add_source, back_terms, precision=lax.Precision.HIGHEST)
     outgoing = outgoing.reshape(2 * REACH + 1, blocks, width_local, tile_size)
+    outgoing, grad = lax.optimization_barrier((outgoing, grad))
     feature_grad = outgoing[REACH]
     for distance in range(-REACH, REACH + 1):
         if distance != 0:

time: 86.6 us -> 81.3 us (0.939)
  waiting for transfers between devices: 24.8 us -> 19.1 us
  local copies, waits for them, and re-layouts: 5.39 us -> 2.26 us
  other arithmetic: 3.62 us -> 5.37 us
  starting transfers between devices: 24.5 us -> 26 us
    ppermute x3, waiting for transfers between devices: 12.7 us -> 0.97 us  [summed_over(): lax.ppermute(block, axis, [(i, i ^ mask) for i in range(size)])]
    ppermute x0 -> x4, waiting for transfers between devices: none -> 7.12 us  [gathered_along(): got = lax.ppermute(held, axis, [(i, i ^ mask) for i in range(size)])]
    ppermute x17 -> x8, starting transfers between devices: 22.5 us -> 18.4 us  [passed_along(): return lax.ppermute(block, axis, route)]
    ppermute x0 -> x4, starting transfers between devices: none -> 3.31 us  [gathered_along(): got = lax.ppermute(held, axis, [(i, i ^ mask) for i in range(size)])]
    dynamic_update_slice x12 -> x7, local copies, waits for them, and re-layouts: 2.59 us -> 0.28 us  [gathered_along(): whole = lax.dynamic_update_slice_in_dim(whole, piece, index * width, dim)]
    ppermute x3, starting transfers between devices: 2 us -> 4.24 us  [summed_over(): lax.ppermute(block, axis, [(i, i ^ mask) for i in range(size)])]
    ppermute x17 -> x8, waiting for transfers between devices: 12.1 us -> 11 us  [passed_along(): return lax.ppermute(block, axis, route)]
    another operation x0 -> x3, other arithmetic: none -> 1.01 us  [gathered_along(): held = jnp.stack([piece for piece, _ in pieces])]
  transfers between devices with their start and end apart: 20 -> 15, of which waited for: 5 -> 9; matrix products, arithmetic and copies ran while one was open for 37% -> 23% of each run, Pallas kernels for 0% -> 0%
where the time goes in v3:
time: 81.3 us; the launch traced here: 81 us
  matrix products  26.6 us (33%)
  starting transfers between devices  26 us (32%)
  waiting for transfers between devices  19.1 us (23%)
  other arithmetic  5.37 us (7%)
  local copies, waits for them, and re-layouts  2.26 us (3%)
  between operations  1.59 us (2%)
    ppermute x8, starting transfers between devices, passed_along(): return lax.ppermute(block, axis, route)  18.4 us
    ppermute x8, waiting for transfers between devices, passed_along(): return lax.ppermute(block, axis, route)  11 us
    dot_general x1, matrix products, per_device(): jnp.einsum('tfj,tjk->tfk', back_sources, tile_values, preferred_element_t...  7.38 us
    dot_general x1, matrix products, per_device(): jnp.einsum('tfk,tjk->tfj', sources, tile_values, preferred_element_type=j...  7.25 us
    ppermute x4, waiting for transfers between devices, gathered_along(): got = lax.ppermute(held, axis, [(i, i ^ mask) for i in range(size)])  7.12 us
    dot_general x1, matrix products, per_device(): jnp.einsum('ts,tfk->sfk', add_source, back_terms, precision=lax.Precision...  4.9 us
    dot_general x1, matrix products, per_device(): jnp.einsum('tb,tfj->bfj', add_row, forward_terms, precision=lax.Precision...  4.36 us
    ppermute x3, starting transfers between devices, summed_over(): lax.ppermute(block, axis, [(i, i ^ mask) for i in range(size)])  4.24 us
  transfers between devices with their start and end apart: 15, of which 9 were waited for; matrix products, arithmetic and copies ran while one was open for 23% of the time, Pallas kernels for 0%

profile of v3, /device:TPU:0, one launch (start us, length us, event | category | flops | bytes accessed | tf_op | source)
XLA Modules:
  0.0 81.0 jit_solution(5605889288658679161)
XLA Ops:
  0.6 6.0 %collective-permute-start.2 = (bf16[16,32,128]{2,1,0:T(8,128)(2,1)}, bf16[16,32,128]{2,1,0:T(8,128)(2,1)S(1)}, u32[]{:S(2)}, u32[]{:S(2)}) collective-permute-start(bf16[16,32,128]{2,1,0:T(8,128)(2,1)} %param.9), channel_id=1, source_target_pairs={{4,0},{8,4},{12,8},{16,12},{20,16},{24,20},{28,24},{0,28},{5,1},{9... | collective-permute-start | bytes 393224 | tf_op jit(solution)/shard_map/ppermute | solution.py:22
  6.7 0.0 collective-permute-start.1
  6.7 0.0 collective-permute-start
  6.7 3.8 %collective-permute-start.3 = (bf16[16,32,128]{2,1,0:T(8,128)(2,1)}, bf16[16,32,128]{2,1,0:T(8,128)(2,1)S(1)}, u32[]{:S(2)}, u32[]{:S(2)}) collective-permute-start(bf16[16,32,128]{2,1,0:T(8,128)(2,1)} %param.9), channel_id=1, source_target_pairs={{8,0},{12,4},{16,8},{20,12},{24,16},{28,20},{0,24},{4,28},{9,1},{1... | collective-permute-start | bytes 393224 | tf_op jit(solution)/shard_map/ppermute | solution.py:22
  10.5 0.7 convert_bitcast_fusion
  11.2 0.1 broadcast_in_dim.11
  11.3 1.0 %fusion.19 = (bf16[1,17,32,128]{3,2,1,0:T(8,128)(2,1)S(1)}, bf16[17,128,128]{2,1,0:T(8,128)(2,1)S(1)}) fusion(bf16[1,32,128]{2,1,0:T(8,128)(2,1)S(1)} %convert_bitcast_fusion, bf16[16,32,128]{2,1,0:T(8,128)(2,1)} %param.17, bf16[17,128,128]{2,1,0:T(8,128)(2,1)S(1)} %broadcast_in_dim.11, s32[]{:T(128)S(6)} %select_n.49), kind=kLoop, calls=%fused_computation.42 | loop fusion | flops 278528 | bytes 417796 | tf_op jit(solution)/shard_map/stack | solution.py:37
  12.3 1.6 %collective-permute-start.4 = (bf16[1,17,32,128]{3,2,1,0:T(8,128)(2,1)S(1)}, bf16[1,17,32,128]{3,2,1,0:T(8,128)(2,1)S(1)}, u32[]{:S(2)}, u32[]{:S(2)}) collective-permute-start(bf16[1,17,32,128]{3,2,1,0:T(8,128)(2,1)S(1)} %get-tuple-element.24), channel_id=1, source_target_pairs={{0,2},{1,3},{2,0},{3,1},{4,6},{5,7},{6,4},{7,5},{8,10},{9,11},{10,... | collective-permute-start | bytes 417800 | tf_op jit(solution)/shard_map/ppermute | solution.py:38
  13.9 0.7 fusion.42
  14.6 0.7 broadcast_subtract_fusion
  15.9 0.0 collective-permute-done
  16.0 0.1 collective-permute-done.1
  16.1 0.9 %constant_dynamic-update-slice_fusion.2 = bf16[80,32,128]{2,1,0:T(8,128)(2,1)S(1)} fusion(bf16[80,32,128]{2,1,0:T(8,128)(2,1)S(1)} %constant_dynamic-update-slice_fusion.3, bf16[16,32,128]{2,1,0:T(8,128)(2,1)} %param.9), kind=kLoop, calls=%fused_computation.66 | loop fusion | bytes 262144
  17.0 0.0 collective-permute-done.2
  17.1 0.3 collective-permute-done.4
  17.4 0.1 collective-permute-start.5
  17.5 0.0 collective-permute-done.3
  17.6 1.5 %collective-permute-done.5 = bf16[2,17,32,128]{3,2,1,0:T(8,128)(2,1)S(1)} collective-permute-done((bf16[2,17,32,128]{3,2,1,0:T(8,128)(2,1)S(1)}, bf16[2,17,32,128]{3,2,1,0:T(8,128)(2,1)S(1)}, u32[]{:S(2)}, u32[]{:S(2)}) %collective-permute-start.5) | collective-permute-done | bytes 278560 | tf_op jit(solution)/shard_map/ppermute | solution.py:38
  19.2 0.8 fusion.10
  19.9 7.2 %fusion.4 = f32[256,32,128]{2,1,0:T(8,128)S(1)} fusion(bf16[256,128,128]{2,1,0:T(8,128)(2,1)} %param.10, bf16[256,32,128]{2,0,1:T(8,128)(2,1)S(1)} %fusion.10), kind=kOutput, calls=%fused_computation.6 | convolution fusion | flops 268435456 | bytes 14680064 | tf_op jit(solution)/shard_map/tfk,tjk->tfj/dot_general | solution.py:113
  27.2 4.4 %fusion.7 = bf16[16,32,128]{2,0,1:T(8,128)(2,1)S(1)} fusion(f32[256,32,128]{2,1,0:T(8,128)S(1)} %fusion.4, f32[256]{0:T(256)S(1)} %compare_convert_fusion, s32[256]{0:T(256)S(1)} %broadcast_subtract_fusion), kind=kOutput, calls=%fused_computation.11 | convolution fusion | flops 201400320 | bytes 4327424 | tf_op jit(solution)/shard_map/tb,tfj->bfj/dot_general | solution.py:116
  31.6 0.0 copy-start
  31.6 1.6 %collective-permute-start.6 = (bf16[1,16,32,128]{3,1,2,0:T(8,128)(2,1)S(1)}, bf16[1,16,32,128]{3,1,2,0:T(8,128)(2,1)S(1)}, u32[]{:S(2)}, u32[]{:S(2)}) collective-permute-start(bf16[1,16,32,128]{3,1,2,0:T(8,128)(2,1)S(1)} %bitcast.74), channel_id=1, source_target_pairs={{0,2},{1,3},{2,0},{3,1},{4,6},{5,7},{6,4},{7,5},{8,10},{9,11},{10,... | collective-permute-start | bytes 393224 | tf_op jit(solution)/shard_map/ppermute | solution.py:38
  33.1 4.0 %collective-permute-done.6 = bf16[1,16,32,128]{3,1,2,0:T(8,128)(2,1)S(1)} collective-permute-done((bf16[1,16,32,128]{3,1,2,0:T(8,128)(2,1)S(1)}, bf16[1,16,32,128]{3,1,2,0:T(8,128)(2,1)S(1)}, u32[]{:S(2)}, u32[]{:S(2)}) %collective-permute-start.6) | collective-permute-done | bytes 131104 | tf_op jit(solution)/shard_map/ppermute | solution.py:38
  37.2 0.1 collective-permute-start.7
  37.3 0.1 broadcast_in_dim.13
  37.4 0.1 copy_dynamic-update-slice_fusion.3
  37.4 0.1 copy_dynamic-update-slice_fusion.2
  37.5 1.3 %collective-permute-done.7 = bf16[2,16,32,128]{3,1,2,0:T(8,128)(2,1)S(1)} collective-permute-done((bf16[2,16,32,128]{3,1,2,0:T(8,128)(2,1)S(1)}, bf16[2,16,32,128]{3,1,2,0:T(8,128)(2,1)S(1)}, u32[]{:S(2)}, u32[]{:S(2)}) %collective-permute-start.7) | collective-permute-done | bytes 262176 | tf_op jit(solution)/shard_map/ppermute | solution.py:38
  38.8 0.1 copy_dynamic-update-slice_fusion.1
  38.9 0.1 copy_dynamic-update-slice_fusion
  38.9 0.3 broadcast_compare_fusion
  39.3 0.4 convolution_bitcast_fusion.1
  39.7 0.0 copy-done
  39.7 0.5 fusion.6
  40.2 0.2 copy.29
  40.4 3.0 %collective-permute-start.8 = (f32[32,128]{1,0:T(8,128)S(1)}, f32[32,128]{1,0:T(8,128)S(1)}, u32[]{:S(2)}, u32[]{:S(2)}) collective-permute-start(f32[32,128]{1,0:T(8,128)S(1)} %convolution_bitcast_fusion.1), channel_id=1, source_target_pairs={{0,4},{4,0},{8,12},{12,8},{16,20},{20,16},{24,28},{28,24},{1,5},{5... | collective-permute-start | bytes 49160 | tf_op jit(solution)/shard_map/ppermute | solution.py:55
  43.5 0.7 fusion.34
  44.2 1.0 %collective-permute-done.8 = f32[32,128]{1,0:T(8,128)S(1)} collective-permute-done((f32[32,128]{1,0:T(8,128)S(1)}, f32[32,128]{1,0:T(8,128)S(1)}, u32[]{:S(2)}, u32[]{:S(2)}) %collective-permute-start.8) | collective-permute-done | bytes 16416 | tf_op jit(solution)/shard_map/ppermute | solution.py:55
  45.2 0.0 collective-permute-start.9
  45.2 7.4 %fusion.5 = f32[256,32,128]{2,1,0:T(8,128)S(1)} fusion(bf16[256,128,128]{2,1,0:T(8,128)(2,1)} %param.10, bf16[256,32,128]{2,0,1:T(8,128)(2,1)S(1)} %fusion.34), kind=kOutput, calls=%fused_computation.7 | convolution fusion | flops 268435456 | bytes 14680064 | tf_op jit(solution)/shard_map/tfj,tjk->tfk/dot_general | solution.py:135
  52.6 0.0 collective-permute-done.9
  52.6 0.0 copy-start.1
  52.6 0.0 copy-start.2
  52.6 1.2 %collective-permute-start.10 = (f32[32,128]{1,0:T(8,128)S(1)}, f32[32,128]{1,0:T(8,128)S(1)}, u32[]{:S(2)}, u32[]{:S(2)}) collective-permute-start(f32[32,128]{1,0:T(8,128)S(1)} %add.81), channel_id=1, source_target_pairs={{0,16},{4,20},{8,24},{12,28},{16,0},{20,4},{24,8},{28,12},{1,17},{... | collective-permute-start | bytes 49160 | tf_op jit(solution)/shard_map/ppermute | solution.py:55
  53.8 4.9 %fusion = f32[80,32,128]{2,0,1:T(8,128)S(1)} fusion(f32[256,32,128]{2,1,0:T(8,128)S(1)} %fusion.5, f32[256]{0:T(256)S(1)} %compare_convert_fusion, s32[256]{0:T(256)S(1)} %fusion.42), kind=kOutput, calls=%fused_computation | convolution fusion | flops 1006673920 | bytes 5507072 | tf_op jit(solution)/shard_map/ts,tfk->sfk/dot_general | solution.py:138
  58.7 0.0 collective-permute-done.10
  58.8 0.4 copy.20
  59.2 0.1 slice_bitcast_fusion.3
  59.2 3.3 %collective-permute-start.11 = (f32[16,32,128]{2,1,0:T(8,128)S(1)}, f32[16,32,128]{2,1,0:T(8,128)S(1)}, u32[]{:S(2)}, u32[]{:S(2)}) collective-permute-start(f32[16,32,128]{2,1,0:T(8,128)S(1)} %get-tuple-element.18), channel_id=1, source_target_pairs={{8,0},{12,4},{16,8},{20,12},{24,16},{28,20},{0,24},{4,28},{9,1},{1... | collective-permute-start | bytes 786440 | tf_op jit(solution)/shard_map/ppermute | solution.py:22
  62.5 0.0 collective-permute-start.14
  62.5 2.0 %collective-permute-start.13 = (f32[16,32,128]{2,1,0:T(8,128)S(1)}, f32[16,32,128]{2,1,0:T(8,128)S(1)}, u32[]{:S(2)}, u32[]{:S(2)}) collective-permute-start(f32[16,32,128]{2,1,0:T(8,128)S(1)} %get-tuple-element.20), channel_id=1, source_target_pairs={{28,0},{0,4},{4,8},{8,12},{12,16},{16,20},{20,24},{24,28},{29,1},{... | collective-permute-start | bytes 786440 | tf_op jit(solution)/shard_map/ppermute | solution.py:22
  64.6 3.3 %collective-permute-start.12 = (f32[16,32,128]{2,1,0:T(8,128)S(1)}, f32[16,32,128]{2,1,0:T(8,128)S(1)}, u32[]{:S(2)}, u32[]{:S(2)}) collective-permute-start(f32[16,32,128]{2,1,0:T(8,128)S(1)} %get-tuple-element.21), channel_id=1, source_target_pairs={{4,0},{8,4},{12,8},{16,12},{20,16},{24,20},{28,24},{0,28},{5,1},{9... | collective-permute-start | bytes 786440 | tf_op jit(solution)/shard_map/ppermute | solution.py:22
  67.8 0.8 select_convert_fusion
  68.6 0.0 copy-done.1
  68.6 0.0 copy-done.2
  68.6 0.6 divide_subtract_fusion
  69.2 0.3 collective-permute-done.11
  69.5 5.9 %collective-permute-done.14 = f32[16,32,128]{2,1,0:T(8,128)S(1)} collective-permute-done((f32[16,32,128]{2,1,0:T(8,128)S(1)}, f32[16,32,128]{2,1,0:T(8,128)S(1)}, u32[]{:S(2)}, u32[]{:S(2)}) %collective-permute-start.14) | collective-permute-done | bytes 262176 | tf_op jit(solution)/shard_map/ppermute | solution.py:22
  75.4 4.7 %collective-permute-done.13 = f32[16,32,128]{2,1,0:T(8,128)S(1)} collective-permute-done((f32[16,32,128]{2,1,0:T(8,128)S(1)}, f32[16,32,128]{2,1,0:T(8,128)S(1)}, u32[]{:S(2)}, u32[]{:S(2)}) %collective-permute-start.13) | collective-permute-done | bytes 262176 | tf_op jit(solution)/shard_map/ppermute | solution.py:22
  80.2 0.0 collective-permute-done.12
  80.2 0.8 %fusion.15 = f32[16,32,128]{2,1,0:T(8,128)} fusion(f32[16,32,128]{2,1,0:T(8,128)S(1)} %collective-permute-done.14, f32[16,32,128]{2,1,0:T(8,128)S(1)} %collective-permute-done.13, f32[16,32,128]{2,1,0:T(8,128)S(1)} %collective-permute-done.12, f32[16,32,128]{2,1,0:T(8,128)S(1)} %collective-permute-done.11, f32[5,16,32,128]{3,2,1,0:T(8,128)S(1)} %copy.20), kind=kLoop, calls=%fused_computation.26 | loop fusion | flops 262144 | bytes 1572864 | tf_op jit(solution)/shard_map/add | solution.py:144
  (16 shorter events, 0.3 us)
Async XLA Ops:
  0.6 16.4 %collective-permute-start.2 = (bf16[16,32,128]{2,1,0:T(8,128)(2,1)}, bf16[16,32,128]{2,1,0:T(8,128)(2,1)S(1)}, u32[]{:S(2)}, u32[]{:S(2)}) collective-permute-start(bf16[16,32,128]{2,1,0:T(8,128)(2,1)} %param.9), channel_id=1, source_target_pairs={{4,0},{8,4},{12,8},{16,12},{20,16},{24,20},{28,24},{0,28},{5,1},{9... | collective-permute-start | bytes 393224 | tf_op jit(solution)/shard_map/ppermute | solution.py:22
  6.7 9.4 %collective-permute-start.1 = (bf16[16,32,128]{2,1,0:T(8,128)(2,1)}, bf16[16,32,128]{2,1,0:T(8,128)(2,1)S(1)}, u32[]{:S(2)}, u32[]{:S(2)}) collective-permute-start(bf16[16,32,128]{2,1,0:T(8,128)(2,1)} %param.9), channel_id=1, source_target_pairs={{28,0},{0,4},{4,8},{8,12},{12,16},{16,20},{20,24},{24,28},{29,1},{... | collective-permute-start | bytes 393224 | tf_op jit(solution)/shard_map/ppermute | solution.py:22
  6.7 9.3 %collective-permute-start = (bf16[16,32,128]{2,1,0:T(8,128)(2,1)}, bf16[16,32,128]{2,1,0:T(8,128)(2,1)S(1)}, u32[]{:S(2)}, u32[]{:S(2)}) collective-permute-start(bf16[16,32,128]{2,1,0:T(8,128)(2,1)} %param.9), channel_id=1, source_target_pairs={{24,0},{28,4},{0,8},{4,12},{8,16},{12,20},{16,24},{20,28},{25,1},{... | collective-permute-start | bytes 393224 | tf_op jit(solution)/shard_map/ppermute | solution.py:22
  6.7 10.9 %collective-permute-start.3 = (bf16[16,32,128]{2,1,0:T(8,128)(2,1)}, bf16[16,32,128]{2,1,0:T(8,128)(2,1)S(1)}, u32[]{:S(2)}, u32[]{:S(2)}) collective-permute-start(bf16[16,32,128]{2,1,0:T(8,128)(2,1)} %param.9), channel_id=1, source_target_pairs={{8,0},{12,4},{16,8},{20,12},{24,16},{28,20},{0,24},{4,28},{9,1},{1... | collective-permute-start | bytes 393224 | tf_op jit(solution)/shard_map/ppermute | solution.py:22
  12.3 5.1 %collective-permute-start.4 = (bf16[1,17,32,128]{3,2,1,0:T(8,128)(2,1)S(1)}, bf16[1,17,32,128]{3,2,1,0:T(8,128)(2,1)S(1)}, u32[]{:S(2)}, u32[]{:S(2)}) collective-permute-start(bf16[1,17,32,128]{3,2,1,0:T(8,128)(2,1)S(1)} %get-tuple-element.24), channel_id=1, source_target_pairs={{0,2},{1,3},{2,0},{3,1},{4,6},{5,7},{6,4},{7,5},{8,10},{9,11},{10,... | collective-permute-start | bytes 417800 | tf_op jit(solution)/shard_map/ppermute | solution.py:38
  17.4 1.6 %collective-permute-start.5 = (bf16[2,17,32,128]{3,2,1,0:T(8,128)(2,1)S(1)}, bf16[2,17,32,128]{3,2,1,0:T(8,128)(2,1)S(1)}, u32[]{:S(2)}, u32[]{:S(2)}) collective-permute-start(bf16[2,17,32,128]{3,2,1,0:T(8,128)(2,1)S(1)} %pad_maximum_fusion), channel_id=1, source_target_pairs={{0,1},{1,0},{2,3},{3,2},{4,5},{5,4},{6,7},{7,6},{8,9},{9,8},{10,11... | collective-permute-start | bytes 835592 | tf_op jit(solution)/shard_map/ppermute | solution.py:38
  31.6 8.1 %copy-start = (f32[32,128]{1,0:T(8,128)S(1)}, f32[32,128]{1,0:T(8,128)}, u32[]{:S(2)}) copy-start(f32[32,128]{1,0:T(8,128)} %param.14) | copy-start | bytes 49156
  31.6 5.6 %collective-permute-start.6 = (bf16[1,16,32,128]{3,1,2,0:T(8,128)(2,1)S(1)}, bf16[1,16,32,128]{3,1,2,0:T(8,128)(2,1)S(1)}, u32[]{:S(2)}, u32[]{:S(2)}) collective-permute-start(bf16[1,16,32,128]{3,1,2,0:T(8,128)(2,1)S(1)} %bitcast.74), channel_id=1, source_target_pairs={{0,2},{1,3},{2,0},{3,1},{4,6},{5,7},{6,4},{7,5},{8,10},{9,11},{10,... | collective-permute-start | bytes 393224 | tf_op jit(solution)/shard_map/ppermute | solution.py:38
  37.2 1.6 %collective-permute-start.7 = (bf16[2,16,32,128]{3,1,2,0:T(8,128)(2,1)S(1)}, bf16[2,16,32,128]{3,1,2,0:T(8,128)(2,1)S(1)}, u32[]{:S(2)}, u32[]{:S(2)}) collective-permute-start(bf16[2,16,32,128]{3,1,2,0:T(8,128)(2,1)S(1)} %pad_maximum_fusion.1), channel_id=1, source_target_pairs={{0,1},{1,0},{2,3},{3,2},{4,5},{5,4},{6,7},{7,6},{8,9},{9,8},{10,11... | collective-permute-start | bytes 786440 | tf_op jit(solution)/shard_map/ppermute | solution.py:38
  40.4 4.8 %collective-permute-start.8 = (f32[32,128]{1,0:T(8,128)S(1)}, f32[32,128]{1,0:T(8,128)S(1)}, u32[]{:S(2)}, u32[]{:S(2)}) collective-permute-start(f32[32,128]{1,0:T(8,128)S(1)} %convolution_bitcast_fusion.1), channel_id=1, source_target_pairs={{0,4},{4,0},{8,12},{12,8},{16,20},{20,16},{24,28},{28,24},{1,5},{5... | collective-permute-start | bytes 49160 | tf_op jit(solution)/shard_map/ppermute | solution.py:55
  45.2 7.4 %collective-permute-start.9 = (f32[32,128]{1,0:T(8,128)S(1)}, f32[32,128]{1,0:T(8,128)S(1)}, u32[]{:S(2)}, u32[]{:S(2)}) collective-permute-start(f32[32,128]{1,0:T(8,128)S(1)} %add.80), channel_id=1, source_target_pairs={{0,8},{4,12},{8,0},{12,4},{16,24},{20,28},{24,16},{28,20},{1,9},{5... | collective-permute-start | bytes 49160 | tf_op jit(solution)/shard_map/ppermute | solution.py:55
  52.6 16.0 %copy-start.1 = (f32[32,128]{1,0:T(8,128)S(1)}, f32[32,128]{1,0:T(8,128)}, u32[]{:S(2)}) copy-start(f32[32,128]{1,0:T(8,128)} %param.15) | copy-start | bytes 49156
  52.6 16.0 %copy-start.2 = (f32[32,128]{1,0:T(8,128)S(1)}, f32[32,128]{1,0:T(8,128)}, u32[]{:S(2)}) copy-start(f32[32,128]{1,0:T(8,128)} %param.16) | copy-start | bytes 49156
  52.6 6.1 %collective-permute-start.10 = (f32[32,128]{1,0:T(8,128)S(1)}, f32[32,128]{1,0:T(8,128)S(1)}, u32[]{:S(2)}, u32[]{:S(2)}) collective-permute-start(f32[32,128]{1,0:T(8,128)S(1)} %add.81), channel_id=1, source_target_pairs={{0,16},{4,20},{8,24},{12,28},{16,0},{20,4},{24,8},{28,12},{1,17},{... | collective-permute-start | bytes 49160 | tf_op jit(solution)/shard_map/ppermute | solution.py:55
  59.2 10.3 %collective-permute-start.11 = (f32[16,32,128]{2,1,0:T(8,128)S(1)}, f32[16,32,128]{2,1,0:T(8,128)S(1)}, u32[]{:S(2)}, u32[]{:S(2)}) collective-permute-start(f32[16,32,128]{2,1,0:T(8,128)S(1)} %get-tuple-element.18), channel_id=1, source_target_pairs={{8,0},{12,4},{16,8},{20,12},{24,16},{28,20},{0,24},{4,28},{9,1},{1... | collective-permute-start | bytes 786440 | tf_op jit(solution)/shard_map/ppermute | solution.py:22
  62.5 12.9 %collective-permute-start.14 = (f32[16,32,128]{2,1,0:T(8,128)S(1)}, f32[16,32,128]{2,1,0:T(8,128)S(1)}, u32[]{:S(2)}, u32[]{:S(2)}) collective-permute-start(f32[16,32,128]{2,1,0:T(8,128)S(1)} %get-tuple-element.19), channel_id=1, source_target_pairs={{24,0},{28,4},{0,8},{4,12},{8,16},{12,20},{16,24},{20,28},{25,1},{... | collective-permute-start | bytes 786440 | tf_op jit(solution)/shard_map/ppermute | solution.py:22
  62.5 17.6 %collective-permute-start.13 = (f32[16,32,128]{2,1,0:T(8,128)S(1)}, f32[16,32,128]{2,1,0:T(8,128)S(1)}, u32[]{:S(2)}, u32[]{:S(2)}) collective-permute-start(f32[16,32,128]{2,1,0:T(8,128)S(1)} %get-tuple-element.20), channel_id=1, source_target_pairs={{28,0},{0,4},{4,8},{8,12},{12,16},{16,20},{20,24},{24,28},{29,1},{... | collective-permute-start | bytes 786440 | tf_op jit(solution)/shard_map/ppermute | solution.py:22
  64.6 15.6 %collective-permute-start.12 = (f32[16,32,128]{2,1,0:T(8,128)S(1)}, f32[16,32,128]{2,1,0:T(8,128)S(1)}, u32[]{:S(2)}, u32[]{:S(2)}) collective-permute-start(f32[16,32,128]{2,1,0:T(8,128)S(1)} %get-tuple-element.21), channel_id=1, source_target_pairs={{4,0},{8,4},{12,8},{16,12},{20,16},{24,20},{28,24},{0,28},{5,1},{9... | collective-permute-start | bytes 786440 | tf_op jit(solution)/shard_map/ppermute | solution.py:22

commit v4 on v3

--- a/solution.py
+++ b/solution.py
@@ -113,7 +113,7 @@
     forward_terms = jnp.einsum(
         "tfk,tjk->tfj", sources, tile_values, preferred_element_type=jnp.float32
     )
-    aggregate = jnp.einsum("tb,tfj->bfj", add_row, forward_terms, precision=lax.Precision.HIGHEST)
+    aggregate = jnp.einsum("tb,tfj->bfj", add_row, forward_terms, precision=lax.Precision.HIGH)
     aggregate = aggregate.astype(jnp.bfloat16)
     aggregate_all = gathered_along(aggregate, "feat", 1)
     column_start = lax.axis_index("feat") * width_local
@@ -135,7 +135,7 @@
     back_terms = jnp.einsum(
         "tfj,tjk->tfk", back_sources, tile_values, preferred_element_type=jnp.float32
     )
-    outgoing = jnp.einsum("ts,tfk->sfk", add_source, back_terms, precision=lax.Precision.HIGHEST)
+    outgoing = jnp.einsum("ts,tfk->sfk", add_source, back_terms, precision=lax.Precision.HIGH)
     outgoing = outgoing.reshape(2 * REACH + 1, blocks, width_local, tile_size)
     outgoing, grad = lax.optimization_barrier((outgoing, grad))
     feature_grad = outgoing[REACH]

time: 81.3 us -> 78.9 us (0.970)
  matrix products: 26.6 us -> 24.2 us
    dot_general x1, matrix products: 4.9 us -> 3.54 us  [per_device(): jnp.einsum('ts,tfk->sfk', add_source, back_terms, precision=lax.Precision...]
    dot_general x1, matrix products: 4.36 us -> 3.29 us  [per_device(): jnp.einsum('tb,tfj->bfj', add_row, forward_terms, precision=lax.Precision...]
  transfers between devices with their start and end apart: 15 -> 15, of which waited for: 9 -> 9; matrix products, arithmetic and copies ran while one was open for 23% -> 22% of each run, Pallas kernels for 0% -> 0%
where the time goes in v4:
time: 78.9 us; the launch traced here: 78.6 us
  starting transfers between devices  26 us (33%)
  matrix products  24.2 us (31%)
  waiting for transfers between devices  19.1 us (24%)
  other arithmetic  5.37 us (7%)
  local copies, waits for them, and re-layouts  2.27 us (3%)
  between operations  1.6 us (2%)
    ppermute x8, starting transfers between devices, passed_along(): return lax.ppermute(block, axis, route)  18.4 us
    ppermute x8, waiting for transfers between devices, passed_along(): return lax.ppermute(block, axis, route)  11 us
    dot_general x1, matrix products, per_device(): jnp.einsum('tfj,tjk->tfk', back_sources, tile_values, preferred_element_t...  7.38 us
    dot_general x1, matrix products, per_device(): jnp.einsum('tfk,tjk->tfj', sources, tile_values, preferred_element_type=j...  7.25 us
    ppermute x4, waiting for transfers between devices, gathered_along(): got = lax.ppermute(held, axis, [(i, i ^ mask) for i in range(size)])  7.12 us
    ppermute x3, starting transfers between devices, summed_over(): lax.ppermute(block, axis, [(i, i ^ mask) for i in range(size)])  4.24 us
    dot_general x1, matrix products, per_device(): jnp.einsum('ts,tfk->sfk', add_source, back_terms, precision=lax.Precision...  3.54 us
    ppermute x4, starting transfers between devices, gathered_along(): got = lax.ppermute(held, axis, [(i, i ^ mask) for i in range(size)])  3.31 us
  transfers between devices with their start and end apart: 15, of which 9 were waited for; matrix products, arithmetic and copies ran while one was open for 22% of the time, Pallas kernels for 0%

profile of v4, /device:TPU:0, one launch (start us, length us, event | category | flops | bytes accessed | tf_op | source)
XLA Modules:
  0.0 78.6 jit_solution(3231636618149563193)
XLA Ops:
  0.6 6.0 %collective-permute-start.2 = (bf16[16,32,128]{2,1,0:T(8,128)(2,1)}, bf16[16,32,128]{2,1,0:T(8,128)(2,1)S(1)}, u32[]{:S(2)}, u32[]{:S(2)}) collective-permute-start(bf16[16,32,128]{2,1,0:T(8,128)(2,1)} %param.9), channel_id=1, source_target_pairs={{4,0},{8,4},{12,8},{16,12},{20,16},{24,20},{28,24},{0,28},{5,1},{9... | collective-permute-start | bytes 393224 | tf_op jit(solution)/shard_map/ppermute | solution.py:22
  6.7 0.0 collective-permute-start.1
  6.7 0.0 collective-permute-start
  6.7 3.8 %collective-permute-start.3 = (bf16[16,32,128]{2,1,0:T(8,128)(2,1)}, bf16[16,32,128]{2,1,0:T(8,128)(2,1)S(1)}, u32[]{:S(2)}, u32[]{:S(2)}) collective-permute-start(bf16[16,32,128]{2,1,0:T(8,128)(2,1)} %param.9), channel_id=1, source_target_pairs={{8,0},{12,4},{16,8},{20,12},{24,16},{28,20},{0,24},{4,28},{9,1},{1... | collective-permute-start | bytes 393224 | tf_op jit(solution)/shard_map/ppermute | solution.py:22
  10.5 0.7 convert_bitcast_fusion
  11.2 0.1 broadcast_in_dim.11
  11.3 1.0 %fusion.19 = (bf16[1,17,32,128]{3,2,1,0:T(8,128)(2,1)S(1)}, bf16[17,128,128]{2,1,0:T(8,128)(2,1)S(1)}) fusion(bf16[1,32,128]{2,1,0:T(8,128)(2,1)S(1)} %convert_bitcast_fusion, bf16[16,32,128]{2,1,0:T(8,128)(2,1)} %param.17, bf16[17,128,128]{2,1,0:T(8,128)(2,1)S(1)} %broadcast_in_dim.11, s32[]{:T(128)S(6)} %select_n.49), kind=kLoop, calls=%fused_computation.42 | loop fusion | flops 278528 | bytes 417796 | tf_op jit(solution)/shard_map/stack | solution.py:37
  12.3 1.6 %collective-permute-start.4 = (bf16[1,17,32,128]{3,2,1,0:T(8,128)(2,1)S(1)}, bf16[1,17,32,128]{3,2,1,0:T(8,128)(2,1)S(1)}, u32[]{:S(2)}, u32[]{:S(2)}) collective-permute-start(bf16[1,17,32,128]{3,2,1,0:T(8,128)(2,1)S(1)} %get-tuple-element.24), channel_id=1, source_target_pairs={{0,2},{1,3},{2,0},{3,1},{4,6},{5,7},{6,4},{7,5},{8,10},{9,11},{10,... | collective-permute-start | bytes 417800 | tf_op jit(solution)/shard_map/ppermute | solution.py:38
  13.9 0.7 fusion.42
  14.6 0.7 broadcast_subtract_fusion
  15.9 0.0 collective-permute-done
  16.0 0.1 collective-permute-done.1
  16.1 0.9 %constant_dynamic-update-slice_fusion.2 = bf16[80,32,128]{2,1,0:T(8,128)(2,1)S(1)} fusion(bf16[80,32,128]{2,1,0:T(8,128)(2,1)S(1)} %constant_dynamic-update-slice_fusion.3, bf16[16,32,128]{2,1,0:T(8,128)(2,1)} %param.9), kind=kLoop, calls=%fused_computation.66 | loop fusion | bytes 262144
  17.0 0.0 collective-permute-done.2
  17.1 0.3 collective-permute-done.4
  17.4 0.1 collective-permute-start.5
  17.5 0.0 collective-permute-done.3
  17.6 1.5 %collective-permute-done.5 = bf16[2,17,32,128]{3,2,1,0:T(8,128)(2,1)S(1)} collective-permute-done((bf16[2,17,32,128]{3,2,1,0:T(8,128)(2,1)S(1)}, bf16[2,17,32,128]{3,2,1,0:T(8,128)(2,1)S(1)}, u32[]{:S(2)}, u32[]{:S(2)}) %collective-permute-start.5) | collective-permute-done | bytes 278560 | tf_op jit(solution)/shard_map/ppermute | solution.py:38
  19.2 0.8 fusion.10
  19.9 7.2 %fusion.4 = f32[256,32,128]{2,1,0:T(8,128)S(1)} fusion(bf16[256,128,128]{2,1,0:T(8,128)(2,1)} %param.10, bf16[256,32,128]{2,0,1:T(8,128)(2,1)S(1)} %fusion.10), kind=kOutput, calls=%fused_computation.6 | convolution fusion | flops 268435456 | bytes 14680064 | tf_op jit(solution)/shard_map/tfk,tjk->tfj/dot_general | solution.py:113
  27.2 3.3 %fusion.7 = bf16[16,32,128]{2,0,1:T(8,128)(2,1)S(1)} fusion(f32[256,32,128]{2,1,0:T(8,128)S(1)} %fusion.4, f32[256]{0:T(256)S(1)} %compare_convert_fusion, s32[256]{0:T(256)S(1)} %broadcast_subtract_fusion), kind=kOutput, calls=%fused_computation.11 | convolution fusion | flops 100737024 | bytes 4327424 | tf_op jit(solution)/shard_map/tb,tfj->bfj/dot_general | solution.py:116
  30.5 0.0 copy-start
  30.5 1.6 %collective-permute-start.6 = (bf16[1,16,32,128]{3,1,2,0:T(8,128)(2,1)S(1)}, bf16[1,16,32,128]{3,1,2,0:T(8,128)(2,1)S(1)}, u32[]{:S(2)}, u32[]{:S(2)}) collective-permute-start(bf16[1,16,32,128]{3,1,2,0:T(8,128)(2,1)S(1)} %bitcast.74), channel_id=1, source_target_pairs={{0,2},{1,3},{2,0},{3,1},{4,6},{5,7},{6,4},{7,5},{8,10},{9,11},{10,... | collective-permute-start | bytes 393224 | tf_op jit(solution)/shard_map/ppermute | solution.py:38
  32.1 4.0 %collective-permute-done.6 = bf16[1,16,32,128]{3,1,2,0:T(8,128)(2,1)S(1)} collective-permute-done((bf16[1,16,32,128]{3,1,2,0:T(8,128)(2,1)S(1)}, bf16[1,16,32,128]{3,1,2,0:T(8,128)(2,1)S(1)}, u32[]{:S(2)}, u32[]{:S(2)}) %collective-permute-start.6) | collective-permute-done | bytes 131104 | tf_op jit(solution)/shard_map/ppermute | solution.py:38
  36.1 0.1 collective-permute-start.7
  36.2 0.1 broadcast_in_dim.13
  36.3 0.1 copy_dynamic-update-slice_fusion.3
  36.4 0.1 copy_dynamic-update-slice_fusion.2
  36.4 1.3 %collective-permute-done.7 = bf16[2,16,32,128]{3,1,2,0:T(8,128)(2,1)S(1)} collective-permute-done((bf16[2,16,32,128]{3,1,2,0:T(8,128)(2,1)S(1)}, bf16[2,16,32,128]{3,1,2,0:T(8,128)(2,1)S(1)}, u32[]{:S(2)}, u32[]{:S(2)}) %collective-permute-start.7) | collective-permute-done | bytes 262176 | tf_op jit(solution)/shard_map/ppermute | solution.py:38
  37.8 0.1 copy_dynamic-update-slice_fusion.1
  37.8 0.1 copy_dynamic-update-slice_fusion
  37.9 0.3 broadcast_compare_fusion
  38.2 0.4 convolution_bitcast_fusion.1
  38.6 0.0 copy-done
  38.6 0.5 fusion.6
  39.1 0.2 copy.29
  39.4 3.0 %collective-permute-start.8 = (f32[32,128]{1,0:T(8,128)S(1)}, f32[32,128]{1,0:T(8,128)S(1)}, u32[]{:S(2)}, u32[]{:S(2)}) collective-permute-start(f32[32,128]{1,0:T(8,128)S(1)} %convolution_bitcast_fusion.1), channel_id=1, source_target_pairs={{0,4},{4,0},{8,12},{12,8},{16,20},{20,16},{24,28},{28,24},{1,5},{5... | collective-permute-start | bytes 49160 | tf_op jit(solution)/shard_map/ppermute | solution.py:55
  42.4 0.7 fusion.34
  43.2 1.0 %collective-permute-done.8 = f32[32,128]{1,0:T(8,128)S(1)} collective-permute-done((f32[32,128]{1,0:T(8,128)S(1)}, f32[32,128]{1,0:T(8,128)S(1)}, u32[]{:S(2)}, u32[]{:S(2)}) %collective-permute-start.8) | collective-permute-done | bytes 16416 | tf_op jit(solution)/shard_map/ppermute | solution.py:55
  44.1 0.0 collective-permute-start.9
  44.2 7.4 %fusion.5 = f32[256,32,128]{2,1,0:T(8,128)S(1)} fusion(bf16[256,128,128]{2,1,0:T(8,128)(2,1)} %param.10, bf16[256,32,128]{2,0,1:T(8,128)(2,1)S(1)} %fusion.34), kind=kOutput, calls=%fused_computation.7 | convolution fusion | flops 268435456 | bytes 14680064 | tf_op jit(solution)/shard_map/tfj,tjk->tfk/dot_general | solution.py:135
  51.5 0.0 collective-permute-done.9
  51.6 0.0 copy-start.1
  51.6 0.0 copy-start.2
  51.6 1.2 %collective-permute-start.10 = (f32[32,128]{1,0:T(8,128)S(1)}, f32[32,128]{1,0:T(8,128)S(1)}, u32[]{:S(2)}, u32[]{:S(2)}) collective-permute-start(f32[32,128]{1,0:T(8,128)S(1)} %add.81), channel_id=1, source_target_pairs={{0,16},{4,20},{8,24},{12,28},{16,0},{20,4},{24,8},{28,12},{1,17},{... | collective-permute-start | bytes 49160 | tf_op jit(solution)/shard_map/ppermute | solution.py:55
  52.8 3.5 %fusion = f32[80,32,128]{2,0,1:T(8,128)S(1)} fusion(f32[256,32,128]{2,1,0:T(8,128)S(1)} %fusion.5, f32[256]{0:T(256)S(1)} %compare_convert_fusion, s32[256]{0:T(256)S(1)} %fusion.42), kind=kOutput, calls=%fused_computation | convolution fusion | flops 503357440 | bytes 5507072 | tf_op jit(solution)/shard_map/ts,tfk->sfk/dot_general | solution.py:138
  56.3 0.0 collective-permute-done.10
  56.3 0.4 copy.20
  56.8 0.1 slice_bitcast_fusion.3
  56.8 3.3 %collective-permute-start.11 = (f32[16,32,128]{2,1,0:T(8,128)S(1)}, f32[16,32,128]{2,1,0:T(8,128)S(1)}, u32[]{:S(2)}, u32[]{:S(2)}) collective-permute-start(f32[16,32,128]{2,1,0:T(8,128)S(1)} %get-tuple-element.18), channel_id=1, source_target_pairs={{8,0},{12,4},{16,8},{20,12},{24,16},{28,20},{0,24},{4,28},{9,1},{1... | collective-permute-start | bytes 786440 | tf_op jit(solution)/shard_map/ppermute | solution.py:22
  60.1 0.0 collective-permute-start.14
  60.1 2.0 %collective-permute-start.13 = (f32[16,32,128]{2,1,0:T(8,128)S(1)}, f32[16,32,128]{2,1,0:T(8,128)S(1)}, u32[]{:S(2)}, u32[]{:S(2)}) collective-permute-start(f32[16,32,128]{2,1,0:T(8,128)S(1)} %get-tuple-element.20), channel_id=1, source_target_pairs={{28,0},{0,4},{4,8},{8,12},{12,16},{16,20},{20,24},{24,28},{29,1},{... | collective-permute-start | bytes 786440 | tf_op jit(solution)/shard_map/ppermute | solution.py:22
  62.2 3.3 %collective-permute-start.12 = (f32[16,32,128]{2,1,0:T(8,128)S(1)}, f32[16,32,128]{2,1,0:T(8,128)S(1)}, u32[]{:S(2)}, u32[]{:S(2)}) collective-permute-start(f32[16,32,128]{2,1,0:T(8,128)S(1)} %get-tuple-element.21), channel_id=1, source_target_pairs={{4,0},{8,4},{12,8},{16,12},{20,16},{24,20},{28,24},{0,28},{5,1},{9... | collective-permute-start | bytes 786440 | tf_op jit(solution)/shard_map/ppermute | solution.py:22
  65.4 0.8 select_convert_fusion
  66.2 0.0 copy-done.1
  66.2 0.0 copy-done.2
  66.2 0.6 divide_subtract_fusion
  66.8 0.3 collective-permute-done.11
  67.2 5.9 %collective-permute-done.14 = f32[16,32,128]{2,1,0:T(8,128)S(1)} collective-permute-done((f32[16,32,128]{2,1,0:T(8,128)S(1)}, f32[16,32,128]{2,1,0:T(8,128)S(1)}, u32[]{:S(2)}, u32[]{:S(2)}) %collective-permute-start.14) | collective-permute-done | bytes 262176 | tf_op jit(solution)/shard_map/ppermute | solution.py:22
  73.0 4.7 %collective-permute-done.13 = f32[16,32,128]{2,1,0:T(8,128)S(1)} collective-permute-done((f32[16,32,128]{2,1,0:T(8,128)S(1)}, f32[16,32,128]{2,1,0:T(8,128)S(1)}, u32[]{:S(2)}, u32[]{:S(2)}) %collective-permute-start.13) | collective-permute-done | bytes 262176 | tf_op jit(solution)/shard_map/ppermute | solution.py:22
  77.7 0.0 collective-permute-done.12
  77.7 0.8 %fusion.15 = f32[16,32,128]{2,1,0:T(8,128)} fusion(f32[16,32,128]{2,1,0:T(8,128)S(1)} %collective-permute-done.14, f32[16,32,128]{2,1,0:T(8,128)S(1)} %collective-permute-done.13, f32[16,32,128]{2,1,0:T(8,128)S(1)} %collective-permute-done.12, f32[16,32,128]{2,1,0:T(8,128)S(1)} %collective-permute-done.11, f32[5,16,32,128]{3,2,1,0:T(8,128)S(1)} %copy.20), kind=kLoop, calls=%fused_computation.26 | loop fusion | flops 262144 | bytes 1572864 | tf_op jit(solution)/shard_map/add | solution.py:144
  (16 shorter events, 0.3 us)
Async XLA Ops:
  0.6 16.4 %collective-permute-start.2 = (bf16[16,32,128]{2,1,0:T(8,128)(2,1)}, bf16[16,32,128]{2,1,0:T(8,128)(2,1)S(1)}, u32[]{:S(2)}, u32[]{:S(2)}) collective-permute-start(bf16[16,32,128]{2,1,0:T(8,128)(2,1)} %param.9), channel_id=1, source_target_pairs={{4,0},{8,4},{12,8},{16,12},{20,16},{24,20},{28,24},{0,28},{5,1},{9... | collective-permute-start | bytes 393224 | tf_op jit(solution)/shard_map/ppermute | solution.py:22
  6.7 9.4 %collective-permute-start.1 = (bf16[16,32,128]{2,1,0:T(8,128)(2,1)}, bf16[16,32,128]{2,1,0:T(8,128)(2,1)S(1)}, u32[]{:S(2)}, u32[]{:S(2)}) collective-permute-start(bf16[16,32,128]{2,1,0:T(8,128)(2,1)} %param.9), channel_id=1, source_target_pairs={{28,0},{0,4},{4,8},{8,12},{12,16},{16,20},{20,24},{24,28},{29,1},{... | collective-permute-start | bytes 393224 | tf_op jit(solution)/shard_map/ppermute | solution.py:22
  6.7 9.3 %collective-permute-start = (bf16[16,32,128]{2,1,0:T(8,128)(2,1)}, bf16[16,32,128]{2,1,0:T(8,128)(2,1)S(1)}, u32[]{:S(2)}, u32[]{:S(2)}) collective-permute-start(bf16[16,32,128]{2,1,0:T(8,128)(2,1)} %param.9), channel_id=1, source_target_pairs={{24,0},{28,4},{0,8},{4,12},{8,16},{12,20},{16,24},{20,28},{25,1},{... | collective-permute-start | bytes 393224 | tf_op jit(solution)/shard_map/ppermute | solution.py:22
  6.7 10.9 %collective-permute-start.3 = (bf16[16,32,128]{2,1,0:T(8,128)(2,1)}, bf16[16,32,128]{2,1,0:T(8,128)(2,1)S(1)}, u32[]{:S(2)}, u32[]{:S(2)}) collective-permute-start(bf16[16,32,128]{2,1,0:T(8,128)(2,1)} %param.9), channel_id=1, source_target_pairs={{8,0},{12,4},{16,8},{20,12},{24,16},{28,20},{0,24},{4,28},{9,1},{1... | collective-permute-start | bytes 393224 | tf_op jit(solution)/shard_map/ppermute | solution.py:22
  12.3 5.1 %collective-permute-start.4 = (bf16[1,17,32,128]{3,2,1,0:T(8,128)(2,1)S(1)}, bf16[1,17,32,128]{3,2,1,0:T(8,128)(2,1)S(1)}, u32[]{:S(2)}, u32[]{:S(2)}) collective-permute-start(bf16[1,17,32,128]{3,2,1,0:T(8,128)(2,1)S(1)} %get-tuple-element.24), channel_id=1, source_target_pairs={{0,2},{1,3},{2,0},{3,1},{4,6},{5,7},{6,4},{7,5},{8,10},{9,11},{10,... | collective-permute-start | bytes 417800 | tf_op jit(solution)/shard_map/ppermute | solution.py:38
  17.4 1.6 %collective-permute-start.5 = (bf16[2,17,32,128]{3,2,1,0:T(8,128)(2,1)S(1)}, bf16[2,17,32,128]{3,2,1,0:T(8,128)(2,1)S(1)}, u32[]{:S(2)}, u32[]{:S(2)}) collective-permute-start(bf16[2,17,32,128]{3,2,1,0:T(8,128)(2,1)S(1)} %pad_maximum_fusion), channel_id=1, source_target_pairs={{0,1},{1,0},{2,3},{3,2},{4,5},{5,4},{6,7},{7,6},{8,9},{9,8},{10,11... | collective-permute-start | bytes 835592 | tf_op jit(solution)/shard_map/ppermute | solution.py:38
  30.5 8.1 %copy-start = (f32[32,128]{1,0:T(8,128)S(1)}, f32[32,128]{1,0:T(8,128)}, u32[]{:S(2)}) copy-start(f32[32,128]{1,0:T(8,128)} %param.14) | copy-start | bytes 49156
  30.5 5.6 %collective-permute-start.6 = (bf16[1,16,32,128]{3,1,2,0:T(8,128)(2,1)S(1)}, bf16[1,16,32,128]{3,1,2,0:T(8,128)(2,1)S(1)}, u32[]{:S(2)}, u32[]{:S(2)}) collective-permute-start(bf16[1,16,32,128]{3,1,2,0:T(8,128)(2,1)S(1)} %bitcast.74), channel_id=1, source_target_pairs={{0,2},{1,3},{2,0},{3,1},{4,6},{5,7},{6,4},{7,5},{8,10},{9,11},{10,... | collective-permute-start | bytes 393224 | tf_op jit(solution)/shard_map/ppermute | solution.py:38
  36.1 1.6 %collective-permute-start.7 = (bf16[2,16,32,128]{3,1,2,0:T(8,128)(2,1)S(1)}, bf16[2,16,32,128]{3,1,2,0:T(8,128)(2,1)S(1)}, u32[]{:S(2)}, u32[]{:S(2)}) collective-permute-start(bf16[2,16,32,128]{3,1,2,0:T(8,128)(2,1)S(1)} %pad_maximum_fusion.1), channel_id=1, source_target_pairs={{0,1},{1,0},{2,3},{3,2},{4,5},{5,4},{6,7},{7,6},{8,9},{9,8},{10,11... | collective-permute-start | bytes 786440 | tf_op jit(solution)/shard_map/ppermute | solution.py:38
  39.4 4.8 %collective-permute-start.8 = (f32[32,128]{1,0:T(8,128)S(1)}, f32[32,128]{1,0:T(8,128)S(1)}, u32[]{:S(2)}, u32[]{:S(2)}) collective-permute-start(f32[32,128]{1,0:T(8,128)S(1)} %convolution_bitcast_fusion.1), channel_id=1, source_target_pairs={{0,4},{4,0},{8,12},{12,8},{16,20},{20,16},{24,28},{28,24},{1,5},{5... | collective-permute-start | bytes 49160 | tf_op jit(solution)/shard_map/ppermute | solution.py:55
  44.1 7.4 %collective-permute-start.9 = (f32[32,128]{1,0:T(8,128)S(1)}, f32[32,128]{1,0:T(8,128)S(1)}, u32[]{:S(2)}, u32[]{:S(2)}) collective-permute-start(f32[32,128]{1,0:T(8,128)S(1)} %add.80), channel_id=1, source_target_pairs={{0,8},{4,12},{8,0},{12,4},{16,24},{20,28},{24,16},{28,20},{1,9},{5... | collective-permute-start | bytes 49160 | tf_op jit(solution)/shard_map/ppermute | solution.py:55
  51.6 14.6 %copy-start.1 = (f32[32,128]{1,0:T(8,128)S(1)}, f32[32,128]{1,0:T(8,128)}, u32[]{:S(2)}) copy-start(f32[32,128]{1,0:T(8,128)} %param.15) | copy-start | bytes 49156
  51.6 14.6 %copy-start.2 = (f32[32,128]{1,0:T(8,128)S(1)}, f32[32,128]{1,0:T(8,128)}, u32[]{:S(2)}) copy-start(f32[32,128]{1,0:T(8,128)} %param.16) | copy-start | bytes 49156
  51.6 4.7 %collective-permute-start.10 = (f32[32,128]{1,0:T(8,128)S(1)}, f32[32,128]{1,0:T(8,128)S(1)}, u32[]{:S(2)}, u32[]{:S(2)}) collective-permute-start(f32[32,128]{1,0:T(8,128)S(1)} %add.81), channel_id=1, source_target_pairs={{0,16},{4,20},{8,24},{12,28},{16,0},{20,4},{24,8},{28,12},{1,17},{... | collective-permute-start | bytes 49160 | tf_op jit(solution)/shard_map/ppermute | solution.py:55
  56.8 10.3 %collective-permute-start.11 = (f32[16,32,128]{2,1,0:T(8,128)S(1)}, f32[16,32,128]{2,1,0:T(8,128)S(1)}, u32[]{:S(2)}, u32[]{:S(2)}) collective-permute-start(f32[16,32,128]{2,1,0:T(8,128)S(1)} %get-tuple-element.18), channel_id=1, source_target_pairs={{8,0},{12,4},{16,8},{20,12},{24,16},{28,20},{0,24},{4,28},{9,1},{1... | collective-permute-start | bytes 786440 | tf_op jit(solution)/shard_map/ppermute | solution.py:22
  60.1 12.9 %collective-permute-start.14 = (f32[16,32,128]{2,1,0:T(8,128)S(1)}, f32[16,32,128]{2,1,0:T(8,128)S(1)}, u32[]{:S(2)}, u32[]{:S(2)}) collective-permute-start(f32[16,32,128]{2,1,0:T(8,128)S(1)} %get-tuple-element.19), channel_id=1, source_target_pairs={{24,0},{28,4},{0,8},{4,12},{8,16},{12,20},{16,24},{20,28},{25,1},{... | collective-permute-start | bytes 786440 | tf_op jit(solution)/shard_map/ppermute | solution.py:22
  60.1 17.6 %collective-permute-start.13 = (f32[16,32,128]{2,1,0:T(8,128)S(1)}, f32[16,32,128]{2,1,0:T(8,128)S(1)}, u32[]{:S(2)}, u32[]{:S(2)}) collective-permute-start(f32[16,32,128]{2,1,0:T(8,128)S(1)} %get-tuple-element.20), channel_id=1, source_target_pairs={{28,0},{0,4},{4,8},{8,12},{12,16},{16,20},{20,24},{24,28},{29,1},{... | collective-permute-start | bytes 786440 | tf_op jit(solution)/shard_map/ppermute | solution.py:22
  62.2 15.6 %collective-permute-start.12 = (f32[16,32,128]{2,1,0:T(8,128)S(1)}, f32[16,32,128]{2,1,0:T(8,128)S(1)}, u32[]{:S(2)}, u32[]{:S(2)}) collective-permute-start(f32[16,32,128]{2,1,0:T(8,128)S(1)} %get-tuple-element.21), channel_id=1, source_target_pairs={{4,0},{8,4},{12,8},{16,12},{20,16},{24,20},{28,24},{0,28},{5,1},{9... | collective-permute-start | bytes 786440 | tf_op jit(solution)/shard_map/ppermute | solution.py:22

commit v5 on v4

--- a/solution.py
+++ b/solution.py
@@ -141,7 +141,8 @@
     feature_grad = outgoing[REACH]
     for distance in range(-REACH, REACH + 1):
         if distance != 0:
-            feature_grad = feature_grad + passed_along(outgoing[distance + REACH], "node", distance)
+            sent = outgoing[distance + REACH].astype(jnp.bfloat16)
+            feature_grad = feature_grad + passed_along(sent, "node", distance).astype(jnp.float32)
     new_first = first_decay * first_moment + (1.0 - first_decay) * grad
     new_second = second_decay * second_moment + (1.0 - second_decay) * grad * grad
     new_weight = weight - learn_rate * (new_first / first_fix) / (

time: 78.9 us -> 72 us (0.913)
  waiting for transfers between devices: 19.1 us -> 13.8 us
  starting transfers between devices: 26 us -> 24.1 us
    ppermute x8, waiting for transfers between devices: 11 us -> 3.52 us  [passed_along(): return lax.ppermute(block, axis, route)]
    ppermute x3, waiting for transfers between devices: 0.97 us -> 3.13 us  [summed_over(): lax.ppermute(block, axis, [(i, i ^ mask) for i in range(size)])]
    ppermute x8, starting transfers between devices: 18.4 us -> 16.7 us  [passed_along(): return lax.ppermute(block, axis, route)]
  transfers between devices with their start and end apart: 15 -> 15, of which waited for: 9 -> 10; matrix products, arithmetic and copies ran while one was open for 22% -> 24% of each run, Pallas kernels for 0% -> 0%
where the time goes in v5:
time: 72 us; the launch traced here: 71.7 us
  matrix products  24.2 us (34%)
  starting transfers between devices  24.1 us (33%)
  waiting for transfers between devices  13.8 us (19%)
  other arithmetic  5.32 us (7%)
  local copies, waits for them, and re-layouts  2.66 us (4%)
  between operations  1.6 us (2%)
    ppermute x8, starting transfers between devices, passed_along(): return lax.ppermute(block, axis, route)  16.7 us
    dot_general x1, matrix products, per_device(): jnp.einsum('tfj,tjk->tfk', back_sources, tile_values, preferred_element_t...  7.38 us
    dot_general x1, matrix products, per_device(): jnp.einsum('tfk,tjk->tfj', sources, tile_values, preferred_element_type=j...  7.25 us
    ppermute x4, waiting for transfers between devices, gathered_along(): got = lax.ppermute(held, axis, [(i, i ^ mask) for i in range(size)])  7.12 us
    ppermute x3, starting transfers between devices, summed_over(): lax.ppermute(block, axis, [(i, i ^ mask) for i in range(size)])  4.17 us
    dot_general x1, matrix products, per_device(): jnp.einsum('ts,tfk->sfk', add_source, back_terms, precision=lax.Precision...  3.54 us
    ppermute x8, waiting for transfers between devices, passed_along(): return lax.ppermute(block, axis, route)  3.52 us
    ppermute x4, starting transfers between devices, gathered_along(): got = lax.ppermute(held, axis, [(i, i ^ mask) for i in range(size)])  3.31 us
  transfers between devices with their start and end apart: 15, of which 10 were waited for; matrix products, arithmetic and copies ran while one was open for 24% of the time, Pallas kernels for 0%

profile of v5, /device:TPU:0, one launch (start us, length us, event | category | flops | bytes accessed | tf_op | source)
XLA Modules:
  0.0 71.7 jit_solution(15222930768536670511)
XLA Ops:
  0.6 6.0 %collective-permute-start.2 = (bf16[16,32,128]{2,1,0:T(8,128)(2,1)}, bf16[16,32,128]{2,1,0:T(8,128)(2,1)S(1)}, u32[]{:S(2)}, u32[]{:S(2)}) collective-permute-start(bf16[16,32,128]{2,1,0:T(8,128)(2,1)} %param.9), channel_id=1, source_target_pairs={{4,0},{8,4},{12,8},{16,12},{20,16},{24,20},{28,24},{0,28},{5,1},{9... | collective-permute-start | bytes 393224 | tf_op jit(solution)/shard_map/ppermute | solution.py:22
  6.7 0.0 collective-permute-start.1
  6.7 0.0 collective-permute-start
  6.7 3.8 %collective-permute-start.3 = (bf16[16,32,128]{2,1,0:T(8,128)(2,1)}, bf16[16,32,128]{2,1,0:T(8,128)(2,1)S(1)}, u32[]{:S(2)}, u32[]{:S(2)}) collective-permute-start(bf16[16,32,128]{2,1,0:T(8,128)(2,1)} %param.9), channel_id=1, source_target_pairs={{8,0},{12,4},{16,8},{20,12},{24,16},{28,20},{0,24},{4,28},{9,1},{1... | collective-permute-start | bytes 393224 | tf_op jit(solution)/shard_map/ppermute | solution.py:22
  10.5 0.7 %convert_bitcast_fusion = bf16[1,32,128]{2,1,0:T(8,128)(2,1)S(1)} fusion(f32[32,128]{1,0:T(8,128)} %param.14), kind=kLoop, calls=%fused_computation.75 | loop fusion | flops 4096 | bytes 24576 | tf_op jit(solution)/shard_map/broadcast_in_dim | solution.py:105
  11.2 0.1 broadcast_in_dim.11
  11.3 1.0 %fusion.19 = (bf16[1,17,32,128]{3,2,1,0:T(8,128)(2,1)S(1)}, bf16[17,128,128]{2,1,0:T(8,128)(2,1)S(1)}) fusion(bf16[1,32,128]{2,1,0:T(8,128)(2,1)S(1)} %convert_bitcast_fusion, bf16[16,32,128]{2,1,0:T(8,128)(2,1)} %param.17, bf16[17,128,128]{2,1,0:T(8,128)(2,1)S(1)} %broadcast_in_dim.11, s32[]{:T(128)S(6)} %select_n.49), kind=kLoop, calls=%fused_computation.42 | loop fusion | flops 278528 | bytes 417796 | tf_op jit(solution)/shard_map/stack | solution.py:37
  12.3 1.6 %collective-permute-start.4 = (bf16[1,17,32,128]{3,2,1,0:T(8,128)(2,1)S(1)}, bf16[1,17,32,128]{3,2,1,0:T(8,128)(2,1)S(1)}, u32[]{:S(2)}, u32[]{:S(2)}) collective-permute-start(bf16[1,17,32,128]{3,2,1,0:T(8,128)(2,1)S(1)} %get-tuple-element.24), channel_id=1, source_target_pairs={{0,2},{1,3},{2,0},{3,1},{4,6},{5,7},{6,4},{7,5},{8,10},{9,11},{10,... | collective-permute-start | bytes 417800 | tf_op jit(solution)/shard_map/ppermute | solution.py:38
  13.9 0.7 fusion.42
  14.6 0.7 broadcast_subtract_fusion
  15.9 0.0 collective-permute-done
  16.0 0.1 collective-permute-done.1
  16.1 0.9 %constant_dynamic-update-slice_fusion.2 = bf16[80,32,128]{2,1,0:T(8,128)(2,1)S(1)} fusion(bf16[80,32,128]{2,1,0:T(8,128)(2,1)S(1)} %constant_dynamic-update-slice_fusion.3, bf16[16,32,128]{2,1,0:T(8,128)(2,1)} %param.9), kind=kLoop, calls=%fused_computation.66 | loop fusion | bytes 262144
  17.0 0.0 collective-permute-done.2
  17.1 0.3 collective-permute-done.4
  17.4 0.1 collective-permute-start.5
  17.5 0.0 collective-permute-done.3
  17.6 1.5 %collective-permute-done.5 = bf16[2,17,32,128]{3,2,1,0:T(8,128)(2,1)S(1)} collective-permute-done((bf16[2,17,32,128]{3,2,1,0:T(8,128)(2,1)S(1)}, bf16[2,17,32,128]{3,2,1,0:T(8,128)(2,1)S(1)}, u32[]{:S(2)}, u32[]{:S(2)}) %collective-permute-start.5) | collective-permute-done | bytes 278560 | tf_op jit(solution)/shard_map/ppermute | solution.py:38
  19.2 0.8 %fusion.10 = bf16[256,32,128]{2,0,1:T(8,128)(2,1)S(1)} fusion(bf16[80,32,128]{2,1,0:T(8,128)(2,1)S(1)} %constant_dynamic-update-slice_fusion, s32[256]{0:T(256)S(1)} %fusion.42), kind=kOutput, calls=%fused_computation.14 | convolution fusion | flops 167792640 | bytes 2753536 | tf_op jit(solution)/shard_map/ts,sfk->tfk/dot_general | solution.py:110
  19.9 7.2 %fusion.4 = f32[256,32,128]{2,1,0:T(8,128)S(1)} fusion(bf16[256,128,128]{2,1,0:T(8,128)(2,1)} %param.10, bf16[256,32,128]{2,0,1:T(8,128)(2,1)S(1)} %fusion.10), kind=kOutput, calls=%fused_computation.6 | convolution fusion | flops 268435456 | bytes 14680064 | tf_op jit(solution)/shard_map/tfk,tjk->tfj/dot_general | solution.py:113
  27.2 3.3 %fusion.7 = bf16[16,32,128]{2,0,1:T(8,128)(2,1)S(1)} fusion(f32[256,32,128]{2,1,0:T(8,128)S(1)} %fusion.4, f32[256]{0:T(256)S(1)} %compare_convert_fusion, s32[256]{0:T(256)S(1)} %broadcast_subtract_fusion), kind=kOutput, calls=%fused_computation.11 | convolution fusion | flops 100737024 | bytes 4327424 | tf_op jit(solution)/shard_map/tb,tfj->bfj/dot_general | solution.py:116
  30.5 0.0 copy-start
  30.5 1.6 %collective-permute-start.6 = (bf16[1,16,32,128]{3,1,2,0:T(8,128)(2,1)S(1)}, bf16[1,16,32,128]{3,1,2,0:T(8,128)(2,1)S(1)}, u32[]{:S(2)}, u32[]{:S(2)}) collective-permute-start(bf16[1,16,32,128]{3,1,2,0:T(8,128)(2,1)S(1)} %bitcast.75), channel_id=1, source_target_pairs={{0,2},{1,3},{2,0},{3,1},{4,6},{5,7},{6,4},{7,5},{8,10},{9,11},{10,... | collective-permute-start | bytes 393224 | tf_op jit(solution)/shard_map/ppermute | solution.py:38
  32.1 4.0 %collective-permute-done.6 = bf16[1,16,32,128]{3,1,2,0:T(8,128)(2,1)S(1)} collective-permute-done((bf16[1,16,32,128]{3,1,2,0:T(8,128)(2,1)S(1)}, bf16[1,16,32,128]{3,1,2,0:T(8,128)(2,1)S(1)}, u32[]{:S(2)}, u32[]{:S(2)}) %collective-permute-start.6) | collective-permute-done | bytes 131104 | tf_op jit(solution)/shard_map/ppermute | solution.py:38
  36.1 0.1 collective-permute-start.7
  36.2 0.1 broadcast_in_dim.13
  36.3 0.1 copy_dynamic-update-slice_fusion.3
  36.4 0.1 copy_dynamic-update-slice_fusion.2
  36.4 1.3 %collective-permute-done.7 = bf16[2,16,32,128]{3,1,2,0:T(8,128)(2,1)S(1)} collective-permute-done((bf16[2,16,32,128]{3,1,2,0:T(8,128)(2,1)S(1)}, bf16[2,16,32,128]{3,1,2,0:T(8,128)(2,1)S(1)}, u32[]{:S(2)}, u32[]{:S(2)}) %collective-permute-start.7) | collective-permute-done | bytes 262176 | tf_op jit(solution)/shard_map/ppermute | solution.py:38
  37.8 0.1 copy_dynamic-update-slice_fusion.1
  37.8 0.1 copy_dynamic-update-slice_fusion
  37.9 0.3 broadcast_compare_fusion
  38.2 0.4 convolution_bitcast_fusion.1
  38.6 0.0 copy-done
  38.6 0.5 fusion.6
  39.1 0.2 copy.26
  39.4 3.0 %collective-permute-start.8 = (f32[32,128]{1,0:T(8,128)S(1)}, f32[32,128]{1,0:T(8,128)S(1)}, u32[]{:S(2)}, u32[]{:S(2)}) collective-permute-start(f32[32,128]{1,0:T(8,128)S(1)} %convolution_bitcast_fusion.1), channel_id=1, source_target_pairs={{0,4},{4,0},{8,12},{12,8},{16,20},{20,16},{24,28},{28,24},{1,5},{5... | collective-permute-start | bytes 49160 | tf_op jit(solution)/shard_map/ppermute | solution.py:55
  42.4 0.7 %fusion.34 = bf16[256,32,128]{2,0,1:T(8,128)(2,1)S(1)} fusion(bf16[16,32,128]{2,0,1:T(8,128)(2,1)S(1)} %copy.26, s32[256]{0:T(256)S(1)} %broadcast_subtract_fusion), kind=kOutput, calls=%fused_computation.63 | convolution fusion | flops 33558528 | bytes 2229248 | tf_op jit(solution)/shard_map/tb,bfj->tfj/dot_general | solution.py:132
  43.2 7.4 %fusion.5 = f32[256,32,128]{2,1,0:T(8,128)S(1)} fusion(bf16[256,128,128]{2,1,0:T(8,128)(2,1)} %param.10, bf16[256,32,128]{2,0,1:T(8,128)(2,1)S(1)} %fusion.34), kind=kOutput, calls=%fused_computation.7 | convolution fusion | flops 268435456 | bytes 14680064 | tf_op jit(solution)/shard_map/tfj,tjk->tfk/dot_general | solution.py:135
  50.6 0.0 collective-permute-done.8
  50.6 0.1 collective-permute-start.9
  50.7 3.5 %fusion = f32[80,32,128]{2,0,1:T(8,128)S(1)} fusion(f32[256,32,128]{2,1,0:T(8,128)S(1)} %fusion.5, f32[256]{0:T(256)S(1)} %compare_convert_fusion, s32[256]{0:T(256)S(1)} %fusion.42), kind=kOutput, calls=%fused_computation | convolution fusion | flops 503357440 | bytes 5507072 | tf_op jit(solution)/shard_map/ts,tfk->sfk/dot_general | solution.py:138
  54.2 0.0 copy-start.1
  54.2 0.0 copy-start.2
  54.2 0.2 collective-permute-done.9
  54.4 1.1 %collective-permute-start.10 = (f32[32,128]{1,0:T(8,128)S(1)}, f32[32,128]{1,0:T(8,128)S(1)}, u32[]{:S(2)}, u32[]{:S(2)}) collective-permute-start(f32[32,128]{1,0:T(8,128)S(1)} %add.81), channel_id=1, source_target_pairs={{0,16},{4,20},{8,24},{12,28},{16,0},{20,4},{24,8},{28,12},{1,17},{... | collective-permute-start | bytes 49160 | tf_op jit(solution)/shard_map/ppermute | solution.py:55
  55.4 0.8 %select_convert_fusion = bf16[16,32,128]{2,1,0:T(8,128)(2,1)} fusion(f32[16,128,128]{2,1,0:T(8,128)S(1)} %get-tuple-element.27, s32[]{:T(128)S(6)} %select_n.49, pred[16,128,128]{2,1,0:T(8,128)(4,1)S(1)} %get-tuple-element.26), kind=kLoop, calls=%fused_computation.24 | loop fusion | flops 196608 | bytes 458756 | tf_op jit(solution)/shard_map/convert_element_type | solution.py:124
  56.2 3.0 %collective-permute-done.10 = f32[32,128]{1,0:T(8,128)S(1)} collective-permute-done((f32[32,128]{1,0:T(8,128)S(1)}, f32[32,128]{1,0:T(8,128)S(1)}, u32[]{:S(2)}, u32[]{:S(2)}) %collective-permute-start.10) | collective-permute-done | bytes 16416 | tf_op jit(solution)/shard_map/ppermute | solution.py:55
  59.2 0.4 copy.49
  59.6 0.4 copy.20
  60.1 1.3 %collective-permute-start.11 = (bf16[16,32,128]{2,1,0:T(8,128)(2,1)S(1)}, bf16[16,32,128]{2,1,0:T(8,128)(2,1)S(1)}, u32[]{:S(2)}, u32[]{:S(2)}) collective-permute-start(bf16[16,32,128]{2,1,0:T(8,128)(2,1)S(1)} %get-tuple-element.18), channel_id=1, source_target_pairs={{8,0},{12,4},{16,8},{20,12},{24,16},{28,20},{0,24},{4,28},{9,1},{1... | collective-permute-start | bytes 393224 | tf_op jit(solution)/shard_map/ppermute | solution.py:22
  61.4 0.8 %collective-permute-start.14 = (bf16[16,32,128]{2,1,0:T(8,128)(2,1)S(1)}, bf16[16,32,128]{2,1,0:T(8,128)(2,1)S(1)}, u32[]{:S(2)}, u32[]{:S(2)}) collective-permute-start(bf16[16,32,128]{2,1,0:T(8,128)(2,1)S(1)} %get-tuple-element.19), channel_id=1, source_target_pairs={{24,0},{28,4},{0,8},{4,12},{8,16},{12,20},{16,24},{20,28},{25,1},{... | collective-permute-start | bytes 393224 | tf_op jit(solution)/shard_map/ppermute | solution.py:22
  62.2 0.0 collective-permute-start.13
  62.2 4.7 %collective-permute-start.12 = (bf16[16,32,128]{2,1,0:T(8,128)(2,1)S(1)}, bf16[16,32,128]{2,1,0:T(8,128)(2,1)S(1)}, u32[]{:S(2)}, u32[]{:S(2)}) collective-permute-start(bf16[16,32,128]{2,1,0:T(8,128)(2,1)S(1)} %get-tuple-element.21), channel_id=1, source_target_pairs={{4,0},{8,4},{12,8},{16,12},{20,16},{24,20},{28,24},{0,28},{5,1},{9... | collective-permute-start | bytes 393224 | tf_op jit(solution)/shard_map/ppermute | solution.py:22
  66.9 0.0 copy-done.1
  66.9 0.0 copy-done.2
  66.9 0.6 divide_subtract_fusion
  67.5 0.0 collective-permute-done.11
  67.5 2.1 %collective-permute-done.14 = bf16[16,32,128]{2,1,0:T(8,128)(2,1)S(1)} collective-permute-done((bf16[16,32,128]{2,1,0:T(8,128)(2,1)S(1)}, bf16[16,32,128]{2,1,0:T(8,128)(2,1)S(1)}, u32[]{:S(2)}, u32[]{:S(2)}) %collective-permute-start.14) | collective-permute-done | bytes 131104 | tf_op jit(solution)/shard_map/ppermute | solution.py:22
  69.6 1.1 %collective-permute-done.13 = bf16[16,32,128]{2,1,0:T(8,128)(2,1)S(1)} collective-permute-done((bf16[16,32,128]{2,1,0:T(8,128)(2,1)S(1)}, bf16[16,32,128]{2,1,0:T(8,128)(2,1)S(1)}, u32[]{:S(2)}, u32[]{:S(2)}) %collective-permute-start.13) | collective-permute-done | bytes 131104 | tf_op jit(solution)/shard_map/ppermute | solution.py:22
  70.7 0.2 collective-permute-done.12
  70.9 0.8 %fusion.15 = f32[16,32,128]{2,1,0:T(8,128)} fusion(f32[5,16,32,128]{3,2,1,0:T(8,128)S(1)} %copy.20, bf16[16,32,128]{2,1,0:T(8,128)(2,1)S(1)} %collective-permute-done.14, bf16[16,32,128]{2,1,0:T(8,128)(2,1)S(1)} %collective-permute-done.13, bf16[16,32,128]{2,1,0:T(8,128)(2,1)S(1)} %collective-permute-done.12, bf16[16,32,128]{2,1,0:T(8,128)(2,1)S(1)} %collective-permute-done.11), kind=kLoop, calls=%fused_computation.22 | loop fusion | flops 524288 | bytes 1048576 | tf_op jit(solution)/shard_map/add | solution.py:145
  (17 shorter events, 0.3 us)
Async XLA Ops:
  0.6 16.4 %collective-permute-start.2 = (bf16[16,32,128]{2,1,0:T(8,128)(2,1)}, bf16[16,32,128]{2,1,0:T(8,128)(2,1)S(1)}, u32[]{:S(2)}, u32[]{:S(2)}) collective-permute-start(bf16[16,32,128]{2,1,0:T(8,128)(2,1)} %param.9), channel_id=1, source_target_pairs={{4,0},{8,4},{12,8},{16,12},{20,16},{24,20},{28,24},{0,28},{5,1},{9... | collective-permute-start | bytes 393224 | tf_op jit(solution)/shard_map/ppermute | solution.py:22
  6.7 9.4 %collective-permute-start.1 = (bf16[16,32,128]{2,1,0:T(8,128)(2,1)}, bf16[16,32,128]{2,1,0:T(8,128)(2,1)S(1)}, u32[]{:S(2)}, u32[]{:S(2)}) collective-permute-start(bf16[16,32,128]{2,1,0:T(8,128)(2,1)} %param.9), channel_id=1, source_target_pairs={{28,0},{0,4},{4,8},{8,12},{12,16},{16,20},{20,24},{24,28},{29,1},{... | collective-permute-start | bytes 393224 | tf_op jit(solution)/shard_map/ppermute | solution.py:22
  6.7 9.3 %collective-permute-start = (bf16[16,32,128]{2,1,0:T(8,128)(2,1)}, bf16[16,32,128]{2,1,0:T(8,128)(2,1)S(1)}, u32[]{:S(2)}, u32[]{:S(2)}) collective-permute-start(bf16[16,32,128]{2,1,0:T(8,128)(2,1)} %param.9), channel_id=1, source_target_pairs={{24,0},{28,4},{0,8},{4,12},{8,16},{12,20},{16,24},{20,28},{25,1},{... | collective-permute-start | bytes 393224 | tf_op jit(solution)/shard_map/ppermute | solution.py:22
  6.7 10.9 %collective-permute-start.3 = (bf16[16,32,128]{2,1,0:T(8,128)(2,1)}, bf16[16,32,128]{2,1,0:T(8,128)(2,1)S(1)}, u32[]{:S(2)}, u32[]{:S(2)}) collective-permute-start(bf16[16,32,128]{2,1,0:T(8,128)(2,1)} %param.9), channel_id=1, source_target_pairs={{8,0},{12,4},{16,8},{20,12},{24,16},{28,20},{0,24},{4,28},{9,1},{1... | collective-permute-start | bytes 393224 | tf_op jit(solution)/shard_map/ppermute | solution.py:22
  12.3 5.1 %collective-permute-start.4 = (bf16[1,17,32,128]{3,2,1,0:T(8,128)(2,1)S(1)}, bf16[1,17,32,128]{3,2,1,0:T(8,128)(2,1)S(1)}, u32[]{:S(2)}, u32[]{:S(2)}) collective-permute-start(bf16[1,17,32,128]{3,2,1,0:T(8,128)(2,1)S(1)} %get-tuple-element.24), channel_id=1, source_target_pairs={{0,2},{1,3},{2,0},{3,1},{4,6},{5,7},{6,4},{7,5},{8,10},{9,11},{10,... | collective-permute-start | bytes 417800 | tf_op jit(solution)/shard_map/ppermute | solution.py:38
  17.4 1.6 %collective-permute-start.5 = (bf16[2,17,32,128]{3,2,1,0:T(8,128)(2,1)S(1)}, bf16[2,17,32,128]{3,2,1,0:T(8,128)(2,1)S(1)}, u32[]{:S(2)}, u32[]{:S(2)}) collective-permute-start(bf16[2,17,32,128]{3,2,1,0:T(8,128)(2,1)S(1)} %pad_maximum_fusion), channel_id=1, source_target_pairs={{0,1},{1,0},{2,3},{3,2},{4,5},{5,4},{6,7},{7,6},{8,9},{9,8},{10,11... | collective-permute-start | bytes 835592 | tf_op jit(solution)/shard_map/ppermute | solution.py:38
  30.5 8.1 %copy-start = (f32[32,128]{1,0:T(8,128)S(1)}, f32[32,128]{1,0:T(8,128)}, u32[]{:S(2)}) copy-start(f32[32,128]{1,0:T(8,128)} %param.14) | copy-start | bytes 49156
  30.5 5.6 %collective-permute-start.6 = (bf16[1,16,32,128]{3,1,2,0:T(8,128)(2,1)S(1)}, bf16[1,16,32,128]{3,1,2,0:T(8,128)(2,1)S(1)}, u32[]{:S(2)}, u32[]{:S(2)}) collective-permute-start(bf16[1,16,32,128]{3,1,2,0:T(8,128)(2,1)S(1)} %bitcast.75), channel_id=1, source_target_pairs={{0,2},{1,3},{2,0},{3,1},{4,6},{5,7},{6,4},{7,5},{8,10},{9,11},{10,... | collective-permute-start | bytes 393224 | tf_op jit(solution)/shard_map/ppermute | solution.py:38
  36.1 1.6 %collective-permute-start.7 = (bf16[2,16,32,128]{3,1,2,0:T(8,128)(2,1)S(1)}, bf16[2,16,32,128]{3,1,2,0:T(8,128)(2,1)S(1)}, u32[]{:S(2)}, u32[]{:S(2)}) collective-permute-start(bf16[2,16,32,128]{3,1,2,0:T(8,128)(2,1)S(1)} %pad_maximum_fusion.1), channel_id=1, source_target_pairs={{0,1},{1,0},{2,3},{3,2},{4,5},{5,4},{6,7},{7,6},{8,9},{9,8},{10,11... | collective-permute-start | bytes 786440 | tf_op jit(solution)/shard_map/ppermute | solution.py:38
  39.4 11.2 %collective-permute-start.8 = (f32[32,128]{1,0:T(8,128)S(1)}, f32[32,128]{1,0:T(8,128)S(1)}, u32[]{:S(2)}, u32[]{:S(2)}) collective-permute-start(f32[32,128]{1,0:T(8,128)S(1)} %convolution_bitcast_fusion.1), channel_id=1, source_target_pairs={{0,4},{4,0},{8,12},{12,8},{16,20},{20,16},{24,28},{28,24},{1,5},{5... | collective-permute-start | bytes 49160 | tf_op jit(solution)/shard_map/ppermute | solution.py:55
  50.6 3.8 %collective-permute-start.9 = (f32[32,128]{1,0:T(8,128)S(1)}, f32[32,128]{1,0:T(8,128)S(1)}, u32[]{:S(2)}, u32[]{:S(2)}) collective-permute-start(f32[32,128]{1,0:T(8,128)S(1)} %add.80), channel_id=1, source_target_pairs={{0,8},{4,12},{8,0},{12,4},{16,24},{20,28},{24,16},{28,20},{1,9},{5... | collective-permute-start | bytes 49160 | tf_op jit(solution)/shard_map/ppermute | solution.py:55
  54.2 12.7 %copy-start.1 = (f32[32,128]{1,0:T(8,128)S(1)}, f32[32,128]{1,0:T(8,128)}, u32[]{:S(2)}) copy-start(f32[32,128]{1,0:T(8,128)} %param.15) | copy-start | bytes 49156
  54.2 12.7 %copy-start.2 = (f32[32,128]{1,0:T(8,128)S(1)}, f32[32,128]{1,0:T(8,128)}, u32[]{:S(2)}) copy-start(f32[32,128]{1,0:T(8,128)} %param.16) | copy-start | bytes 49156
  54.4 4.8 %collective-permute-start.10 = (f32[32,128]{1,0:T(8,128)S(1)}, f32[32,128]{1,0:T(8,128)S(1)}, u32[]{:S(2)}, u32[]{:S(2)}) collective-permute-start(f32[32,128]{1,0:T(8,128)S(1)} %add.81), channel_id=1, source_target_pairs={{0,16},{4,20},{8,24},{12,28},{16,0},{20,4},{24,8},{28,12},{1,17},{... | collective-permute-start | bytes 49160 | tf_op jit(solution)/shard_map/ppermute | solution.py:55
  60.1 7.4 %collective-permute-start.11 = (bf16[16,32,128]{2,1,0:T(8,128)(2,1)S(1)}, bf16[16,32,128]{2,1,0:T(8,128)(2,1)S(1)}, u32[]{:S(2)}, u32[]{:S(2)}) collective-permute-start(bf16[16,32,128]{2,1,0:T(8,128)(2,1)S(1)} %get-tuple-element.18), channel_id=1, source_target_pairs={{8,0},{12,4},{16,8},{20,12},{24,16},{28,20},{0,24},{4,28},{9,1},{1... | collective-permute-start | bytes 393224 | tf_op jit(solution)/shard_map/ppermute | solution.py:22
  61.4 8.2 %collective-permute-start.14 = (bf16[16,32,128]{2,1,0:T(8,128)(2,1)S(1)}, bf16[16,32,128]{2,1,0:T(8,128)(2,1)S(1)}, u32[]{:S(2)}, u32[]{:S(2)}) collective-permute-start(bf16[16,32,128]{2,1,0:T(8,128)(2,1)S(1)} %get-tuple-element.19), channel_id=1, source_target_pairs={{24,0},{28,4},{0,8},{4,12},{8,16},{12,20},{16,24},{20,28},{25,1},{... | collective-permute-start | bytes 393224 | tf_op jit(solution)/shard_map/ppermute | solution.py:22
  62.2 8.5 %collective-permute-start.13 = (bf16[16,32,128]{2,1,0:T(8,128)(2,1)S(1)}, bf16[16,32,128]{2,1,0:T(8,128)(2,1)S(1)}, u32[]{:S(2)}, u32[]{:S(2)}) collective-permute-start(bf16[16,32,128]{2,1,0:T(8,128)(2,1)S(1)} %get-tuple-element.20), channel_id=1, source_target_pairs={{28,0},{0,4},{4,8},{8,12},{12,16},{16,20},{20,24},{24,28},{29,1},{... | collective-permute-start | bytes 393224 | tf_op jit(solution)/shard_map/ppermute | solution.py:22
  62.2 8.7 %collective-permute-start.12 = (bf16[16,32,128]{2,1,0:T(8,128)(2,1)S(1)}, bf16[16,32,128]{2,1,0:T(8,128)(2,1)S(1)}, u32[]{:S(2)}, u32[]{:S(2)}) collective-permute-start(bf16[16,32,128]{2,1,0:T(8,128)(2,1)S(1)} %get-tuple-element.21), channel_id=1, source_target_pairs={{4,0},{8,4},{12,8},{16,12},{20,16},{24,20},{28,24},{0,28},{5,1},{9... | collective-permute-start | bytes 393224 | tf_op jit(solution)/shard_map/ppermute | solution.py:22

commit v6 on v5

--- a/solution.py
+++ b/solution.py
@@ -57,6 +57,14 @@
     return block
 
 
+def summed_by_table(table, terms, spec):
+    high = terms.astype(jnp.bfloat16)
+    low = (terms - high.astype(jnp.float32)).astype(jnp.bfloat16)
+    both = jnp.concatenate([high, low], axis=0)
+    doubled = jnp.concatenate([table, table], axis=0).astype(jnp.bfloat16)
+    return jnp.einsum(spec, doubled, both, preferred_element_type=jnp.float32)
+
+
 def elu_slope(preact):
     return jnp.where(preact > 0, 1.0, jnp.exp(jnp.minimum(preact, 0.0)))
 
@@ -113,7 +121,7 @@
     forward_terms = jnp.einsum(
         "tfk,tjk->tfj", sources, tile_values, preferred_element_type=jnp.float32
     )
-    aggregate = jnp.einsum("tb,tfj->bfj", add_row, forward_terms, precision=lax.Precision.HIGH)
+    aggregate = summed_by_table(add_row, forward_terms, "tb,tfj->bfj")
     aggregate = aggregate.astype(jnp.bfloat16)
     aggregate_all = gathered_along(aggregate, "feat", 1)
     column_start = lax.axis_index("feat") * width_local
@@ -135,7 +143,7 @@
     back_terms = jnp.einsum(
         "tfj,tjk->tfk", back_sources, tile_values, preferred_element_type=jnp.float32
     )
-    outgoing = jnp.einsum("ts,tfk->sfk", add_source, back_terms, precision=lax.Precision.HIGH)
+    outgoing = summed_by_table(add_source, back_terms, "ts,tfk->sfk")
     outgoing = outgoing.reshape(2 * REACH + 1, blocks, width_local, tile_size)
     outgoing, grad = lax.optimization_barrier((outgoing, grad))
     feature_grad = outgoing[REACH]

time: 72 us -> 68.6 us (0.953)
  matrix products: 24.2 us -> 19.3 us
  waiting for transfers between devices: 13.8 us -> 15.6 us
  starting transfers between devices: 24.1 us -> 23 us
  other arithmetic: 5.32 us -> 6.09 us
    dot_general x2, matrix products: 6.83 us -> 2.69 us  [summed_by_table(): return jnp.einsum(spec, doubled, both, preferred_element_type=jnp.float32)]
    ppermute x3, waiting for transfers between devices: 3.13 us -> 6.1 us  [summed_over(): lax.ppermute(block, axis, [(i, i ^ mask) for i in range(size)])]
    dot_general x1, matrix products: 7.38 us -> 5.99 us  [per_device(): jnp.einsum('tfj,tjk->tfk', back_sources, tile_values, preferred_element_t...]
    ppermute x8, waiting for transfers between devices: 3.52 us -> 2.43 us  [passed_along(): return lax.ppermute(block, axis, route)]
    ppermute x3, starting transfers between devices: 4.17 us -> 3.12 us  [summed_over(): lax.ppermute(block, axis, [(i, i ^ mask) for i in range(size)])]
    concatenate x0 -> x2, other arithmetic: none -> 0.73 us  [summed_by_table(): both = jnp.concatenate([high, low], axis=0)]
  transfers between devices with their start and end apart: 15 -> 15, of which waited for: 10 -> 9; matrix products, arithmetic and copies ran while one was open for 24% -> 21% of each run, Pallas kernels for 0% -> 0%
where the time goes in v6:
time: 68.6 us; the launch traced here: 68.3 us
  starting transfers between devices  23 us (34%)
  matrix products  19.3 us (28%)
  waiting for transfers between devices  15.6 us (23%)
  other arithmetic  6.09 us (9%)
  local copies, waits for them, and re-layouts  2.65 us (4%)
  between operations  1.59 us (2%)
    ppermute x8, starting transfers between devices, passed_along(): return lax.ppermute(block, axis, route)  16.7 us
    dot_general x1, matrix products, per_device(): jnp.einsum('tfk,tjk->tfj', sources, tile_values, preferred_element_type=j...  7.88 us
    ppermute x4, waiting for transfers between devices, gathered_along(): got = lax.ppermute(held, axis, [(i, i ^ mask) for i in range(size)])  7.11 us
    ppermute x3, waiting for transfers between devices, summed_over(): lax.ppermute(block, axis, [(i, i ^ mask) for i in range(size)])  6.1 us
    dot_general x1, matrix products, per_device(): jnp.einsum('tfj,tjk->tfk', back_sources, tile_values, preferred_element_t...  5.99 us
    ppermute x4, starting transfers between devices, gathered_along(): got = lax.ppermute(held, axis, [(i, i ^ mask) for i in range(size)])  3.26 us
    ppermute x3, starting transfers between devices, summed_over(): lax.ppermute(block, axis, [(i, i ^ mask) for i in range(size)])  3.12 us
    dot_general x2, matrix products, summed_by_table(): return jnp.einsum(spec, doubled, both, preferred_element_type=jnp.float32)  2.69 us
  transfers between devices with their start and end apart: 15, of which 9 were waited for; matrix products, arithmetic and copies ran while one was open for 21% of the time, Pallas kernels for 0%

profile of v6, /device:TPU:0, one launch (start us, length us, event | category | flops | bytes accessed | tf_op | source)
XLA Modules:
  0.0 68.3 jit_solution(7511429393297703581)
XLA Ops:
  0.6 6.0 %collective-permute-start.2 = (bf16[16,32,128]{2,1,0:T(8,128)(2,1)}, bf16[16,32,128]{2,1,0:T(8,128)(2,1)S(1)}, u32[]{:S(2)}, u32[]{:S(2)}) collective-permute-start(bf16[16,32,128]{2,1,0:T(8,128)(2,1)} %param.9), channel_id=1, source_target_pairs={{4,0},{8,4},{12,8},{16,12},{20,16},{24,20},{28,24},{0,28},{5,1},{9... | collective-permute-start | bytes 393224 | tf_op jit(solution)/shard_map/ppermute | solution.py:22
  6.7 0.0 collective-permute-start.1
  6.7 0.0 collective-permute-start
  6.7 3.8 %collective-permute-start.3 = (bf16[16,32,128]{2,1,0:T(8,128)(2,1)}, bf16[16,32,128]{2,1,0:T(8,128)(2,1)S(1)}, u32[]{:S(2)}, u32[]{:S(2)}) collective-permute-start(bf16[16,32,128]{2,1,0:T(8,128)(2,1)} %param.9), channel_id=1, source_target_pairs={{8,0},{12,4},{16,8},{20,12},{24,16},{28,20},{0,24},{4,28},{9,1},{1... | collective-permute-start | bytes 393224 | tf_op jit(solution)/shard_map/ppermute | solution.py:22
  10.5 0.7 %convert_bitcast_fusion = bf16[1,32,128]{2,1,0:T(8,128)(2,1)S(1)} fusion(f32[32,128]{1,0:T(8,128)} %param.14), kind=kLoop, calls=%fused_computation.77 | loop fusion | flops 4096 | bytes 24576 | tf_op jit(solution)/shard_map/broadcast_in_dim | solution.py:113
  11.2 0.1 broadcast_in_dim.11
  11.3 1.0 %fusion.19 = (bf16[1,17,32,128]{3,2,1,0:T(8,128)(2,1)S(1)}, bf16[17,128,128]{2,1,0:T(8,128)(2,1)S(1)}) fusion(bf16[1,32,128]{2,1,0:T(8,128)(2,1)S(1)} %convert_bitcast_fusion, bf16[16,32,128]{2,1,0:T(8,128)(2,1)} %param.17, bf16[17,128,128]{2,1,0:T(8,128)(2,1)S(1)} %broadcast_in_dim.11, s32[]{:T(128)S(6)} %select_n.49), kind=kLoop, calls=%fused_computation.46 | loop fusion | flops 278528 | bytes 417796 | tf_op jit(solution)/shard_map/stack | solution.py:37
  12.3 1.6 %collective-permute-start.4 = (bf16[1,17,32,128]{3,2,1,0:T(8,128)(2,1)S(1)}, bf16[1,17,32,128]{3,2,1,0:T(8,128)(2,1)S(1)}, u32[]{:S(2)}, u32[]{:S(2)}) collective-permute-start(bf16[1,17,32,128]{3,2,1,0:T(8,128)(2,1)S(1)} %get-tuple-element.28), channel_id=1, source_target_pairs={{0,2},{1,3},{2,0},{3,1},{4,6},{5,7},{6,4},{7,5},{8,10},{9,11},{10,... | collective-permute-start | bytes 417800 | tf_op jit(solution)/shard_map/ppermute | solution.py:38
  14.5 0.7 %broadcast_subtract_fusion = s32[256]{0:T(256)S(1)} fusion(s32[256]{0:T(256)} %param.11, s32[]{:T(128)S(6)} %mul.86), kind=kLoop, calls=%fused_computation.92 | loop fusion | flops 256 | bytes 2052 | tf_op jit(solution)/shard_map/sub | solution.py:94
  15.2 0.7 %fusion.36 = s32[256]{0:T(256)S(1)} fusion(s32[256]{0:T(256)} %param.12, s32[]{:T(128)S(6)} %axis_index.33), kind=kLoop, calls=%fused_computation.88 | loop fusion | flops 9472 | bytes 2052 | tf_op jit(solution)/shard_map/add | solution.py:99
  15.9 0.0 collective-permute-done
  16.0 0.1 collective-permute-done.1
  16.1 0.9 %constant_dynamic-update-slice_fusion.2 = bf16[80,32,128]{2,1,0:T(8,128)(2,1)S(1)} fusion(bf16[80,32,128]{2,1,0:T(8,128)(2,1)S(1)} %constant_dynamic-update-slice_fusion.3, bf16[16,32,128]{2,1,0:T(8,128)(2,1)} %param.9), kind=kLoop, calls=%fused_computation.71 | loop fusion | bytes 262144
  17.0 0.0 collective-permute-done.2
  17.1 0.3 collective-permute-done.4
  17.4 0.1 collective-permute-start.5
  17.5 0.0 collective-permute-done.3
  17.6 1.5 %collective-permute-done.5 = bf16[2,17,32,128]{3,2,1,0:T(8,128)(2,1)S(1)} collective-permute-done((bf16[2,17,32,128]{3,2,1,0:T(8,128)(2,1)S(1)}, bf16[2,17,32,128]{3,2,1,0:T(8,128)(2,1)S(1)}, u32[]{:S(2)}, u32[]{:S(2)}) %collective-permute-start.5) | collective-permute-done | bytes 278560 | tf_op jit(solution)/shard_map/ppermute | solution.py:38
  19.2 0.8 %fusion.10 = bf16[256,32,128]{2,0,1:T(8,128)(2,1)S(1)} fusion(bf16[80,32,128]{2,1,0:T(8,128)(2,1)S(1)} %constant_dynamic-update-slice_fusion, s32[256]{0:T(256)S(1)} %fusion.36), kind=kOutput, calls=%fused_computation.18 | convolution fusion | flops 167792640 | bytes 2753536 | tf_op jit(solution)/shard_map/ts,sfk->tfk/dot_general | solution.py:118
  19.9 7.9 %subtract_convert_fusion.1 = (bf16[256,32,128]{2,1,0:T(8,128)(2,1)S(1)}, bf16[256,32,128]{2,1,0:T(8,128)(2,1)S(1)}) fusion(bf16[256,128,128]{2,1,0:T(8,128)(2,1)} %param.10, bf16[256,32,128]{2,0,1:T(8,128)(2,1)S(1)} %fusion.10), kind=kOutput, calls=%fused_computation.9 | convolution fusion | flops 272629760 | bytes 14680064 | tf_op jit(solution)/shard_map/tfk,tjk->tfj/dot_general | solution.py:121
  27.8 0.4 pad_maximum_fusion
  28.2 1.2 %fusion.7 = bf16[16,32,128]{2,0,1:T(8,128)(2,1)S(1)} fusion(bf16[512,32,128]{2,1,0:T(8,128)(2,1)S(1)} %pad_maximum_fusion, bf16[256,16]{0,1:T(8,128)(2,1)S(1)} %select_convert_fusion.2), kind=kOutput, calls=%fused_computation.15 | convolution fusion | flops 67207168 | bytes 4333568 | tf_op jit(solution)/shard_map/tb,tfj->bfj/dot_general | solution.py:65
  29.4 0.0 copy-start
  29.4 1.5 %collective-permute-start.6 = (bf16[1,16,32,128]{3,1,2,0:T(8,128)(2,1)S(1)}, bf16[1,16,32,128]{3,1,2,0:T(8,128)(2,1)S(1)}, u32[]{:S(2)}, u32[]{:S(2)}) collective-permute-start(bf16[1,16,32,128]{3,1,2,0:T(8,128)(2,1)S(1)} %bitcast.75), channel_id=1, source_target_pairs={{0,2},{1,3},{2,0},{3,1},{4,6},{5,7},{6,4},{7,5},{8,10},{9,11},{10,... | collective-permute-start | bytes 393224 | tf_op jit(solution)/shard_map/ppermute | solution.py:38
  31.0 4.0 %collective-permute-done.6 = bf16[1,16,32,128]{3,1,2,0:T(8,128)(2,1)S(1)} collective-permute-done((bf16[1,16,32,128]{3,1,2,0:T(8,128)(2,1)S(1)}, bf16[1,16,32,128]{3,1,2,0:T(8,128)(2,1)S(1)}, u32[]{:S(2)}, u32[]{:S(2)}) %collective-permute-start.6) | collective-permute-done | bytes 131104 | tf_op jit(solution)/shard_map/ppermute | solution.py:38
  35.0 0.1 collective-permute-start.7
  35.1 0.1 broadcast_in_dim.13
  35.2 0.1 copy_dynamic-update-slice_fusion.3
  35.3 0.1 copy_dynamic-update-slice_fusion.2
  35.3 1.3 %collective-permute-done.7 = bf16[2,16,32,128]{3,1,2,0:T(8,128)(2,1)S(1)} collective-permute-done((bf16[2,16,32,128]{3,1,2,0:T(8,128)(2,1)S(1)}, bf16[2,16,32,128]{3,1,2,0:T(8,128)(2,1)S(1)}, u32[]{:S(2)}, u32[]{:S(2)}) %collective-permute-start.7) | collective-permute-done | bytes 262176 | tf_op jit(solution)/shard_map/ppermute | solution.py:38
  36.6 0.1 copy_dynamic-update-slice_fusion.1
  36.7 0.1 copy_dynamic-update-slice_fusion
  36.8 0.3 broadcast_compare_fusion
  37.1 0.4 convolution_bitcast_fusion.1
  37.5 0.0 copy-done
  37.5 0.5 fusion.6
  38.0 0.2 copy.27
  38.3 3.0 %collective-permute-start.8 = (f32[32,128]{1,0:T(8,128)S(1)}, f32[32,128]{1,0:T(8,128)S(1)}, u32[]{:S(2)}, u32[]{:S(2)}) collective-permute-start(f32[32,128]{1,0:T(8,128)S(1)} %convolution_bitcast_fusion.1), channel_id=1, source_target_pairs={{0,4},{4,0},{8,12},{12,8},{16,20},{20,16},{24,28},{28,24},{1,5},{5... | collective-permute-start | bytes 49160 | tf_op jit(solution)/shard_map/ppermute | solution.py:55
  41.3 0.7 %fusion.31 = bf16[256,32,128]{2,0,1:T(8,128)(2,1)S(1)} fusion(bf16[16,32,128]{2,0,1:T(8,128)(2,1)S(1)} %copy.27, s32[256]{0:T(256)S(1)} %broadcast_subtract_fusion), kind=kOutput, calls=%fused_computation.68 | convolution fusion | flops 33558528 | bytes 2229248 | tf_op jit(solution)/shard_map/tb,bfj->tfj/dot_general | solution.py:140
  42.1 6.0 %subtract_convert_fusion = (bf16[256,32,128]{2,1,0:T(8,128)(2,1)S(1)}, bf16[256,32,128]{2,1,0:T(8,128)(2,1)S(1)}) fusion(bf16[256,128,128]{2,1,0:T(8,128)(2,1)} %param.10, bf16[256,32,128]{2,0,1:T(8,128)(2,1)S(1)} %fusion.31), kind=kOutput, calls=%fused_computation.8 | convolution fusion | flops 272629760 | bytes 14680064 | tf_op jit(solution)/shard_map/tfj,tjk->tfk/dot_general | solution.py:143
  48.1 0.4 pad_maximum_fusion.1
  48.4 0.0 collective-permute-done.8
  48.4 0.1 collective-permute-start.9
  48.5 1.5 %fusion = f32[80,32,128]{2,0,1:T(8,128)S(1)} fusion(bf16[512,32,128]{2,1,0:T(8,128)(2,1)S(1)} %pad_maximum_fusion.1, bf16[256,80]{0,1:T(8,128)(2,1)S(1)} %select_convert_fusion.1), kind=kOutput, calls=%fused_computation.4 | convolution fusion | flops 335708160 | bytes 5545984 | tf_op jit(solution)/shard_map/ts,tfk->sfk/dot_general | solution.py:65
  50.0 0.0 copy-start.1
  50.0 0.0 copy-start.2
  50.0 2.2 %collective-permute-done.9 = f32[32,128]{1,0:T(8,128)S(1)} collective-permute-done((f32[32,128]{1,0:T(8,128)S(1)}, f32[32,128]{1,0:T(8,128)S(1)}, u32[]{:S(2)}, u32[]{:S(2)}) %collective-permute-start.9) | collective-permute-done | bytes 16416 | tf_op jit(solution)/shard_map/ppermute | solution.py:55
  52.3 0.0 collective-permute-start.10
  52.3 0.8 %select_convert_fusion = bf16[16,32,128]{2,1,0:T(8,128)(2,1)} fusion(f32[16,128,128]{2,1,0:T(8,128)S(1)} %get-tuple-element.31, s32[]{:T(128)S(6)} %select_n.49, pred[16,128,128]{2,1,0:T(8,128)(4,1)S(1)} %get-tuple-element.30), kind=kLoop, calls=%fused_computation.28 | loop fusion | flops 196608 | bytes 458756 | tf_op jit(solution)/shard_map/convert_element_type | solution.py:132
  53.0 3.8 %collective-permute-done.10 = f32[32,128]{1,0:T(8,128)S(1)} collective-permute-done((f32[32,128]{1,0:T(8,128)S(1)}, f32[32,128]{1,0:T(8,128)S(1)}, u32[]{:S(2)}, u32[]{:S(2)}) %collective-permute-start.10) | collective-permute-done | bytes 16416 | tf_op jit(solution)/shard_map/ppermute | solution.py:55
  56.9 0.4 copy.49
  57.3 0.4 copy.22
  57.8 0.6 collective-permute-start.11
  58.4 1.4 %collective-permute-start.14 = (bf16[16,32,128]{2,1,0:T(8,128)(2,1)S(1)}, bf16[16,32,128]{2,1,0:T(8,128)(2,1)S(1)}, u32[]{:S(2)}, u32[]{:S(2)}) collective-permute-start(bf16[16,32,128]{2,1,0:T(8,128)(2,1)S(1)} %get-tuple-element.23), channel_id=1, source_target_pairs={{24,0},{28,4},{0,8},{4,12},{8,16},{12,20},{16,24},{20,28},{25,1},{... | collective-permute-start | bytes 393224 | tf_op jit(solution)/shard_map/ppermute | solution.py:22
  59.9 0.0 collective-permute-start.13
  59.9 4.7 %collective-permute-start.12 = (bf16[16,32,128]{2,1,0:T(8,128)(2,1)S(1)}, bf16[16,32,128]{2,1,0:T(8,128)(2,1)S(1)}, u32[]{:S(2)}, u32[]{:S(2)}) collective-permute-start(bf16[16,32,128]{2,1,0:T(8,128)(2,1)S(1)} %get-tuple-element.25), channel_id=1, source_target_pairs={{4,0},{8,4},{12,8},{16,12},{20,16},{24,20},{28,24},{0,28},{5,1},{9... | collective-permute-start | bytes 393224 | tf_op jit(solution)/shard_map/ppermute | solution.py:22
  64.6 0.0 copy-done.1
  64.6 0.0 copy-done.2
  64.6 0.6 divide_subtract_fusion
  65.2 0.0 collective-permute-done.11
  65.2 0.6 collective-permute-done.14
  65.8 1.7 %collective-permute-done.13 = bf16[16,32,128]{2,1,0:T(8,128)(2,1)S(1)} collective-permute-done((bf16[16,32,128]{2,1,0:T(8,128)(2,1)S(1)}, bf16[16,32,128]{2,1,0:T(8,128)(2,1)S(1)}, u32[]{:S(2)}, u32[]{:S(2)}) %collective-permute-start.13) | collective-permute-done | bytes 131104 | tf_op jit(solution)/shard_map/ppermute | solution.py:22
  67.5 0.0 collective-permute-done.12
  67.5 0.8 %fusion.15 = f32[16,32,128]{2,1,0:T(8,128)} fusion(f32[5,16,32,128]{3,2,1,0:T(8,128)S(1)} %copy.22, bf16[16,32,128]{2,1,0:T(8,128)(2,1)S(1)} %collective-permute-done.14, bf16[16,32,128]{2,1,0:T(8,128)(2,1)S(1)} %collective-permute-done.13, bf16[16,32,128]{2,1,0:T(8,128)(2,1)S(1)} %collective-permute-done.12, bf16[16,32,128]{2,1,0:T(8,128)(2,1)S(1)} %collective-permute-done.11), kind=kLoop, calls=%fused_computation.26 | loop fusion | flops 524288 | bytes 1048576 | tf_op jit(solution)/shard_map/add | solution.py:153
  (19 shorter events, 0.3 us)
Async XLA Ops:
  0.6 16.4 %collective-permute-start.2 = (bf16[16,32,128]{2,1,0:T(8,128)(2,1)}, bf16[16,32,128]{2,1,0:T(8,128)(2,1)S(1)}, u32[]{:S(2)}, u32[]{:S(2)}) collective-permute-start(bf16[16,32,128]{2,1,0:T(8,128)(2,1)} %param.9), channel_id=1, source_target_pairs={{4,0},{8,4},{12,8},{16,12},{20,16},{24,20},{28,24},{0,28},{5,1},{9... | collective-permute-start | bytes 393224 | tf_op jit(solution)/shard_map/ppermute | solution.py:22
  6.7 9.4 %collective-permute-start.1 = (bf16[16,32,128]{2,1,0:T(8,128)(2,1)}, bf16[16,32,128]{2,1,0:T(8,128)(2,1)S(1)}, u32[]{:S(2)}, u32[]{:S(2)}) collective-permute-start(bf16[16,32,128]{2,1,0:T(8,128)(2,1)} %param.9), channel_id=1, source_target_pairs={{28,0},{0,4},{4,8},{8,12},{12,16},{16,20},{20,24},{24,28},{29,1},{... | collective-permute-start | bytes 393224 | tf_op jit(solution)/shard_map/ppermute | solution.py:22
  6.7 9.3 %collective-permute-start = (bf16[16,32,128]{2,1,0:T(8,128)(2,1)}, bf16[16,32,128]{2,1,0:T(8,128)(2,1)S(1)}, u32[]{:S(2)}, u32[]{:S(2)}) collective-permute-start(bf16[16,32,128]{2,1,0:T(8,128)(2,1)} %param.9), channel_id=1, source_target_pairs={{24,0},{28,4},{0,8},{4,12},{8,16},{12,20},{16,24},{20,28},{25,1},{... | collective-permute-start | bytes 393224 | tf_op jit(solution)/shard_map/ppermute | solution.py:22
  6.7 10.9 %collective-permute-start.3 = (bf16[16,32,128]{2,1,0:T(8,128)(2,1)}, bf16[16,32,128]{2,1,0:T(8,128)(2,1)S(1)}, u32[]{:S(2)}, u32[]{:S(2)}) collective-permute-start(bf16[16,32,128]{2,1,0:T(8,128)(2,1)} %param.9), channel_id=1, source_target_pairs={{8,0},{12,4},{16,8},{20,12},{24,16},{28,20},{0,24},{4,28},{9,1},{1... | collective-permute-start | bytes 393224 | tf_op jit(solution)/shard_map/ppermute | solution.py:22
  12.3 5.1 %collective-permute-start.4 = (bf16[1,17,32,128]{3,2,1,0:T(8,128)(2,1)S(1)}, bf16[1,17,32,128]{3,2,1,0:T(8,128)(2,1)S(1)}, u32[]{:S(2)}, u32[]{:S(2)}) collective-permute-start(bf16[1,17,32,128]{3,2,1,0:T(8,128)(2,1)S(1)} %get-tuple-element.28), channel_id=1, source_target_pairs={{0,2},{1,3},{2,0},{3,1},{4,6},{5,7},{6,4},{7,5},{8,10},{9,11},{10,... | collective-permute-start | bytes 417800 | tf_op jit(solution)/shard_map/ppermute | solution.py:38
  17.4 1.6 %collective-permute-start.5 = (bf16[2,17,32,128]{3,2,1,0:T(8,128)(2,1)S(1)}, bf16[2,17,32,128]{3,2,1,0:T(8,128)(2,1)S(1)}, u32[]{:S(2)}, u32[]{:S(2)}) collective-permute-start(bf16[2,17,32,128]{3,2,1,0:T(8,128)(2,1)S(1)} %pad_maximum_fusion.2), channel_id=1, source_target_pairs={{0,1},{1,0},{2,3},{3,2},{4,5},{5,4},{6,7},{7,6},{8,9},{9,8},{10,11... | collective-permute-start | bytes 835592 | tf_op jit(solution)/shard_map/ppermute | solution.py:38
  29.4 8.1 %copy-start = (f32[32,128]{1,0:T(8,128)S(1)}, f32[32,128]{1,0:T(8,128)}, u32[]{:S(2)}) copy-start(f32[32,128]{1,0:T(8,128)} %param.14) | copy-start | bytes 49156
  29.4 5.6 %collective-permute-start.6 = (bf16[1,16,32,128]{3,1,2,0:T(8,128)(2,1)S(1)}, bf16[1,16,32,128]{3,1,2,0:T(8,128)(2,1)S(1)}, u32[]{:S(2)}, u32[]{:S(2)}) collective-permute-start(bf16[1,16,32,128]{3,1,2,0:T(8,128)(2,1)S(1)} %bitcast.75), channel_id=1, source_target_pairs={{0,2},{1,3},{2,0},{3,1},{4,6},{5,7},{6,4},{7,5},{8,10},{9,11},{10,... | collective-permute-start | bytes 393224 | tf_op jit(solution)/shard_map/ppermute | solution.py:38
  35.0 1.6 %collective-permute-start.7 = (bf16[2,16,32,128]{3,1,2,0:T(8,128)(2,1)S(1)}, bf16[2,16,32,128]{3,1,2,0:T(8,128)(2,1)S(1)}, u32[]{:S(2)}, u32[]{:S(2)}) collective-permute-start(bf16[2,16,32,128]{3,1,2,0:T(8,128)(2,1)S(1)} %pad_maximum_fusion.3), channel_id=1, source_target_pairs={{0,1},{1,0},{2,3},{3,2},{4,5},{5,4},{6,7},{7,6},{8,9},{9,8},{10,11... | collective-permute-start | bytes 786440 | tf_op jit(solution)/shard_map/ppermute | solution.py:38
  38.3 10.2 %collective-permute-start.8 = (f32[32,128]{1,0:T(8,128)S(1)}, f32[32,128]{1,0:T(8,128)S(1)}, u32[]{:S(2)}, u32[]{:S(2)}) collective-permute-start(f32[32,128]{1,0:T(8,128)S(1)} %convolution_bitcast_fusion.1), channel_id=1, source_target_pairs={{0,4},{4,0},{8,12},{12,8},{16,20},{20,16},{24,28},{28,24},{1,5},{5... | collective-permute-start | bytes 49160 | tf_op jit(solution)/shard_map/ppermute | solution.py:55
  48.4 3.8 %collective-permute-start.9 = (f32[32,128]{1,0:T(8,128)S(1)}, f32[32,128]{1,0:T(8,128)S(1)}, u32[]{:S(2)}, u32[]{:S(2)}) collective-permute-start(f32[32,128]{1,0:T(8,128)S(1)} %add.80), channel_id=1, source_target_pairs={{0,8},{4,12},{8,0},{12,4},{16,24},{20,28},{24,16},{28,20},{1,9},{5... | collective-permute-start | bytes 49160 | tf_op jit(solution)/shard_map/ppermute | solution.py:55
  50.0 14.6 %copy-start.1 = (f32[32,128]{1,0:T(8,128)S(1)}, f32[32,128]{1,0:T(8,128)}, u32[]{:S(2)}) copy-start(f32[32,128]{1,0:T(8,128)} %param.15) | copy-start | bytes 49156
  50.0 14.6 %copy-start.2 = (f32[32,128]{1,0:T(8,128)S(1)}, f32[32,128]{1,0:T(8,128)}, u32[]{:S(2)}) copy-start(f32[32,128]{1,0:T(8,128)} %param.16) | copy-start | bytes 49156
  52.3 4.6 %collective-permute-start.10 = (f32[32,128]{1,0:T(8,128)S(1)}, f32[32,128]{1,0:T(8,128)S(1)}, u32[]{:S(2)}, u32[]{:S(2)}) collective-permute-start(f32[32,128]{1,0:T(8,128)S(1)} %add.81), channel_id=1, source_target_pairs={{0,16},{4,20},{8,24},{12,28},{16,0},{20,4},{24,8},{28,12},{1,17},{... | collective-permute-start | bytes 49160 | tf_op jit(solution)/shard_map/ppermute | solution.py:55
  57.8 7.4 %collective-permute-start.11 = (bf16[16,32,128]{2,1,0:T(8,128)(2,1)S(1)}, bf16[16,32,128]{2,1,0:T(8,128)(2,1)S(1)}, u32[]{:S(2)}, u32[]{:S(2)}) collective-permute-start(bf16[16,32,128]{2,1,0:T(8,128)(2,1)S(1)} %get-tuple-element.22), channel_id=1, source_target_pairs={{8,0},{12,4},{16,8},{20,12},{24,16},{28,20},{0,24},{4,28},{9,1},{1... | collective-permute-start | bytes 393224 | tf_op jit(solution)/shard_map/ppermute | solution.py:22
  58.4 7.4 %collective-permute-start.14 = (bf16[16,32,128]{2,1,0:T(8,128)(2,1)S(1)}, bf16[16,32,128]{2,1,0:T(8,128)(2,1)S(1)}, u32[]{:S(2)}, u32[]{:S(2)}) collective-permute-start(bf16[16,32,128]{2,1,0:T(8,128)(2,1)S(1)} %get-tuple-element.23), channel_id=1, source_target_pairs={{24,0},{28,4},{0,8},{4,12},{8,16},{12,20},{16,24},{20,28},{25,1},{... | collective-permute-start | bytes 393224 | tf_op jit(solution)/shard_map/ppermute | solution.py:22
  59.9 7.7 %collective-permute-start.13 = (bf16[16,32,128]{2,1,0:T(8,128)(2,1)S(1)}, bf16[16,32,128]{2,1,0:T(8,128)(2,1)S(1)}, u32[]{:S(2)}, u32[]{:S(2)}) collective-permute-start(bf16[16,32,128]{2,1,0:T(8,128)(2,1)S(1)} %get-tuple-element.24), channel_id=1, source_target_pairs={{28,0},{0,4},{4,8},{8,12},{12,16},{16,20},{20,24},{24,28},{29,1},{... | collective-permute-start | bytes 393224 | tf_op jit(solution)/shard_map/ppermute | solution.py:22
  59.9 7.7 %collective-permute-start.12 = (bf16[16,32,128]{2,1,0:T(8,128)(2,1)S(1)}, bf16[16,32,128]{2,1,0:T(8,128)(2,1)S(1)}, u32[]{:S(2)}, u32[]{:S(2)}) collective-permute-start(bf16[16,32,128]{2,1,0:T(8,128)(2,1)S(1)} %get-tuple-element.25), channel_id=1, source_target_pairs={{4,0},{8,4},{12,8},{16,12},{20,16},{24,20},{28,24},{0,28},{5,1},{9... | collective-permute-start | bytes 393224 | tf_op jit(solution)/shard_map/ppermute | solution.py:22

commit v7 on v6

--- a/solution.py
+++ b/solution.py
@@ -58,8 +58,9 @@
 
 
 def summed_by_table(table, terms, spec):
-    high = terms.astype(jnp.bfloat16)
-    low = (terms - high.astype(jnp.float32)).astype(jnp.bfloat16)
+    rounded = lax.reduce_precision(terms, exponent_bits=8, mantissa_bits=7)
+    high = rounded.astype(jnp.bfloat16)
+    low = (terms - rounded).astype(jnp.bfloat16)
     both = jnp.concatenate([high, low], axis=0)
     doubled = jnp.concatenate([table, table], axis=0).astype(jnp.bfloat16)
     return jnp.einsum(spec, doubled, both, preferred_element_type=jnp.float32)

time: 68.6 us -> 68.7 us (level)
  no operation moved by 1% of the time
where the time goes in v7:
time: 68.7 us; the launch traced here: 68.4 us
  starting transfers between devices  23 us (33%)
  matrix products  19.5 us (28%)
  waiting for transfers between devices  15.5 us (23%)
  other arithmetic  6.09 us (9%)
  local copies, waits for them, and re-layouts  2.65 us (4%)
  between operations  1.59 us (2%)
    ppermute x8, starting transfers between devices, passed_along(): return lax.ppermute(block, axis, route)  16.7 us
    dot_general x1, matrix products, per_device(): jnp.einsum('tfk,tjk->tfj', sources, tile_values, preferred_element_type=j...  7.92 us
    ppermute x4, waiting for transfers between devices, gathered_along(): got = lax.ppermute(held, axis, [(i, i ^ mask) for i in range(size)])  7.11 us
    dot_general x1, matrix products, per_device(): jnp.einsum('tfj,tjk->tfk', back_sources, tile_values, preferred_element_t...  5.99 us
    ppermute x3, waiting for transfers between devices, summed_over(): lax.ppermute(block, axis, [(i, i ^ mask) for i in range(size)])  5.92 us
    ppermute x4, starting transfers between devices, gathered_along(): got = lax.ppermute(held, axis, [(i, i ^ mask) for i in range(size)])  3.26 us
    ppermute x3, starting transfers between devices, summed_over(): lax.ppermute(block, axis, [(i, i ^ mask) for i in range(size)])  3.12 us
    dot_general x2, matrix products, summed_by_table(): return jnp.einsum(spec, doubled, both, preferred_element_type=jnp.float32)  2.87 us
  transfers between devices with their start and end apart: 15, of which 9 were waited for; matrix products, arithmetic and copies ran while one was open for 21% of the time, Pallas kernels for 0%

profile of v7, /device:TPU:0, one launch (start us, length us, event | category | flops | bytes accessed | tf_op | source)
XLA Modules:
  0.0 68.4 jit_solution(11714898246700774498)
XLA Ops:
  0.6 6.0 %collective-permute-start.2 = (bf16[16,32,128]{2,1,0:T(8,128)(2,1)}, bf16[16,32,128]{2,1,0:T(8,128)(2,1)S(1)}, u32[]{:S(2)}, u32[]{:S(2)}) collective-permute-start(bf16[16,32,128]{2,1,0:T(8,128)(2,1)} %param.9), channel_id=1, source_target_pairs={{4,0},{8,4},{12,8},{16,12},{20,16},{24,20},{28,24},{0,28},{5,1},{9... | collective-permute-start | bytes 393224 | tf_op jit(solution)/shard_map/ppermute | solution.py:22
  6.7 0.0 collective-permute-start.1
  6.7 0.0 collective-permute-start
  6.7 3.8 %collective-permute-start.3 = (bf16[16,32,128]{2,1,0:T(8,128)(2,1)}, bf16[16,32,128]{2,1,0:T(8,128)(2,1)S(1)}, u32[]{:S(2)}, u32[]{:S(2)}) collective-permute-start(bf16[16,32,128]{2,1,0:T(8,128)(2,1)} %param.9), channel_id=1, source_target_pairs={{8,0},{12,4},{16,8},{20,12},{24,16},{28,20},{0,24},{4,28},{9,1},{1... | collective-permute-start | bytes 393224 | tf_op jit(solution)/shard_map/ppermute | solution.py:22
  10.5 0.7 %convert_bitcast_fusion = bf16[1,32,128]{2,1,0:T(8,128)(2,1)S(1)} fusion(f32[32,128]{1,0:T(8,128)} %param.14), kind=kLoop, calls=%fused_computation.81 | loop fusion | flops 4096 | bytes 24576 | tf_op jit(solution)/shard_map/broadcast_in_dim | solution.py:114
  11.2 0.1 broadcast_in_dim.11
  11.3 1.0 %fusion.21 = (bf16[1,17,32,128]{3,2,1,0:T(8,128)(2,1)S(1)}, bf16[17,128,128]{2,1,0:T(8,128)(2,1)S(1)}) fusion(bf16[1,32,128]{2,1,0:T(8,128)(2,1)S(1)} %convert_bitcast_fusion, bf16[16,32,128]{2,1,0:T(8,128)(2,1)} %param.17, bf16[17,128,128]{2,1,0:T(8,128)(2,1)S(1)} %broadcast_in_dim.11, s32[]{:T(128)S(6)} %select_n.49), kind=kLoop, calls=%fused_computation.50 | loop fusion | flops 278528 | bytes 417796 | tf_op jit(solution)/shard_map/stack | solution.py:37
  12.3 1.6 %collective-permute-start.4 = (bf16[1,17,32,128]{3,2,1,0:T(8,128)(2,1)S(1)}, bf16[1,17,32,128]{3,2,1,0:T(8,128)(2,1)S(1)}, u32[]{:S(2)}, u32[]{:S(2)}) collective-permute-start(bf16[1,17,32,128]{3,2,1,0:T(8,128)(2,1)S(1)} %get-tuple-element.28), channel_id=1, source_target_pairs={{0,2},{1,3},{2,0},{3,1},{4,6},{5,7},{6,4},{7,5},{8,10},{9,11},{10,... | collective-permute-start | bytes 417800 | tf_op jit(solution)/shard_map/ppermute | solution.py:38
  14.5 0.7 broadcast_subtract_fusion
  15.2 0.7 %fusion.38 = s32[256]{0:T(256)S(1)} fusion(s32[256]{0:T(256)} %param.12, s32[]{:T(128)S(6)} %axis_index.33), kind=kLoop, calls=%fused_computation.92 | loop fusion | flops 9472 | bytes 2052 | tf_op jit(solution)/shard_map/add | solution.py:100
  15.9 0.0 collective-permute-done
  16.0 0.1 collective-permute-done.1
  16.1 0.9 %constant_dynamic-update-slice_fusion.2 = bf16[80,32,128]{2,1,0:T(8,128)(2,1)S(1)} fusion(bf16[80,32,128]{2,1,0:T(8,128)(2,1)S(1)} %constant_dynamic-update-slice_fusion.3, bf16[16,32,128]{2,1,0:T(8,128)(2,1)} %param.9), kind=kLoop, calls=%fused_computation.75 | loop fusion | bytes 262144
  17.0 0.0 collective-permute-done.2
  17.1 0.3 collective-permute-done.4
  17.4 0.1 collective-permute-start.5
  17.5 0.0 collective-permute-done.3
  17.6 1.5 %collective-permute-done.5 = bf16[2,17,32,128]{3,2,1,0:T(8,128)(2,1)S(1)} collective-permute-done((bf16[2,17,32,128]{3,2,1,0:T(8,128)(2,1)S(1)}, bf16[2,17,32,128]{3,2,1,0:T(8,128)(2,1)S(1)}, u32[]{:S(2)}, u32[]{:S(2)}) %collective-permute-start.5) | collective-permute-done | bytes 278560 | tf_op jit(solution)/shard_map/ppermute | solution.py:38
  19.2 0.8 %fusion.12 = bf16[256,32,128]{2,0,1:T(8,128)(2,1)S(1)} fusion(bf16[80,32,128]{2,1,0:T(8,128)(2,1)S(1)} %constant_dynamic-update-slice_fusion, s32[256]{0:T(256)S(1)} %fusion.38), kind=kOutput, calls=%fused_computation.22 | convolution fusion | flops 167792640 | bytes 2753536 | tf_op jit(solution)/shard_map/ts,sfk->tfk/dot_general | solution.py:119
  20.0 7.9 %reduce-precision_convert_fusion.1 = (bf16[256,32,128]{2,1,0:T(8,128)(2,1)S(1)}, bf16[256,32,128]{2,1,0:T(8,128)(2,1)S(1)}) fusion(bf16[256,128,128]{2,1,0:T(8,128)(2,1)} %param.10, bf16[256,32,128]{2,0,1:T(8,128)(2,1)S(1)} %fusion.12), kind=kOutput, calls=%fused_computation.3 | convolution fusion | flops 272629760 | bytes 14680064 | tf_op jit(solution)/shard_map/tfk,tjk->tfj/dot_general | solution.py:122
  27.9 0.4 pad_maximum_fusion
  28.3 1.2 %fusion.9 = bf16[16,32,128]{2,0,1:T(8,128)(2,1)S(1)} fusion(bf16[512,32,128]{2,1,0:T(8,128)(2,1)S(1)} %pad_maximum_fusion, bf16[256,16]{0,1:T(8,128)(2,1)S(1)} %select_convert_fusion.2), kind=kOutput, calls=%fused_computation.19 | convolution fusion | flops 67207168 | bytes 4333568 | tf_op jit(solution)/shard_map/tb,tfj->bfj/dot_general | solution.py:66
  29.5 0.0 copy-start
  29.5 1.5 %collective-permute-start.6 = (bf16[1,16,32,128]{3,1,2,0:T(8,128)(2,1)S(1)}, bf16[1,16,32,128]{3,1,2,0:T(8,128)(2,1)S(1)}, u32[]{:S(2)}, u32[]{:S(2)}) collective-permute-start(bf16[1,16,32,128]{3,1,2,0:T(8,128)(2,1)S(1)} %bitcast.75), channel_id=1, source_target_pairs={{0,2},{1,3},{2,0},{3,1},{4,6},{5,7},{6,4},{7,5},{8,10},{9,11},{10,... | collective-permute-start | bytes 393224 | tf_op jit(solution)/shard_map/ppermute | solution.py:38
  31.0 4.0 %collective-permute-done.6 = bf16[1,16,32,128]{3,1,2,0:T(8,128)(2,1)S(1)} collective-permute-done((bf16[1,16,32,128]{3,1,2,0:T(8,128)(2,1)S(1)}, bf16[1,16,32,128]{3,1,2,0:T(8,128)(2,1)S(1)}, u32[]{:S(2)}, u32[]{:S(2)}) %collective-permute-start.6) | collective-permute-done | bytes 131104 | tf_op jit(solution)/shard_map/ppermute | solution.py:38
  35.1 0.1 collective-permute-start.7
  35.1 0.1 broadcast_in_dim.13
  35.2 0.1 copy_dynamic-update-slice_fusion.3
  35.3 0.1 copy_dynamic-update-slice_fusion.2
  35.4 1.3 %collective-permute-done.7 = bf16[2,16,32,128]{3,1,2,0:T(8,128)(2,1)S(1)} collective-permute-done((bf16[2,16,32,128]{3,1,2,0:T(8,128)(2,1)S(1)}, bf16[2,16,32,128]{3,1,2,0:T(8,128)(2,1)S(1)}, u32[]{:S(2)}, u32[]{:S(2)}) %collective-permute-start.7) | collective-permute-done | bytes 262176 | tf_op jit(solution)/shard_map/ppermute | solution.py:38
  36.7 0.1 copy_dynamic-update-slice_fusion.1
  36.7 0.1 copy_dynamic-update-slice_fusion
  36.8 0.3 broadcast_compare_fusion
  37.1 0.4 convolution_bitcast_fusion.1
  37.5 0.0 copy-done
  37.6 0.5 fusion.8
  38.1 0.2 copy.27
  38.3 3.0 %collective-permute-start.8 = (f32[32,128]{1,0:T(8,128)S(1)}, f32[32,128]{1,0:T(8,128)S(1)}, u32[]{:S(2)}, u32[]{:S(2)}) collective-permute-start(f32[32,128]{1,0:T(8,128)S(1)} %convolution_bitcast_fusion.1), channel_id=1, source_target_pairs={{0,4},{4,0},{8,12},{12,8},{16,20},{20,16},{24,28},{28,24},{1,5},{5... | collective-permute-start | bytes 49160 | tf_op jit(solution)/shard_map/ppermute | solution.py:55
  41.4 0.7 %fusion.33 = bf16[256,32,128]{2,0,1:T(8,128)(2,1)S(1)} fusion(bf16[16,32,128]{2,0,1:T(8,128)(2,1)S(1)} %copy.27, s32[256]{0:T(256)S(1)} %broadcast_subtract_fusion), kind=kOutput, calls=%fused_computation.72 | convolution fusion | flops 33558528 | bytes 2229248 | tf_op jit(solution)/shard_map/tb,bfj->tfj/dot_general | solution.py:141
  42.1 6.0 %reduce-precision_convert_fusion = (bf16[256,32,128]{2,1,0:T(8,128)(2,1)S(1)}, bf16[256,32,128]{2,1,0:T(8,128)(2,1)S(1)}) fusion(bf16[256,128,128]{2,1,0:T(8,128)(2,1)} %param.10, bf16[256,32,128]{2,0,1:T(8,128)(2,1)S(1)} %fusion.33), kind=kOutput, calls=%fused_computation.1 | convolution fusion | flops 272629760 | bytes 14680064 | tf_op jit(solution)/shard_map/tfj,tjk->tfk/dot_general | solution.py:144
  48.1 0.4 pad_maximum_fusion.1
  48.5 0.0 collective-permute-done.8
  48.5 0.1 collective-permute-start.9
  48.6 1.6 %fusion.2 = f32[80,32,128]{2,0,1:T(8,128)S(1)} fusion(bf16[512,32,128]{2,1,0:T(8,128)(2,1)S(1)} %pad_maximum_fusion.1, bf16[256,80]{0,1:T(8,128)(2,1)S(1)} %select_convert_fusion.1), kind=kOutput, calls=%fused_computation.10 | convolution fusion | flops 335708160 | bytes 5545984 | tf_op jit(solution)/shard_map/ts,tfk->sfk/dot_general | solution.py:66
  50.2 0.0 copy-start.1
  50.2 0.0 copy-start.2
  50.2 2.1 %collective-permute-done.9 = f32[32,128]{1,0:T(8,128)S(1)} collective-permute-done((f32[32,128]{1,0:T(8,128)S(1)}, f32[32,128]{1,0:T(8,128)S(1)}, u32[]{:S(2)}, u32[]{:S(2)}) %collective-permute-start.9) | collective-permute-done | bytes 16416 | tf_op jit(solution)/shard_map/ppermute | solution.py:55
  52.3 0.0 collective-permute-start.10
  52.3 0.8 %select_convert_fusion = bf16[16,32,128]{2,1,0:T(8,128)(2,1)} fusion(f32[16,128,128]{2,1,0:T(8,128)S(1)} %get-tuple-element.31, s32[]{:T(128)S(6)} %select_n.49, pred[16,128,128]{2,1,0:T(8,128)(4,1)S(1)} %get-tuple-element.30), kind=kLoop, calls=%fused_computation.32 | loop fusion | flops 196608 | bytes 458756 | tf_op jit(solution)/shard_map/convert_element_type | solution.py:133
  53.1 3.8 %collective-permute-done.10 = f32[32,128]{1,0:T(8,128)S(1)} collective-permute-done((f32[32,128]{1,0:T(8,128)S(1)}, f32[32,128]{1,0:T(8,128)S(1)}, u32[]{:S(2)}, u32[]{:S(2)}) %collective-permute-start.10) | collective-permute-done | bytes 16416 | tf_op jit(solution)/shard_map/ppermute | solution.py:55
  57.0 0.4 copy.49
  57.4 0.4 copy.22
  57.8 0.6 collective-permute-start.11
  58.5 1.4 %collective-permute-start.14 = (bf16[16,32,128]{2,1,0:T(8,128)(2,1)S(1)}, bf16[16,32,128]{2,1,0:T(8,128)(2,1)S(1)}, u32[]{:S(2)}, u32[]{:S(2)}) collective-permute-start(bf16[16,32,128]{2,1,0:T(8,128)(2,1)S(1)} %get-tuple-element.23), channel_id=1, source_target_pairs={{24,0},{28,4},{0,8},{4,12},{8,16},{12,20},{16,24},{20,28},{25,1},{... | collective-permute-start | bytes 393224 | tf_op jit(solution)/shard_map/ppermute | solution.py:22
  59.9 0.0 collective-permute-start.13
  59.9 4.7 %collective-permute-start.12 = (bf16[16,32,128]{2,1,0:T(8,128)(2,1)S(1)}, bf16[16,32,128]{2,1,0:T(8,128)(2,1)S(1)}, u32[]{:S(2)}, u32[]{:S(2)}) collective-permute-start(bf16[16,32,128]{2,1,0:T(8,128)(2,1)S(1)} %get-tuple-element.25), channel_id=1, source_target_pairs={{4,0},{8,4},{12,8},{16,12},{20,16},{24,20},{28,24},{0,28},{5,1},{9... | collective-permute-start | bytes 393224 | tf_op jit(solution)/shard_map/ppermute | solution.py:22
  64.6 0.0 copy-done.1
  64.6 0.0 copy-done.2
  64.6 0.6 divide_subtract_fusion
  65.3 0.0 collective-permute-done.11
  65.3 0.6 collective-permute-done.14
  65.9 1.7 %collective-permute-done.13 = bf16[16,32,128]{2,1,0:T(8,128)(2,1)S(1)} collective-permute-done((bf16[16,32,128]{2,1,0:T(8,128)(2,1)S(1)}, bf16[16,32,128]{2,1,0:T(8,128)(2,1)S(1)}, u32[]{:S(2)}, u32[]{:S(2)}) %collective-permute-start.13) | collective-permute-done | bytes 131104 | tf_op jit(solution)/shard_map/ppermute | solution.py:22
  67.6 0.0 collective-permute-done.12
  67.6 0.8 %fusion.17 = f32[16,32,128]{2,1,0:T(8,128)} fusion(f32[5,16,32,128]{3,2,1,0:T(8,128)S(1)} %copy.22, bf16[16,32,128]{2,1,0:T(8,128)(2,1)S(1)} %collective-permute-done.14, bf16[16,32,128]{2,1,0:T(8,128)(2,1)S(1)} %collective-permute-done.13, bf16[16,32,128]{2,1,0:T(8,128)(2,1)S(1)} %collective-permute-done.12, bf16[16,32,128]{2,1,0:T(8,128)(2,1)S(1)} %collective-permute-done.11), kind=kLoop, calls=%fused_computation.30 | loop fusion | flops 524288 | bytes 1048576 | tf_op jit(solution)/shard_map/add | solution.py:154
  (19 shorter events, 0.3 us)
Async XLA Ops:
  0.6 16.4 %collective-permute-start.2 = (bf16[16,32,128]{2,1,0:T(8,128)(2,1)}, bf16[16,32,128]{2,1,0:T(8,128)(2,1)S(1)}, u32[]{:S(2)}, u32[]{:S(2)}) collective-permute-start(bf16[16,32,128]{2,1,0:T(8,128)(2,1)} %param.9), channel_id=1, source_target_pairs={{4,0},{8,4},{12,8},{16,12},{20,16},{24,20},{28,24},{0,28},{5,1},{9... | collective-permute-start | bytes 393224 | tf_op jit(solution)/shard_map/ppermute | solution.py:22
  6.7 9.4 %collective-permute-start.1 = (bf16[16,32,128]{2,1,0:T(8,128)(2,1)}, bf16[16,32,128]{2,1,0:T(8,128)(2,1)S(1)}, u32[]{:S(2)}, u32[]{:S(2)}) collective-permute-start(bf16[16,32,128]{2,1,0:T(8,128)(2,1)} %param.9), channel_id=1, source_target_pairs={{28,0},{0,4},{4,8},{8,12},{12,16},{16,20},{20,24},{24,28},{29,1},{... | collective-permute-start | bytes 393224 | tf_op jit(solution)/shard_map/ppermute | solution.py:22
  6.7 9.3 %collective-permute-start = (bf16[16,32,128]{2,1,0:T(8,128)(2,1)}, bf16[16,32,128]{2,1,0:T(8,128)(2,1)S(1)}, u32[]{:S(2)}, u32[]{:S(2)}) collective-permute-start(bf16[16,32,128]{2,1,0:T(8,128)(2,1)} %param.9), channel_id=1, source_target_pairs={{24,0},{28,4},{0,8},{4,12},{8,16},{12,20},{16,24},{20,28},{25,1},{... | collective-permute-start | bytes 393224 | tf_op jit(solution)/shard_map/ppermute | solution.py:22
  6.7 10.9 %collective-permute-start.3 = (bf16[16,32,128]{2,1,0:T(8,128)(2,1)}, bf16[16,32,128]{2,1,0:T(8,128)(2,1)S(1)}, u32[]{:S(2)}, u32[]{:S(2)}) collective-permute-start(bf16[16,32,128]{2,1,0:T(8,128)(2,1)} %param.9), channel_id=1, source_target_pairs={{8,0},{12,4},{16,8},{20,12},{24,16},{28,20},{0,24},{4,28},{9,1},{1... | collective-permute-start | bytes 393224 | tf_op jit(solution)/shard_map/ppermute | solution.py:22
  12.3 5.1 %collective-permute-start.4 = (bf16[1,17,32,128]{3,2,1,0:T(8,128)(2,1)S(1)}, bf16[1,17,32,128]{3,2,1,0:T(8,128)(2,1)S(1)}, u32[]{:S(2)}, u32[]{:S(2)}) collective-permute-start(bf16[1,17,32,128]{3,2,1,0:T(8,128)(2,1)S(1)} %get-tuple-element.28), channel_id=1, source_target_pairs={{0,2},{1,3},{2,0},{3,1},{4,6},{5,7},{6,4},{7,5},{8,10},{9,11},{10,... | collective-permute-start | bytes 417800 | tf_op jit(solution)/shard_map/ppermute | solution.py:38
  17.4 1.6 %collective-permute-start.5 = (bf16[2,17,32,128]{3,2,1,0:T(8,128)(2,1)S(1)}, bf16[2,17,32,128]{3,2,1,0:T(8,128)(2,1)S(1)}, u32[]{:S(2)}, u32[]{:S(2)}) collective-permute-start(bf16[2,17,32,128]{3,2,1,0:T(8,128)(2,1)S(1)} %pad_maximum_fusion.2), channel_id=1, source_target_pairs={{0,1},{1,0},{2,3},{3,2},{4,5},{5,4},{6,7},{7,6},{8,9},{9,8},{10,11... | collective-permute-start | bytes 835592 | tf_op jit(solution)/shard_map/ppermute | solution.py:38
  29.5 8.1 %copy-start = (f32[32,128]{1,0:T(8,128)S(1)}, f32[32,128]{1,0:T(8,128)}, u32[]{:S(2)}) copy-start(f32[32,128]{1,0:T(8,128)} %param.14) | copy-start | bytes 49156
  29.5 5.6 %collective-permute-start.6 = (bf16[1,16,32,128]{3,1,2,0:T(8,128)(2,1)S(1)}, bf16[1,16,32,128]{3,1,2,0:T(8,128)(2,1)S(1)}, u32[]{:S(2)}, u32[]{:S(2)}) collective-permute-start(bf16[1,16,32,128]{3,1,2,0:T(8,128)(2,1)S(1)} %bitcast.75), channel_id=1, source_target_pairs={{0,2},{1,3},{2,0},{3,1},{4,6},{5,7},{6,4},{7,5},{8,10},{9,11},{10,... | collective-permute-start | bytes 393224 | tf_op jit(solution)/shard_map/ppermute | solution.py:38
  35.1 1.6 %collective-permute-start.7 = (bf16[2,16,32,128]{3,1,2,0:T(8,128)(2,1)S(1)}, bf16[2,16,32,128]{3,1,2,0:T(8,128)(2,1)S(1)}, u32[]{:S(2)}, u32[]{:S(2)}) collective-permute-start(bf16[2,16,32,128]{3,1,2,0:T(8,128)(2,1)S(1)} %pad_maximum_fusion.3), channel_id=1, source_target_pairs={{0,1},{1,0},{2,3},{3,2},{4,5},{5,4},{6,7},{7,6},{8,9},{9,8},{10,11... | collective-permute-start | bytes 786440 | tf_op jit(solution)/shard_map/ppermute | solution.py:38
  38.3 10.2 %collective-permute-start.8 = (f32[32,128]{1,0:T(8,128)S(1)}, f32[32,128]{1,0:T(8,128)S(1)}, u32[]{:S(2)}, u32[]{:S(2)}) collective-permute-start(f32[32,128]{1,0:T(8,128)S(1)} %convolution_bitcast_fusion.1), channel_id=1, source_target_pairs={{0,4},{4,0},{8,12},{12,8},{16,20},{20,16},{24,28},{28,24},{1,5},{5... | collective-permute-start | bytes 49160 | tf_op jit(solution)/shard_map/ppermute | solution.py:55
  48.5 3.8 %collective-permute-start.9 = (f32[32,128]{1,0:T(8,128)S(1)}, f32[32,128]{1,0:T(8,128)S(1)}, u32[]{:S(2)}, u32[]{:S(2)}) collective-permute-start(f32[32,128]{1,0:T(8,128)S(1)} %add.80), channel_id=1, source_target_pairs={{0,8},{4,12},{8,0},{12,4},{16,24},{20,28},{24,16},{28,20},{1,9},{5... | collective-permute-start | bytes 49160 | tf_op jit(solution)/shard_map/ppermute | solution.py:55
  50.2 14.4 %copy-start.1 = (f32[32,128]{1,0:T(8,128)S(1)}, f32[32,128]{1,0:T(8,128)}, u32[]{:S(2)}) copy-start(f32[32,128]{1,0:T(8,128)} %param.15) | copy-start | bytes 49156
  50.2 14.4 %copy-start.2 = (f32[32,128]{1,0:T(8,128)S(1)}, f32[32,128]{1,0:T(8,128)}, u32[]{:S(2)}) copy-start(f32[32,128]{1,0:T(8,128)} %param.16) | copy-start | bytes 49156
  52.3 4.6 %collective-permute-start.10 = (f32[32,128]{1,0:T(8,128)S(1)}, f32[32,128]{1,0:T(8,128)S(1)}, u32[]{:S(2)}, u32[]{:S(2)}) collective-permute-start(f32[32,128]{1,0:T(8,128)S(1)} %add.81), channel_id=1, source_target_pairs={{0,16},{4,20},{8,24},{12,28},{16,0},{20,4},{24,8},{28,12},{1,17},{... | collective-permute-start | bytes 49160 | tf_op jit(solution)/shard_map/ppermute | solution.py:55
  57.8 7.4 %collective-permute-start.11 = (bf16[16,32,128]{2,1,0:T(8,128)(2,1)S(1)}, bf16[16,32,128]{2,1,0:T(8,128)(2,1)S(1)}, u32[]{:S(2)}, u32[]{:S(2)}) collective-permute-start(bf16[16,32,128]{2,1,0:T(8,128)(2,1)S(1)} %get-tuple-element.22), channel_id=1, source_target_pairs={{8,0},{12,4},{16,8},{20,12},{24,16},{28,20},{0,24},{4,28},{9,1},{1... | collective-permute-start | bytes 393224 | tf_op jit(solution)/shard_map/ppermute | solution.py:22
  58.5 7.4 %collective-permute-start.14 = (bf16[16,32,128]{2,1,0:T(8,128)(2,1)S(1)}, bf16[16,32,128]{2,1,0:T(8,128)(2,1)S(1)}, u32[]{:S(2)}, u32[]{:S(2)}) collective-permute-start(bf16[16,32,128]{2,1,0:T(8,128)(2,1)S(1)} %get-tuple-element.23), channel_id=1, source_target_pairs={{24,0},{28,4},{0,8},{4,12},{8,16},{12,20},{16,24},{20,28},{25,1},{... | collective-permute-start | bytes 393224 | tf_op jit(solution)/shard_map/ppermute | solution.py:22
  59.9 7.7 %collective-permute-start.13 = (bf16[16,32,128]{2,1,0:T(8,128)(2,1)S(1)}, bf16[16,32,128]{2,1,0:T(8,128)(2,1)S(1)}, u32[]{:S(2)}, u32[]{:S(2)}) collective-permute-start(bf16[16,32,128]{2,1,0:T(8,128)(2,1)S(1)} %get-tuple-element.24), channel_id=1, source_target_pairs={{28,0},{0,4},{4,8},{8,12},{12,16},{16,20},{20,24},{24,28},{29,1},{... | collective-permute-start | bytes 393224 | tf_op jit(solution)/shard_map/ppermute | solution.py:22
  59.9 7.7 %collective-permute-start.12 = (bf16[16,32,128]{2,1,0:T(8,128)(2,1)S(1)}, bf16[16,32,128]{2,1,0:T(8,128)(2,1)S(1)}, u32[]{:S(2)}, u32[]{:S(2)}) collective-permute-start(bf16[16,32,128]{2,1,0:T(8,128)(2,1)S(1)} %get-tuple-element.25), channel_id=1, source_target_pairs={{4,0},{8,4},{12,8},{16,12},{20,16},{24,20},{28,24},{0,28},{5,1},{9... | collective-permute-start | bytes 393224 | tf_op jit(solution)/shard_map/ppermute | solution.py:22

commit v8 on v7

--- a/solution.py
+++ b/solution.py
@@ -146,7 +146,6 @@
     )
     outgoing = summed_by_table(add_source, back_terms, "ts,tfk->sfk")
     outgoing = outgoing.reshape(2 * REACH + 1, blocks, width_local, tile_size)
-    outgoing, grad = lax.optimization_barrier((outgoing, grad))
     feature_grad = outgoing[REACH]
     for distance in range(-REACH, REACH + 1):
         if distance != 0:

time: 68.7 us -> 67.8 us (0.987)
  other arithmetic: 6.09 us -> 5.4 us
    ppermute x3, waiting for transfers between devices: 5.92 us -> 3.69 us  [summed_over(): lax.ppermute(block, axis, [(i, i ^ mask) for i in range(size)])]
    ppermute x8, waiting for transfers between devices: 2.43 us -> 4.32 us  [passed_along(): return lax.ppermute(block, axis, route)]
    optimization_barrier x2 -> x0, local copies, waits for them, and re-layouts: 0.84 us -> none  [per_device(): outgoing, grad = lax.optimization_barrier((outgoing, grad))]
    unnamed x10 -> x11, local copies, waits for them, and re-layouts: 0.99 us -> 1.78 us
    add x1, other arithmetic: 0.79 us -> 0.1 us  [per_device(): feature_grad + passed_along(sent, 'node', distance).astype(jnp.float32)]
  transfers between devices with their start and end apart: 15 -> 15, of which waited for: 9 -> 8; matrix products, arithmetic and copies ran while one was open for 21% -> 22% of each run, Pallas kernels for 0% -> 0%
where the time goes in v8:
time: 67.8 us; the launch traced here: 67.4 us
  starting transfers between devices  23.3 us (34%)
  matrix products  19.4 us (29%)
  waiting for transfers between devices  15.1 us (22%)
  other arithmetic  5.4 us (8%)
  local copies, waits for them, and re-layouts  2.61 us (4%)
  between operations  1.59 us (2%)
    ppermute x8, starting transfers between devices, passed_along(): return lax.ppermute(block, axis, route)  16.9 us
    dot_general x1, matrix products, per_device(): jnp.einsum('tfk,tjk->tfj', sources, tile_values, preferred_element_type=j...  7.92 us
    ppermute x4, waiting for transfers between devices, gathered_along(): got = lax.ppermute(held, axis, [(i, i ^ mask) for i in range(size)])  7.11 us
    dot_general x1, matrix products, per_device(): jnp.einsum('tfj,tjk->tfk', back_sources, tile_values, preferred_element_t...  5.99 us
    ppermute x8, waiting for transfers between devices, passed_along(): return lax.ppermute(block, axis, route)  4.32 us
    ppermute x3, waiting for transfers between devices, summed_over(): lax.ppermute(block, axis, [(i, i ^ mask) for i in range(size)])  3.69 us
    ppermute x4, starting transfers between devices, gathered_along(): got = lax.ppermute(held, axis, [(i, i ^ mask) for i in range(size)])  3.26 us
    ppermute x3, starting transfers between devices, summed_over(): lax.ppermute(block, axis, [(i, i ^ mask) for i in range(size)])  3.12 us
  transfers between devices with their start and end apart: 15, of which 8 were waited for; matrix products, arithmetic and copies ran while one was open for 22% of the time, Pallas kernels for 0%

profile of v8, /device:TPU:0, one launch (start us, length us, event | category | flops | bytes accessed | tf_op | source)
XLA Modules:
  0.0 67.4 jit_solution(12622929646462378571)
XLA Ops:
  0.6 6.0 %collective-permute-start.2 = (bf16[16,32,128]{2,1,0:T(8,128)(2,1)}, bf16[16,32,128]{2,1,0:T(8,128)(2,1)S(1)}, u32[]{:S(2)}, u32[]{:S(2)}) collective-permute-start(bf16[16,32,128]{2,1,0:T(8,128)(2,1)} %param.9), channel_id=1, source_target_pairs={{4,0},{8,4},{12,8},{16,12},{20,16},{24,20},{28,24},{0,28},{5,1},{9... | collective-permute-start | bytes 393224 | tf_op jit(solution)/shard_map/ppermute | solution.py:22
  6.7 0.0 collective-permute-start.1
  6.7 0.0 collective-permute-start
  6.7 3.8 %collective-permute-start.3 = (bf16[16,32,128]{2,1,0:T(8,128)(2,1)}, bf16[16,32,128]{2,1,0:T(8,128)(2,1)S(1)}, u32[]{:S(2)}, u32[]{:S(2)}) collective-permute-start(bf16[16,32,128]{2,1,0:T(8,128)(2,1)} %param.9), channel_id=1, source_target_pairs={{8,0},{12,4},{16,8},{20,12},{24,16},{28,20},{0,24},{4,28},{9,1},{1... | collective-permute-start | bytes 393224 | tf_op jit(solution)/shard_map/ppermute | solution.py:22
  10.5 0.7 %convert_bitcast_fusion = bf16[1,32,128]{2,1,0:T(8,128)(2,1)S(1)} fusion(f32[32,128]{1,0:T(8,128)} %param.14), kind=kLoop, calls=%fused_computation.74 | loop fusion | flops 4096 | bytes 24576 | tf_op jit(solution)/shard_map/broadcast_in_dim | solution.py:114
  11.2 0.1 broadcast_in_dim.11
  11.3 1.0 %fusion.20 = (bf16[1,17,32,128]{3,2,1,0:T(8,128)(2,1)S(1)}, bf16[17,128,128]{2,1,0:T(8,128)(2,1)S(1)}) fusion(bf16[1,32,128]{2,1,0:T(8,128)(2,1)S(1)} %convert_bitcast_fusion, bf16[16,32,128]{2,1,0:T(8,128)(2,1)} %param.17, bf16[17,128,128]{2,1,0:T(8,128)(2,1)S(1)} %broadcast_in_dim.11, s32[]{:T(128)S(6)} %select_n.49), kind=kLoop, calls=%fused_computation.45 | loop fusion | flops 278528 | bytes 417796 | tf_op jit(solution)/shard_map/stack | solution.py:37
  12.3 1.6 %collective-permute-start.4 = (bf16[1,17,32,128]{3,2,1,0:T(8,128)(2,1)S(1)}, bf16[1,17,32,128]{3,2,1,0:T(8,128)(2,1)S(1)}, u32[]{:S(2)}, u32[]{:S(2)}) collective-permute-start(bf16[1,17,32,128]{3,2,1,0:T(8,128)(2,1)S(1)} %get-tuple-element.29), channel_id=1, source_target_pairs={{0,2},{1,3},{2,0},{3,1},{4,6},{5,7},{6,4},{7,5},{8,10},{9,11},{10,... | collective-permute-start | bytes 417800 | tf_op jit(solution)/shard_map/ppermute | solution.py:38
  14.5 0.7 %broadcast_subtract_fusion = s32[256]{0:T(256)S(1)} fusion(s32[256]{0:T(256)} %param.11, s32[]{:T(128)S(6)} %mul.86), kind=kLoop, calls=%fused_computation.89 | loop fusion | flops 256 | bytes 2052 | tf_op jit(solution)/shard_map/sub | solution.py:95
  15.2 0.7 %fusion.36 = s32[256]{0:T(256)S(1)} fusion(s32[256]{0:T(256)} %param.12, s32[]{:T(128)S(6)} %axis_index.33), kind=kLoop, calls=%fused_computation.85 | loop fusion | flops 9472 | bytes 2052 | tf_op jit(solution)/shard_map/add | solution.py:100
  15.9 0.0 collective-permute-done
  16.0 0.1 collective-permute-done.1
  16.1 0.9 %constant_dynamic-update-slice_fusion.2 = bf16[80,32,128]{2,1,0:T(8,128)(2,1)S(1)} fusion(bf16[80,32,128]{2,1,0:T(8,128)(2,1)S(1)} %constant_dynamic-update-slice_fusion.3, bf16[16,32,128]{2,1,0:T(8,128)(2,1)} %param.9), kind=kLoop, calls=%fused_computation.68 | loop fusion | bytes 262144
  17.0 0.0 collective-permute-done.2
  17.1 0.3 collective-permute-done.4
  17.4 0.1 collective-permute-start.5
  17.5 0.0 collective-permute-done.3
  17.6 1.5 %collective-permute-done.5 = bf16[2,17,32,128]{3,2,1,0:T(8,128)(2,1)S(1)} collective-permute-done((bf16[2,17,32,128]{3,2,1,0:T(8,128)(2,1)S(1)}, bf16[2,17,32,128]{3,2,1,0:T(8,128)(2,1)S(1)}, u32[]{:S(2)}, u32[]{:S(2)}) %collective-permute-start.5) | collective-permute-done | bytes 278560 | tf_op jit(solution)/shard_map/ppermute | solution.py:38
  19.2 0.8 %fusion.12 = bf16[256,32,128]{2,0,1:T(8,128)(2,1)S(1)} fusion(bf16[80,32,128]{2,1,0:T(8,128)(2,1)S(1)} %constant_dynamic-update-slice_fusion, s32[256]{0:T(256)S(1)} %fusion.36), kind=kOutput, calls=%fused_computation.22 | convolution fusion | flops 167792640 | bytes 2753536 | tf_op jit(solution)/shard_map/ts,sfk->tfk/dot_general | solution.py:119
  19.9 7.9 %reduce-precision_convert_fusion.1 = (bf16[256,32,128]{2,1,0:T(8,128)(2,1)S(1)}, bf16[256,32,128]{2,1,0:T(8,128)(2,1)S(1)}) fusion(bf16[256,128,128]{2,1,0:T(8,128)(2,1)} %param.10, bf16[256,32,128]{2,0,1:T(8,128)(2,1)S(1)} %fusion.12), kind=kOutput, calls=%fused_computation.3 | convolution fusion | flops 272629760 | bytes 14680064 | tf_op jit(solution)/shard_map/tfk,tjk->tfj/dot_general | solution.py:122
  27.9 0.4 pad_maximum_fusion
  28.3 1.2 %fusion.9 = bf16[16,32,128]{2,0,1:T(8,128)(2,1)S(1)} fusion(bf16[512,32,128]{2,1,0:T(8,128)(2,1)S(1)} %pad_maximum_fusion, bf16[256,16]{0,1:T(8,128)(2,1)S(1)} %select_convert_fusion.2), kind=kOutput, calls=%fused_computation.19 | convolution fusion | flops 67207168 | bytes 4333568 | tf_op jit(solution)/shard_map/tb,tfj->bfj/dot_general | solution.py:66
  29.5 0.0 copy-start
  29.5 1.5 %collective-permute-start.6 = (bf16[1,16,32,128]{3,1,2,0:T(8,128)(2,1)S(1)}, bf16[1,16,32,128]{3,1,2,0:T(8,128)(2,1)S(1)}, u32[]{:S(2)}, u32[]{:S(2)}) collective-permute-start(bf16[1,16,32,128]{3,1,2,0:T(8,128)(2,1)S(1)} %bitcast.56), channel_id=1, source_target_pairs={{0,2},{1,3},{2,0},{3,1},{4,6},{5,7},{6,4},{7,5},{8,10},{9,11},{10,... | collective-permute-start | bytes 393224 | tf_op jit(solution)/shard_map/ppermute | solution.py:38
  31.0 4.0 %collective-permute-done.6 = bf16[1,16,32,128]{3,1,2,0:T(8,128)(2,1)S(1)} collective-permute-done((bf16[1,16,32,128]{3,1,2,0:T(8,128)(2,1)S(1)}, bf16[1,16,32,128]{3,1,2,0:T(8,128)(2,1)S(1)}, u32[]{:S(2)}, u32[]{:S(2)}) %collective-permute-start.6) | collective-permute-done | bytes 131104 | tf_op jit(solution)/shard_map/ppermute | solution.py:38
  35.1 0.1 collective-permute-start.7
  35.1 0.1 broadcast_in_dim.13
  35.3 0.1 copy_dynamic-update-slice_fusion.3
  35.3 0.1 copy_dynamic-update-slice_fusion.2
  35.4 1.3 %collective-permute-done.7 = bf16[2,16,32,128]{3,1,2,0:T(8,128)(2,1)S(1)} collective-permute-done((bf16[2,16,32,128]{3,1,2,0:T(8,128)(2,1)S(1)}, bf16[2,16,32,128]{3,1,2,0:T(8,128)(2,1)S(1)}, u32[]{:S(2)}, u32[]{:S(2)}) %collective-permute-start.7) | collective-permute-done | bytes 262176 | tf_op jit(solution)/shard_map/ppermute | solution.py:38
  36.7 0.1 copy_dynamic-update-slice_fusion.1
  36.7 0.1 copy_dynamic-update-slice_fusion
  36.8 0.3 broadcast_compare_fusion
  37.1 0.4 convolution_bitcast_fusion.1
  37.5 0.0 copy-done
  37.6 0.5 fusion.8
  38.1 0.2 copy.26
  38.3 3.0 %collective-permute-start.12 = (f32[32,128]{1,0:T(8,128)S(1)}, f32[32,128]{1,0:T(8,128)S(1)}, u32[]{:S(2)}, u32[]{:S(2)}) collective-permute-start(f32[32,128]{1,0:T(8,128)S(1)} %convolution_bitcast_fusion.1), channel_id=1, source_target_pairs={{0,4},{4,0},{8,12},{12,8},{16,20},{20,16},{24,28},{28,24},{1,5},{5... | collective-permute-start | bytes 49160 | tf_op jit(solution)/shard_map/ppermute | solution.py:55
  41.4 0.7 %fusion.31 = bf16[256,32,128]{2,0,1:T(8,128)(2,1)S(1)} fusion(bf16[16,32,128]{2,0,1:T(8,128)(2,1)S(1)} %copy.26, s32[256]{0:T(256)S(1)} %broadcast_subtract_fusion), kind=kOutput, calls=%fused_computation.65 | convolution fusion | flops 33558528 | bytes 2229248 | tf_op jit(solution)/shard_map/tb,bfj->tfj/dot_general | solution.py:141
  42.1 6.0 %reduce-precision_convert_fusion = (bf16[256,32,128]{2,1,0:T(8,128)(2,1)S(1)}, bf16[256,32,128]{2,1,0:T(8,128)(2,1)S(1)}) fusion(bf16[256,128,128]{2,1,0:T(8,128)(2,1)} %param.10, bf16[256,32,128]{2,0,1:T(8,128)(2,1)S(1)} %fusion.31), kind=kOutput, calls=%fused_computation.1 | convolution fusion | flops 272629760 | bytes 14680064 | tf_op jit(solution)/shard_map/tfj,tjk->tfk/dot_general | solution.py:144
  48.1 0.4 pad_maximum_fusion.1
  48.5 0.0 copy-start.1
  48.5 0.0 copy-start.2
  48.5 1.5 %fusion.43 = (bf16[80,32,128]{2,0,1:T(8,128)(2,1)S(1)}, f32[80,32,128]{2,0,1:T(8,128)S(1)}) fusion(bf16[512,32,128]{2,1,0:T(8,128)(2,1)S(1)} %pad_maximum_fusion.1, bf16[256,80]{0,1:T(8,128)(2,1)S(1)} %select_convert_fusion.1), kind=kOutput, calls=%fused_computation.93 | convolution fusion | flops 336035840 | bytes 6201344 | tf_op jit(solution)/shard_map/ts,tfk->sfk/dot_general | solution.py:66
  50.0 0.0 collective-permute-done.12
  50.0 0.1 collective-permute-start.13
  50.2 3.7 %collective-permute-done.13 = f32[32,128]{1,0:T(8,128)S(1)} collective-permute-done((f32[32,128]{1,0:T(8,128)S(1)}, f32[32,128]{1,0:T(8,128)S(1)}, u32[]{:S(2)}, u32[]{:S(2)}) %collective-permute-start.13) | collective-permute-done | bytes 16416 | tf_op jit(solution)/shard_map/ppermute | solution.py:55
  53.8 0.0 collective-permute-start.14
  53.8 0.8 %select_convert_fusion = bf16[16,32,128]{2,1,0:T(8,128)(2,1)} fusion(f32[16,128,128]{2,1,0:T(8,128)S(1)} %get-tuple-element.32, s32[]{:T(128)S(6)} %select_n.49, pred[16,128,128]{2,1,0:T(8,128)(4,1)S(1)} %get-tuple-element.31), kind=kLoop, calls=%fused_computation.31 | loop fusion | flops 196608 | bytes 458756 | tf_op jit(solution)/shard_map/convert_element_type | solution.py:133
  54.6 2.4 %collective-permute-start.8 = (bf16[16,32,128]{2,0,1:T(8,128)(2,1)S(1)}, bf16[16,32,128]{2,0,1:T(8,128)(2,1)S(1)}, u32[]{:S(2)}, u32[]{:S(2)}) collective-permute-start(bf16[16,32,128]{2,0,1:T(8,128)(2,1)S(1)} %get-tuple-element.23), channel_id=1, source_target_pairs={{8,0},{12,4},{16,8},{20,12},{24,16},{28,20},{0,24},{4,28},{9,1},{1... | collective-permute-start | bytes 393224 | tf_op jit(solution)/shard_map/ppermute | solution.py:22
  57.0 0.0 collective-permute-start.11
  57.0 0.0 collective-permute-start.10
  57.0 4.7 %collective-permute-start.9 = (bf16[16,32,128]{2,0,1:T(8,128)(2,1)S(1)}, bf16[16,32,128]{2,0,1:T(8,128)(2,1)S(1)}, u32[]{:S(2)}, u32[]{:S(2)}) collective-permute-start(bf16[16,32,128]{2,0,1:T(8,128)(2,1)S(1)} %get-tuple-element.26), channel_id=1, source_target_pairs={{4,0},{8,4},{12,8},{16,12},{20,16},{24,20},{28,24},{0,28},{5,1},{9... | collective-permute-start | bytes 393224 | tf_op jit(solution)/shard_map/ppermute | solution.py:22
  61.7 0.0 collective-permute-done.14
  61.7 0.0 copy-done.1
  61.7 0.0 copy-done.2
  61.7 0.6 divide_subtract_fusion
  62.4 0.0 collective-permute-done.8
  62.4 3.2 %collective-permute-done.11 = bf16[16,32,128]{2,0,1:T(8,128)(2,1)S(1)} collective-permute-done((bf16[16,32,128]{2,0,1:T(8,128)(2,1)S(1)}, bf16[16,32,128]{2,0,1:T(8,128)(2,1)S(1)}, u32[]{:S(2)}, u32[]{:S(2)}) %collective-permute-start.11) | collective-permute-done | bytes 131104 | tf_op jit(solution)/shard_map/ppermute | solution.py:22
  65.5 1.0 %collective-permute-done.10 = bf16[16,32,128]{2,0,1:T(8,128)(2,1)S(1)} collective-permute-done((bf16[16,32,128]{2,0,1:T(8,128)(2,1)S(1)}, bf16[16,32,128]{2,0,1:T(8,128)(2,1)S(1)}, u32[]{:S(2)}, u32[]{:S(2)}) %collective-permute-start.10) | collective-permute-done | bytes 131104 | tf_op jit(solution)/shard_map/ppermute | solution.py:22
  66.6 0.0 collective-permute-done.9
  66.6 0.1 fusion.16
  66.7 0.8 %copy.22 = f32[16,32,128]{2,1,0:T(8,128)} copy(f32[16,32,128]{2,0,1:T(8,128)S(1)} %fusion.16) | data formatting | bytes 524288
  (18 shorter events, 0.3 us)
Async XLA Ops:
  0.6 16.4 %collective-permute-start.2 = (bf16[16,32,128]{2,1,0:T(8,128)(2,1)}, bf16[16,32,128]{2,1,0:T(8,128)(2,1)S(1)}, u32[]{:S(2)}, u32[]{:S(2)}) collective-permute-start(bf16[16,32,128]{2,1,0:T(8,128)(2,1)} %param.9), channel_id=1, source_target_pairs={{4,0},{8,4},{12,8},{16,12},{20,16},{24,20},{28,24},{0,28},{5,1},{9... | collective-permute-start | bytes 393224 | tf_op jit(solution)/shard_map/ppermute | solution.py:22
  6.7 9.4 %collective-permute-start.1 = (bf16[16,32,128]{2,1,0:T(8,128)(2,1)}, bf16[16,32,128]{2,1,0:T(8,128)(2,1)S(1)}, u32[]{:S(2)}, u32[]{:S(2)}) collective-permute-start(bf16[16,32,128]{2,1,0:T(8,128)(2,1)} %param.9), channel_id=1, source_target_pairs={{28,0},{0,4},{4,8},{8,12},{12,16},{16,20},{20,24},{24,28},{29,1},{... | collective-permute-start | bytes 393224 | tf_op jit(solution)/shard_map/ppermute | solution.py:22
  6.7 9.3 %collective-permute-start = (bf16[16,32,128]{2,1,0:T(8,128)(2,1)}, bf16[16,32,128]{2,1,0:T(8,128)(2,1)S(1)}, u32[]{:S(2)}, u32[]{:S(2)}) collective-permute-start(bf16[16,32,128]{2,1,0:T(8,128)(2,1)} %param.9), channel_id=1, source_target_pairs={{24,0},{28,4},{0,8},{4,12},{8,16},{12,20},{16,24},{20,28},{25,1},{... | collective-permute-start | bytes 393224 | tf_op jit(solution)/shard_map/ppermute | solution.py:22
  6.7 10.9 %collective-permute-start.3 = (bf16[16,32,128]{2,1,0:T(8,128)(2,1)}, bf16[16,32,128]{2,1,0:T(8,128)(2,1)S(1)}, u32[]{:S(2)}, u32[]{:S(2)}) collective-permute-start(bf16[16,32,128]{2,1,0:T(8,128)(2,1)} %param.9), channel_id=1, source_target_pairs={{8,0},{12,4},{16,8},{20,12},{24,16},{28,20},{0,24},{4,28},{9,1},{1... | collective-permute-start | bytes 393224 | tf_op jit(solution)/shard_map/ppermute | solution.py:22
  12.3 5.1 %collective-permute-start.4 = (bf16[1,17,32,128]{3,2,1,0:T(8,128)(2,1)S(1)}, bf16[1,17,32,128]{3,2,1,0:T(8,128)(2,1)S(1)}, u32[]{:S(2)}, u32[]{:S(2)}) collective-permute-start(bf16[1,17,32,128]{3,2,1,0:T(8,128)(2,1)S(1)} %get-tuple-element.29), channel_id=1, source_target_pairs={{0,2},{1,3},{2,0},{3,1},{4,6},{5,7},{6,4},{7,5},{8,10},{9,11},{10,... | collective-permute-start | bytes 417800 | tf_op jit(solution)/shard_map/ppermute | solution.py:38
  17.4 1.6 %collective-permute-start.5 = (bf16[2,17,32,128]{3,2,1,0:T(8,128)(2,1)S(1)}, bf16[2,17,32,128]{3,2,1,0:T(8,128)(2,1)S(1)}, u32[]{:S(2)}, u32[]{:S(2)}) collective-permute-start(bf16[2,17,32,128]{3,2,1,0:T(8,128)(2,1)S(1)} %pad_maximum_fusion.2), channel_id=1, source_target_pairs={{0,1},{1,0},{2,3},{3,2},{4,5},{5,4},{6,7},{7,6},{8,9},{9,8},{10,11... | collective-permute-start | bytes 835592 | tf_op jit(solution)/shard_map/ppermute | solution.py:38
  29.5 8.1 %copy-start = (f32[32,128]{1,0:T(8,128)S(1)}, f32[32,128]{1,0:T(8,128)}, u32[]{:S(2)}) copy-start(f32[32,128]{1,0:T(8,128)} %param.14) | copy-start | bytes 49156
  29.5 5.6 %collective-permute-start.6 = (bf16[1,16,32,128]{3,1,2,0:T(8,128)(2,1)S(1)}, bf16[1,16,32,128]{3,1,2,0:T(8,128)(2,1)S(1)}, u32[]{:S(2)}, u32[]{:S(2)}) collective-permute-start(bf16[1,16,32,128]{3,1,2,0:T(8,128)(2,1)S(1)} %bitcast.56), channel_id=1, source_target_pairs={{0,2},{1,3},{2,0},{3,1},{4,6},{5,7},{6,4},{7,5},{8,10},{9,11},{10,... | collective-permute-start | bytes 393224 | tf_op jit(solution)/shard_map/ppermute | solution.py:38
  35.1 1.6 %collective-permute-start.7 = (bf16[2,16,32,128]{3,1,2,0:T(8,128)(2,1)S(1)}, bf16[2,16,32,128]{3,1,2,0:T(8,128)(2,1)S(1)}, u32[]{:S(2)}, u32[]{:S(2)}) collective-permute-start(bf16[2,16,32,128]{3,1,2,0:T(8,128)(2,1)S(1)} %pad_maximum_fusion.3), channel_id=1, source_target_pairs={{0,1},{1,0},{2,3},{3,2},{4,5},{5,4},{6,7},{7,6},{8,9},{9,8},{10,11... | collective-permute-start | bytes 786440 | tf_op jit(solution)/shard_map/ppermute | solution.py:38
  38.3 11.7 %collective-permute-start.12 = (f32[32,128]{1,0:T(8,128)S(1)}, f32[32,128]{1,0:T(8,128)S(1)}, u32[]{:S(2)}, u32[]{:S(2)}) collective-permute-start(f32[32,128]{1,0:T(8,128)S(1)} %convolution_bitcast_fusion.1), channel_id=1, source_target_pairs={{0,4},{4,0},{8,12},{12,8},{16,20},{20,16},{24,28},{28,24},{1,5},{5... | collective-permute-start | bytes 49160 | tf_op jit(solution)/shard_map/ppermute | solution.py:55
  48.5 13.2 %copy-start.1 = (f32[32,128]{1,0:T(8,128)S(1)}, f32[32,128]{1,0:T(8,128)}, u32[]{:S(2)}) copy-start(f32[32,128]{1,0:T(8,128)} %param.15) | copy-start | bytes 49156
  48.5 13.2 %copy-start.2 = (f32[32,128]{1,0:T(8,128)S(1)}, f32[32,128]{1,0:T(8,128)}, u32[]{:S(2)}) copy-start(f32[32,128]{1,0:T(8,128)} %param.16) | copy-start | bytes 49156
  50.0 3.8 %collective-permute-start.13 = (f32[32,128]{1,0:T(8,128)S(1)}, f32[32,128]{1,0:T(8,128)S(1)}, u32[]{:S(2)}, u32[]{:S(2)}) collective-permute-start(f32[32,128]{1,0:T(8,128)S(1)} %add.84), channel_id=1, source_target_pairs={{0,8},{4,12},{8,0},{12,4},{16,24},{20,28},{24,16},{28,20},{1,9},{5... | collective-permute-start | bytes 49160 | tf_op jit(solution)/shard_map/ppermute | solution.py:55
  53.8 7.9 %collective-permute-start.14 = (f32[32,128]{1,0:T(8,128)S(1)}, f32[32,128]{1,0:T(8,128)S(1)}, u32[]{:S(2)}, u32[]{:S(2)}) collective-permute-start(f32[32,128]{1,0:T(8,128)S(1)} %add.85), channel_id=1, source_target_pairs={{0,16},{4,20},{8,24},{12,28},{16,0},{20,4},{24,8},{28,12},{1,17},{... | collective-permute-start | bytes 49160 | tf_op jit(solution)/shard_map/ppermute | solution.py:55
  54.6 7.7 %collective-permute-start.8 = (bf16[16,32,128]{2,0,1:T(8,128)(2,1)S(1)}, bf16[16,32,128]{2,0,1:T(8,128)(2,1)S(1)}, u32[]{:S(2)}, u32[]{:S(2)}) collective-permute-start(bf16[16,32,128]{2,0,1:T(8,128)(2,1)S(1)} %get-tuple-element.23), channel_id=1, source_target_pairs={{8,0},{12,4},{16,8},{20,12},{24,16},{28,20},{0,24},{4,28},{9,1},{1... | collective-permute-start | bytes 393224 | tf_op jit(solution)/shard_map/ppermute | solution.py:22
  57.0 8.5 %collective-permute-start.11 = (bf16[16,32,128]{2,0,1:T(8,128)(2,1)S(1)}, bf16[16,32,128]{2,0,1:T(8,128)(2,1)S(1)}, u32[]{:S(2)}, u32[]{:S(2)}) collective-permute-start(bf16[16,32,128]{2,0,1:T(8,128)(2,1)S(1)} %get-tuple-element.24), channel_id=1, source_target_pairs={{24,0},{28,4},{0,8},{4,12},{8,16},{12,20},{16,24},{20,28},{25,1},{... | collective-permute-start | bytes 393224 | tf_op jit(solution)/shard_map/ppermute | solution.py:22
  57.0 9.6 %collective-permute-start.10 = (bf16[16,32,128]{2,0,1:T(8,128)(2,1)S(1)}, bf16[16,32,128]{2,0,1:T(8,128)(2,1)S(1)}, u32[]{:S(2)}, u32[]{:S(2)}) collective-permute-start(bf16[16,32,128]{2,0,1:T(8,128)(2,1)S(1)} %get-tuple-element.25), channel_id=1, source_target_pairs={{28,0},{0,4},{4,8},{8,12},{12,16},{16,20},{20,24},{24,28},{29,1},{... | collective-permute-start | bytes 393224 | tf_op jit(solution)/shard_map/ppermute | solution.py:22
  57.0 9.6 %collective-permute-start.9 = (bf16[16,32,128]{2,0,1:T(8,128)(2,1)S(1)}, bf16[16,32,128]{2,0,1:T(8,128)(2,1)S(1)}, u32[]{:S(2)}, u32[]{:S(2)}) collective-permute-start(bf16[16,32,128]{2,0,1:T(8,128)(2,1)S(1)} %get-tuple-element.26), channel_id=1, source_target_pairs={{4,0},{8,4},{12,8},{16,12},{20,16},{24,20},{28,24},{0,28},{5,1},{9... | collective-permute-start | bytes 393224 | tf_op jit(solution)/shard_map/ppermute | solution.py:22

commit v9 on v8

--- a/solution.py
+++ b/solution.py
@@ -120,9 +120,9 @@
         "ts,sfk->tfk", pick_source, nearby, preferred_element_type=jnp.float32
     ).astype(jnp.bfloat16)
     forward_terms = jnp.einsum(
-        "tfk,tjk->tfj", sources, tile_values, preferred_element_type=jnp.float32
+        "tjk,tfk->tjf", tile_values, sources, preferred_element_type=jnp.float32
     )
-    aggregate = summed_by_table(add_row, forward_terms, "tb,tfj->bfj")
+    aggregate = summed_by_table(add_row, forward_terms, "tb,tjf->bfj")
     aggregate = aggregate.astype(jnp.bfloat16)
     aggregate_all = gathered_along(aggregate, "feat", 1)
     column_start = lax.axis_index("feat") * width_local

time: 67.8 us -> 67.8 us (level)
  no operation moved by 1% of the time
where the time goes in v9:
time: 67.8 us; the launch traced here: 67.4 us
  starting transfers between devices  23.3 us (34%)
  matrix products  19.4 us (29%)
  waiting for transfers between devices  15.1 us (22%)
  other arithmetic  5.4 us (8%)
  local copies, waits for them, and re-layouts  2.61 us (4%)
  between operations  1.59 us (2%)
    ppermute x8, starting transfers between devices, passed_along(): return lax.ppermute(block, axis, route)  16.9 us
    dot_general x1, matrix products, per_device(): jnp.einsum('tjk,tfk->tjf', tile_values, sources, preferred_element_type=j...  7.92 us
    ppermute x4, waiting for transfers between devices, gathered_along(): got = lax.ppermute(held, axis, [(i, i ^ mask) for i in range(size)])  7.11 us
    dot_general x1, matrix products, per_device(): jnp.einsum('tfj,tjk->tfk', back_sources, tile_values, preferred_element_t...  5.99 us
    ppermute x8, waiting for transfers between devices, passed_along(): return lax.ppermute(block, axis, route)  4.32 us
    ppermute x3, waiting for transfers between devices, summed_over(): lax.ppermute(block, axis, [(i, i ^ mask) for i in range(size)])  3.69 us
    ppermute x4, starting transfers between devices, gathered_along(): got = lax.ppermute(held, axis, [(i, i ^ mask) for i in range(size)])  3.26 us
    ppermute x3, starting transfers between devices, summed_over(): lax.ppermute(block, axis, [(i, i ^ mask) for i in range(size)])  3.12 us
  transfers between devices with their start and end apart: 15, of which 8 were waited for; matrix products, arithmetic and copies ran while one was open for 22% of the time, Pallas kernels for 0%

profile of v9, /device:TPU:0, one launch (start us, length us, event | category | flops | bytes accessed | tf_op | source)
XLA Modules:
  0.0 67.4 jit_solution(12622929646462378571)
XLA Ops:
  0.6 6.0 %collective-permute-start.2 = (bf16[16,32,128]{2,1,0:T(8,128)(2,1)}, bf16[16,32,128]{2,1,0:T(8,128)(2,1)S(1)}, u32[]{:S(2)}, u32[]{:S(2)}) collective-permute-start(bf16[16,32,128]{2,1,0:T(8,128)(2,1)} %param.9), channel_id=1, source_target_pairs={{4,0},{8,4},{12,8},{16,12},{20,16},{24,20},{28,24},{0,28},{5,1},{9... | collective-permute-start | bytes 393224 | tf_op jit(solution)/shard_map/ppermute | solution.py:22
  6.7 0.0 collective-permute-start.1
  6.7 0.0 collective-permute-start
  6.7 3.8 %collective-permute-start.3 = (bf16[16,32,128]{2,1,0:T(8,128)(2,1)}, bf16[16,32,128]{2,1,0:T(8,128)(2,1)S(1)}, u32[]{:S(2)}, u32[]{:S(2)}) collective-permute-start(bf16[16,32,128]{2,1,0:T(8,128)(2,1)} %param.9), channel_id=1, source_target_pairs={{8,0},{12,4},{16,8},{20,12},{24,16},{28,20},{0,24},{4,28},{9,1},{1... | collective-permute-start | bytes 393224 | tf_op jit(solution)/shard_map/ppermute | solution.py:22
  10.5 0.7 %convert_bitcast_fusion = bf16[1,32,128]{2,1,0:T(8,128)(2,1)S(1)} fusion(f32[32,128]{1,0:T(8,128)} %param.14), kind=kLoop, calls=%fused_computation.74 | loop fusion | flops 4096 | bytes 24576 | tf_op jit(solution)/shard_map/broadcast_in_dim | solution.py:114
  11.2 0.1 broadcast_in_dim.11
  11.3 1.0 %fusion.20 = (bf16[1,17,32,128]{3,2,1,0:T(8,128)(2,1)S(1)}, bf16[17,128,128]{2,1,0:T(8,128)(2,1)S(1)}) fusion(bf16[1,32,128]{2,1,0:T(8,128)(2,1)S(1)} %convert_bitcast_fusion, bf16[16,32,128]{2,1,0:T(8,128)(2,1)} %param.17, bf16[17,128,128]{2,1,0:T(8,128)(2,1)S(1)} %broadcast_in_dim.11, s32[]{:T(128)S(6)} %select_n.49), kind=kLoop, calls=%fused_computation.45 | loop fusion | flops 278528 | bytes 417796 | tf_op jit(solution)/shard_map/stack | solution.py:37
  12.3 1.6 %collective-permute-start.4 = (bf16[1,17,32,128]{3,2,1,0:T(8,128)(2,1)S(1)}, bf16[1,17,32,128]{3,2,1,0:T(8,128)(2,1)S(1)}, u32[]{:S(2)}, u32[]{:S(2)}) collective-permute-start(bf16[1,17,32,128]{3,2,1,0:T(8,128)(2,1)S(1)} %get-tuple-element.29), channel_id=1, source_target_pairs={{0,2},{1,3},{2,0},{3,1},{4,6},{5,7},{6,4},{7,5},{8,10},{9,11},{10,... | collective-permute-start | bytes 417800 | tf_op jit(solution)/shard_map/ppermute | solution.py:38
  14.5 0.7 %broadcast_subtract_fusion = s32[256]{0:T(256)S(1)} fusion(s32[256]{0:T(256)} %param.11, s32[]{:T(128)S(6)} %mul.87), kind=kLoop, calls=%fused_computation.89 | loop fusion | flops 256 | bytes 2052 | tf_op jit(solution)/shard_map/sub | solution.py:95
  15.2 0.7 %fusion.36 = s32[256]{0:T(256)S(1)} fusion(s32[256]{0:T(256)} %param.12, s32[]{:T(128)S(6)} %axis_index.33), kind=kLoop, calls=%fused_computation.85 | loop fusion | flops 9472 | bytes 2052 | tf_op jit(solution)/shard_map/add | solution.py:100
  15.9 0.0 collective-permute-done
  16.0 0.1 collective-permute-done.1
  16.1 0.9 %constant_dynamic-update-slice_fusion.2 = bf16[80,32,128]{2,1,0:T(8,128)(2,1)S(1)} fusion(bf16[80,32,128]{2,1,0:T(8,128)(2,1)S(1)} %constant_dynamic-update-slice_fusion.3, bf16[16,32,128]{2,1,0:T(8,128)(2,1)} %param.9), kind=kLoop, calls=%fused_computation.68 | loop fusion | bytes 262144
  17.0 0.0 collective-permute-done.2
  17.1 0.3 collective-permute-done.4
  17.4 0.1 collective-permute-start.5
  17.5 0.0 collective-permute-done.3
  17.6 1.5 %collective-permute-done.5 = bf16[2,17,32,128]{3,2,1,0:T(8,128)(2,1)S(1)} collective-permute-done((bf16[2,17,32,128]{3,2,1,0:T(8,128)(2,1)S(1)}, bf16[2,17,32,128]{3,2,1,0:T(8,128)(2,1)S(1)}, u32[]{:S(2)}, u32[]{:S(2)}) %collective-permute-start.5) | collective-permute-done | bytes 278560 | tf_op jit(solution)/shard_map/ppermute | solution.py:38
  19.2 0.8 %fusion.12 = bf16[256,32,128]{2,0,1:T(8,128)(2,1)S(1)} fusion(bf16[80,32,128]{2,1,0:T(8,128)(2,1)S(1)} %constant_dynamic-update-slice_fusion, s32[256]{0:T(256)S(1)} %fusion.36), kind=kOutput, calls=%fused_computation.22 | convolution fusion | flops 167792640 | bytes 2753536 | tf_op jit(solution)/shard_map/ts,sfk->tfk/dot_general | solution.py:119
  19.9 7.9 %reduce-precision_convert_fusion.1 = (bf16[256,128,32]{1,2,0:T(8,128)(2,1)S(1)}, bf16[256,128,32]{1,2,0:T(8,128)(2,1)S(1)}) fusion(bf16[256,128,128]{2,1,0:T(8,128)(2,1)} %param.10, bf16[256,32,128]{2,0,1:T(8,128)(2,1)S(1)} %fusion.12), kind=kOutput, calls=%fused_computation.3 | convolution fusion | flops 272629760 | bytes 14680064 | tf_op jit(solution)/shard_map/tjk,tfk->tjf/dot_general | solution.py:122
  27.9 0.4 pad_maximum_fusion
  28.3 1.2 %fusion.9 = bf16[128,32,16]{0,2,1:T(8,128)(2,1)S(1)} fusion(bf16[512,128,32]{1,2,0:T(8,128)(2,1)S(1)} %pad_maximum_fusion, bf16[256,16]{0,1:T(8,128)(2,1)S(1)} %select_convert_fusion.2), kind=kOutput, calls=%fused_computation.19 | convolution fusion | flops 67207168 | bytes 4333568 | tf_op jit(solution)/shard_map/tb,tjf->bfj/dot_general | solution.py:66
  29.5 0.0 copy-start
  29.5 1.5 %collective-permute-start.6 = (bf16[1,16,32,128]{3,1,2,0:T(8,128)(2,1)S(1)}, bf16[1,16,32,128]{3,1,2,0:T(8,128)(2,1)S(1)}, u32[]{:S(2)}, u32[]{:S(2)}) collective-permute-start(bf16[1,16,32,128]{3,1,2,0:T(8,128)(2,1)S(1)} %bitcast.61), channel_id=1, source_target_pairs={{0,2},{1,3},{2,0},{3,1},{4,6},{5,7},{6,4},{7,5},{8,10},{9,11},{10,... | collective-permute-start | bytes 393224 | tf_op jit(solution)/shard_map/ppermute | solution.py:38
  31.0 4.0 %collective-permute-done.6 = bf16[1,16,32,128]{3,1,2,0:T(8,128)(2,1)S(1)} collective-permute-done((bf16[1,16,32,128]{3,1,2,0:T(8,128)(2,1)S(1)}, bf16[1,16,32,128]{3,1,2,0:T(8,128)(2,1)S(1)}, u32[]{:S(2)}, u32[]{:S(2)}) %collective-permute-start.6) | collective-permute-done | bytes 131104 | tf_op jit(solution)/shard_map/ppermute | solution.py:38
  35.1 0.1 collective-permute-start.7
  35.1 0.1 broadcast_in_dim.13
  35.3 0.1 copy_dynamic-update-slice_fusion.3
  35.3 0.1 copy_dynamic-update-slice_fusion.2
  35.4 1.3 %collective-permute-done.7 = bf16[2,16,32,128]{3,1,2,0:T(8,128)(2,1)S(1)} collective-permute-done((bf16[2,16,32,128]{3,1,2,0:T(8,128)(2,1)S(1)}, bf16[2,16,32,128]{3,1,2,0:T(8,128)(2,1)S(1)}, u32[]{:S(2)}, u32[]{:S(2)}) %collective-permute-start.7) | collective-permute-done | bytes 262176 | tf_op jit(solution)/shard_map/ppermute | solution.py:38
  36.7 0.1 copy_dynamic-update-slice_fusion.1
  36.7 0.1 copy_dynamic-update-slice_fusion
  36.8 0.3 broadcast_compare_fusion
  37.1 0.4 convolution_bitcast_fusion.1
  37.5 0.0 copy-done
  37.6 0.5 fusion.8
  38.1 0.2 copy.26
  38.3 3.0 %collective-permute-start.12 = (f32[32,128]{1,0:T(8,128)S(1)}, f32[32,128]{1,0:T(8,128)S(1)}, u32[]{:S(2)}, u32[]{:S(2)}) collective-permute-start(f32[32,128]{1,0:T(8,128)S(1)} %convolution_bitcast_fusion.1), channel_id=1, source_target_pairs={{0,4},{4,0},{8,12},{12,8},{16,20},{20,16},{24,28},{28,24},{1,5},{5... | collective-permute-start | bytes 49160 | tf_op jit(solution)/shard_map/ppermute | solution.py:55
  41.4 0.7 %fusion.31 = bf16[256,32,128]{2,0,1:T(8,128)(2,1)S(1)} fusion(bf16[16,32,128]{2,0,1:T(8,128)(2,1)S(1)} %copy.26, s32[256]{0:T(256)S(1)} %broadcast_subtract_fusion), kind=kOutput, calls=%fused_computation.65 | convolution fusion | flops 33558528 | bytes 2229248 | tf_op jit(solution)/shard_map/tb,bfj->tfj/dot_general | solution.py:141
  42.1 6.0 %reduce-precision_convert_fusion = (bf16[256,32,128]{2,1,0:T(8,128)(2,1)S(1)}, bf16[256,32,128]{2,1,0:T(8,128)(2,1)S(1)}) fusion(bf16[256,128,128]{2,1,0:T(8,128)(2,1)} %param.10, bf16[256,32,128]{2,0,1:T(8,128)(2,1)S(1)} %fusion.31), kind=kOutput, calls=%fused_computation.1 | convolution fusion | flops 272629760 | bytes 14680064 | tf_op jit(solution)/shard_map/tfj,tjk->tfk/dot_general | solution.py:144
  48.1 0.4 pad_maximum_fusion.1
  48.5 0.0 copy-start.1
  48.5 0.0 copy-start.2
  48.5 1.5 %fusion.43 = (bf16[80,32,128]{2,0,1:T(8,128)(2,1)S(1)}, f32[80,32,128]{2,0,1:T(8,128)S(1)}) fusion(bf16[512,32,128]{2,1,0:T(8,128)(2,1)S(1)} %pad_maximum_fusion.1, bf16[256,80]{0,1:T(8,128)(2,1)S(1)} %select_convert_fusion.1), kind=kOutput, calls=%fused_computation.93 | convolution fusion | flops 336035840 | bytes 6201344 | tf_op jit(solution)/shard_map/ts,tfk->sfk/dot_general | solution.py:66
  50.0 0.0 collective-permute-done.12
  50.0 0.1 collective-permute-start.13
  50.2 3.7 %collective-permute-done.13 = f32[32,128]{1,0:T(8,128)S(1)} collective-permute-done((f32[32,128]{1,0:T(8,128)S(1)}, f32[32,128]{1,0:T(8,128)S(1)}, u32[]{:S(2)}, u32[]{:S(2)}) %collective-permute-start.13) | collective-permute-done | bytes 16416 | tf_op jit(solution)/shard_map/ppermute | solution.py:55
  53.8 0.0 collective-permute-start.14
  53.8 0.8 %select_convert_fusion = bf16[16,32,128]{2,1,0:T(8,128)(2,1)} fusion(f32[16,128,128]{2,1,0:T(8,128)S(1)} %get-tuple-element.32, s32[]{:T(128)S(6)} %select_n.49, pred[16,128,128]{2,1,0:T(8,128)(4,1)S(1)} %get-tuple-element.31), kind=kLoop, calls=%fused_computation.31 | loop fusion | flops 196608 | bytes 458756 | tf_op jit(solution)/shard_map/convert_element_type | solution.py:133
  54.6 2.4 %collective-permute-start.8 = (bf16[16,32,128]{2,0,1:T(8,128)(2,1)S(1)}, bf16[16,32,128]{2,0,1:T(8,128)(2,1)S(1)}, u32[]{:S(2)}, u32[]{:S(2)}) collective-permute-start(bf16[16,32,128]{2,0,1:T(8,128)(2,1)S(1)} %get-tuple-element.23), channel_id=1, source_target_pairs={{8,0},{12,4},{16,8},{20,12},{24,16},{28,20},{0,24},{4,28},{9,1},{1... | collective-permute-start | bytes 393224 | tf_op jit(solution)/shard_map/ppermute | solution.py:22
  57.0 0.0 collective-permute-start.11
  57.0 0.0 collective-permute-start.10
  57.0 4.7 %collective-permute-start.9 = (bf16[16,32,128]{2,0,1:T(8,128)(2,1)S(1)}, bf16[16,32,128]{2,0,1:T(8,128)(2,1)S(1)}, u32[]{:S(2)}, u32[]{:S(2)}) collective-permute-start(bf16[16,32,128]{2,0,1:T(8,128)(2,1)S(1)} %get-tuple-element.26), channel_id=1, source_target_pairs={{4,0},{8,4},{12,8},{16,12},{20,16},{24,20},{28,24},{0,28},{5,1},{9... | collective-permute-start | bytes 393224 | tf_op jit(solution)/shard_map/ppermute | solution.py:22
  61.7 0.0 collective-permute-done.14
  61.7 0.0 copy-done.1
  61.7 0.0 copy-done.2
  61.7 0.6 divide_subtract_fusion
  62.4 0.0 collective-permute-done.8
  62.4 3.2 %collective-permute-done.11 = bf16[16,32,128]{2,0,1:T(8,128)(2,1)S(1)} collective-permute-done((bf16[16,32,128]{2,0,1:T(8,128)(2,1)S(1)}, bf16[16,32,128]{2,0,1:T(8,128)(2,1)S(1)}, u32[]{:S(2)}, u32[]{:S(2)}) %collective-permute-start.11) | collective-permute-done | bytes 131104 | tf_op jit(solution)/shard_map/ppermute | solution.py:22
  65.5 1.0 %collective-permute-done.10 = bf16[16,32,128]{2,0,1:T(8,128)(2,1)S(1)} collective-permute-done((bf16[16,32,128]{2,0,1:T(8,128)(2,1)S(1)}, bf16[16,32,128]{2,0,1:T(8,128)(2,1)S(1)}, u32[]{:S(2)}, u32[]{:S(2)}) %collective-permute-start.10) | collective-permute-done | bytes 131104 | tf_op jit(solution)/shard_map/ppermute | solution.py:22
  66.6 0.0 collective-permute-done.9
  66.6 0.1 fusion.16
  66.7 0.8 %copy.22 = f32[16,32,128]{2,1,0:T(8,128)} copy(f32[16,32,128]{2,0,1:T(8,128)S(1)} %fusion.16) | data formatting | bytes 524288
  (18 shorter events, 0.3 us)
Async XLA Ops:
  0.6 16.4 %collective-permute-start.2 = (bf16[16,32,128]{2,1,0:T(8,128)(2,1)}, bf16[16,32,128]{2,1,0:T(8,128)(2,1)S(1)}, u32[]{:S(2)}, u32[]{:S(2)}) collective-permute-start(bf16[16,32,128]{2,1,0:T(8,128)(2,1)} %param.9), channel_id=1, source_target_pairs={{4,0},{8,4},{12,8},{16,12},{20,16},{24,20},{28,24},{0,28},{5,1},{9... | collective-permute-start | bytes 393224 | tf_op jit(solution)/shard_map/ppermute | solution.py:22
  6.7 9.4 %collective-permute-start.1 = (bf16[16,32,128]{2,1,0:T(8,128)(2,1)}, bf16[16,32,128]{2,1,0:T(8,128)(2,1)S(1)}, u32[]{:S(2)}, u32[]{:S(2)}) collective-permute-start(bf16[16,32,128]{2,1,0:T(8,128)(2,1)} %param.9), channel_id=1, source_target_pairs={{28,0},{0,4},{4,8},{8,12},{12,16},{16,20},{20,24},{24,28},{29,1},{... | collective-permute-start | bytes 393224 | tf_op jit(solution)/shard_map/ppermute | solution.py:22
  6.7 9.3 %collective-permute-start = (bf16[16,32,128]{2,1,0:T(8,128)(2,1)}, bf16[16,32,128]{2,1,0:T(8,128)(2,1)S(1)}, u32[]{:S(2)}, u32[]{:S(2)}) collective-permute-start(bf16[16,32,128]{2,1,0:T(8,128)(2,1)} %param.9), channel_id=1, source_target_pairs={{24,0},{28,4},{0,8},{4,12},{8,16},{12,20},{16,24},{20,28},{25,1},{... | collective-permute-start | bytes 393224 | tf_op jit(solution)/shard_map/ppermute | solution.py:22
  6.7 10.9 %collective-permute-start.3 = (bf16[16,32,128]{2,1,0:T(8,128)(2,1)}, bf16[16,32,128]{2,1,0:T(8,128)(2,1)S(1)}, u32[]{:S(2)}, u32[]{:S(2)}) collective-permute-start(bf16[16,32,128]{2,1,0:T(8,128)(2,1)} %param.9), channel_id=1, source_target_pairs={{8,0},{12,4},{16,8},{20,12},{24,16},{28,20},{0,24},{4,28},{9,1},{1... | collective-permute-start | bytes 393224 | tf_op jit(solution)/shard_map/ppermute | solution.py:22
  12.3 5.1 %collective-permute-start.4 = (bf16[1,17,32,128]{3,2,1,0:T(8,128)(2,1)S(1)}, bf16[1,17,32,128]{3,2,1,0:T(8,128)(2,1)S(1)}, u32[]{:S(2)}, u32[]{:S(2)}) collective-permute-start(bf16[1,17,32,128]{3,2,1,0:T(8,128)(2,1)S(1)} %get-tuple-element.29), channel_id=1, source_target_pairs={{0,2},{1,3},{2,0},{3,1},{4,6},{5,7},{6,4},{7,5},{8,10},{9,11},{10,... | collective-permute-start | bytes 417800 | tf_op jit(solution)/shard_map/ppermute | solution.py:38
  17.4 1.6 %collective-permute-start.5 = (bf16[2,17,32,128]{3,2,1,0:T(8,128)(2,1)S(1)}, bf16[2,17,32,128]{3,2,1,0:T(8,128)(2,1)S(1)}, u32[]{:S(2)}, u32[]{:S(2)}) collective-permute-start(bf16[2,17,32,128]{3,2,1,0:T(8,128)(2,1)S(1)} %pad_maximum_fusion.2), channel_id=1, source_target_pairs={{0,1},{1,0},{2,3},{3,2},{4,5},{5,4},{6,7},{7,6},{8,9},{9,8},{10,11... | collective-permute-start | bytes 835592 | tf_op jit(solution)/shard_map/ppermute | solution.py:38
  29.5 8.1 %copy-start = (f32[32,128]{1,0:T(8,128)S(1)}, f32[32,128]{1,0:T(8,128)}, u32[]{:S(2)}) copy-start(f32[32,128]{1,0:T(8,128)} %param.14) | copy-start | bytes 49156
  29.5 5.6 %collective-permute-start.6 = (bf16[1,16,32,128]{3,1,2,0:T(8,128)(2,1)S(1)}, bf16[1,16,32,128]{3,1,2,0:T(8,128)(2,1)S(1)}, u32[]{:S(2)}, u32[]{:S(2)}) collective-permute-start(bf16[1,16,32,128]{3,1,2,0:T(8,128)(2,1)S(1)} %bitcast.61), channel_id=1, source_target_pairs={{0,2},{1,3},{2,0},{3,1},{4,6},{5,7},{6,4},{7,5},{8,10},{9,11},{10,... | collective-permute-start | bytes 393224 | tf_op jit(solution)/shard_map/ppermute | solution.py:38
  35.1 1.6 %collective-permute-start.7 = (bf16[2,16,32,128]{3,1,2,0:T(8,128)(2,1)S(1)}, bf16[2,16,32,128]{3,1,2,0:T(8,128)(2,1)S(1)}, u32[]{:S(2)}, u32[]{:S(2)}) collective-permute-start(bf16[2,16,32,128]{3,1,2,0:T(8,128)(2,1)S(1)} %pad_maximum_fusion.3), channel_id=1, source_target_pairs={{0,1},{1,0},{2,3},{3,2},{4,5},{5,4},{6,7},{7,6},{8,9},{9,8},{10,11... | collective-permute-start | bytes 786440 | tf_op jit(solution)/shard_map/ppermute | solution.py:38
  38.3 11.7 %collective-permute-start.12 = (f32[32,128]{1,0:T(8,128)S(1)}, f32[32,128]{1,0:T(8,128)S(1)}, u32[]{:S(2)}, u32[]{:S(2)}) collective-permute-start(f32[32,128]{1,0:T(8,128)S(1)} %convolution_bitcast_fusion.1), channel_id=1, source_target_pairs={{0,4},{4,0},{8,12},{12,8},{16,20},{20,16},{24,28},{28,24},{1,5},{5... | collective-permute-start | bytes 49160 | tf_op jit(solution)/shard_map/ppermute | solution.py:55
  48.5 13.2 %copy-start.1 = (f32[32,128]{1,0:T(8,128)S(1)}, f32[32,128]{1,0:T(8,128)}, u32[]{:S(2)}) copy-start(f32[32,128]{1,0:T(8,128)} %param.15) | copy-start | bytes 49156
  48.5 13.2 %copy-start.2 = (f32[32,128]{1,0:T(8,128)S(1)}, f32[32,128]{1,0:T(8,128)}, u32[]{:S(2)}) copy-start(f32[32,128]{1,0:T(8,128)} %param.16) | copy-start | bytes 49156
  50.0 3.8 %collective-permute-start.13 = (f32[32,128]{1,0:T(8,128)S(1)}, f32[32,128]{1,0:T(8,128)S(1)}, u32[]{:S(2)}, u32[]{:S(2)}) collective-permute-start(f32[32,128]{1,0:T(8,128)S(1)} %add.84), channel_id=1, source_target_pairs={{0,8},{4,12},{8,0},{12,4},{16,24},{20,28},{24,16},{28,20},{1,9},{5... | collective-permute-start | bytes 49160 | tf_op jit(solution)/shard_map/ppermute | solution.py:55
  53.8 7.9 %collective-permute-start.14 = (f32[32,128]{1,0:T(8,128)S(1)}, f32[32,128]{1,0:T(8,128)S(1)}, u32[]{:S(2)}, u32[]{:S(2)}) collective-permute-start(f32[32,128]{1,0:T(8,128)S(1)} %add.85), channel_id=1, source_target_pairs={{0,16},{4,20},{8,24},{12,28},{16,0},{20,4},{24,8},{28,12},{1,17},{... | collective-permute-start | bytes 49160 | tf_op jit(solution)/shard_map/ppermute | solution.py:55
  54.6 7.7 %collective-permute-start.8 = (bf16[16,32,128]{2,0,1:T(8,128)(2,1)S(1)}, bf16[16,32,128]{2,0,1:T(8,128)(2,1)S(1)}, u32[]{:S(2)}, u32[]{:S(2)}) collective-permute-start(bf16[16,32,128]{2,0,1:T(8,128)(2,1)S(1)} %get-tuple-element.23), channel_id=1, source_target_pairs={{8,0},{12,4},{16,8},{20,12},{24,16},{28,20},{0,24},{4,28},{9,1},{1... | collective-permute-start | bytes 393224 | tf_op jit(solution)/shard_map/ppermute | solution.py:22
  57.0 8.5 %collective-permute-start.11 = (bf16[16,32,128]{2,0,1:T(8,128)(2,1)S(1)}, bf16[16,32,128]{2,0,1:T(8,128)(2,1)S(1)}, u32[]{:S(2)}, u32[]{:S(2)}) collective-permute-start(bf16[16,32,128]{2,0,1:T(8,128)(2,1)S(1)} %get-tuple-element.24), channel_id=1, source_target_pairs={{24,0},{28,4},{0,8},{4,12},{8,16},{12,20},{16,24},{20,28},{25,1},{... | collective-permute-start | bytes 393224 | tf_op jit(solution)/shard_map/ppermute | solution.py:22
  57.0 9.6 %collective-permute-start.10 = (bf16[16,32,128]{2,0,1:T(8,128)(2,1)S(1)}, bf16[16,32,128]{2,0,1:T(8,128)(2,1)S(1)}, u32[]{:S(2)}, u32[]{:S(2)}) collective-permute-start(bf16[16,32,128]{2,0,1:T(8,128)(2,1)S(1)} %get-tuple-element.25), channel_id=1, source_target_pairs={{28,0},{0,4},{4,8},{8,12},{12,16},{16,20},{20,24},{24,28},{29,1},{... | collective-permute-start | bytes 393224 | tf_op jit(solution)/shard_map/ppermute | solution.py:22
  57.0 9.6 %collective-permute-start.9 = (bf16[16,32,128]{2,0,1:T(8,128)(2,1)S(1)}, bf16[16,32,128]{2,0,1:T(8,128)(2,1)S(1)}, u32[]{:S(2)}, u32[]{:S(2)}) collective-permute-start(bf16[16,32,128]{2,0,1:T(8,128)(2,1)S(1)} %get-tuple-element.26), channel_id=1, source_target_pairs={{4,0},{8,4},{12,8},{16,12},{20,16},{24,20},{28,24},{0,28},{5,1},{9... | collective-permute-start | bytes 393224 | tf_op jit(solution)/shard_map/ppermute | solution.py:22

commit v10 on v9

--- a/solution.py
+++ b/solution.py
@@ -50,10 +50,22 @@
     size = lax.axis_size(axis)
     if size & (size - 1):
         return lax.psum(block, axis)
-    mask = 1
-    while mask < size:
-        block = block + lax.ppermute(block, axis, [(i, i ^ mask) for i in range(size)])
-        mask *= 2
+    own = lax.axis_index(axis)
+    stride = 1
+    while stride < size:
+        if stride * 4 <= size:
+            held = [block]
+            for k in (1, 2, 3):
+                route = [(i, i ^ (k * stride)) for i in range(size)]
+                held.append(lax.ppermute(block, axis, route))
+            held = jnp.stack(held)
+            member = (own // stride) % 4
+            ordered = [held[m ^ member] for m in range(4)]
+            block = (ordered[0] + ordered[1]) + (ordered[2] + ordered[3])
+            stride *= 4
+        else:
+            block = block + lax.ppermute(block, axis, [(i, i ^ stride) for i in range(size)])
+            stride *= 2
     return block
 
 

time: 67.8 us -> 68 us (level)
  starting transfers between devices: 23.3 us -> 25.4 us
  waiting for transfers between devices: 15.1 us -> 13.2 us
    ppermute x3 -> x4, waiting for transfers between devices: 3.69 us -> 0.01 us  [the longest x3 0.01 us: summed_over(): held.append(lax.ppermute(block, axis, route))]
    ppermute x8, waiting for transfers between devices: 4.32 us -> 6.03 us  [passed_along(): return lax.ppermute(block, axis, route)]
    ppermute x3 -> x4, starting transfers between devices: 3.12 us -> 4.57 us  [the longest x3 4.5 us: summed_over(): held.append(lax.ppermute(block, axis, route))]
  transfers between devices with their start and end apart: 15 -> 16, of which waited for: 8 -> 7; matrix products, arithmetic and copies ran while one was open for 22% -> 22% of each run, Pallas kernels for 0% -> 0%
where the time goes in v10:
time: 68 us; the launch traced here: 67.6 us
  starting transfers between devices  25.4 us (37%)
  matrix products  19.4 us (29%)
  waiting for transfers between devices  13.2 us (19%)
  other arithmetic  5.43 us (8%)
  local copies, waits for them, and re-layouts  2.6 us (4%)
  between operations  1.65 us (2%)
    ppermute x8, starting transfers between devices, passed_along(): return lax.ppermute(block, axis, route)  17.6 us
    dot_general x1, matrix products, per_device(): jnp.einsum('tjk,tfk->tjf', tile_values, sources, preferred_element_type=j...  7.92 us
    ppermute x4, waiting for transfers between devices, gathered_along(): got = lax.ppermute(held, axis, [(i, i ^ mask) for i in range(size)])  7.11 us
    ppermute x8, waiting for transfers between devices, passed_along(): return lax.ppermute(block, axis, route)  6.03 us
    dot_general x1, matrix products, per_device(): jnp.einsum('tfj,tjk->tfk', back_sources, tile_values, preferred_element_t...  5.99 us
    ppermute x3, starting transfers between devices, summed_over(): held.append(lax.ppermute(block, axis, route))  4.5 us
    ppermute x4, starting transfers between devices, gathered_along(): got = lax.ppermute(held, axis, [(i, i ^ mask) for i in range(size)])  3.26 us
    dot_general x2, matrix products, summed_by_table(): return jnp.einsum(spec, doubled, both, preferred_element_type=jnp.float32)  2.74 us
  transfers between devices with their start and end apart: 16, of which 7 were waited for; matrix products, arithmetic and copies ran while one was open for 22% of the time, Pallas kernels for 0%

profile of v10, /device:TPU:0, one launch (start us, length us, event | category | flops | bytes accessed | tf_op | source)
XLA Modules:
  0.0 67.6 jit_solution(4087845602297089247)
XLA Ops:
  0.6 6.0 %collective-permute-start.2 = (bf16[16,32,128]{2,1,0:T(8,128)(2,1)}, bf16[16,32,128]{2,1,0:T(8,128)(2,1)S(1)}, u32[]{:S(2)}, u32[]{:S(2)}) collective-permute-start(bf16[16,32,128]{2,1,0:T(8,128)(2,1)} %param.9), channel_id=1, source_target_pairs={{4,0},{8,4},{12,8},{16,12},{20,16},{24,20},{28,24},{0,28},{5,1},{9... | collective-permute-start | bytes 393224 | tf_op jit(solution)/shard_map/ppermute | solution.py:22
  6.7 0.0 collective-permute-start.1
  6.7 0.0 collective-permute-start
  6.7 3.8 %collective-permute-start.3 = (bf16[16,32,128]{2,1,0:T(8,128)(2,1)}, bf16[16,32,128]{2,1,0:T(8,128)(2,1)S(1)}, u32[]{:S(2)}, u32[]{:S(2)}) collective-permute-start(bf16[16,32,128]{2,1,0:T(8,128)(2,1)} %param.9), channel_id=1, source_target_pairs={{8,0},{12,4},{16,8},{20,12},{24,16},{28,20},{0,24},{4,28},{9,1},{1... | collective-permute-start | bytes 393224 | tf_op jit(solution)/shard_map/ppermute | solution.py:22
  10.5 0.7 %convert_bitcast_fusion = bf16[1,32,128]{2,1,0:T(8,128)(2,1)S(1)} fusion(f32[32,128]{1,0:T(8,128)} %param.14), kind=kLoop, calls=%fused_computation.76 | loop fusion | flops 4096 | bytes 24576 | tf_op jit(solution)/shard_map/broadcast_in_dim | solution.py:126
  11.2 0.1 broadcast_in_dim.11
  11.3 1.0 %fusion.21 = (bf16[1,17,32,128]{3,2,1,0:T(8,128)(2,1)S(1)}, bf16[17,128,128]{2,1,0:T(8,128)(2,1)S(1)}) fusion(bf16[1,32,128]{2,1,0:T(8,128)(2,1)S(1)} %convert_bitcast_fusion, bf16[16,32,128]{2,1,0:T(8,128)(2,1)} %param.17, bf16[17,128,128]{2,1,0:T(8,128)(2,1)S(1)} %broadcast_in_dim.11, s32[]{:T(128)S(6)} %select_n.69), kind=kLoop, calls=%fused_computation.45 | loop fusion | flops 278528 | bytes 417796 | tf_op jit(solution)/shard_map/stack | solution.py:37
  12.3 1.6 %collective-permute-start.4 = (bf16[1,17,32,128]{3,2,1,0:T(8,128)(2,1)S(1)}, bf16[1,17,32,128]{3,2,1,0:T(8,128)(2,1)S(1)}, u32[]{:S(2)}, u32[]{:S(2)}) collective-permute-start(bf16[1,17,32,128]{3,2,1,0:T(8,128)(2,1)S(1)} %get-tuple-element.29), channel_id=1, source_target_pairs={{0,2},{1,3},{2,0},{3,1},{4,6},{5,7},{6,4},{7,5},{8,10},{9,11},{10,... | collective-permute-start | bytes 417800 | tf_op jit(solution)/shard_map/ppermute | solution.py:38
  14.5 0.7 %broadcast_subtract_fusion = s32[256]{0:T(256)S(1)} fusion(s32[256]{0:T(256)} %param.11, s32[]{:T(128)S(6)} %mul.87), kind=kLoop, calls=%fused_computation.91 | loop fusion | flops 256 | bytes 2052 | tf_op jit(solution)/shard_map/sub | solution.py:107
  15.2 0.7 %fusion.37 = s32[256]{0:T(256)S(1)} fusion(s32[256]{0:T(256)} %param.12, s32[]{:T(128)S(6)} %axis_index.17), kind=kLoop, calls=%fused_computation.87 | loop fusion | flops 9472 | bytes 2052 | tf_op jit(solution)/shard_map/add | solution.py:112
  16.0 0.0 collective-permute-done
  16.0 0.1 collective-permute-done.1
  16.1 0.9 %constant_dynamic-update-slice_fusion.2 = bf16[80,32,128]{2,1,0:T(8,128)(2,1)S(1)} fusion(bf16[80,32,128]{2,1,0:T(8,128)(2,1)S(1)} %constant_dynamic-update-slice_fusion.3, bf16[16,32,128]{2,1,0:T(8,128)(2,1)} %param.9), kind=kLoop, calls=%fused_computation.70 | loop fusion | bytes 262144
  17.0 0.0 collective-permute-done.2
  17.1 0.3 collective-permute-done.4
  17.4 0.1 collective-permute-start.5
  17.5 0.0 collective-permute-done.3
  17.6 1.5 %collective-permute-done.5 = bf16[2,17,32,128]{3,2,1,0:T(8,128)(2,1)S(1)} collective-permute-done((bf16[2,17,32,128]{3,2,1,0:T(8,128)(2,1)S(1)}, bf16[2,17,32,128]{3,2,1,0:T(8,128)(2,1)S(1)}, u32[]{:S(2)}, u32[]{:S(2)}) %collective-permute-start.5) | collective-permute-done | bytes 278560 | tf_op jit(solution)/shard_map/ppermute | solution.py:38
  19.2 0.8 %fusion.12 = bf16[256,32,128]{2,0,1:T(8,128)(2,1)S(1)} fusion(bf16[80,32,128]{2,1,0:T(8,128)(2,1)S(1)} %constant_dynamic-update-slice_fusion, s32[256]{0:T(256)S(1)} %fusion.37), kind=kOutput, calls=%fused_computation.21 | convolution fusion | flops 167792640 | bytes 2753536 | tf_op jit(solution)/shard_map/ts,sfk->tfk/dot_general | solution.py:131
  19.9 7.9 %reduce-precision_convert_fusion.1 = (bf16[256,128,32]{1,2,0:T(8,128)(2,1)S(1)}, bf16[256,128,32]{1,2,0:T(8,128)(2,1)S(1)}) fusion(bf16[256,128,128]{2,1,0:T(8,128)(2,1)} %param.10, bf16[256,32,128]{2,0,1:T(8,128)(2,1)S(1)} %fusion.12), kind=kOutput, calls=%fused_computation.3 | convolution fusion | flops 272629760 | bytes 14680064 | tf_op jit(solution)/shard_map/tjk,tfk->tjf/dot_general | solution.py:134
  27.9 0.4 pad_maximum_fusion
  28.3 1.2 %fusion.9 = bf16[128,32,16]{0,2,1:T(8,128)(2,1)S(1)} fusion(bf16[512,128,32]{1,2,0:T(8,128)(2,1)S(1)} %pad_maximum_fusion, bf16[256,16]{0,1:T(8,128)(2,1)S(1)} %select_convert_fusion.2), kind=kOutput, calls=%fused_computation.19 | convolution fusion | flops 67207168 | bytes 4333568 | tf_op jit(solution)/shard_map/tb,tjf->bfj/dot_general | solution.py:78
  29.5 1.5 %collective-permute-start.6 = (bf16[1,16,32,128]{3,1,2,0:T(8,128)(2,1)S(1)}, bf16[1,16,32,128]{3,1,2,0:T(8,128)(2,1)S(1)}, u32[]{:S(2)}, u32[]{:S(2)}) collective-permute-start(bf16[1,16,32,128]{3,1,2,0:T(8,128)(2,1)S(1)} %bitcast.68), channel_id=1, source_target_pairs={{0,2},{1,3},{2,0},{3,1},{4,6},{5,7},{6,4},{7,5},{8,10},{9,11},{10,... | collective-permute-start | bytes 393224 | tf_op jit(solution)/shard_map/ppermute | solution.py:38
  31.0 4.0 %collective-permute-done.6 = bf16[1,16,32,128]{3,1,2,0:T(8,128)(2,1)S(1)} collective-permute-done((bf16[1,16,32,128]{3,1,2,0:T(8,128)(2,1)S(1)}, bf16[1,16,32,128]{3,1,2,0:T(8,128)(2,1)S(1)}, u32[]{:S(2)}, u32[]{:S(2)}) %collective-permute-start.6) | collective-permute-done | bytes 131104 | tf_op jit(solution)/shard_map/ppermute | solution.py:38
  35.1 0.1 collective-permute-start.7
  35.1 0.1 broadcast_in_dim.13
  35.3 0.1 copy_dynamic-update-slice_fusion.3
  35.3 0.1 copy_dynamic-update-slice_fusion.2
  35.4 1.3 %collective-permute-done.7 = bf16[2,16,32,128]{3,1,2,0:T(8,128)(2,1)S(1)} collective-permute-done((bf16[2,16,32,128]{3,1,2,0:T(8,128)(2,1)S(1)}, bf16[2,16,32,128]{3,1,2,0:T(8,128)(2,1)S(1)}, u32[]{:S(2)}, u32[]{:S(2)}) %collective-permute-start.7) | collective-permute-done | bytes 262176 | tf_op jit(solution)/shard_map/ppermute | solution.py:38
  36.7 0.1 copy_dynamic-update-slice_fusion.1
  36.7 0.1 copy_dynamic-update-slice_fusion
  36.8 0.3 broadcast_compare_fusion
  37.1 0.4 fusion.19
  37.5 0.0 copy-done
  37.6 0.5 fusion.8
  38.1 0.1 collective-permute-start.13
  38.2 3.0 %collective-permute-start.12 = (f32[32,128]{1,0:T(8,128)S(1)}, f32[32,128]{1,0:T(8,128)S(1)}, u32[]{:S(2)}, u32[]{:S(2)}) collective-permute-start(f32[32,128]{1,0:T(8,128)S(1)} %bitcast.74), channel_id=1, source_target_pairs={{0,4},{4,0},{8,12},{12,8},{16,20},{20,16},{24,28},{28,24},{1,5},{5... | collective-permute-start | bytes 49160 | tf_op jit(solution)/shard_map/ppermute | solution.py:60
  41.2 1.4 %collective-permute-start.14 = (f32[32,128]{1,0:T(8,128)S(1)}, f32[32,128]{1,0:T(8,128)S(1)}, u32[]{:S(2)}, u32[]{:S(2)}) collective-permute-start(f32[32,128]{1,0:T(8,128)S(1)} %bitcast.75), channel_id=1, source_target_pairs={{0,12},{4,8},{8,4},{12,0},{16,28},{20,24},{24,20},{28,16},{1,13},{... | collective-permute-start | bytes 49160 | tf_op jit(solution)/shard_map/ppermute | solution.py:60
  42.6 0.2 copy.26
  42.8 0.7 %fusion.32 = bf16[256,32,128]{2,0,1:T(8,128)(2,1)S(1)} fusion(bf16[16,32,128]{2,0,1:T(8,128)(2,1)S(1)} %copy.26, s32[256]{0:T(256)S(1)} %broadcast_subtract_fusion), kind=kOutput, calls=%fused_computation.67 | convolution fusion | flops 33558528 | bytes 2229248 | tf_op jit(solution)/shard_map/tb,bfj->tfj/dot_general | solution.py:153
  43.6 6.0 %reduce-precision_convert_fusion = (bf16[256,32,128]{2,1,0:T(8,128)(2,1)S(1)}, bf16[256,32,128]{2,1,0:T(8,128)(2,1)S(1)}) fusion(bf16[256,128,128]{2,1,0:T(8,128)(2,1)} %param.10, bf16[256,32,128]{2,0,1:T(8,128)(2,1)S(1)} %fusion.32), kind=kOutput, calls=%fused_computation.1 | convolution fusion | flops 272629760 | bytes 14680064 | tf_op jit(solution)/shard_map/tfj,tjk->tfk/dot_general | solution.py:156
  49.6 0.4 pad_maximum_fusion.1
  49.9 0.0 copy-start.1
  49.9 0.0 copy-start.2
  50.0 1.5 %fusion.44 = (bf16[80,32,128]{2,0,1:T(8,128)(2,1)S(1)}, f32[80,32,128]{2,0,1:T(8,128)S(1)}) fusion(bf16[512,32,128]{2,1,0:T(8,128)(2,1)S(1)} %pad_maximum_fusion.1, bf16[256,80]{0,1:T(8,128)(2,1)S(1)} %select_convert_fusion.1), kind=kOutput, calls=%fused_computation.95 | convolution fusion | flops 336035840 | bytes 6201344 | tf_op jit(solution)/shard_map/ts,tfk->sfk/dot_general | solution.py:78
  51.5 0.0 collective-permute-done.13
  51.5 0.0 collective-permute-done.12
  51.5 0.0 collective-permute-done.14
  51.6 0.1 collective-permute-start.15
  51.7 0.8 %select_convert_fusion = bf16[16,32,128]{2,1,0:T(8,128)(2,1)} fusion(f32[16,128,128]{2,1,0:T(8,128)S(1)} %get-tuple-element.32, s32[]{:T(128)S(6)} %select_n.69, pred[16,128,128]{2,1,0:T(8,128)(4,1)S(1)} %get-tuple-element.31), kind=kLoop, calls=%fused_computation.30 | loop fusion | flops 196608 | bytes 458756 | tf_op jit(solution)/shard_map/convert_element_type | solution.py:145
  52.4 2.9 %collective-permute-start.8 = (bf16[16,32,128]{2,0,1:T(8,128)(2,1)S(1)}, bf16[16,32,128]{2,0,1:T(8,128)(2,1)S(1)}, u32[]{:S(2)}, u32[]{:S(2)}) collective-permute-start(bf16[16,32,128]{2,0,1:T(8,128)(2,1)S(1)} %get-tuple-element.23), channel_id=1, source_target_pairs={{8,0},{12,4},{16,8},{20,12},{24,16},{28,20},{0,24},{4,28},{9,1},{1... | collective-permute-start | bytes 393224 | tf_op jit(solution)/shard_map/ppermute | solution.py:22
  55.3 0.0 collective-permute-start.11
  55.3 1.5 %collective-permute-start.10 = (bf16[16,32,128]{2,0,1:T(8,128)(2,1)S(1)}, bf16[16,32,128]{2,0,1:T(8,128)(2,1)S(1)}, u32[]{:S(2)}, u32[]{:S(2)}) collective-permute-start(bf16[16,32,128]{2,0,1:T(8,128)(2,1)S(1)} %get-tuple-element.25), channel_id=1, source_target_pairs={{28,0},{0,4},{4,8},{8,12},{12,16},{16,20},{20,24},{24,28},{29,1},{... | collective-permute-start | bytes 393224 | tf_op jit(solution)/shard_map/ppermute | solution.py:22
  56.9 3.3 %collective-permute-start.9 = (bf16[16,32,128]{2,0,1:T(8,128)(2,1)S(1)}, bf16[16,32,128]{2,0,1:T(8,128)(2,1)S(1)}, u32[]{:S(2)}, u32[]{:S(2)}) collective-permute-start(bf16[16,32,128]{2,0,1:T(8,128)(2,1)S(1)} %get-tuple-element.26), channel_id=1, source_target_pairs={{4,0},{8,4},{12,8},{16,12},{20,16},{24,20},{28,24},{0,28},{5,1},{9... | collective-permute-start | bytes 393224 | tf_op jit(solution)/shard_map/ppermute | solution.py:22
  60.1 0.0 collective-permute-done.15
  60.1 0.0 copy-done.1
  60.2 0.0 copy-done.2
  60.2 0.6 divide_subtract_fusion
  60.8 0.0 collective-permute-done.8
  60.8 2.8 %collective-permute-done.11 = bf16[16,32,128]{2,0,1:T(8,128)(2,1)S(1)} collective-permute-done((bf16[16,32,128]{2,0,1:T(8,128)(2,1)S(1)}, bf16[16,32,128]{2,0,1:T(8,128)(2,1)S(1)}, u32[]{:S(2)}, u32[]{:S(2)}) %collective-permute-start.11) | collective-permute-done | bytes 131104 | tf_op jit(solution)/shard_map/ppermute | solution.py:22
  63.6 3.1 %collective-permute-done.10 = bf16[16,32,128]{2,0,1:T(8,128)(2,1)S(1)} collective-permute-done((bf16[16,32,128]{2,0,1:T(8,128)(2,1)S(1)}, bf16[16,32,128]{2,0,1:T(8,128)(2,1)S(1)}, u32[]{:S(2)}, u32[]{:S(2)}) %collective-permute-start.10) | collective-permute-done | bytes 131104 | tf_op jit(solution)/shard_map/ppermute | solution.py:22
  66.7 0.0 collective-permute-done.9
  66.8 0.1 fusion.16
  66.9 0.8 %copy.22 = f32[16,32,128]{2,1,0:T(8,128)} copy(f32[16,32,128]{2,0,1:T(8,128)S(1)} %fusion.16) | data formatting | bytes 524288
  (19 shorter events, 0.3 us)
Async XLA Ops:
  0.6 16.4 %collective-permute-start.2 = (bf16[16,32,128]{2,1,0:T(8,128)(2,1)}, bf16[16,32,128]{2,1,0:T(8,128)(2,1)S(1)}, u32[]{:S(2)}, u32[]{:S(2)}) collective-permute-start(bf16[16,32,128]{2,1,0:T(8,128)(2,1)} %param.9), channel_id=1, source_target_pairs={{4,0},{8,4},{12,8},{16,12},{20,16},{24,20},{28,24},{0,28},{5,1},{9... | collective-permute-start | bytes 393224 | tf_op jit(solution)/shard_map/ppermute | solution.py:22
  6.7 9.4 %collective-permute-start.1 = (bf16[16,32,128]{2,1,0:T(8,128)(2,1)}, bf16[16,32,128]{2,1,0:T(8,128)(2,1)S(1)}, u32[]{:S(2)}, u32[]{:S(2)}) collective-permute-start(bf16[16,32,128]{2,1,0:T(8,128)(2,1)} %param.9), channel_id=1, source_target_pairs={{28,0},{0,4},{4,8},{8,12},{12,16},{16,20},{20,24},{24,28},{29,1},{... | collective-permute-start | bytes 393224 | tf_op jit(solution)/shard_map/ppermute | solution.py:22
  6.7 9.3 %collective-permute-start = (bf16[16,32,128]{2,1,0:T(8,128)(2,1)}, bf16[16,32,128]{2,1,0:T(8,128)(2,1)S(1)}, u32[]{:S(2)}, u32[]{:S(2)}) collective-permute-start(bf16[16,32,128]{2,1,0:T(8,128)(2,1)} %param.9), channel_id=1, source_target_pairs={{24,0},{28,4},{0,8},{4,12},{8,16},{12,20},{16,24},{20,28},{25,1},{... | collective-permute-start | bytes 393224 | tf_op jit(solution)/shard_map/ppermute | solution.py:22
  6.7 10.9 %collective-permute-start.3 = (bf16[16,32,128]{2,1,0:T(8,128)(2,1)}, bf16[16,32,128]{2,1,0:T(8,128)(2,1)S(1)}, u32[]{:S(2)}, u32[]{:S(2)}) collective-permute-start(bf16[16,32,128]{2,1,0:T(8,128)(2,1)} %param.9), channel_id=1, source_target_pairs={{8,0},{12,4},{16,8},{20,12},{24,16},{28,20},{0,24},{4,28},{9,1},{1... | collective-permute-start | bytes 393224 | tf_op jit(solution)/shard_map/ppermute | solution.py:22
  12.3 5.1 %collective-permute-start.4 = (bf16[1,17,32,128]{3,2,1,0:T(8,128)(2,1)S(1)}, bf16[1,17,32,128]{3,2,1,0:T(8,128)(2,1)S(1)}, u32[]{:S(2)}, u32[]{:S(2)}) collective-permute-start(bf16[1,17,32,128]{3,2,1,0:T(8,128)(2,1)S(1)} %get-tuple-element.29), channel_id=1, source_target_pairs={{0,2},{1,3},{2,0},{3,1},{4,6},{5,7},{6,4},{7,5},{8,10},{9,11},{10,... | collective-permute-start | bytes 417800 | tf_op jit(solution)/shard_map/ppermute | solution.py:38
  17.4 1.6 %collective-permute-start.5 = (bf16[2,17,32,128]{3,2,1,0:T(8,128)(2,1)S(1)}, bf16[2,17,32,128]{3,2,1,0:T(8,128)(2,1)S(1)}, u32[]{:S(2)}, u32[]{:S(2)}) collective-permute-start(bf16[2,17,32,128]{3,2,1,0:T(8,128)(2,1)S(1)} %pad_maximum_fusion.2), channel_id=1, source_target_pairs={{0,1},{1,0},{2,3},{3,2},{4,5},{5,4},{6,7},{7,6},{8,9},{9,8},{10,11... | collective-permute-start | bytes 835592 | tf_op jit(solution)/shard_map/ppermute | solution.py:38
  29.5 8.1 %copy-start = (f32[32,128]{1,0:T(8,128)S(1)}, f32[32,128]{1,0:T(8,128)}, u32[]{:S(2)}) copy-start(f32[32,128]{1,0:T(8,128)} %param.14) | copy-start | bytes 49156
  29.5 5.6 %collective-permute-start.6 = (bf16[1,16,32,128]{3,1,2,0:T(8,128)(2,1)S(1)}, bf16[1,16,32,128]{3,1,2,0:T(8,128)(2,1)S(1)}, u32[]{:S(2)}, u32[]{:S(2)}) collective-permute-start(bf16[1,16,32,128]{3,1,2,0:T(8,128)(2,1)S(1)} %bitcast.68), channel_id=1, source_target_pairs={{0,2},{1,3},{2,0},{3,1},{4,6},{5,7},{6,4},{7,5},{8,10},{9,11},{10,... | collective-permute-start | bytes 393224 | tf_op jit(solution)/shard_map/ppermute | solution.py:38
  35.1 1.6 %collective-permute-start.7 = (bf16[2,16,32,128]{3,1,2,0:T(8,128)(2,1)S(1)}, bf16[2,16,32,128]{3,1,2,0:T(8,128)(2,1)S(1)}, u32[]{:S(2)}, u32[]{:S(2)}) collective-permute-start(bf16[2,16,32,128]{3,1,2,0:T(8,128)(2,1)S(1)} %pad_maximum_fusion.3), channel_id=1, source_target_pairs={{0,1},{1,0},{2,3},{3,2},{4,5},{5,4},{6,7},{7,6},{8,9},{9,8},{10,11... | collective-permute-start | bytes 786440 | tf_op jit(solution)/shard_map/ppermute | solution.py:38
  38.1 13.4 %collective-permute-start.13 = (f32[32,128]{1,0:T(8,128)S(1)}, f32[32,128]{1,0:T(8,128)S(1)}, u32[]{:S(2)}, u32[]{:S(2)}) collective-permute-start(f32[32,128]{1,0:T(8,128)S(1)} %bitcast.73), channel_id=1, source_target_pairs={{0,8},{4,12},{8,0},{12,4},{16,24},{20,28},{24,16},{28,20},{1,9},{5... | collective-permute-start | bytes 49160 | tf_op jit(solution)/shard_map/ppermute | solution.py:60
  38.2 13.4 %collective-permute-start.12 = (f32[32,128]{1,0:T(8,128)S(1)}, f32[32,128]{1,0:T(8,128)S(1)}, u32[]{:S(2)}, u32[]{:S(2)}) collective-permute-start(f32[32,128]{1,0:T(8,128)S(1)} %bitcast.74), channel_id=1, source_target_pairs={{0,4},{4,0},{8,12},{12,8},{16,20},{20,16},{24,28},{28,24},{1,5},{5... | collective-permute-start | bytes 49160 | tf_op jit(solution)/shard_map/ppermute | solution.py:60
  41.2 10.3 %collective-permute-start.14 = (f32[32,128]{1,0:T(8,128)S(1)}, f32[32,128]{1,0:T(8,128)S(1)}, u32[]{:S(2)}, u32[]{:S(2)}) collective-permute-start(f32[32,128]{1,0:T(8,128)S(1)} %bitcast.75), channel_id=1, source_target_pairs={{0,12},{4,8},{8,4},{12,0},{16,28},{20,24},{24,20},{28,16},{1,13},{... | collective-permute-start | bytes 49160 | tf_op jit(solution)/shard_map/ppermute | solution.py:60
  49.9 10.2 %copy-start.1 = (f32[32,128]{1,0:T(8,128)S(1)}, f32[32,128]{1,0:T(8,128)}, u32[]{:S(2)}) copy-start(f32[32,128]{1,0:T(8,128)} %param.15) | copy-start | bytes 49156
  49.9 10.2 %copy-start.2 = (f32[32,128]{1,0:T(8,128)S(1)}, f32[32,128]{1,0:T(8,128)}, u32[]{:S(2)}) copy-start(f32[32,128]{1,0:T(8,128)} %param.16) | copy-start | bytes 49156
  51.6 8.6 %collective-permute-start.15 = (f32[32,128]{1,0:T(8,128)S(1)}, f32[32,128]{1,0:T(8,128)S(1)}, u32[]{:S(2)}, u32[]{:S(2)}) collective-permute-start(f32[32,128]{1,0:T(8,128)S(1)} %add_bitcast_fusion), channel_id=1, source_target_pairs={{0,16},{4,20},{8,24},{12,28},{16,0},{20,4},{24,8},{28,12},{1,17},{... | collective-permute-start | bytes 49160 | tf_op jit(solution)/shard_map/ppermute | solution.py:67
  52.4 8.4 %collective-permute-start.8 = (bf16[16,32,128]{2,0,1:T(8,128)(2,1)S(1)}, bf16[16,32,128]{2,0,1:T(8,128)(2,1)S(1)}, u32[]{:S(2)}, u32[]{:S(2)}) collective-permute-start(bf16[16,32,128]{2,0,1:T(8,128)(2,1)S(1)} %get-tuple-element.23), channel_id=1, source_target_pairs={{8,0},{12,4},{16,8},{20,12},{24,16},{28,20},{0,24},{4,28},{9,1},{1... | collective-permute-start | bytes 393224 | tf_op jit(solution)/shard_map/ppermute | solution.py:22
  55.3 8.3 %collective-permute-start.11 = (bf16[16,32,128]{2,0,1:T(8,128)(2,1)S(1)}, bf16[16,32,128]{2,0,1:T(8,128)(2,1)S(1)}, u32[]{:S(2)}, u32[]{:S(2)}) collective-permute-start(bf16[16,32,128]{2,0,1:T(8,128)(2,1)S(1)} %get-tuple-element.24), channel_id=1, source_target_pairs={{24,0},{28,4},{0,8},{4,12},{8,16},{12,20},{16,24},{20,28},{25,1},{... | collective-permute-start | bytes 393224 | tf_op jit(solution)/shard_map/ppermute | solution.py:22
  55.3 11.4 %collective-permute-start.10 = (bf16[16,32,128]{2,0,1:T(8,128)(2,1)S(1)}, bf16[16,32,128]{2,0,1:T(8,128)(2,1)S(1)}, u32[]{:S(2)}, u32[]{:S(2)}) collective-permute-start(bf16[16,32,128]{2,0,1:T(8,128)(2,1)S(1)} %get-tuple-element.25), channel_id=1, source_target_pairs={{28,0},{0,4},{4,8},{8,12},{12,16},{16,20},{20,24},{24,28},{29,1},{... | collective-permute-start | bytes 393224 | tf_op jit(solution)/shard_map/ppermute | solution.py:22
  56.9 9.9 %collective-permute-start.9 = (bf16[16,32,128]{2,0,1:T(8,128)(2,1)S(1)}, bf16[16,32,128]{2,0,1:T(8,128)(2,1)S(1)}, u32[]{:S(2)}, u32[]{:S(2)}) collective-permute-start(bf16[16,32,128]{2,0,1:T(8,128)(2,1)S(1)} %get-tuple-element.26), channel_id=1, source_target_pairs={{4,0},{8,4},{12,8},{16,12},{20,16},{24,20},{28,24},{0,28},{5,1},{9... | collective-permute-start | bytes 393224 | tf_op jit(solution)/shard_map/ppermute | solution.py:22

commit v11 on v10

--- a/solution.py
+++ b/solution.py
@@ -131,10 +131,12 @@
     sources = jnp.einsum(
         "ts,sfk->tfk", pick_source, nearby, preferred_element_type=jnp.float32
     ).astype(jnp.bfloat16)
+    tiles_turned = jnp.swapaxes(tile_values, 1, 2)
+    tiles_turned, nearby = lax.optimization_barrier((tiles_turned, nearby))
     forward_terms = jnp.einsum(
-        "tjk,tfk->tjf", tile_values, sources, preferred_element_type=jnp.float32
+        "tfk,tkj->tfj", sources, tiles_turned, preferred_element_type=jnp.float32
     )
-    aggregate = summed_by_table(add_row, forward_terms, "tb,tjf->bfj")
+    aggregate = summed_by_table(add_row, forward_terms, "tb,tfj->bfj")
     aggregate = aggregate.astype(jnp.bfloat16)
     aggregate_all = gathered_along(aggregate, "feat", 1)
     column_start = lax.axis_index("feat") * width_local

time: 68 us -> 68 us (level)
  no operation moved by 1% of the time
where the time goes in v11:
time: 68 us; the launch traced here: 67.6 us
  starting transfers between devices  25.4 us (37%)
  matrix products  19.4 us (29%)
  waiting for transfers between devices  13.2 us (19%)
  other arithmetic  5.43 us (8%)
  local copies, waits for them, and re-layouts  2.6 us (4%)
  between operations  1.65 us (2%)
    ppermute x8, starting transfers between devices, passed_along(): return lax.ppermute(block, axis, route)  17.6 us
    dot_general x1, matrix products, per_device(): jnp.einsum('tfk,tkj->tfj', sources, tiles_turned, preferred_element_type=...  7.92 us
    ppermute x4, waiting for transfers between devices, gathered_along(): got = lax.ppermute(held, axis, [(i, i ^ mask) for i in range(size)])  7.11 us
    ppermute x8, waiting for transfers between devices, passed_along(): return lax.ppermute(block, axis, route)  6.03 us
    dot_general x1, matrix products, per_device(): jnp.einsum('tfj,tjk->tfk', back_sources, tile_values, preferred_element_t...  5.99 us
    ppermute x3, starting transfers between devices, summed_over(): held.append(lax.ppermute(block, axis, route))  4.5 us
    ppermute x4, starting transfers between devices, gathered_along(): got = lax.ppermute(held, axis, [(i, i ^ mask) for i in range(size)])  3.26 us
    dot_general x2, matrix products, summed_by_table(): return jnp.einsum(spec, doubled, both, preferred_element_type=jnp.float32)  2.74 us
  transfers between devices with their start and end apart: 16, of which 7 were waited for; matrix products, arithmetic and copies ran while one was open for 22% of the time, Pallas kernels for 0%

profile of v11, /device:TPU:0, one launch (start us, length us, event | category | flops | bytes accessed | tf_op | source)
XLA Modules:
  0.0 67.6 jit_solution(4087845602297089247)
XLA Ops:
  0.6 6.0 %collective-permute-start.2 = (bf16[16,32,128]{2,1,0:T(8,128)(2,1)}, bf16[16,32,128]{2,1,0:T(8,128)(2,1)S(1)}, u32[]{:S(2)}, u32[]{:S(2)}) collective-permute-start(bf16[16,32,128]{2,1,0:T(8,128)(2,1)} %param.9), channel_id=1, source_target_pairs={{4,0},{8,4},{12,8},{16,12},{20,16},{24,20},{28,24},{0,28},{5,1},{9... | collective-permute-start | bytes 393224 | tf_op jit(solution)/shard_map/ppermute | solution.py:22
  6.7 0.0 collective-permute-start.1
  6.7 0.0 collective-permute-start
  6.7 3.8 %collective-permute-start.3 = (bf16[16,32,128]{2,1,0:T(8,128)(2,1)}, bf16[16,32,128]{2,1,0:T(8,128)(2,1)S(1)}, u32[]{:S(2)}, u32[]{:S(2)}) collective-permute-start(bf16[16,32,128]{2,1,0:T(8,128)(2,1)} %param.9), channel_id=1, source_target_pairs={{8,0},{12,4},{16,8},{20,12},{24,16},{28,20},{0,24},{4,28},{9,1},{1... | collective-permute-start | bytes 393224 | tf_op jit(solution)/shard_map/ppermute | solution.py:22
  10.5 0.7 %convert_bitcast_fusion = bf16[1,32,128]{2,1,0:T(8,128)(2,1)S(1)} fusion(f32[32,128]{1,0:T(8,128)} %param.14), kind=kLoop, calls=%fused_computation.76 | loop fusion | flops 4096 | bytes 24576 | tf_op jit(solution)/shard_map/broadcast_in_dim | solution.py:126
  11.2 0.1 broadcast_in_dim.11
  11.3 1.0 %fusion.21 = (bf16[1,17,32,128]{3,2,1,0:T(8,128)(2,1)S(1)}, bf16[17,128,128]{2,1,0:T(8,128)(2,1)S(1)}) fusion(bf16[1,32,128]{2,1,0:T(8,128)(2,1)S(1)} %convert_bitcast_fusion, bf16[16,32,128]{2,1,0:T(8,128)(2,1)} %param.17, bf16[17,128,128]{2,1,0:T(8,128)(2,1)S(1)} %broadcast_in_dim.11, s32[]{:T(128)S(6)} %select_n.69), kind=kLoop, calls=%fused_computation.45 | loop fusion | flops 278528 | bytes 417796 | tf_op jit(solution)/shard_map/stack | solution.py:37
  12.3 1.6 %collective-permute-start.4 = (bf16[1,17,32,128]{3,2,1,0:T(8,128)(2,1)S(1)}, bf16[1,17,32,128]{3,2,1,0:T(8,128)(2,1)S(1)}, u32[]{:S(2)}, u32[]{:S(2)}) collective-permute-start(bf16[1,17,32,128]{3,2,1,0:T(8,128)(2,1)S(1)} %get-tuple-element.31), channel_id=1, source_target_pairs={{0,2},{1,3},{2,0},{3,1},{4,6},{5,7},{6,4},{7,5},{8,10},{9,11},{10,... | collective-permute-start | bytes 417800 | tf_op jit(solution)/shard_map/ppermute | solution.py:38
  14.5 0.7 %broadcast_subtract_fusion = s32[256]{0:T(256)S(1)} fusion(s32[256]{0:T(256)} %param.11, s32[]{:T(128)S(6)} %mul.86), kind=kLoop, calls=%fused_computation.91 | loop fusion | flops 256 | bytes 2052 | tf_op jit(solution)/shard_map/sub | solution.py:107
  15.2 0.7 %fusion.37 = s32[256]{0:T(256)S(1)} fusion(s32[256]{0:T(256)} %param.12, s32[]{:T(128)S(6)} %axis_index.17), kind=kLoop, calls=%fused_computation.87 | loop fusion | flops 9472 | bytes 2052 | tf_op jit(solution)/shard_map/add | solution.py:112
  16.0 0.0 collective-permute-done
  16.0 0.1 collective-permute-done.1
  16.1 0.9 %constant_dynamic-update-slice_fusion.2 = bf16[80,32,128]{2,1,0:T(8,128)(2,1)S(1)} fusion(bf16[80,32,128]{2,1,0:T(8,128)(2,1)S(1)} %constant_dynamic-update-slice_fusion.3, bf16[16,32,128]{2,1,0:T(8,128)(2,1)} %param.9), kind=kLoop, calls=%fused_computation.70 | loop fusion | bytes 262144
  17.0 0.0 collective-permute-done.2
  17.1 0.3 collective-permute-done.4
  17.4 0.1 collective-permute-start.5
  17.5 0.0 collective-permute-done.3
  17.6 1.5 %collective-permute-done.5 = bf16[2,17,32,128]{3,2,1,0:T(8,128)(2,1)S(1)} collective-permute-done((bf16[2,17,32,128]{3,2,1,0:T(8,128)(2,1)S(1)}, bf16[2,17,32,128]{3,2,1,0:T(8,128)(2,1)S(1)}, u32[]{:S(2)}, u32[]{:S(2)}) %collective-permute-start.5) | collective-permute-done | bytes 278560 | tf_op jit(solution)/shard_map/ppermute | solution.py:38
  19.2 0.8 %fusion.12 = bf16[256,32,128]{2,0,1:T(8,128)(2,1)S(1)} fusion(bf16[80,32,128]{2,1,0:T(8,128)(2,1)S(1)} %constant_dynamic-update-slice_fusion, s32[256]{0:T(256)S(1)} %fusion.37), kind=kOutput, calls=%fused_computation.21 | convolution fusion | flops 167792640 | bytes 2753536 | tf_op jit(solution)/shard_map/ts,sfk->tfk/dot_general | solution.py:131
  19.9 7.9 %reduce-precision_convert_fusion.1 = (bf16[256,32,128]{2,1,0:T(8,128)(2,1)S(1)}, bf16[256,32,128]{2,1,0:T(8,128)(2,1)S(1)}) fusion(bf16[256,128,128]{1,2,0:T(8,128)(2,1)} %bitcast.64, bf16[256,32,128]{2,0,1:T(8,128)(2,1)S(1)} %fusion.12), kind=kOutput, calls=%fused_computation.3 | convolution fusion | flops 272629760 | bytes 14680064 | tf_op jit(solution)/shard_map/tfk,tkj->tfj/dot_general | solution.py:136
  27.9 0.4 pad_maximum_fusion
  28.3 1.2 %fusion.9 = bf16[16,32,128]{2,0,1:T(8,128)(2,1)S(1)} fusion(bf16[512,32,128]{2,1,0:T(8,128)(2,1)S(1)} %pad_maximum_fusion, bf16[256,16]{0,1:T(8,128)(2,1)S(1)} %select_convert_fusion.2), kind=kOutput, calls=%fused_computation.19 | convolution fusion | flops 67207168 | bytes 4333568 | tf_op jit(solution)/shard_map/tb,tfj->bfj/dot_general | solution.py:78
  29.5 1.5 %collective-permute-start.6 = (bf16[1,16,32,128]{3,1,2,0:T(8,128)(2,1)S(1)}, bf16[1,16,32,128]{3,1,2,0:T(8,128)(2,1)S(1)}, u32[]{:S(2)}, u32[]{:S(2)}) collective-permute-start(bf16[1,16,32,128]{3,1,2,0:T(8,128)(2,1)S(1)} %bitcast.65), channel_id=1, source_target_pairs={{0,2},{1,3},{2,0},{3,1},{4,6},{5,7},{6,4},{7,5},{8,10},{9,11},{10,... | collective-permute-start | bytes 393224 | tf_op jit(solution)/shard_map/ppermute | solution.py:38
  31.0 4.0 %collective-permute-done.6 = bf16[1,16,32,128]{3,1,2,0:T(8,128)(2,1)S(1)} collective-permute-done((bf16[1,16,32,128]{3,1,2,0:T(8,128)(2,1)S(1)}, bf16[1,16,32,128]{3,1,2,0:T(8,128)(2,1)S(1)}, u32[]{:S(2)}, u32[]{:S(2)}) %collective-permute-start.6) | collective-permute-done | bytes 131104 | tf_op jit(solution)/shard_map/ppermute | solution.py:38
  35.1 0.1 collective-permute-start.7
  35.1 0.1 broadcast_in_dim.13
  35.3 0.1 copy_dynamic-update-slice_fusion.3
  35.3 0.1 copy_dynamic-update-slice_fusion.2
  35.4 1.3 %collective-permute-done.7 = bf16[2,16,32,128]{3,1,2,0:T(8,128)(2,1)S(1)} collective-permute-done((bf16[2,16,32,128]{3,1,2,0:T(8,128)(2,1)S(1)}, bf16[2,16,32,128]{3,1,2,0:T(8,128)(2,1)S(1)}, u32[]{:S(2)}, u32[]{:S(2)}) %collective-permute-start.7) | collective-permute-done | bytes 262176 | tf_op jit(solution)/shard_map/ppermute | solution.py:38
  36.7 0.1 copy_dynamic-update-slice_fusion.1
  36.7 0.1 copy_dynamic-update-slice_fusion
  36.8 0.3 broadcast_compare_fusion
  37.1 0.4 fusion.19
  37.5 0.0 copy-done
  37.6 0.5 fusion.8
  38.1 0.1 collective-permute-start.13
  38.2 3.0 %collective-permute-start.12 = (f32[32,128]{1,0:T(8,128)S(1)}, f32[32,128]{1,0:T(8,128)S(1)}, u32[]{:S(2)}, u32[]{:S(2)}) collective-permute-start(f32[32,128]{1,0:T(8,128)S(1)} %bitcast.69), channel_id=1, source_target_pairs={{0,4},{4,0},{8,12},{12,8},{16,20},{20,16},{24,28},{28,24},{1,5},{5... | collective-permute-start | bytes 49160 | tf_op jit(solution)/shard_map/ppermute | solution.py:60
  41.2 1.4 %collective-permute-start.14 = (f32[32,128]{1,0:T(8,128)S(1)}, f32[32,128]{1,0:T(8,128)S(1)}, u32[]{:S(2)}, u32[]{:S(2)}) collective-permute-start(f32[32,128]{1,0:T(8,128)S(1)} %bitcast.70), channel_id=1, source_target_pairs={{0,12},{4,8},{8,4},{12,0},{16,28},{20,24},{24,20},{28,16},{1,13},{... | collective-permute-start | bytes 49160 | tf_op jit(solution)/shard_map/ppermute | solution.py:60
  42.6 0.2 copy.28
  42.8 0.7 %fusion.32 = bf16[256,32,128]{2,0,1:T(8,128)(2,1)S(1)} fusion(bf16[16,32,128]{2,0,1:T(8,128)(2,1)S(1)} %copy.28, s32[256]{0:T(256)S(1)} %broadcast_subtract_fusion), kind=kOutput, calls=%fused_computation.67 | convolution fusion | flops 33558528 | bytes 2229248 | tf_op jit(solution)/shard_map/tb,bfj->tfj/dot_general | solution.py:155
  43.6 6.0 %reduce-precision_convert_fusion = (bf16[256,32,128]{2,1,0:T(8,128)(2,1)S(1)}, bf16[256,32,128]{2,1,0:T(8,128)(2,1)S(1)}) fusion(bf16[256,128,128]{2,1,0:T(8,128)(2,1)} %param.10, bf16[256,32,128]{2,0,1:T(8,128)(2,1)S(1)} %fusion.32), kind=kOutput, calls=%fused_computation.1 | convolution fusion | flops 272629760 | bytes 14680064 | tf_op jit(solution)/shard_map/tfj,tjk->tfk/dot_general | solution.py:158
  49.6 0.4 pad_maximum_fusion.1
  49.9 0.0 copy-start.1
  49.9 0.0 copy-start.2
  50.0 1.5 %fusion.44 = (bf16[80,32,128]{2,0,1:T(8,128)(2,1)S(1)}, f32[80,32,128]{2,0,1:T(8,128)S(1)}) fusion(bf16[512,32,128]{2,1,0:T(8,128)(2,1)S(1)} %pad_maximum_fusion.1, bf16[256,80]{0,1:T(8,128)(2,1)S(1)} %select_convert_fusion.1), kind=kOutput, calls=%fused_computation.95 | convolution fusion | flops 336035840 | bytes 6201344 | tf_op jit(solution)/shard_map/ts,tfk->sfk/dot_general | solution.py:78
  51.5 0.0 collective-permute-done.13
  51.5 0.0 collective-permute-done.12
  51.5 0.0 collective-permute-done.14
  51.6 0.1 collective-permute-start.15
  51.7 0.8 %select_convert_fusion = bf16[16,32,128]{2,1,0:T(8,128)(2,1)} fusion(f32[16,128,128]{2,1,0:T(8,128)S(1)} %get-tuple-element.34, s32[]{:T(128)S(6)} %select_n.69, pred[16,128,128]{2,1,0:T(8,128)(4,1)S(1)} %get-tuple-element.33), kind=kLoop, calls=%fused_computation.30 | loop fusion | flops 196608 | bytes 458756 | tf_op jit(solution)/shard_map/convert_element_type | solution.py:147
  52.4 2.9 %collective-permute-start.8 = (bf16[16,32,128]{2,0,1:T(8,128)(2,1)S(1)}, bf16[16,32,128]{2,0,1:T(8,128)(2,1)S(1)}, u32[]{:S(2)}, u32[]{:S(2)}) collective-permute-start(bf16[16,32,128]{2,0,1:T(8,128)(2,1)S(1)} %get-tuple-element.25), channel_id=1, source_target_pairs={{8,0},{12,4},{16,8},{20,12},{24,16},{28,20},{0,24},{4,28},{9,1},{1... | collective-permute-start | bytes 393224 | tf_op jit(solution)/shard_map/ppermute | solution.py:22
  55.3 0.0 collective-permute-start.11
  55.3 1.5 %collective-permute-start.10 = (bf16[16,32,128]{2,0,1:T(8,128)(2,1)S(1)}, bf16[16,32,128]{2,0,1:T(8,128)(2,1)S(1)}, u32[]{:S(2)}, u32[]{:S(2)}) collective-permute-start(bf16[16,32,128]{2,0,1:T(8,128)(2,1)S(1)} %get-tuple-element.27), channel_id=1, source_target_pairs={{28,0},{0,4},{4,8},{8,12},{12,16},{16,20},{20,24},{24,28},{29,1},{... | collective-permute-start | bytes 393224 | tf_op jit(solution)/shard_map/ppermute | solution.py:22
  56.9 3.3 %collective-permute-start.9 = (bf16[16,32,128]{2,0,1:T(8,128)(2,1)S(1)}, bf16[16,32,128]{2,0,1:T(8,128)(2,1)S(1)}, u32[]{:S(2)}, u32[]{:S(2)}) collective-permute-start(bf16[16,32,128]{2,0,1:T(8,128)(2,1)S(1)} %get-tuple-element.28), channel_id=1, source_target_pairs={{4,0},{8,4},{12,8},{16,12},{20,16},{24,20},{28,24},{0,28},{5,1},{9... | collective-permute-start | bytes 393224 | tf_op jit(solution)/shard_map/ppermute | solution.py:22
  60.1 0.0 collective-permute-done.15
  60.1 0.0 copy-done.1
  60.2 0.0 copy-done.2
  60.2 0.6 divide_subtract_fusion
  60.8 0.0 collective-permute-done.8
  60.8 2.8 %collective-permute-done.11 = bf16[16,32,128]{2,0,1:T(8,128)(2,1)S(1)} collective-permute-done((bf16[16,32,128]{2,0,1:T(8,128)(2,1)S(1)}, bf16[16,32,128]{2,0,1:T(8,128)(2,1)S(1)}, u32[]{:S(2)}, u32[]{:S(2)}) %collective-permute-start.11) | collective-permute-done | bytes 131104 | tf_op jit(solution)/shard_map/ppermute | solution.py:22
  63.6 3.1 %collective-permute-done.10 = bf16[16,32,128]{2,0,1:T(8,128)(2,1)S(1)} collective-permute-done((bf16[16,32,128]{2,0,1:T(8,128)(2,1)S(1)}, bf16[16,32,128]{2,0,1:T(8,128)(2,1)S(1)}, u32[]{:S(2)}, u32[]{:S(2)}) %collective-permute-start.10) | collective-permute-done | bytes 131104 | tf_op jit(solution)/shard_map/ppermute | solution.py:22
  66.7 0.0 collective-permute-done.9
  66.8 0.1 fusion.16
  66.9 0.8 %copy.23 = f32[16,32,128]{2,1,0:T(8,128)} copy(f32[16,32,128]{2,0,1:T(8,128)S(1)} %fusion.16) | data formatting | bytes 524288
  (19 shorter events, 0.3 us)
Async XLA Ops:
  0.6 16.4 %collective-permute-start.2 = (bf16[16,32,128]{2,1,0:T(8,128)(2,1)}, bf16[16,32,128]{2,1,0:T(8,128)(2,1)S(1)}, u32[]{:S(2)}, u32[]{:S(2)}) collective-permute-start(bf16[16,32,128]{2,1,0:T(8,128)(2,1)} %param.9), channel_id=1, source_target_pairs={{4,0},{8,4},{12,8},{16,12},{20,16},{24,20},{28,24},{0,28},{5,1},{9... | collective-permute-start | bytes 393224 | tf_op jit(solution)/shard_map/ppermute | solution.py:22
  6.7 9.4 %collective-permute-start.1 = (bf16[16,32,128]{2,1,0:T(8,128)(2,1)}, bf16[16,32,128]{2,1,0:T(8,128)(2,1)S(1)}, u32[]{:S(2)}, u32[]{:S(2)}) collective-permute-start(bf16[16,32,128]{2,1,0:T(8,128)(2,1)} %param.9), channel_id=1, source_target_pairs={{28,0},{0,4},{4,8},{8,12},{12,16},{16,20},{20,24},{24,28},{29,1},{... | collective-permute-start | bytes 393224 | tf_op jit(solution)/shard_map/ppermute | solution.py:22
  6.7 9.3 %collective-permute-start = (bf16[16,32,128]{2,1,0:T(8,128)(2,1)}, bf16[16,32,128]{2,1,0:T(8,128)(2,1)S(1)}, u32[]{:S(2)}, u32[]{:S(2)}) collective-permute-start(bf16[16,32,128]{2,1,0:T(8,128)(2,1)} %param.9), channel_id=1, source_target_pairs={{24,0},{28,4},{0,8},{4,12},{8,16},{12,20},{16,24},{20,28},{25,1},{... | collective-permute-start | bytes 393224 | tf_op jit(solution)/shard_map/ppermute | solution.py:22
  6.7 10.9 %collective-permute-start.3 = (bf16[16,32,128]{2,1,0:T(8,128)(2,1)}, bf16[16,32,128]{2,1,0:T(8,128)(2,1)S(1)}, u32[]{:S(2)}, u32[]{:S(2)}) collective-permute-start(bf16[16,32,128]{2,1,0:T(8,128)(2,1)} %param.9), channel_id=1, source_target_pairs={{8,0},{12,4},{16,8},{20,12},{24,16},{28,20},{0,24},{4,28},{9,1},{1... | collective-permute-start | bytes 393224 | tf_op jit(solution)/shard_map/ppermute | solution.py:22
  12.3 5.1 %collective-permute-start.4 = (bf16[1,17,32,128]{3,2,1,0:T(8,128)(2,1)S(1)}, bf16[1,17,32,128]{3,2,1,0:T(8,128)(2,1)S(1)}, u32[]{:S(2)}, u32[]{:S(2)}) collective-permute-start(bf16[1,17,32,128]{3,2,1,0:T(8,128)(2,1)S(1)} %get-tuple-element.31), channel_id=1, source_target_pairs={{0,2},{1,3},{2,0},{3,1},{4,6},{5,7},{6,4},{7,5},{8,10},{9,11},{10,... | collective-permute-start | bytes 417800 | tf_op jit(solution)/shard_map/ppermute | solution.py:38
  17.4 1.6 %collective-permute-start.5 = (bf16[2,17,32,128]{3,2,1,0:T(8,128)(2,1)S(1)}, bf16[2,17,32,128]{3,2,1,0:T(8,128)(2,1)S(1)}, u32[]{:S(2)}, u32[]{:S(2)}) collective-permute-start(bf16[2,17,32,128]{3,2,1,0:T(8,128)(2,1)S(1)} %pad_maximum_fusion.2), channel_id=1, source_target_pairs={{0,1},{1,0},{2,3},{3,2},{4,5},{5,4},{6,7},{7,6},{8,9},{9,8},{10,11... | collective-permute-start | bytes 835592 | tf_op jit(solution)/shard_map/ppermute | solution.py:38
  29.5 8.1 %copy-start = (f32[32,128]{1,0:T(8,128)S(1)}, f32[32,128]{1,0:T(8,128)}, u32[]{:S(2)}) copy-start(f32[32,128]{1,0:T(8,128)} %param.14) | copy-start | bytes 49156
  29.5 5.6 %collective-permute-start.6 = (bf16[1,16,32,128]{3,1,2,0:T(8,128)(2,1)S(1)}, bf16[1,16,32,128]{3,1,2,0:T(8,128)(2,1)S(1)}, u32[]{:S(2)}, u32[]{:S(2)}) collective-permute-start(bf16[1,16,32,128]{3,1,2,0:T(8,128)(2,1)S(1)} %bitcast.65), channel_id=1, source_target_pairs={{0,2},{1,3},{2,0},{3,1},{4,6},{5,7},{6,4},{7,5},{8,10},{9,11},{10,... | collective-permute-start | bytes 393224 | tf_op jit(solution)/shard_map/ppermute | solution.py:38
  35.1 1.6 %collective-permute-start.7 = (bf16[2,16,32,128]{3,1,2,0:T(8,128)(2,1)S(1)}, bf16[2,16,32,128]{3,1,2,0:T(8,128)(2,1)S(1)}, u32[]{:S(2)}, u32[]{:S(2)}) collective-permute-start(bf16[2,16,32,128]{3,1,2,0:T(8,128)(2,1)S(1)} %pad_maximum_fusion.3), channel_id=1, source_target_pairs={{0,1},{1,0},{2,3},{3,2},{4,5},{5,4},{6,7},{7,6},{8,9},{9,8},{10,11... | collective-permute-start | bytes 786440 | tf_op jit(solution)/shard_map/ppermute | solution.py:38
  38.1 13.4 %collective-permute-start.13 = (f32[32,128]{1,0:T(8,128)S(1)}, f32[32,128]{1,0:T(8,128)S(1)}, u32[]{:S(2)}, u32[]{:S(2)}) collective-permute-start(f32[32,128]{1,0:T(8,128)S(1)} %bitcast.68), channel_id=1, source_target_pairs={{0,8},{4,12},{8,0},{12,4},{16,24},{20,28},{24,16},{28,20},{1,9},{5... | collective-permute-start | bytes 49160 | tf_op jit(solution)/shard_map/ppermute | solution.py:60
  38.2 13.4 %collective-permute-start.12 = (f32[32,128]{1,0:T(8,128)S(1)}, f32[32,128]{1,0:T(8,128)S(1)}, u32[]{:S(2)}, u32[]{:S(2)}) collective-permute-start(f32[32,128]{1,0:T(8,128)S(1)} %bitcast.69), channel_id=1, source_target_pairs={{0,4},{4,0},{8,12},{12,8},{16,20},{20,16},{24,28},{28,24},{1,5},{5... | collective-permute-start | bytes 49160 | tf_op jit(solution)/shard_map/ppermute | solution.py:60
  41.2 10.3 %collective-permute-start.14 = (f32[32,128]{1,0:T(8,128)S(1)}, f32[32,128]{1,0:T(8,128)S(1)}, u32[]{:S(2)}, u32[]{:S(2)}) collective-permute-start(f32[32,128]{1,0:T(8,128)S(1)} %bitcast.70), channel_id=1, source_target_pairs={{0,12},{4,8},{8,4},{12,0},{16,28},{20,24},{24,20},{28,16},{1,13},{... | collective-permute-start | bytes 49160 | tf_op jit(solution)/shard_map/ppermute | solution.py:60
  49.9 10.2 %copy-start.1 = (f32[32,128]{1,0:T(8,128)S(1)}, f32[32,128]{1,0:T(8,128)}, u32[]{:S(2)}) copy-start(f32[32,128]{1,0:T(8,128)} %param.15) | copy-start | bytes 49156
  49.9 10.2 %copy-start.2 = (f32[32,128]{1,0:T(8,128)S(1)}, f32[32,128]{1,0:T(8,128)}, u32[]{:S(2)}) copy-start(f32[32,128]{1,0:T(8,128)} %param.16) | copy-start | bytes 49156
  51.6 8.6 %collective-permute-start.15 = (f32[32,128]{1,0:T(8,128)S(1)}, f32[32,128]{1,0:T(8,128)S(1)}, u32[]{:S(2)}, u32[]{:S(2)}) collective-permute-start(f32[32,128]{1,0:T(8,128)S(1)} %add_bitcast_fusion), channel_id=1, source_target_pairs={{0,16},{4,20},{8,24},{12,28},{16,0},{20,4},{24,8},{28,12},{1,17},{... | collective-permute-start | bytes 49160 | tf_op jit(solution)/shard_map/ppermute | solution.py:67
  52.4 8.4 %collective-permute-start.8 = (bf16[16,32,128]{2,0,1:T(8,128)(2,1)S(1)}, bf16[16,32,128]{2,0,1:T(8,128)(2,1)S(1)}, u32[]{:S(2)}, u32[]{:S(2)}) collective-permute-start(bf16[16,32,128]{2,0,1:T(8,128)(2,1)S(1)} %get-tuple-element.25), channel_id=1, source_target_pairs={{8,0},{12,4},{16,8},{20,12},{24,16},{28,20},{0,24},{4,28},{9,1},{1... | collective-permute-start | bytes 393224 | tf_op jit(solution)/shard_map/ppermute | solution.py:22
  55.3 8.3 %collective-permute-start.11 = (bf16[16,32,128]{2,0,1:T(8,128)(2,1)S(1)}, bf16[16,32,128]{2,0,1:T(8,128)(2,1)S(1)}, u32[]{:S(2)}, u32[]{:S(2)}) collective-permute-start(bf16[16,32,128]{2,0,1:T(8,128)(2,1)S(1)} %get-tuple-element.26), channel_id=1, source_target_pairs={{24,0},{28,4},{0,8},{4,12},{8,16},{12,20},{16,24},{20,28},{25,1},{... | collective-permute-start | bytes 393224 | tf_op jit(solution)/shard_map/ppermute | solution.py:22
  55.3 11.4 %collective-permute-start.10 = (bf16[16,32,128]{2,0,1:T(8,128)(2,1)S(1)}, bf16[16,32,128]{2,0,1:T(8,128)(2,1)S(1)}, u32[]{:S(2)}, u32[]{:S(2)}) collective-permute-start(bf16[16,32,128]{2,0,1:T(8,128)(2,1)S(1)} %get-tuple-element.27), channel_id=1, source_target_pairs={{28,0},{0,4},{4,8},{8,12},{12,16},{16,20},{20,24},{24,28},{29,1},{... | collective-permute-start | bytes 393224 | tf_op jit(solution)/shard_map/ppermute | solution.py:22
  56.9 9.9 %collective-permute-start.9 = (bf16[16,32,128]{2,0,1:T(8,128)(2,1)S(1)}, bf16[16,32,128]{2,0,1:T(8,128)(2,1)S(1)}, u32[]{:S(2)}, u32[]{:S(2)}) collective-permute-start(bf16[16,32,128]{2,0,1:T(8,128)(2,1)S(1)} %get-tuple-element.28), channel_id=1, source_target_pairs={{4,0},{8,4},{12,8},{16,12},{20,16},{24,20},{28,24},{0,28},{5,1},{9... | collective-permute-start | bytes 393224 | tf_op jit(solution)/shard_map/ppermute | solution.py:22

commit v12 on v10

--- a/solution.py
+++ b/solution.py
@@ -3,6 +3,8 @@
 import jax
 import jax.numpy as jnp
 from jax import lax
+from jax.experimental import pallas as pl
+from jax.experimental.pallas import tpu as pltpu
 from jax.sharding import PartitionSpec as P
 
 REACH = 2
@@ -80,6 +82,51 @@
 
 def elu_slope(preact):
     return jnp.where(preact > 0, 1.0, jnp.exp(jnp.minimum(preact, 0.0)))
+
+
+def gathered_terms_kernel(source_ref, row_ref, count_ref, nearby_ref, tiles_ref, out_ref, acc_ref):
+    step = pl.program_id(0)
+    per_step = tiles_ref.shape[0]
+
+    @pl.when(step == 0)
+    def _():
+        acc_ref[...] = jnp.zeros_like(acc_ref)
+
+    for t in range(per_step):
+        slot = step * per_step + t
+
+        @pl.when(slot < count_ref[0])
+        def _():
+            picked = nearby_ref[source_ref[slot]]
+            term = jnp.dot(tiles_ref[t], picked, preferred_element_type=jnp.float32)
+            row = row_ref[slot]
+            acc_ref[row] = acc_ref[row] + term
+
+    @pl.when(step == pl.num_programs(0) - 1)
+    def _():
+        out_ref[...] = acc_ref[...]
+
+
+def aggregate_by_kernel(source_slot, local_row, count, nearby_turned, tile_values, blocks):
+    slots, tile, _ = tile_values.shape
+    width = nearby_turned.shape[2]
+    per_step = 16
+    spec = pltpu.PrefetchScalarGridSpec(
+        num_scalar_prefetch=3,
+        grid=(slots // per_step,),
+        in_specs=[
+            pl.BlockSpec(nearby_turned.shape, lambda i, *_: (0, 0, 0)),
+            pl.BlockSpec((per_step, tile, tile), lambda i, *_: (i, 0, 0)),
+        ],
+        out_specs=pl.BlockSpec((blocks, tile, width), lambda i, *_: (0, 0, 0)),
+        scratch_shapes=[pltpu.VMEM((blocks, tile, width), jnp.float32)],
+    )
+    return pl.pallas_call(
+        gathered_terms_kernel,
+        grid_spec=spec,
+        out_shape=jax.ShapeDtypeStruct((blocks, tile, width), jnp.float32),
+        compiler_params=pltpu.CompilerParams(dimension_semantics=("arbitrary",)),
+    )(source_slot, local_row, count, nearby_turned, tile_values)
 
 
 def one_hot_table(indices, count, dtype):
@@ -111,9 +158,9 @@
     offset = jnp.where(offset > cycle_size // 2, offset - cycle_size, offset)
     source_slot = (offset + REACH) * blocks + col_block
     targets = (2 * REACH + 1) * blocks
-    pick_source = one_hot_table(source_slot, targets, jnp.bfloat16)
+    source_slot = jnp.clip(source_slot, 0, targets - 1)
+    local_row = jnp.clip(local_row, 0, blocks - 1)
     pick_row = one_hot_table(local_row, blocks, jnp.bfloat16)
-    add_row = one_hot_table(local_row, blocks, jnp.float32) * live[:, None]
     add_source = one_hot_table(source_slot, targets, jnp.float32) * live[:, None]
     pieces = []
     for distance in range(-REACH, REACH + 1):
@@ -128,13 +175,10 @@
     cotangent_all = packed_all[:blocks]
     weight_all = packed_all[blocks]
     nearby, cotangent_all, weight_all = lax.optimization_barrier((nearby, cotangent_all, weight_all))
-    sources = jnp.einsum(
-        "ts,sfk->tfk", pick_source, nearby, preferred_element_type=jnp.float32
-    ).astype(jnp.bfloat16)
-    forward_terms = jnp.einsum(
-        "tjk,tfk->tjf", tile_values, sources, preferred_element_type=jnp.float32
-    )
-    aggregate = summed_by_table(add_row, forward_terms, "tb,tjf->bfj")
+    turned = aggregate_by_kernel(
+        source_slot, local_row, tile_count, jnp.swapaxes(nearby, 1, 2), tile_values, blocks
+    )
+    aggregate = jnp.swapaxes(turned, 1, 2)
     aggregate = aggregate.astype(jnp.bfloat16)
     aggregate_all = gathered_along(aggregate, "feat", 1)
     column_start = lax.axis_index("feat") * width_local

time: 68 us -> 108 us (1.59)
  Pallas kernels: 0 us -> 39.6 us
  matrix products: 19.4 us -> 9.18 us
  waiting for transfers between devices: 13.2 us -> 19.8 us
  local copies, waits for them, and re-layouts: 2.6 us -> 6.29 us
  starting transfers between devices: 25.4 us -> 23.9 us
  other arithmetic: 5.43 us -> 6.68 us
    pallas_call x0 -> x1, Pallas kernels: none -> 39.6 us  [aggregate_by_kernel(): pl.pallas_call(gathered_terms_kernel, grid_spec=spec, out_shape=jax.Shape...]
    dot_general x2 -> x0, matrix products: 8.69 us -> none  [the longest x1 7.92 us: per_device(): jnp.einsum('tjk,tfk->tjf', tile_values, sources, preferred_element_type=j...]
    ppermute x4, waiting for transfers between devices: 7.11 us -> 14.9 us  [gathered_along(): got = lax.ppermute(held, axis, [(i, i ^ mask) for i in range(size)])]
    optimization_barrier x0 -> x1, local copies, waits for them, and re-layouts: none -> 3.02 us  [per_device(): lax.optimization_barrier((nearby, cotangent_all, weight_all))]
    another operation x3 -> x4, other arithmetic: 1.01 us -> 2.49 us  [gathered_along(): held = jnp.stack([piece for piece, _ in pieces])]
    min x0 -> x1, other arithmetic: none -> 1.28 us  [per_device(): local_row = jnp.clip(local_row, 0, blocks - 1)]
    dot_general x2 -> x1, matrix products: 2.74 us -> 1.51 us  [summed_by_table(): return jnp.einsum(spec, doubled, both, preferred_element_type=jnp.float32)]
    ppermute x8, waiting for transfers between devices: 6.03 us -> 4.82 us  [passed_along(): return lax.ppermute(block, axis, route)]
  transfers between devices with their start and end apart: 16 -> 16, of which waited for: 7 -> 7; matrix products, arithmetic and copies ran while one was open for 22% -> 14% of each run, Pallas kernels for 0% -> 0%
where the time goes in v12:
time: 108 us; the launch traced here: 107 us
  Pallas kernels  39.6 us (37%)
  starting transfers between devices  23.9 us (22%)
  waiting for transfers between devices  19.8 us (18%)
  matrix products  9.18 us (8%)
  other arithmetic  6.68 us (6%)
  local copies, waits for them, and re-layouts  6.29 us (6%)
  between operations  1.73 us (2%)
    pallas_call x1, Pallas kernels, aggregate_by_kernel(): pl.pallas_call(gathered_terms_kernel, grid_spec=spec, out_shape=jax.Shape...  39.6 us
    ppermute x8, starting transfers between devices, passed_along(): return lax.ppermute(block, axis, route)  17 us
    ppermute x4, waiting for transfers between devices, gathered_along(): got = lax.ppermute(held, axis, [(i, i ^ mask) for i in range(size)])  14.9 us
    dot_general x1, matrix products, per_device(): jnp.einsum('tfj,tjk->tfk', back_sources, tile_values, preferred_element_t...  5.99 us
    ppermute x8, waiting for transfers between devices, passed_along(): return lax.ppermute(block, axis, route)  4.82 us
    ppermute x3, starting transfers between devices, summed_over(): held.append(lax.ppermute(block, axis, route))  3.54 us
    ppermute x4, starting transfers between devices, gathered_along(): got = lax.ppermute(held, axis, [(i, i ^ mask) for i in range(size)])  3.31 us
    optimization_barrier x1, local copies, waits for them, and re-layouts, per_device(): lax.optimization_barrier((nearby, cotangent_all, weight_all))  3.02 us
  transfers between devices with their start and end apart: 16, of which 7 were waited for; matrix products, arithmetic and copies ran while one was open for 14% of the time, Pallas kernels for 0%

profile of v12, /device:TPU:0, one launch (start us, length us, event | category | flops | bytes accessed | tf_op | source)
XLA Modules:
  0.0 107.2 jit_solution(11271362800673490776)
XLA Ops:
  0.6 6.0 %collective-permute-start.2 = (bf16[16,32,128]{2,1,0:T(8,128)(2,1)}, bf16[16,32,128]{2,1,0:T(8,128)(2,1)S(1)}, u32[]{:S(2)}, u32[]{:S(2)}) collective-permute-start(bf16[16,32,128]{2,1,0:T(8,128)(2,1)} %param.9), channel_id=1, source_target_pairs={{4,0},{8,4},{12,8},{16,12},{20,16},{24,20},{28,24},{0,28},{5,1},{9... | collective-permute-start | bytes 393224 | tf_op jit(solution)/shard_map/ppermute | solution.py:24
  6.7 0.0 collective-permute-start.1
  6.7 0.0 collective-permute-start
  6.7 3.8 %collective-permute-start.3 = (bf16[16,32,128]{2,1,0:T(8,128)(2,1)}, bf16[16,32,128]{2,1,0:T(8,128)(2,1)S(1)}, u32[]{:S(2)}, u32[]{:S(2)}) collective-permute-start(bf16[16,32,128]{2,1,0:T(8,128)(2,1)} %param.9), channel_id=1, source_target_pairs={{8,0},{12,4},{16,8},{20,12},{24,16},{28,20},{0,24},{4,28},{9,1},{1... | collective-permute-start | bytes 393224 | tf_op jit(solution)/shard_map/ppermute | solution.py:24
  10.5 0.7 convert_bitcast_fusion.2
  11.2 0.1 broadcast_in_dim.20
  11.3 1.0 fusion.15
  12.3 1.6 %collective-permute-start.4 = (bf16[1,17,32,128]{3,2,1,0:T(8,128)(2,1)S(1)}, bf16[1,17,32,128]{3,2,1,0:T(8,128)(2,1)S(1)}, u32[]{:S(2)}, u32[]{:S(2)}) collective-permute-start(bf16[1,17,32,128]{3,2,1,0:T(8,128)(2,1)S(1)} %get-tuple-element.32), channel_id=1, source_target_pairs={{0,2},{1,3},{2,0},{3,1},{4,6},{5,7},{6,4},{7,5},{8,10},{9,11},{10,... | collective-permute-start | bytes 417800 | tf_op jit(solution)/shard_map/ppermute | solution.py:40
  13.9 1.3 %subtract_clamp_fusion = (s32[256]{0:T(256)}, s32[256]{0:T(256)}) fusion(s32[256]{0:T(256)} %param.11, s32[]{:T(128)S(6)} %mul.79, s32[]{:T(128)S(6)} %axis_index.17, s32[256]{0:T(256)} %param.12), kind=kLoop, calls=%fused_computation.74 | loop fusion | flops 10240 | bytes 4104 | tf_op jit(solution)/shard_map/jit(clip)/min | solution.py:162
  15.8 0.0 collective-permute-done
  15.8 0.3 collective-permute-done.1
  16.1 0.9 constant_dynamic-update-slice_fusion.2
  17.0 0.0 collective-permute-done.2
  17.1 0.3 collective-permute-done.4
  17.4 0.1 collective-permute-start.5
  17.5 0.0 collective-permute-done.3
  17.6 1.5 %collective-permute-done.5 = bf16[2,17,32,128]{3,2,1,0:T(8,128)(2,1)S(1)} collective-permute-done((bf16[2,17,32,128]{3,2,1,0:T(8,128)(2,1)S(1)}, bf16[2,17,32,128]{3,2,1,0:T(8,128)(2,1)S(1)}, u32[]{:S(2)}, u32[]{:S(2)}) %collective-permute-start.5) | collective-permute-done | bytes 278560 | tf_op jit(solution)/shard_map/ppermute | solution.py:40
  19.2 3.0 %copy.27 = bf16[80,32,128]{1,2,0:T(8,128)(2,1)} copy(bf16[80,32,128]{2,1,0:T(8,128)(2,1)S(1)} %constant_dynamic-update-slice_fusion) | data formatting | bytes 1310720 | tf_op jit(solution)/shard_map/optimization_barrier | solution.py:177
  22.2 39.6 %shard_map.128 = f32[16,128,32]{2,1,0:T(8,128)} custom-call(s32[256]{0:T(256)} %get-tuple-element.39.source_ref, s32[256]{0:T(256)} %get-tuple-element.38.row_ref, s32[1]{0:T(128)} %copy.61.count_ref, bf16[80,128,32]{2,1,0:T(8,128)(2,1)} %bitcast.68, bf16[256,128,128]{2,1,0:T(8,128)(2,1)} %tiles_ref.1), custom_call_target="tpu_custom_call" | custom-call | tf_op jit(solution)/shard_map/pallas_call | solution.py:124
  61.8 1.5 %convert_bitcast_fusion = (bf16[1,16,32,128]{2,3,1,0:T(8,128)(2,1)S(1)}, bf16[16,32,128]{1,2,0:T(8,128)(2,1)S(1)}) fusion(f32[16,128,32]{2,1,0:T(8,128)} %shard_map.128), kind=kLoop, calls=%fused_computation.20 | loop fusion | flops 65536 | bytes 524288 | tf_op jit(solution)/shard_map/stack | solution.py:39
  63.3 1.6 %collective-permute-start.6 = (bf16[1,16,32,128]{2,3,1,0:T(8,128)(2,1)S(1)}, bf16[1,16,32,128]{2,3,1,0:T(8,128)(2,1)S(1)}, u32[]{:S(2)}, u32[]{:S(2)}) collective-permute-start(bf16[1,16,32,128]{2,3,1,0:T(8,128)(2,1)S(1)} %get-tuple-element.26), channel_id=1, source_target_pairs={{0,2},{1,3},{2,0},{3,1},{4,6},{5,7},{6,4},{7,5},{8,10},{9,11},{10,... | collective-permute-start | bytes 393224 | tf_op jit(solution)/shard_map/ppermute | solution.py:40
  64.9 0.2 copy.30
  65.1 12.2 %collective-permute-done.6 = bf16[1,16,32,128]{2,3,1,0:T(8,128)(2,1)S(1)} collective-permute-done((bf16[1,16,32,128]{2,3,1,0:T(8,128)(2,1)S(1)}, bf16[1,16,32,128]{2,3,1,0:T(8,128)(2,1)S(1)}, u32[]{:S(2)}, u32[]{:S(2)}) %collective-permute-start.6) | collective-permute-done | bytes 131104 | tf_op jit(solution)/shard_map/ppermute | solution.py:40
  77.3 0.2 copy.31
  77.6 0.1 collective-permute-start.7
  77.7 0.2 copy.28
  77.9 0.1 broadcast_in_dim.22
  78.1 0.2 copy.29
  78.3 0.9 collective-permute-done.7
  79.2 0.0 copy-start
  79.2 0.3 broadcast_compare_fusion
  79.6 0.0 copy-start.3
  79.6 0.3 multiply_convert_fusion
  79.9 0.3 fusion.31
  80.2 0.0 copy-done
  80.2 0.3 fusion.4
  80.5 0.1 collective-permute-start.13
  80.6 0.1 collective-permute-start.12
  80.7 3.4 %collective-permute-start.14 = (f32[32,128]{1,0:T(8,128)S(1)}, f32[32,128]{1,0:T(8,128)S(1)}, u32[]{:S(2)}, u32[]{:S(2)}) collective-permute-start(f32[32,128]{1,0:T(8,128)S(1)} %bitcast.72), channel_id=1, source_target_pairs={{0,12},{4,8},{8,4},{12,0},{16,28},{20,24},{24,20},{28,16},{1,13},{... | collective-permute-start | bytes 49160 | tf_op jit(solution)/shard_map/ppermute | solution.py:62
  84.1 0.2 copy.37
  84.3 0.7 fusion.13
  85.1 6.0 %reduce-precision_convert_fusion = (bf16[256,32,128]{2,1,0:T(8,128)(2,1)S(1)}, bf16[256,32,128]{2,1,0:T(8,128)(2,1)S(1)}) fusion(bf16[256,128,128]{2,1,0:T(8,128)(2,1)} %tiles_ref.1, bf16[256,32,128]{2,0,1:T(8,128)(2,1)S(1)} %fusion.13), kind=kOutput, calls=%fused_computation.1 | convolution fusion | flops 272629760 | bytes 14680064 | tf_op jit(solution)/shard_map/tfj,tjk->tfk/dot_general | solution.py:200
  91.1 0.4 pad_maximum_fusion
  91.4 0.0 copy-start.1
  91.4 0.0 copy-start.2
  91.5 1.5 %fusion.30 = (bf16[80,32,128]{2,0,1:T(8,128)(2,1)S(1)}, f32[80,32,128]{2,0,1:T(8,128)S(1)}) fusion(bf16[512,32,128]{2,1,0:T(8,128)(2,1)S(1)} %pad_maximum_fusion, bf16[256,80]{0,1:T(8,128)(2,1)S(1)} %select_convert_fusion.1), kind=kOutput, calls=%fused_computation.78 | convolution fusion | flops 336035840 | bytes 6201344 | tf_op jit(solution)/shard_map/ts,tfk->sfk/dot_general | solution.py:80
  93.0 0.0 collective-permute-done.13
  93.0 0.0 collective-permute-done.12
  93.0 0.0 collective-permute-done.14
  93.1 0.1 collective-permute-start.15
  93.2 0.8 select_convert_fusion
  93.9 2.4 %collective-permute-start.8 = (bf16[16,32,128]{2,0,1:T(8,128)(2,1)S(1)}, bf16[16,32,128]{2,0,1:T(8,128)(2,1)S(1)}, u32[]{:S(2)}, u32[]{:S(2)}) collective-permute-start(bf16[16,32,128]{2,0,1:T(8,128)(2,1)S(1)} %get-tuple-element.28), channel_id=1, source_target_pairs={{8,0},{12,4},{16,8},{20,12},{24,16},{28,20},{0,24},{4,28},{9,1},{1... | collective-permute-start | bytes 393224 | tf_op jit(solution)/shard_map/ppermute | solution.py:24
  96.4 0.0 collective-permute-start.11
  96.4 0.5 collective-permute-start.10
  96.8 4.2 %collective-permute-start.9 = (bf16[16,32,128]{2,0,1:T(8,128)(2,1)S(1)}, bf16[16,32,128]{2,0,1:T(8,128)(2,1)S(1)}, u32[]{:S(2)}, u32[]{:S(2)}) collective-permute-start(bf16[16,32,128]{2,0,1:T(8,128)(2,1)S(1)} %get-tuple-element.31), channel_id=1, source_target_pairs={{4,0},{8,4},{12,8},{16,12},{20,16},{24,20},{28,24},{0,28},{5,1},{9... | collective-permute-start | bytes 393224 | tf_op jit(solution)/shard_map/ppermute | solution.py:24
  101.1 0.0 collective-permute-done.15
  101.1 0.0 copy-done.1
  101.1 0.6 divide_subtract_fusion
  101.7 0.0 collective-permute-done.8
  101.7 3.6 %collective-permute-done.11 = bf16[16,32,128]{2,0,1:T(8,128)(2,1)S(1)} collective-permute-done((bf16[16,32,128]{2,0,1:T(8,128)(2,1)S(1)}, bf16[16,32,128]{2,0,1:T(8,128)(2,1)S(1)}, u32[]{:S(2)}, u32[]{:S(2)}) %collective-permute-start.11) | collective-permute-done | bytes 131104 | tf_op jit(solution)/shard_map/ppermute | solution.py:24
  105.4 0.9 collective-permute-done.10
  106.3 0.0 collective-permute-done.9
  106.3 0.1 fusion.7
  106.4 0.8 copy.35
  (24 shorter events, 0.4 us)
Async XLA Ops:
  0.6 16.4 %collective-permute-start.2 = (bf16[16,32,128]{2,1,0:T(8,128)(2,1)}, bf16[16,32,128]{2,1,0:T(8,128)(2,1)S(1)}, u32[]{:S(2)}, u32[]{:S(2)}) collective-permute-start(bf16[16,32,128]{2,1,0:T(8,128)(2,1)} %param.9), channel_id=1, source_target_pairs={{4,0},{8,4},{12,8},{16,12},{20,16},{24,20},{28,24},{0,28},{5,1},{9... | collective-permute-start | bytes 393224 | tf_op jit(solution)/shard_map/ppermute | solution.py:24
  6.7 9.4 %collective-permute-start.1 = (bf16[16,32,128]{2,1,0:T(8,128)(2,1)}, bf16[16,32,128]{2,1,0:T(8,128)(2,1)S(1)}, u32[]{:S(2)}, u32[]{:S(2)}) collective-permute-start(bf16[16,32,128]{2,1,0:T(8,128)(2,1)} %param.9), channel_id=1, source_target_pairs={{28,0},{0,4},{4,8},{8,12},{12,16},{16,20},{20,24},{24,28},{29,1},{... | collective-permute-start | bytes 393224 | tf_op jit(solution)/shard_map/ppermute | solution.py:24
  6.7 9.1 %collective-permute-start = (bf16[16,32,128]{2,1,0:T(8,128)(2,1)}, bf16[16,32,128]{2,1,0:T(8,128)(2,1)S(1)}, u32[]{:S(2)}, u32[]{:S(2)}) collective-permute-start(bf16[16,32,128]{2,1,0:T(8,128)(2,1)} %param.9), channel_id=1, source_target_pairs={{24,0},{28,4},{0,8},{4,12},{8,16},{12,20},{16,24},{20,28},{25,1},{... | collective-permute-start | bytes 393224 | tf_op jit(solution)/shard_map/ppermute | solution.py:24
  6.7 10.9 %collective-permute-start.3 = (bf16[16,32,128]{2,1,0:T(8,128)(2,1)}, bf16[16,32,128]{2,1,0:T(8,128)(2,1)S(1)}, u32[]{:S(2)}, u32[]{:S(2)}) collective-permute-start(bf16[16,32,128]{2,1,0:T(8,128)(2,1)} %param.9), channel_id=1, source_target_pairs={{8,0},{12,4},{16,8},{20,12},{24,16},{28,20},{0,24},{4,28},{9,1},{1... | collective-permute-start | bytes 393224 | tf_op jit(solution)/shard_map/ppermute | solution.py:24
  12.3 5.1 %collective-permute-start.4 = (bf16[1,17,32,128]{3,2,1,0:T(8,128)(2,1)S(1)}, bf16[1,17,32,128]{3,2,1,0:T(8,128)(2,1)S(1)}, u32[]{:S(2)}, u32[]{:S(2)}) collective-permute-start(bf16[1,17,32,128]{3,2,1,0:T(8,128)(2,1)S(1)} %get-tuple-element.32), channel_id=1, source_target_pairs={{0,2},{1,3},{2,0},{3,1},{4,6},{5,7},{6,4},{7,5},{8,10},{9,11},{10,... | collective-permute-start | bytes 417800 | tf_op jit(solution)/shard_map/ppermute | solution.py:40
  17.4 1.6 %collective-permute-start.5 = (bf16[2,17,32,128]{3,2,1,0:T(8,128)(2,1)S(1)}, bf16[2,17,32,128]{3,2,1,0:T(8,128)(2,1)S(1)}, u32[]{:S(2)}, u32[]{:S(2)}) collective-permute-start(bf16[2,17,32,128]{3,2,1,0:T(8,128)(2,1)S(1)} %pad_maximum_fusion.1), channel_id=1, source_target_pairs={{0,1},{1,0},{2,3},{3,2},{4,5},{5,4},{6,7},{7,6},{8,9},{9,8},{10,11... | collective-permute-start | bytes 835592 | tf_op jit(solution)/shard_map/ppermute | solution.py:40
  61.8 15.8 %copy-start.4 = (s32[256]{0:T(256)S(1)}, s32[256]{0:T(256)}, u32[]{:S(2)}) copy-start(s32[256]{0:T(256)} %get-tuple-element.39.source_ref) | copy-start | bytes 3076
  63.3 14.0 %collective-permute-start.6 = (bf16[1,16,32,128]{2,3,1,0:T(8,128)(2,1)S(1)}, bf16[1,16,32,128]{2,3,1,0:T(8,128)(2,1)S(1)}, u32[]{:S(2)}, u32[]{:S(2)}) collective-permute-start(bf16[1,16,32,128]{2,3,1,0:T(8,128)(2,1)S(1)} %get-tuple-element.26), channel_id=1, source_target_pairs={{0,2},{1,3},{2,0},{3,1},{4,6},{5,7},{6,4},{7,5},{8,10},{9,11},{10,... | collective-permute-start | bytes 393224 | tf_op jit(solution)/shard_map/ppermute | solution.py:40
  77.6 1.6 %collective-permute-start.7 = (bf16[2,16,32,128]{3,2,1,0:T(8,128)(2,1)S(1)}, bf16[2,16,32,128]{3,2,1,0:T(8,128)(2,1)S(1)}, u32[]{:S(2)}, u32[]{:S(2)}) collective-permute-start(bf16[2,16,32,128]{3,2,1,0:T(8,128)(2,1)S(1)} %pad_maximum_fusion.2), channel_id=1, source_target_pairs={{0,1},{1,0},{2,3},{3,2},{4,5},{5,4},{6,7},{7,6},{8,9},{9,8},{10,11... | collective-permute-start | bytes 786440 | tf_op jit(solution)/shard_map/ppermute | solution.py:40
  79.2 1.0 copy-start
  79.6 4.7 %copy-start.3 = (s32[256]{0:T(256)S(1)}, s32[256]{0:T(256)}, u32[]{:S(2)}) copy-start(s32[256]{0:T(256)} %get-tuple-element.38.row_ref) | copy-start | bytes 3076
  80.5 12.5 %collective-permute-start.13 = (f32[32,128]{1,0:T(8,128)S(1)}, f32[32,128]{1,0:T(8,128)S(1)}, u32[]{:S(2)}, u32[]{:S(2)}) collective-permute-start(f32[32,128]{1,0:T(8,128)S(1)} %bitcast.70), channel_id=1, source_target_pairs={{0,8},{4,12},{8,0},{12,4},{16,24},{20,28},{24,16},{28,20},{1,9},{5... | collective-permute-start | bytes 49160 | tf_op jit(solution)/shard_map/ppermute | solution.py:62
  80.6 12.4 %collective-permute-start.12 = (f32[32,128]{1,0:T(8,128)S(1)}, f32[32,128]{1,0:T(8,128)S(1)}, u32[]{:S(2)}, u32[]{:S(2)}) collective-permute-start(f32[32,128]{1,0:T(8,128)S(1)} %bitcast.71), channel_id=1, source_target_pairs={{0,4},{4,0},{8,12},{12,8},{16,20},{20,16},{24,28},{28,24},{1,5},{5... | collective-permute-start | bytes 49160 | tf_op jit(solution)/shard_map/ppermute | solution.py:62
  80.7 12.4 %collective-permute-start.14 = (f32[32,128]{1,0:T(8,128)S(1)}, f32[32,128]{1,0:T(8,128)S(1)}, u32[]{:S(2)}, u32[]{:S(2)}) collective-permute-start(f32[32,128]{1,0:T(8,128)S(1)} %bitcast.72), channel_id=1, source_target_pairs={{0,12},{4,8},{8,4},{12,0},{16,28},{20,24},{24,20},{28,16},{1,13},{... | collective-permute-start | bytes 49160 | tf_op jit(solution)/shard_map/ppermute | solution.py:62
  91.4 9.7 %copy-start.1 = (f32[32,128]{1,0:T(8,128)S(1)}, f32[32,128]{1,0:T(8,128)}, u32[]{:S(2)}) copy-start(f32[32,128]{1,0:T(8,128)} %param.15) | copy-start | bytes 49156
  91.4 9.6 %copy-start.2 = (f32[32,128]{1,0:T(8,128)S(1)}, f32[32,128]{1,0:T(8,128)}, u32[]{:S(2)}) copy-start(f32[32,128]{1,0:T(8,128)} %param.16) | copy-start | bytes 49156
  93.1 8.0 %collective-permute-start.15 = (f32[32,128]{1,0:T(8,128)S(1)}, f32[32,128]{1,0:T(8,128)S(1)}, u32[]{:S(2)}, u32[]{:S(2)}) collective-permute-start(f32[32,128]{1,0:T(8,128)S(1)} %add_bitcast_fusion), channel_id=1, source_target_pairs={{0,16},{4,20},{8,24},{12,28},{16,0},{20,4},{24,8},{28,12},{1,17},{... | collective-permute-start | bytes 49160 | tf_op jit(solution)/shard_map/ppermute | solution.py:69
  93.9 7.8 %collective-permute-start.8 = (bf16[16,32,128]{2,0,1:T(8,128)(2,1)S(1)}, bf16[16,32,128]{2,0,1:T(8,128)(2,1)S(1)}, u32[]{:S(2)}, u32[]{:S(2)}) collective-permute-start(bf16[16,32,128]{2,0,1:T(8,128)(2,1)S(1)} %get-tuple-element.28), channel_id=1, source_target_pairs={{8,0},{12,4},{16,8},{20,12},{24,16},{28,20},{0,24},{4,28},{9,1},{1... | collective-permute-start | bytes 393224 | tf_op jit(solution)/shard_map/ppermute | solution.py:24
  96.4 9.0 %collective-permute-start.11 = (bf16[16,32,128]{2,0,1:T(8,128)(2,1)S(1)}, bf16[16,32,128]{2,0,1:T(8,128)(2,1)S(1)}, u32[]{:S(2)}, u32[]{:S(2)}) collective-permute-start(bf16[16,32,128]{2,0,1:T(8,128)(2,1)S(1)} %get-tuple-element.29), channel_id=1, source_target_pairs={{24,0},{28,4},{0,8},{4,12},{8,16},{12,20},{16,24},{20,28},{25,1},{... | collective-permute-start | bytes 393224 | tf_op jit(solution)/shard_map/ppermute | solution.py:24
  96.4 9.9 %collective-permute-start.10 = (bf16[16,32,128]{2,0,1:T(8,128)(2,1)S(1)}, bf16[16,32,128]{2,0,1:T(8,128)(2,1)S(1)}, u32[]{:S(2)}, u32[]{:S(2)}) collective-permute-start(bf16[16,32,128]{2,0,1:T(8,128)(2,1)S(1)} %get-tuple-element.30), channel_id=1, source_target_pairs={{28,0},{0,4},{4,8},{8,12},{12,16},{16,20},{20,24},{24,28},{29,1},{... | collective-permute-start | bytes 393224 | tf_op jit(solution)/shard_map/ppermute | solution.py:24
  96.8 9.5 %collective-permute-start.9 = (bf16[16,32,128]{2,0,1:T(8,128)(2,1)S(1)}, bf16[16,32,128]{2,0,1:T(8,128)(2,1)S(1)}, u32[]{:S(2)}, u32[]{:S(2)}) collective-permute-start(bf16[16,32,128]{2,0,1:T(8,128)(2,1)S(1)} %get-tuple-element.31), channel_id=1, source_target_pairs={{4,0},{8,4},{12,8},{16,12},{20,16},{24,20},{28,24},{0,28},{5,1},{9... | collective-permute-start | bytes 393224 | tf_op jit(solution)/shard_map/ppermute | solution.py:24

commit v13 on v12

--- a/solution.py
+++ b/solution.py
@@ -92,30 +92,32 @@
     def _():
         acc_ref[...] = jnp.zeros_like(acc_ref)
 
+    terms = []
     for t in range(per_step):
         slot = step * per_step + t
-
-        @pl.when(slot < count_ref[0])
-        def _():
-            picked = nearby_ref[source_ref[slot]]
-            term = jnp.dot(tiles_ref[t], picked, preferred_element_type=jnp.float32)
-            row = row_ref[slot]
-            acc_ref[row] = acc_ref[row] + term
+        picked = nearby_ref[source_ref[slot]]
+        term = lax.dot_general(
+            tiles_ref[t], picked, (((1,), (1,)), ((), ())), preferred_element_type=jnp.float32
+        )
+        terms.append(jnp.where(slot < count_ref[0], term, 0.0))
+    for t in range(per_step):
+        row = row_ref[step * per_step + t]
+        acc_ref[row] = acc_ref[row] + terms[t]
 
     @pl.when(step == pl.num_programs(0) - 1)
     def _():
         out_ref[...] = acc_ref[...]
 
 
-def aggregate_by_kernel(source_slot, local_row, count, nearby_turned, tile_values, blocks):
+def aggregate_by_kernel(source_slot, local_row, count, nearby, tile_values, blocks):
     slots, tile, _ = tile_values.shape
-    width = nearby_turned.shape[2]
+    width = nearby.shape[1]
     per_step = 16
     spec = pltpu.PrefetchScalarGridSpec(
         num_scalar_prefetch=3,
         grid=(slots // per_step,),
         in_specs=[
-            pl.BlockSpec(nearby_turned.shape, lambda i, *_: (0, 0, 0)),
+            pl.BlockSpec(nearby.shape, lambda i, *_: (0, 0, 0)),
             pl.BlockSpec((per_step, tile, tile), lambda i, *_: (i, 0, 0)),
         ],
         out_specs=pl.BlockSpec((blocks, tile, width), lambda i, *_: (0, 0, 0)),
@@ -126,7 +128,7 @@
         grid_spec=spec,
         out_shape=jax.ShapeDtypeStruct((blocks, tile, width), jnp.float32),
         compiler_params=pltpu.CompilerParams(dimension_semantics=("arbitrary",)),
-    )(source_slot, local_row, count, nearby_turned, tile_values)
+    )(source_slot, local_row, count, nearby, tile_values)
 
 
 def one_hot_table(indices, count, dtype):
@@ -176,7 +178,7 @@
     weight_all = packed_all[blocks]
     nearby, cotangent_all, weight_all = lax.optimization_barrier((nearby, cotangent_all, weight_all))
     turned = aggregate_by_kernel(
-        source_slot, local_row, tile_count, jnp.swapaxes(nearby, 1, 2), tile_values, blocks
+        source_slot, local_row, tile_count, nearby, tile_values, blocks
     )
     aggregate = jnp.swapaxes(turned, 1, 2)
     aggregate = aggregate.astype(jnp.bfloat16)

time: 108 us -> 81.5 us (0.75)
  Pallas kernels: 39.6 us -> 13.5 us
  local copies, waits for them, and re-layouts: 6.29 us -> 3.28 us
  starting transfers between devices: 23.9 us -> 25.4 us
  waiting for transfers between devices: 19.8 us -> 21.1 us
    pallas_call x1, Pallas kernels: 39.6 us -> 13.5 us  [aggregate_by_kernel(): pl.pallas_call(gathered_terms_kernel, grid_spec=spec, out_shape=jax.Shape...]
    optimization_barrier x1 -> x0, local copies, waits for them, and re-layouts: 3.02 us -> none  [per_device(): lax.optimization_barrier((nearby, cotangent_all, weight_all))]
    ppermute x8, waiting for transfers between devices: 4.82 us -> 6.21 us  [passed_along(): return lax.ppermute(block, axis, route)]
  transfers between devices with their start and end apart: 16 -> 16, of which waited for: 7 -> 7; matrix products, arithmetic and copies ran while one was open for 14% -> 19% of each run, Pallas kernels for 0% -> 0%
where the time goes in v13:
time: 81.5 us; the launch traced here: 81 us
  starting transfers between devices  25.4 us (31%)
  waiting for transfers between devices  21.1 us (26%)
  Pallas kernels  13.5 us (17%)
  matrix products  9.18 us (11%)
  other arithmetic  6.66 us (8%)
  local copies, waits for them, and re-layouts  3.28 us (4%)
  between operations  1.75 us (2%)
    ppermute x8, starting transfers between devices, passed_along(): return lax.ppermute(block, axis, route)  17.6 us
    ppermute x4, waiting for transfers between devices, gathered_along(): got = lax.ppermute(held, axis, [(i, i ^ mask) for i in range(size)])  14.9 us
    pallas_call x1, Pallas kernels, aggregate_by_kernel(): pl.pallas_call(gathered_terms_kernel, grid_spec=spec, out_shape=jax.Shape...  13.5 us
    ppermute x8, waiting for transfers between devices, passed_along(): return lax.ppermute(block, axis, route)  6.21 us
    dot_general x1, matrix products, per_device(): jnp.einsum('tfj,tjk->tfk', back_sources, tile_values, preferred_element_t...  5.99 us
    ppermute x3, starting transfers between devices, summed_over(): held.append(lax.ppermute(block, axis, route))  4.5 us
    ppermute x4, starting transfers between devices, gathered_along(): got = lax.ppermute(held, axis, [(i, i ^ mask) for i in range(size)])  3.31 us
    another operation x4, other arithmetic, gathered_along(): held = jnp.stack([piece for piece, _ in pieces])  2.48 us
  transfers between devices with their start and end apart: 16, of which 7 were waited for; matrix products, arithmetic and copies ran while one was open for 19% of the time, Pallas kernels for 0%

profile of v13, /device:TPU:0, one launch (start us, length us, event | category | flops | bytes accessed | tf_op | source)
XLA Modules:
  0.0 81.0 jit_solution(4927198934521435784)
XLA Ops:
  0.6 6.0 %collective-permute-start.2 = (bf16[16,32,128]{2,1,0:T(8,128)(2,1)}, bf16[16,32,128]{2,1,0:T(8,128)(2,1)S(1)}, u32[]{:S(2)}, u32[]{:S(2)}) collective-permute-start(bf16[16,32,128]{2,1,0:T(8,128)(2,1)} %param.9), channel_id=1, source_target_pairs={{4,0},{8,4},{12,8},{16,12},{20,16},{24,20},{28,24},{0,28},{5,1},{9... | collective-permute-start | bytes 393224 | tf_op jit(solution)/shard_map/ppermute | solution.py:24
  6.7 0.0 collective-permute-start.1
  6.7 0.0 collective-permute-start
  6.7 3.8 %collective-permute-start.3 = (bf16[16,32,128]{2,1,0:T(8,128)(2,1)}, bf16[16,32,128]{2,1,0:T(8,128)(2,1)S(1)}, u32[]{:S(2)}, u32[]{:S(2)}) collective-permute-start(bf16[16,32,128]{2,1,0:T(8,128)(2,1)} %param.9), channel_id=1, source_target_pairs={{8,0},{12,4},{16,8},{20,12},{24,16},{28,20},{0,24},{4,28},{9,1},{1... | collective-permute-start | bytes 393224 | tf_op jit(solution)/shard_map/ppermute | solution.py:24
  10.5 0.7 convert_bitcast_fusion.2
  11.2 0.1 broadcast_in_dim.20
  11.3 1.0 %fusion.15 = (bf16[1,17,32,128]{3,2,1,0:T(8,128)(2,1)S(1)}, bf16[17,128,128]{2,1,0:T(8,128)(2,1)S(1)}) fusion(bf16[1,32,128]{2,1,0:T(8,128)(2,1)S(1)} %convert_bitcast_fusion.2, bf16[16,32,128]{2,1,0:T(8,128)(2,1)} %param.17, bf16[17,128,128]{2,1,0:T(8,128)(2,1)S(1)} %broadcast_in_dim.20, s32[]{:T(128)S(6)} %select_n.69), kind=kLoop, calls=%fused_computation.35 | loop fusion | flops 278528 | bytes 417796 | tf_op jit(solution)/shard_map/stack | solution.py:39
  12.3 1.6 %collective-permute-start.4 = (bf16[1,17,32,128]{3,2,1,0:T(8,128)(2,1)S(1)}, bf16[1,17,32,128]{3,2,1,0:T(8,128)(2,1)S(1)}, u32[]{:S(2)}, u32[]{:S(2)}) collective-permute-start(bf16[1,17,32,128]{3,2,1,0:T(8,128)(2,1)S(1)} %get-tuple-element.32), channel_id=1, source_target_pairs={{0,2},{1,3},{2,0},{3,1},{4,6},{5,7},{6,4},{7,5},{8,10},{9,11},{10,... | collective-permute-start | bytes 417800 | tf_op jit(solution)/shard_map/ppermute | solution.py:40
  13.9 1.3 %subtract_clamp_fusion = (s32[256]{0:T(256)}, s32[256]{0:T(256)}) fusion(s32[256]{0:T(256)} %param.11, s32[]{:T(128)S(6)} %mul.79, s32[]{:T(128)S(6)} %axis_index.17, s32[256]{0:T(256)} %param.12), kind=kLoop, calls=%fused_computation.74 | loop fusion | flops 10240 | bytes 4104 | tf_op jit(solution)/shard_map/jit(clip)/min | solution.py:164
  15.8 0.0 collective-permute-done
  15.8 0.3 collective-permute-done.1
  16.1 0.9 %constant_dynamic-update-slice_fusion.2 = bf16[80,32,128]{2,1,0:T(8,128)(2,1)S(1)} fusion(bf16[80,32,128]{2,1,0:T(8,128)(2,1)S(1)} %constant_dynamic-update-slice_fusion.3, bf16[16,32,128]{2,1,0:T(8,128)(2,1)} %param.9), kind=kLoop, calls=%fused_computation.52 | loop fusion | bytes 262144
  17.0 0.0 collective-permute-done.2
  17.1 0.3 collective-permute-done.4
  17.4 0.1 collective-permute-start.5
  17.5 0.0 collective-permute-done.3
  17.6 1.5 %collective-permute-done.5 = bf16[2,17,32,128]{3,2,1,0:T(8,128)(2,1)S(1)} collective-permute-done((bf16[2,17,32,128]{3,2,1,0:T(8,128)(2,1)S(1)}, bf16[2,17,32,128]{3,2,1,0:T(8,128)(2,1)S(1)}, u32[]{:S(2)}, u32[]{:S(2)}) %collective-permute-start.5) | collective-permute-done | bytes 278560 | tf_op jit(solution)/shard_map/ppermute | solution.py:40
  19.2 0.0 copy-start.5
  19.2 13.5 %shard_map.128 = f32[16,128,32]{2,1,0:T(8,128)} custom-call(s32[256]{0:T(256)} %get-tuple-element.39.source_ref, s32[256]{0:T(256)} %get-tuple-element.38.row_ref, s32[1]{0:T(128)} %copy.55.count_ref, bf16[80,32,128]{2,1,0:T(8,128)(2,1)} %copy-done, bf16[256,128,128]{2,1,0:T(8,128)(2,1)} %tiles_ref.1), custom_call_target="tpu_custom_call" | custom-call | tf_op jit(solution)/shard_map/pallas_call | solution.py:126
  32.7 1.5 %convert_bitcast_fusion = (bf16[1,16,32,128]{2,3,1,0:T(8,128)(2,1)S(1)}, bf16[16,32,128]{1,2,0:T(8,128)(2,1)S(1)}) fusion(f32[16,128,32]{2,1,0:T(8,128)} %shard_map.128), kind=kLoop, calls=%fused_computation.20 | loop fusion | flops 65536 | bytes 524288 | tf_op jit(solution)/shard_map/stack | solution.py:39
  34.2 1.6 %collective-permute-start.6 = (bf16[1,16,32,128]{2,3,1,0:T(8,128)(2,1)S(1)}, bf16[1,16,32,128]{2,3,1,0:T(8,128)(2,1)S(1)}, u32[]{:S(2)}, u32[]{:S(2)}) collective-permute-start(bf16[1,16,32,128]{2,3,1,0:T(8,128)(2,1)S(1)} %get-tuple-element.26), channel_id=1, source_target_pairs={{0,2},{1,3},{2,0},{3,1},{4,6},{5,7},{6,4},{7,5},{8,10},{9,11},{10,... | collective-permute-start | bytes 393224 | tf_op jit(solution)/shard_map/ppermute | solution.py:40
  35.8 0.2 copy.24
  36.0 12.2 %collective-permute-done.6 = bf16[1,16,32,128]{2,3,1,0:T(8,128)(2,1)S(1)} collective-permute-done((bf16[1,16,32,128]{2,3,1,0:T(8,128)(2,1)S(1)}, bf16[1,16,32,128]{2,3,1,0:T(8,128)(2,1)S(1)}, u32[]{:S(2)}, u32[]{:S(2)}) %collective-permute-start.6) | collective-permute-done | bytes 131104 | tf_op jit(solution)/shard_map/ppermute | solution.py:40
  48.2 0.2 copy.25
  48.4 0.0 copy-start.1
  48.5 0.1 collective-permute-start.7
  48.6 0.0 copy-done.5
  48.6 0.2 copy.22
  48.8 0.1 broadcast_in_dim.22
  48.9 0.0 copy-start.4
  49.0 0.2 copy.23
  49.2 0.9 %collective-permute-done.7 = bf16[2,16,32,128]{3,2,1,0:T(8,128)(2,1)S(1)} collective-permute-done((bf16[2,16,32,128]{3,2,1,0:T(8,128)(2,1)S(1)}, bf16[2,16,32,128]{3,2,1,0:T(8,128)(2,1)S(1)}, u32[]{:S(2)}, u32[]{:S(2)}) %collective-permute-start.7) | collective-permute-done | bytes 262176 | tf_op jit(solution)/shard_map/ppermute | solution.py:40
  50.1 0.3 broadcast_compare_fusion
  50.5 0.3 multiply_convert_fusion
  50.8 0.3 fusion.31
  51.0 0.0 copy-done.1
  51.1 0.3 fusion.4
  51.4 0.1 collective-permute-start.13
  51.5 3.0 %collective-permute-start.12 = (f32[32,128]{1,0:T(8,128)S(1)}, f32[32,128]{1,0:T(8,128)S(1)}, u32[]{:S(2)}, u32[]{:S(2)}) collective-permute-start(f32[32,128]{1,0:T(8,128)S(1)} %bitcast.69), channel_id=1, source_target_pairs={{0,4},{4,0},{8,12},{12,8},{16,20},{20,16},{24,28},{28,24},{1,5},{5... | collective-permute-start | bytes 49160 | tf_op jit(solution)/shard_map/ppermute | solution.py:62
  54.5 1.4 %collective-permute-start.14 = (f32[32,128]{1,0:T(8,128)S(1)}, f32[32,128]{1,0:T(8,128)S(1)}, u32[]{:S(2)}, u32[]{:S(2)}) collective-permute-start(f32[32,128]{1,0:T(8,128)S(1)} %bitcast.70), channel_id=1, source_target_pairs={{0,12},{4,8},{8,4},{12,0},{16,28},{20,24},{24,20},{28,16},{1,13},{... | collective-permute-start | bytes 49160 | tf_op jit(solution)/shard_map/ppermute | solution.py:62
  55.9 0.2 copy.31
  56.2 0.7 fusion.13
  56.9 6.0 %reduce-precision_convert_fusion = (bf16[256,32,128]{2,1,0:T(8,128)(2,1)S(1)}, bf16[256,32,128]{2,1,0:T(8,128)(2,1)S(1)}) fusion(bf16[256,128,128]{2,1,0:T(8,128)(2,1)} %tiles_ref.1, bf16[256,32,128]{2,0,1:T(8,128)(2,1)S(1)} %fusion.13), kind=kOutput, calls=%fused_computation.1 | convolution fusion | flops 272629760 | bytes 14680064 | tf_op jit(solution)/shard_map/tfj,tjk->tfk/dot_general | solution.py:202
  62.9 0.4 pad_maximum_fusion
  63.3 0.0 copy-start.2
  63.3 0.0 copy-start.3
  63.3 1.5 %fusion.30 = (bf16[80,32,128]{2,0,1:T(8,128)(2,1)S(1)}, f32[80,32,128]{2,0,1:T(8,128)S(1)}) fusion(bf16[512,32,128]{2,1,0:T(8,128)(2,1)S(1)} %pad_maximum_fusion, bf16[256,80]{0,1:T(8,128)(2,1)S(1)} %select_convert_fusion.1), kind=kOutput, calls=%fused_computation.78 | convolution fusion | flops 336035840 | bytes 6201344 | tf_op jit(solution)/shard_map/ts,tfk->sfk/dot_general | solution.py:80
  64.8 0.0 collective-permute-done.13
  64.9 0.0 collective-permute-done.12
  64.9 0.0 collective-permute-done.14
  64.9 0.1 collective-permute-start.15
  65.0 0.8 select_convert_fusion
  65.8 2.9 %collective-permute-start.8 = (bf16[16,32,128]{2,0,1:T(8,128)(2,1)S(1)}, bf16[16,32,128]{2,0,1:T(8,128)(2,1)S(1)}, u32[]{:S(2)}, u32[]{:S(2)}) collective-permute-start(bf16[16,32,128]{2,0,1:T(8,128)(2,1)S(1)} %get-tuple-element.28), channel_id=1, source_target_pairs={{8,0},{12,4},{16,8},{20,12},{24,16},{28,20},{0,24},{4,28},{9,1},{1... | collective-permute-start | bytes 393224 | tf_op jit(solution)/shard_map/ppermute | solution.py:24
  68.7 0.0 collective-permute-start.11
  68.7 1.5 %collective-permute-start.10 = (bf16[16,32,128]{2,0,1:T(8,128)(2,1)S(1)}, bf16[16,32,128]{2,0,1:T(8,128)(2,1)S(1)}, u32[]{:S(2)}, u32[]{:S(2)}) collective-permute-start(bf16[16,32,128]{2,0,1:T(8,128)(2,1)S(1)} %get-tuple-element.30), channel_id=1, source_target_pairs={{28,0},{0,4},{4,8},{8,12},{12,16},{16,20},{20,24},{24,28},{29,1},{... | collective-permute-start | bytes 393224 | tf_op jit(solution)/shard_map/ppermute | solution.py:24
  70.2 3.3 %collective-permute-start.9 = (bf16[16,32,128]{2,0,1:T(8,128)(2,1)S(1)}, bf16[16,32,128]{2,0,1:T(8,128)(2,1)S(1)}, u32[]{:S(2)}, u32[]{:S(2)}) collective-permute-start(bf16[16,32,128]{2,0,1:T(8,128)(2,1)S(1)} %get-tuple-element.31), channel_id=1, source_target_pairs={{4,0},{8,4},{12,8},{16,12},{20,16},{24,20},{28,24},{0,28},{5,1},{9... | collective-permute-start | bytes 393224 | tf_op jit(solution)/shard_map/ppermute | solution.py:24
  73.5 0.0 collective-permute-done.15
  73.5 0.6 divide_subtract_fusion
  74.1 0.0 collective-permute-done.8
  74.1 2.8 %collective-permute-done.11 = bf16[16,32,128]{2,0,1:T(8,128)(2,1)S(1)} collective-permute-done((bf16[16,32,128]{2,0,1:T(8,128)(2,1)S(1)}, bf16[16,32,128]{2,0,1:T(8,128)(2,1)S(1)}, u32[]{:S(2)}, u32[]{:S(2)}) %collective-permute-start.11) | collective-permute-done | bytes 131104 | tf_op jit(solution)/shard_map/ppermute | solution.py:24
  77.0 3.1 %collective-permute-done.10 = bf16[16,32,128]{2,0,1:T(8,128)(2,1)S(1)} collective-permute-done((bf16[16,32,128]{2,0,1:T(8,128)(2,1)S(1)}, bf16[16,32,128]{2,0,1:T(8,128)(2,1)S(1)}, u32[]{:S(2)}, u32[]{:S(2)}) %collective-permute-start.10) | collective-permute-done | bytes 131104 | tf_op jit(solution)/shard_map/ppermute | solution.py:24
  80.1 0.0 collective-permute-done.9
  80.1 0.1 fusion.7
  80.2 0.8 copy.29
  (25 shorter events, 0.4 us)
Async XLA Ops:
  0.6 16.4 %collective-permute-start.2 = (bf16[16,32,128]{2,1,0:T(8,128)(2,1)}, bf16[16,32,128]{2,1,0:T(8,128)(2,1)S(1)}, u32[]{:S(2)}, u32[]{:S(2)}) collective-permute-start(bf16[16,32,128]{2,1,0:T(8,128)(2,1)} %param.9), channel_id=1, source_target_pairs={{4,0},{8,4},{12,8},{16,12},{20,16},{24,20},{28,24},{0,28},{5,1},{9... | collective-permute-start | bytes 393224 | tf_op jit(solution)/shard_map/ppermute | solution.py:24
  6.7 9.4 %collective-permute-start.1 = (bf16[16,32,128]{2,1,0:T(8,128)(2,1)}, bf16[16,32,128]{2,1,0:T(8,128)(2,1)S(1)}, u32[]{:S(2)}, u32[]{:S(2)}) collective-permute-start(bf16[16,32,128]{2,1,0:T(8,128)(2,1)} %param.9), channel_id=1, source_target_pairs={{28,0},{0,4},{4,8},{8,12},{12,16},{16,20},{20,24},{24,28},{29,1},{... | collective-permute-start | bytes 393224 | tf_op jit(solution)/shard_map/ppermute | solution.py:24
  6.7 9.1 %collective-permute-start = (bf16[16,32,128]{2,1,0:T(8,128)(2,1)}, bf16[16,32,128]{2,1,0:T(8,128)(2,1)S(1)}, u32[]{:S(2)}, u32[]{:S(2)}) collective-permute-start(bf16[16,32,128]{2,1,0:T(8,128)(2,1)} %param.9), channel_id=1, source_target_pairs={{24,0},{28,4},{0,8},{4,12},{8,16},{12,20},{16,24},{20,28},{25,1},{... | collective-permute-start | bytes 393224 | tf_op jit(solution)/shard_map/ppermute | solution.py:24
  6.7 10.9 %collective-permute-start.3 = (bf16[16,32,128]{2,1,0:T(8,128)(2,1)}, bf16[16,32,128]{2,1,0:T(8,128)(2,1)S(1)}, u32[]{:S(2)}, u32[]{:S(2)}) collective-permute-start(bf16[16,32,128]{2,1,0:T(8,128)(2,1)} %param.9), channel_id=1, source_target_pairs={{8,0},{12,4},{16,8},{20,12},{24,16},{28,20},{0,24},{4,28},{9,1},{1... | collective-permute-start | bytes 393224 | tf_op jit(solution)/shard_map/ppermute | solution.py:24
  12.3 5.1 %collective-permute-start.4 = (bf16[1,17,32,128]{3,2,1,0:T(8,128)(2,1)S(1)}, bf16[1,17,32,128]{3,2,1,0:T(8,128)(2,1)S(1)}, u32[]{:S(2)}, u32[]{:S(2)}) collective-permute-start(bf16[1,17,32,128]{3,2,1,0:T(8,128)(2,1)S(1)} %get-tuple-element.32), channel_id=1, source_target_pairs={{0,2},{1,3},{2,0},{3,1},{4,6},{5,7},{6,4},{7,5},{8,10},{9,11},{10,... | collective-permute-start | bytes 417800 | tf_op jit(solution)/shard_map/ppermute | solution.py:40
  17.4 1.6 %collective-permute-start.5 = (bf16[2,17,32,128]{3,2,1,0:T(8,128)(2,1)S(1)}, bf16[2,17,32,128]{3,2,1,0:T(8,128)(2,1)S(1)}, u32[]{:S(2)}, u32[]{:S(2)}) collective-permute-start(bf16[2,17,32,128]{3,2,1,0:T(8,128)(2,1)S(1)} %pad_maximum_fusion.1), channel_id=1, source_target_pairs={{0,1},{1,0},{2,3},{3,2},{4,5},{5,4},{6,7},{7,6},{8,9},{9,8},{10,11... | collective-permute-start | bytes 835592 | tf_op jit(solution)/shard_map/ppermute | solution.py:40
  17.6 1.6 %copy-start = (bf16[80,32,128]{2,1,0:T(8,128)(2,1)}, bf16[80,32,128]{2,1,0:T(8,128)(2,1)S(1)}, u32[]{:S(2)}) copy-start(bf16[80,32,128]{2,1,0:T(8,128)(2,1)S(1)} %constant_dynamic-update-slice_fusion.nearby_ref) | copy-start | bytes 1966084
  19.2 29.4 %copy-start.5 = (s32[256]{0:T(256)S(1)}, s32[256]{0:T(256)}, u32[]{:S(2)}) copy-start(s32[256]{0:T(256)} %get-tuple-element.39.source_ref) | copy-start | bytes 3076
  34.2 14.0 %collective-permute-start.6 = (bf16[1,16,32,128]{2,3,1,0:T(8,128)(2,1)S(1)}, bf16[1,16,32,128]{2,3,1,0:T(8,128)(2,1)S(1)}, u32[]{:S(2)}, u32[]{:S(2)}) collective-permute-start(bf16[1,16,32,128]{2,3,1,0:T(8,128)(2,1)S(1)} %get-tuple-element.26), channel_id=1, source_target_pairs={{0,2},{1,3},{2,0},{3,1},{4,6},{5,7},{6,4},{7,5},{8,10},{9,11},{10,... | collective-permute-start | bytes 393224 | tf_op jit(solution)/shard_map/ppermute | solution.py:40
  48.4 2.6 %copy-start.1 = (f32[32,128]{1,0:T(8,128)S(1)}, f32[32,128]{1,0:T(8,128)}, u32[]{:S(2)}) copy-start(f32[32,128]{1,0:T(8,128)} %param.14) | copy-start | bytes 49156
  48.5 1.6 %collective-permute-start.7 = (bf16[2,16,32,128]{3,2,1,0:T(8,128)(2,1)S(1)}, bf16[2,16,32,128]{3,2,1,0:T(8,128)(2,1)S(1)}, u32[]{:S(2)}, u32[]{:S(2)}) collective-permute-start(bf16[2,16,32,128]{3,2,1,0:T(8,128)(2,1)S(1)} %pad_maximum_fusion.2), channel_id=1, source_target_pairs={{0,1},{1,0},{2,3},{3,2},{4,5},{5,4},{6,7},{7,6},{8,9},{9,8},{10,11... | collective-permute-start | bytes 786440 | tf_op jit(solution)/shard_map/ppermute | solution.py:40
  48.9 7.2 %copy-start.4 = (s32[256]{0:T(256)S(1)}, s32[256]{0:T(256)}, u32[]{:S(2)}) copy-start(s32[256]{0:T(256)} %get-tuple-element.38.row_ref) | copy-start | bytes 3076
  51.4 13.4 %collective-permute-start.13 = (f32[32,128]{1,0:T(8,128)S(1)}, f32[32,128]{1,0:T(8,128)S(1)}, u32[]{:S(2)}, u32[]{:S(2)}) collective-permute-start(f32[32,128]{1,0:T(8,128)S(1)} %bitcast.68), channel_id=1, source_target_pairs={{0,8},{4,12},{8,0},{12,4},{16,24},{20,28},{24,16},{28,20},{1,9},{5... | collective-permute-start | bytes 49160 | tf_op jit(solution)/shard_map/ppermute | solution.py:62
  51.5 13.4 %collective-permute-start.12 = (f32[32,128]{1,0:T(8,128)S(1)}, f32[32,128]{1,0:T(8,128)S(1)}, u32[]{:S(2)}, u32[]{:S(2)}) collective-permute-start(f32[32,128]{1,0:T(8,128)S(1)} %bitcast.69), channel_id=1, source_target_pairs={{0,4},{4,0},{8,12},{12,8},{16,20},{20,16},{24,28},{28,24},{1,5},{5... | collective-permute-start | bytes 49160 | tf_op jit(solution)/shard_map/ppermute | solution.py:62
  54.5 10.3 %collective-permute-start.14 = (f32[32,128]{1,0:T(8,128)S(1)}, f32[32,128]{1,0:T(8,128)S(1)}, u32[]{:S(2)}, u32[]{:S(2)}) collective-permute-start(f32[32,128]{1,0:T(8,128)S(1)} %bitcast.70), channel_id=1, source_target_pairs={{0,12},{4,8},{8,4},{12,0},{16,28},{20,24},{24,20},{28,16},{1,13},{... | collective-permute-start | bytes 49160 | tf_op jit(solution)/shard_map/ppermute | solution.py:62
  63.3 10.2 %copy-start.2 = (f32[32,128]{1,0:T(8,128)S(1)}, f32[32,128]{1,0:T(8,128)}, u32[]{:S(2)}) copy-start(f32[32,128]{1,0:T(8,128)} %param.15) | copy-start | bytes 49156
  63.3 10.2 %copy-start.3 = (f32[32,128]{1,0:T(8,128)S(1)}, f32[32,128]{1,0:T(8,128)}, u32[]{:S(2)}) copy-start(f32[32,128]{1,0:T(8,128)} %param.16) | copy-start | bytes 49156
  64.9 8.6 %collective-permute-start.15 = (f32[32,128]{1,0:T(8,128)S(1)}, f32[32,128]{1,0:T(8,128)S(1)}, u32[]{:S(2)}, u32[]{:S(2)}) collective-permute-start(f32[32,128]{1,0:T(8,128)S(1)} %add_bitcast_fusion), channel_id=1, source_target_pairs={{0,16},{4,20},{8,24},{12,28},{16,0},{20,4},{24,8},{28,12},{1,17},{... | collective-permute-start | bytes 49160 | tf_op jit(solution)/shard_map/ppermute | solution.py:69
  65.8 8.4 %collective-permute-start.8 = (bf16[16,32,128]{2,0,1:T(8,128)(2,1)S(1)}, bf16[16,32,128]{2,0,1:T(8,128)(2,1)S(1)}, u32[]{:S(2)}, u32[]{:S(2)}) collective-permute-start(bf16[16,32,128]{2,0,1:T(8,128)(2,1)S(1)} %get-tuple-element.28), channel_id=1, source_target_pairs={{8,0},{12,4},{16,8},{20,12},{24,16},{28,20},{0,24},{4,28},{9,1},{1... | collective-permute-start | bytes 393224 | tf_op jit(solution)/shard_map/ppermute | solution.py:24
  68.7 8.3 %collective-permute-start.11 = (bf16[16,32,128]{2,0,1:T(8,128)(2,1)S(1)}, bf16[16,32,128]{2,0,1:T(8,128)(2,1)S(1)}, u32[]{:S(2)}, u32[]{:S(2)}) collective-permute-start(bf16[16,32,128]{2,0,1:T(8,128)(2,1)S(1)} %get-tuple-element.29), channel_id=1, source_target_pairs={{24,0},{28,4},{0,8},{4,12},{8,16},{12,20},{16,24},{20,28},{25,1},{... | collective-permute-start | bytes 393224 | tf_op jit(solution)/shard_map/ppermute | solution.py:24
  68.7 11.4 %collective-permute-start.10 = (bf16[16,32,128]{2,0,1:T(8,128)(2,1)S(1)}, bf16[16,32,128]{2,0,1:T(8,128)(2,1)S(1)}, u32[]{:S(2)}, u32[]{:S(2)}) collective-permute-start(bf16[16,32,128]{2,0,1:T(8,128)(2,1)S(1)} %get-tuple-element.30), channel_id=1, source_target_pairs={{28,0},{0,4},{4,8},{8,12},{12,16},{16,20},{20,24},{24,28},{29,1},{... | collective-permute-start | bytes 393224 | tf_op jit(solution)/shard_map/ppermute | solution.py:24
  70.2 9.9 %collective-permute-start.9 = (bf16[16,32,128]{2,0,1:T(8,128)(2,1)S(1)}, bf16[16,32,128]{2,0,1:T(8,128)(2,1)S(1)}, u32[]{:S(2)}, u32[]{:S(2)}) collective-permute-start(bf16[16,32,128]{2,0,1:T(8,128)(2,1)S(1)} %get-tuple-element.31), channel_id=1, source_target_pairs={{4,0},{8,4},{12,8},{16,12},{20,16},{24,20},{28,24},{0,28},{5,1},{9... | collective-permute-start | bytes 393224 | tf_op jit(solution)/shard_map/ppermute | solution.py:24

commit v14 on v13

--- a/solution.py
+++ b/solution.py
@@ -97,7 +97,7 @@
         slot = step * per_step + t
         picked = nearby_ref[source_ref[slot]]
         term = lax.dot_general(
-            tiles_ref[t], picked, (((1,), (1,)), ((), ())), preferred_element_type=jnp.float32
+            picked, tiles_ref[t], (((1,), (1,)), ((), ())), preferred_element_type=jnp.float32
         )
         terms.append(jnp.where(slot < count_ref[0], term, 0.0))
     for t in range(per_step):
@@ -120,13 +120,13 @@
             pl.BlockSpec(nearby.shape, lambda i, *_: (0, 0, 0)),
             pl.BlockSpec((per_step, tile, tile), lambda i, *_: (i, 0, 0)),
         ],
-        out_specs=pl.BlockSpec((blocks, tile, width), lambda i, *_: (0, 0, 0)),
-        scratch_shapes=[pltpu.VMEM((blocks, tile, width), jnp.float32)],
+        out_specs=pl.BlockSpec((blocks, width, tile), lambda i, *_: (0, 0, 0)),
+        scratch_shapes=[pltpu.VMEM((blocks, width, tile), jnp.float32)],
     )
     return pl.pallas_call(
         gathered_terms_kernel,
         grid_spec=spec,
-        out_shape=jax.ShapeDtypeStruct((blocks, tile, width), jnp.float32),
+        out_shape=jax.ShapeDtypeStruct((blocks, width, tile), jnp.float32),
         compiler_params=pltpu.CompilerParams(dimension_semantics=("arbitrary",)),
     )(source_slot, local_row, count, nearby, tile_values)
 
@@ -180,7 +180,7 @@
     turned = aggregate_by_kernel(
         source_slot, local_row, tile_count, nearby, tile_values, blocks
     )
-    aggregate = jnp.swapaxes(turned, 1, 2)
+    aggregate = turned
     aggregate = aggregate.astype(jnp.bfloat16)
     aggregate_all = gathered_along(aggregate, "feat", 1)
     column_start = lax.axis_index("feat") * width_local

time: 81.5 us -> 72.8 us (0.89)
  waiting for transfers between devices: 21.1 us -> 12.3 us
  local copies, waits for them, and re-layouts: 3.28 us -> 2.46 us
    ppermute x4, waiting for transfers between devices: 14.9 us -> 6.19 us  [gathered_along(): got = lax.ppermute(held, axis, [(i, i ^ mask) for i in range(size)])]
    dynamic_update_slice x0 -> x1, other arithmetic: none -> 0.99 us  [gathered_along(): whole = lax.dynamic_update_slice_in_dim(whole, piece, index * width, dim)]
    unnamed x17 -> x19, local copies, waits for them, and re-layouts: 1.8 us -> 1.79 us
  transfers between devices with their start and end apart: 16 -> 16, of which waited for: 7 -> 7; matrix products, arithmetic and copies ran while one was open for 19% -> 21% of each run, Pallas kernels for 0% -> 0%
where the time goes in v14:
time: 72.8 us; the launch traced here: 72.3 us
  starting transfers between devices  25.5 us (35%)
  Pallas kernels  13.9 us (19%)
  waiting for transfers between devices  12.3 us (17%)
  matrix products  9.19 us (13%)
  other arithmetic  7.22 us (10%)
  local copies, waits for them, and re-layouts  2.46 us (3%)
  between operations  1.7 us (2%)
    ppermute x8, starting transfers between devices, passed_along(): return lax.ppermute(block, axis, route)  17.6 us
    pallas_call x1, Pallas kernels, aggregate_by_kernel(): pl.pallas_call(gathered_terms_kernel, grid_spec=spec, out_shape=jax.Shape...  13.9 us
    ppermute x4, waiting for transfers between devices, gathered_along(): got = lax.ppermute(held, axis, [(i, i ^ mask) for i in range(size)])  6.19 us
    ppermute x8, waiting for transfers between devices, passed_along(): return lax.ppermute(block, axis, route)  6.15 us
    dot_general x1, matrix products, per_device(): jnp.einsum('tfj,tjk->tfk', back_sources, tile_values, preferred_element_t...  5.99 us
    ppermute x3, starting transfers between devices, summed_over(): held.append(lax.ppermute(block, axis, route))  4.51 us
    ppermute x4, starting transfers between devices, gathered_along(): got = lax.ppermute(held, axis, [(i, i ^ mask) for i in range(size)])  3.31 us
    another operation x4, other arithmetic, gathered_along(): held = jnp.stack([piece for piece, _ in pieces])  2.05 us
  transfers between devices with their start and end apart: 16, of which 7 were waited for; matrix products, arithmetic and copies ran while one was open for 21% of the time, Pallas kernels for 0%

profile of v14, /device:TPU:0, one launch (start us, length us, event | category | flops | bytes accessed | tf_op | source)
XLA Modules:
  0.0 72.3 jit_solution(4539085989075044715)
XLA Ops:
  0.6 6.0 %collective-permute-start.2 = (bf16[16,32,128]{2,1,0:T(8,128)(2,1)}, bf16[16,32,128]{2,1,0:T(8,128)(2,1)S(1)}, u32[]{:S(2)}, u32[]{:S(2)}) collective-permute-start(bf16[16,32,128]{2,1,0:T(8,128)(2,1)} %param.9), channel_id=1, source_target_pairs={{4,0},{8,4},{12,8},{16,12},{20,16},{24,20},{28,24},{0,28},{5,1},{9... | collective-permute-start | bytes 393224 | tf_op jit(solution)/shard_map/ppermute | solution.py:24
  6.7 0.0 collective-permute-start.1
  6.7 0.0 collective-permute-start
  6.7 3.8 %collective-permute-start.3 = (bf16[16,32,128]{2,1,0:T(8,128)(2,1)}, bf16[16,32,128]{2,1,0:T(8,128)(2,1)S(1)}, u32[]{:S(2)}, u32[]{:S(2)}) collective-permute-start(bf16[16,32,128]{2,1,0:T(8,128)(2,1)} %param.9), channel_id=1, source_target_pairs={{8,0},{12,4},{16,8},{20,12},{24,16},{28,20},{0,24},{4,28},{9,1},{1... | collective-permute-start | bytes 393224 | tf_op jit(solution)/shard_map/ppermute | solution.py:24
  10.5 0.7 convert_bitcast_fusion
  11.2 0.1 broadcast_in_dim.20
  11.3 1.0 %fusion.15 = (bf16[1,17,32,128]{3,2,1,0:T(8,128)(2,1)S(1)}, bf16[17,128,128]{2,1,0:T(8,128)(2,1)S(1)}) fusion(bf16[1,32,128]{2,1,0:T(8,128)(2,1)S(1)} %convert_bitcast_fusion, bf16[16,32,128]{2,1,0:T(8,128)(2,1)} %param.17, bf16[17,128,128]{2,1,0:T(8,128)(2,1)S(1)} %broadcast_in_dim.20, s32[]{:T(128)S(6)} %select_n.69), kind=kLoop, calls=%fused_computation.34 | loop fusion | flops 278528 | bytes 417796 | tf_op jit(solution)/shard_map/stack | solution.py:39
  12.3 1.6 %collective-permute-start.4 = (bf16[1,17,32,128]{3,2,1,0:T(8,128)(2,1)S(1)}, bf16[1,17,32,128]{3,2,1,0:T(8,128)(2,1)S(1)}, u32[]{:S(2)}, u32[]{:S(2)}) collective-permute-start(bf16[1,17,32,128]{3,2,1,0:T(8,128)(2,1)S(1)} %get-tuple-element.25), channel_id=1, source_target_pairs={{0,2},{1,3},{2,0},{3,1},{4,6},{5,7},{6,4},{7,5},{8,10},{9,11},{10,... | collective-permute-start | bytes 417800 | tf_op jit(solution)/shard_map/ppermute | solution.py:40
  13.9 1.3 %subtract_clamp_fusion = (s32[256]{0:T(256)}, s32[256]{0:T(256)}) fusion(s32[256]{0:T(256)} %param.11, s32[]{:T(128)S(6)} %mul.79, s32[]{:T(128)S(6)} %axis_index.17, s32[256]{0:T(256)} %param.12), kind=kLoop, calls=%fused_computation.72 | loop fusion | flops 10240 | bytes 4104 | tf_op jit(solution)/shard_map/jit(clip)/min | solution.py:164
  15.9 0.0 collective-permute-done
  15.9 0.2 collective-permute-done.1
  16.1 0.9 %constant_dynamic-update-slice_fusion.2 = bf16[80,32,128]{2,1,0:T(8,128)(2,1)S(1)} fusion(bf16[80,32,128]{2,1,0:T(8,128)(2,1)S(1)} %constant_dynamic-update-slice_fusion.3, bf16[16,32,128]{2,1,0:T(8,128)(2,1)} %param.9), kind=kLoop, calls=%fused_computation.51 | loop fusion | bytes 262144
  17.0 0.0 collective-permute-done.2
  17.1 0.3 collective-permute-done.4
  17.4 0.1 collective-permute-start.5
  17.5 0.0 collective-permute-done.3
  17.6 0.0 copy-start.1
  17.6 1.5 %collective-permute-done.5 = bf16[2,17,32,128]{3,2,1,0:T(8,128)(2,1)S(1)} collective-permute-done((bf16[2,17,32,128]{3,2,1,0:T(8,128)(2,1)S(1)}, bf16[2,17,32,128]{3,2,1,0:T(8,128)(2,1)S(1)}, u32[]{:S(2)}, u32[]{:S(2)}) %collective-permute-start.5) | collective-permute-done | bytes 278560 | tf_op jit(solution)/shard_map/ppermute | solution.py:40
  19.2 0.0 copy-done.1
  19.2 0.0 copy-start.6
  19.2 13.9 %shard_map.128 = f32[16,32,128]{2,1,0:T(8,128)} custom-call(s32[256]{0:T(256)} %get-tuple-element.32.source_ref, s32[256]{0:T(256)} %get-tuple-element.31.row_ref, s32[1]{0:T(128)} %copy.41.count_ref, bf16[80,32,128]{2,1,0:T(8,128)(2,1)} %copy-done.1, bf16[256,128,128]{2,1,0:T(8,128)(2,1)} %tiles_ref.1), custom_call_target="tpu_custom_call" | custom-call | tf_op jit(solution)/shard_map/pallas_call | solution.py:126
  33.1 1.0 %convert_bitcast_fusion.1 = bf16[1,16,32,128]{3,2,1,0:T(8,128)(2,1)S(1)} fusion(f32[16,32,128]{2,1,0:T(8,128)} %shard_map.128), kind=kLoop, calls=%fused_computation.77 | loop fusion | flops 65536 | bytes 393216 | tf_op jit(solution)/shard_map/stack | solution.py:39
  34.2 1.6 %collective-permute-start.6 = (bf16[1,16,32,128]{3,2,1,0:T(8,128)(2,1)S(1)}, bf16[1,16,32,128]{3,2,1,0:T(8,128)(2,1)S(1)}, u32[]{:S(2)}, u32[]{:S(2)}) collective-permute-start(bf16[1,16,32,128]{3,2,1,0:T(8,128)(2,1)S(1)} %convert_bitcast_fusion.1), channel_id=1, source_target_pairs={{0,2},{1,3},{2,0},{3,1},{4,6},{5,7},{6,4},{7,5},{8,10},{9,11},{10,... | collective-permute-start | bytes 393224 | tf_op jit(solution)/shard_map/ppermute | solution.py:40
  35.8 0.0 copy-done.6
  35.8 4.0 %collective-permute-done.6 = bf16[1,16,32,128]{3,2,1,0:T(8,128)(2,1)S(1)} collective-permute-done((bf16[1,16,32,128]{3,2,1,0:T(8,128)(2,1)S(1)}, bf16[1,16,32,128]{3,2,1,0:T(8,128)(2,1)S(1)}, u32[]{:S(2)}, u32[]{:S(2)}) %collective-permute-start.6) | collective-permute-done | bytes 131104 | tf_op jit(solution)/shard_map/ppermute | solution.py:40
  39.8 0.0 copy-start.5
  39.8 0.1 collective-permute-start.7
  39.9 0.1 broadcast_in_dim.22
  40.0 1.0 %constant_dynamic-update-slice_fusion.5 = bf16[16,128,128]{2,1,0:T(8,128)(2,1)S(1)} fusion(bf16[16,128,128]{2,1,0:T(8,128)(2,1)S(1)} %broadcast_in_dim.22, s32[]{:T(128)S(6)} %select_n.69, f32[16,32,128]{2,1,0:T(8,128)} %shard_map.128), kind=kLoop, calls=%fused_computation.58 | loop fusion | flops 65536 | bytes 393220 | tf_op jit(solution)/shard_map/dynamic_update_slice | solution.py:47
  41.0 0.4 collective-permute-done.7
  41.5 0.3 broadcast_compare_fusion
  41.8 0.3 multiply_convert_fusion
  42.1 0.3 fusion.29
  42.4 0.0 copy-done.2
  42.4 0.4 fusion.4
  42.7 0.1 collective-permute-start.13
  42.8 3.1 %collective-permute-start.12 = (f32[32,128]{1,0:T(8,128)S(1)}, f32[32,128]{1,0:T(8,128)S(1)}, u32[]{:S(2)}, u32[]{:S(2)}) collective-permute-start(f32[32,128]{1,0:T(8,128)S(1)} %bitcast.65), channel_id=1, source_target_pairs={{0,4},{4,0},{8,12},{12,8},{16,20},{20,16},{24,28},{28,24},{1,5},{5... | collective-permute-start | bytes 49160 | tf_op jit(solution)/shard_map/ppermute | solution.py:62
  45.9 1.4 %collective-permute-start.14 = (f32[32,128]{1,0:T(8,128)S(1)}, f32[32,128]{1,0:T(8,128)S(1)}, u32[]{:S(2)}, u32[]{:S(2)}) collective-permute-start(f32[32,128]{1,0:T(8,128)S(1)} %bitcast.66), channel_id=1, source_target_pairs={{0,12},{4,8},{8,4},{12,0},{16,28},{20,24},{24,20},{28,16},{1,13},{... | collective-permute-start | bytes 49160 | tf_op jit(solution)/shard_map/ppermute | solution.py:62
  47.3 0.2 copy.18
  47.5 0.0 copy-done.5
  47.5 0.7 %fusion.13 = bf16[256,32,128]{2,0,1:T(8,128)(2,1)S(1)} fusion(bf16[16,32,128]{2,0,1:T(8,128)(2,1)S(1)} %copy.18, s32[256]{0:T(256)S(1)} %copy-done.5), kind=kOutput, calls=%fused_computation.33 | convolution fusion | flops 33558528 | bytes 2229248 | tf_op jit(solution)/shard_map/tb,bfj->tfj/dot_general | solution.py:199
  48.2 6.0 %reduce-precision_convert_fusion = (bf16[256,32,128]{2,1,0:T(8,128)(2,1)S(1)}, bf16[256,32,128]{2,1,0:T(8,128)(2,1)S(1)}) fusion(bf16[256,128,128]{2,1,0:T(8,128)(2,1)} %tiles_ref.1, bf16[256,32,128]{2,0,1:T(8,128)(2,1)S(1)} %fusion.13), kind=kOutput, calls=%fused_computation.1 | convolution fusion | flops 272629760 | bytes 14680064 | tf_op jit(solution)/shard_map/tfj,tjk->tfk/dot_general | solution.py:202
  54.2 0.4 pad_maximum_fusion
  54.6 0.0 copy-start.3
  54.6 0.0 copy-start.4
  54.6 1.5 %fusion.32 = (bf16[80,32,128]{2,0,1:T(8,128)(2,1)S(1)}, f32[80,32,128]{2,0,1:T(8,128)S(1)}) fusion(bf16[512,32,128]{2,1,0:T(8,128)(2,1)S(1)} %pad_maximum_fusion, bf16[256,80]{0,1:T(8,128)(2,1)S(1)} %select_convert_fusion.1), kind=kOutput, calls=%fused_computation.79 | convolution fusion | flops 336035840 | bytes 6201344 | tf_op jit(solution)/shard_map/ts,tfk->sfk/dot_general | solution.py:80
  56.2 0.0 collective-permute-done.13
  56.2 0.0 collective-permute-done.12
  56.2 0.0 collective-permute-done.14
  56.3 0.1 collective-permute-start.15
  56.3 0.8 %select_convert_fusion = bf16[16,32,128]{2,1,0:T(8,128)(2,1)} fusion(f32[16,128,128]{2,1,0:T(8,128)S(1)} %get-tuple-element.28, s32[]{:T(128)S(6)} %select_n.69, pred[16,128,128]{2,1,0:T(8,128)(4,1)S(1)} %get-tuple-element.27), kind=kLoop, calls=%fused_computation.19 | loop fusion | flops 196608 | bytes 458756 | tf_op jit(solution)/shard_map/convert_element_type | solution.py:191
  57.1 2.9 %collective-permute-start.8 = (bf16[16,32,128]{2,0,1:T(8,128)(2,1)S(1)}, bf16[16,32,128]{2,0,1:T(8,128)(2,1)S(1)}, u32[]{:S(2)}, u32[]{:S(2)}) collective-permute-start(bf16[16,32,128]{2,0,1:T(8,128)(2,1)S(1)} %get-tuple-element.21), channel_id=1, source_target_pairs={{8,0},{12,4},{16,8},{20,12},{24,16},{28,20},{0,24},{4,28},{9,1},{1... | collective-permute-start | bytes 393224 | tf_op jit(solution)/shard_map/ppermute | solution.py:24
  60.0 0.0 collective-permute-start.11
  60.0 1.5 %collective-permute-start.10 = (bf16[16,32,128]{2,0,1:T(8,128)(2,1)S(1)}, bf16[16,32,128]{2,0,1:T(8,128)(2,1)S(1)}, u32[]{:S(2)}, u32[]{:S(2)}) collective-permute-start(bf16[16,32,128]{2,0,1:T(8,128)(2,1)S(1)} %get-tuple-element.23), channel_id=1, source_target_pairs={{28,0},{0,4},{4,8},{8,12},{12,16},{16,20},{20,24},{24,28},{29,1},{... | collective-permute-start | bytes 393224 | tf_op jit(solution)/shard_map/ppermute | solution.py:24
  61.6 3.3 %collective-permute-start.9 = (bf16[16,32,128]{2,0,1:T(8,128)(2,1)S(1)}, bf16[16,32,128]{2,0,1:T(8,128)(2,1)S(1)}, u32[]{:S(2)}, u32[]{:S(2)}) collective-permute-start(bf16[16,32,128]{2,0,1:T(8,128)(2,1)S(1)} %get-tuple-element.24), channel_id=1, source_target_pairs={{4,0},{8,4},{12,8},{16,12},{20,16},{24,20},{28,24},{0,28},{5,1},{9... | collective-permute-start | bytes 393224 | tf_op jit(solution)/shard_map/ppermute | solution.py:24
  64.8 0.0 collective-permute-done.15
  64.8 0.0 copy-done.4
  64.8 0.6 divide_subtract_fusion
  65.5 0.0 collective-permute-done.8
  65.5 2.8 %collective-permute-done.11 = bf16[16,32,128]{2,0,1:T(8,128)(2,1)S(1)} collective-permute-done((bf16[16,32,128]{2,0,1:T(8,128)(2,1)S(1)}, bf16[16,32,128]{2,0,1:T(8,128)(2,1)S(1)}, u32[]{:S(2)}, u32[]{:S(2)}) %collective-permute-start.11) | collective-permute-done | bytes 131104 | tf_op jit(solution)/shard_map/ppermute | solution.py:24
  68.3 3.1 %collective-permute-done.10 = bf16[16,32,128]{2,0,1:T(8,128)(2,1)S(1)} collective-permute-done((bf16[16,32,128]{2,0,1:T(8,128)(2,1)S(1)}, bf16[16,32,128]{2,0,1:T(8,128)(2,1)S(1)}, u32[]{:S(2)}, u32[]{:S(2)}) %collective-permute-start.10) | collective-permute-done | bytes 131104 | tf_op jit(solution)/shard_map/ppermute | solution.py:24
  71.4 0.0 collective-permute-done.9
  71.4 0.1 fusion.7
  71.5 0.8 %copy.16 = f32[16,32,128]{2,1,0:T(8,128)} copy(f32[16,32,128]{2,0,1:T(8,128)S(1)} %fusion.7) | data formatting | bytes 524288
  (23 shorter events, 0.4 us)
Async XLA Ops:
  0.6 16.4 %collective-permute-start.2 = (bf16[16,32,128]{2,1,0:T(8,128)(2,1)}, bf16[16,32,128]{2,1,0:T(8,128)(2,1)S(1)}, u32[]{:S(2)}, u32[]{:S(2)}) collective-permute-start(bf16[16,32,128]{2,1,0:T(8,128)(2,1)} %param.9), channel_id=1, source_target_pairs={{4,0},{8,4},{12,8},{16,12},{20,16},{24,20},{28,24},{0,28},{5,1},{9... | collective-permute-start | bytes 393224 | tf_op jit(solution)/shard_map/ppermute | solution.py:24
  6.7 9.4 %collective-permute-start.1 = (bf16[16,32,128]{2,1,0:T(8,128)(2,1)}, bf16[16,32,128]{2,1,0:T(8,128)(2,1)S(1)}, u32[]{:S(2)}, u32[]{:S(2)}) collective-permute-start(bf16[16,32,128]{2,1,0:T(8,128)(2,1)} %param.9), channel_id=1, source_target_pairs={{28,0},{0,4},{4,8},{8,12},{12,16},{16,20},{20,24},{24,28},{29,1},{... | collective-permute-start | bytes 393224 | tf_op jit(solution)/shard_map/ppermute | solution.py:24
  6.7 9.2 %collective-permute-start = (bf16[16,32,128]{2,1,0:T(8,128)(2,1)}, bf16[16,32,128]{2,1,0:T(8,128)(2,1)S(1)}, u32[]{:S(2)}, u32[]{:S(2)}) collective-permute-start(bf16[16,32,128]{2,1,0:T(8,128)(2,1)} %param.9), channel_id=1, source_target_pairs={{24,0},{28,4},{0,8},{4,12},{8,16},{12,20},{16,24},{20,28},{25,1},{... | collective-permute-start | bytes 393224 | tf_op jit(solution)/shard_map/ppermute | solution.py:24
  6.7 10.9 %collective-permute-start.3 = (bf16[16,32,128]{2,1,0:T(8,128)(2,1)}, bf16[16,32,128]{2,1,0:T(8,128)(2,1)S(1)}, u32[]{:S(2)}, u32[]{:S(2)}) collective-permute-start(bf16[16,32,128]{2,1,0:T(8,128)(2,1)} %param.9), channel_id=1, source_target_pairs={{8,0},{12,4},{16,8},{20,12},{24,16},{28,20},{0,24},{4,28},{9,1},{1... | collective-permute-start | bytes 393224 | tf_op jit(solution)/shard_map/ppermute | solution.py:24
  12.3 5.1 %collective-permute-start.4 = (bf16[1,17,32,128]{3,2,1,0:T(8,128)(2,1)S(1)}, bf16[1,17,32,128]{3,2,1,0:T(8,128)(2,1)S(1)}, u32[]{:S(2)}, u32[]{:S(2)}) collective-permute-start(bf16[1,17,32,128]{3,2,1,0:T(8,128)(2,1)S(1)} %get-tuple-element.25), channel_id=1, source_target_pairs={{0,2},{1,3},{2,0},{3,1},{4,6},{5,7},{6,4},{7,5},{8,10},{9,11},{10,... | collective-permute-start | bytes 417800 | tf_op jit(solution)/shard_map/ppermute | solution.py:40
  17.4 1.6 %collective-permute-start.5 = (bf16[2,17,32,128]{3,2,1,0:T(8,128)(2,1)S(1)}, bf16[2,17,32,128]{3,2,1,0:T(8,128)(2,1)S(1)}, u32[]{:S(2)}, u32[]{:S(2)}) collective-permute-start(bf16[2,17,32,128]{3,2,1,0:T(8,128)(2,1)S(1)} %pad_maximum_fusion.1), channel_id=1, source_target_pairs={{0,1},{1,0},{2,3},{3,2},{4,5},{5,4},{6,7},{7,6},{8,9},{9,8},{10,11... | collective-permute-start | bytes 835592 | tf_op jit(solution)/shard_map/ppermute | solution.py:40
  17.6 1.6 %copy-start.1 = (bf16[80,32,128]{2,1,0:T(8,128)(2,1)}, bf16[80,32,128]{2,1,0:T(8,128)(2,1)S(1)}, u32[]{:S(2)}) copy-start(bf16[80,32,128]{2,1,0:T(8,128)(2,1)S(1)} %constant_dynamic-update-slice_fusion.nearby_ref) | copy-start | bytes 1966084
  19.2 16.6 %copy-start.6 = (s32[256]{0:T(256)S(1)}, s32[256]{0:T(256)}, u32[]{:S(2)}) copy-start(s32[256]{0:T(256)} %get-tuple-element.32.source_ref) | copy-start | bytes 3076
  33.1 9.0 %copy-start = (f32[16,32,128]{2,1,0:T(8,128)S(1)}, f32[16,32,128]{2,1,0:T(8,128)}, u32[]{:S(2)}) copy-start(f32[16,32,128]{2,1,0:T(8,128)} %shard_map.128) | copy-start | bytes 786436
  33.1 9.2 %copy-start.2 = (f32[32,128]{1,0:T(8,128)S(1)}, f32[32,128]{1,0:T(8,128)}, u32[]{:S(2)}) copy-start(f32[32,128]{1,0:T(8,128)} %param.14) | copy-start | bytes 49156
  34.2 5.6 %collective-permute-start.6 = (bf16[1,16,32,128]{3,2,1,0:T(8,128)(2,1)S(1)}, bf16[1,16,32,128]{3,2,1,0:T(8,128)(2,1)S(1)}, u32[]{:S(2)}, u32[]{:S(2)}) collective-permute-start(bf16[1,16,32,128]{3,2,1,0:T(8,128)(2,1)S(1)} %convert_bitcast_fusion.1), channel_id=1, source_target_pairs={{0,2},{1,3},{2,0},{3,1},{4,6},{5,7},{6,4},{7,5},{8,10},{9,11},{10,... | collective-permute-start | bytes 393224 | tf_op jit(solution)/shard_map/ppermute | solution.py:40
  39.8 7.7 %copy-start.5 = (s32[256]{0:T(256)S(1)}, s32[256]{0:T(256)}, u32[]{:S(2)}) copy-start(s32[256]{0:T(256)} %get-tuple-element.31.row_ref) | copy-start | bytes 3076
  39.8 1.6 %collective-permute-start.7 = (bf16[2,16,32,128]{3,2,1,0:T(8,128)(2,1)S(1)}, bf16[2,16,32,128]{3,2,1,0:T(8,128)(2,1)S(1)}, u32[]{:S(2)}, u32[]{:S(2)}) collective-permute-start(bf16[2,16,32,128]{3,2,1,0:T(8,128)(2,1)S(1)} %pad_maximum_fusion.2), channel_id=1, source_target_pairs={{0,1},{1,0},{2,3},{3,2},{4,5},{5,4},{6,7},{7,6},{8,9},{9,8},{10,11... | collective-permute-start | bytes 786440 | tf_op jit(solution)/shard_map/ppermute | solution.py:40
  42.7 13.5 %collective-permute-start.13 = (f32[32,128]{1,0:T(8,128)S(1)}, f32[32,128]{1,0:T(8,128)S(1)}, u32[]{:S(2)}, u32[]{:S(2)}) collective-permute-start(f32[32,128]{1,0:T(8,128)S(1)} %bitcast.64), channel_id=1, source_target_pairs={{0,8},{4,12},{8,0},{12,4},{16,24},{20,28},{24,16},{28,20},{1,9},{5... | collective-permute-start | bytes 49160 | tf_op jit(solution)/shard_map/ppermute | solution.py:62
  42.8 13.4 %collective-permute-start.12 = (f32[32,128]{1,0:T(8,128)S(1)}, f32[32,128]{1,0:T(8,128)S(1)}, u32[]{:S(2)}, u32[]{:S(2)}) collective-permute-start(f32[32,128]{1,0:T(8,128)S(1)} %bitcast.65), channel_id=1, source_target_pairs={{0,4},{4,0},{8,12},{12,8},{16,20},{20,16},{24,28},{28,24},{1,5},{5... | collective-permute-start | bytes 49160 | tf_op jit(solution)/shard_map/ppermute | solution.py:62
  45.9 10.3 %collective-permute-start.14 = (f32[32,128]{1,0:T(8,128)S(1)}, f32[32,128]{1,0:T(8,128)S(1)}, u32[]{:S(2)}, u32[]{:S(2)}) collective-permute-start(f32[32,128]{1,0:T(8,128)S(1)} %bitcast.66), channel_id=1, source_target_pairs={{0,12},{4,8},{8,4},{12,0},{16,28},{20,24},{24,20},{28,16},{1,13},{... | collective-permute-start | bytes 49160 | tf_op jit(solution)/shard_map/ppermute | solution.py:62
  54.6 10.2 %copy-start.3 = (f32[32,128]{1,0:T(8,128)S(1)}, f32[32,128]{1,0:T(8,128)}, u32[]{:S(2)}) copy-start(f32[32,128]{1,0:T(8,128)} %param.15) | copy-start | bytes 49156
  54.6 10.2 %copy-start.4 = (f32[32,128]{1,0:T(8,128)S(1)}, f32[32,128]{1,0:T(8,128)}, u32[]{:S(2)}) copy-start(f32[32,128]{1,0:T(8,128)} %param.16) | copy-start | bytes 49156
  56.3 8.6 %collective-permute-start.15 = (f32[32,128]{1,0:T(8,128)S(1)}, f32[32,128]{1,0:T(8,128)S(1)}, u32[]{:S(2)}, u32[]{:S(2)}) collective-permute-start(f32[32,128]{1,0:T(8,128)S(1)} %add_bitcast_fusion), channel_id=1, source_target_pairs={{0,16},{4,20},{8,24},{12,28},{16,0},{20,4},{24,8},{28,12},{1,17},{... | collective-permute-start | bytes 49160 | tf_op jit(solution)/shard_map/ppermute | solution.py:69
  57.1 8.4 %collective-permute-start.8 = (bf16[16,32,128]{2,0,1:T(8,128)(2,1)S(1)}, bf16[16,32,128]{2,0,1:T(8,128)(2,1)S(1)}, u32[]{:S(2)}, u32[]{:S(2)}) collective-permute-start(bf16[16,32,128]{2,0,1:T(8,128)(2,1)S(1)} %get-tuple-element.21), channel_id=1, source_target_pairs={{8,0},{12,4},{16,8},{20,12},{24,16},{28,20},{0,24},{4,28},{9,1},{1... | collective-permute-start | bytes 393224 | tf_op jit(solution)/shard_map/ppermute | solution.py:24
  60.0 8.3 %collective-permute-start.11 = (bf16[16,32,128]{2,0,1:T(8,128)(2,1)S(1)}, bf16[16,32,128]{2,0,1:T(8,128)(2,1)S(1)}, u32[]{:S(2)}, u32[]{:S(2)}) collective-permute-start(bf16[16,32,128]{2,0,1:T(8,128)(2,1)S(1)} %get-tuple-element.22), channel_id=1, source_target_pairs={{24,0},{28,4},{0,8},{4,12},{8,16},{12,20},{16,24},{20,28},{25,1},{... | collective-permute-start | bytes 393224 | tf_op jit(solution)/shard_map/ppermute | solution.py:24
  60.0 11.4 %collective-permute-start.10 = (bf16[16,32,128]{2,0,1:T(8,128)(2,1)S(1)}, bf16[16,32,128]{2,0,1:T(8,128)(2,1)S(1)}, u32[]{:S(2)}, u32[]{:S(2)}) collective-permute-start(bf16[16,32,128]{2,0,1:T(8,128)(2,1)S(1)} %get-tuple-element.23), channel_id=1, source_target_pairs={{28,0},{0,4},{4,8},{8,12},{12,16},{16,20},{20,24},{24,28},{29,1},{... | collective-permute-start | bytes 393224 | tf_op jit(solution)/shard_map/ppermute | solution.py:24
  61.6 9.9 %collective-permute-start.9 = (bf16[16,32,128]{2,0,1:T(8,128)(2,1)S(1)}, bf16[16,32,128]{2,0,1:T(8,128)(2,1)S(1)}, u32[]{:S(2)}, u32[]{:S(2)}) collective-permute-start(bf16[16,32,128]{2,0,1:T(8,128)(2,1)S(1)} %get-tuple-element.24), channel_id=1, source_target_pairs={{4,0},{8,4},{12,8},{16,12},{20,16},{24,20},{28,24},{0,28},{5,1},{9... | collective-permute-start | bytes 393224 | tf_op jit(solution)/shard_map/ppermute | solution.py:24

commit v15 on v10

--- a/solution.py
+++ b/solution.py
@@ -111,8 +111,6 @@
     offset = jnp.where(offset > cycle_size // 2, offset - cycle_size, offset)
     source_slot = (offset + REACH) * blocks + col_block
     targets = (2 * REACH + 1) * blocks
-    pick_source = one_hot_table(source_slot, targets, jnp.bfloat16)
-    pick_row = one_hot_table(local_row, blocks, jnp.bfloat16)
     add_row = one_hot_table(local_row, blocks, jnp.float32) * live[:, None]
     add_source = one_hot_table(source_slot, targets, jnp.float32) * live[:, None]
     pieces = []
@@ -128,9 +126,7 @@
     cotangent_all = packed_all[:blocks]
     weight_all = packed_all[blocks]
     nearby, cotangent_all, weight_all = lax.optimization_barrier((nearby, cotangent_all, weight_all))
-    sources = jnp.einsum(
-        "ts,sfk->tfk", pick_source, nearby, preferred_element_type=jnp.float32
-    ).astype(jnp.bfloat16)
+    sources = jnp.take(nearby, jnp.clip(source_slot, 0, targets - 1), axis=0)
     forward_terms = jnp.einsum(
         "tjk,tfk->tjf", tile_values, sources, preferred_element_type=jnp.float32
     )
@@ -150,9 +146,7 @@
     back_rows = jnp.einsum(
         "io,boj->bij", weight_half, slope_all, preferred_element_type=jnp.float32
     ).astype(jnp.bfloat16)
-    back_sources = jnp.einsum(
-        "tb,bfj->tfj", pick_row, back_rows, preferred_element_type=jnp.float32
-    ).astype(jnp.bfloat16)
+    back_sources = jnp.take(back_rows, jnp.clip(local_row, 0, blocks - 1), axis=0)
     back_terms = jnp.einsum(
         "tfj,tjk->tfk", back_sources, tile_values, preferred_element_type=jnp.float32
     )

time: 68 us -> 71.2 us (1.047)
  local copies, waits for them, and re-layouts: 2.6 us -> 6.33 us
  other arithmetic: 5.43 us -> 7.92 us
  waiting for transfers between devices: 13.2 us -> 11.7 us
  matrix products: 19.4 us -> 18.1 us
    gather x0 -> x2, local copies, waits for them, and re-layouts: none -> 2.12 us  [the longest x1 1.13 us: per_device(): jnp.take(back_rows, jnp.clip(local_row, 0, blocks - 1), axis=0)]
    and x0 -> x2, other arithmetic: none -> 1.91 us  [the longest x1 1.2 us: per_device(): jnp.take(back_rows, jnp.clip(local_row, 0, blocks - 1), axis=0)]
    dot_general x2 -> x0, matrix products: 1.51 us -> none  [the longest x1 0.77 us: per_device(): jnp.einsum('ts,sfk->tfk', pick_source, nearby, preferred_element_type=jnp...]
    ppermute x4, waiting for transfers between devices: 7.11 us -> 5.72 us  [gathered_along(): got = lax.ppermute(held, axis, [(i, i ^ mask) for i in range(size)])]
    slice x1, local copies, waits for them, and re-layouts: 0.04 us -> 0.84 us  [per_device(): cotangent_all = packed_all[:blocks]]
    another operation x1, other arithmetic: 0.01 us -> 0.78 us  [summed_over(): held = jnp.stack(held)]
    unnamed x11 -> x17, local copies, waits for them, and re-layouts: 1.78 us -> 2.18 us
  transfers between devices with their start and end apart: 16 -> 16, of which waited for: 7 -> 5; matrix products, arithmetic and copies ran while one was open for 22% -> 23% of each run, Pallas kernels for 0% -> 0%
where the time goes in v15:
time: 71.2 us; the launch traced here: 70.8 us
  starting transfers between devices  25.1 us (35%)
  matrix products  18.1 us (25%)
  waiting for transfers between devices  11.7 us (16%)
  other arithmetic  7.92 us (11%)
  local copies, waits for them, and re-layouts  6.33 us (9%)
  between operations  1.64 us (2%)
    ppermute x8, starting transfers between devices, passed_along(): return lax.ppermute(block, axis, route)  17.6 us
    dot_general x1, matrix products, per_device(): jnp.einsum('tjk,tfk->tjf', tile_values, sources, preferred_element_type=j...  7.89 us
    ppermute x8, waiting for transfers between devices, passed_along(): return lax.ppermute(block, axis, route)  5.96 us
    dot_general x1, matrix products, per_device(): jnp.einsum('tfj,tjk->tfk', back_sources, tile_values, preferred_element_t...  5.77 us
    ppermute x4, waiting for transfers between devices, gathered_along(): got = lax.ppermute(held, axis, [(i, i ^ mask) for i in range(size)])  5.72 us
    ppermute x3, starting transfers between devices, summed_over(): held.append(lax.ppermute(block, axis, route))  4.34 us
    ppermute x4, starting transfers between devices, gathered_along(): got = lax.ppermute(held, axis, [(i, i ^ mask) for i in range(size)])  3.12 us
    dot_general x2, matrix products, summed_by_table(): return jnp.einsum(spec, doubled, both, preferred_element_type=jnp.float32)  2.74 us
  transfers between devices with their start and end apart: 16, of which 5 were waited for; matrix products, arithmetic and copies ran while one was open for 23% of the time, Pallas kernels for 0%

profile of v15, /device:TPU:0, one launch (start us, length us, event | category | flops | bytes accessed | tf_op | source)
XLA Modules:
  0.0 70.8 jit_solution(1011163865016232565)
XLA Ops:
  0.6 6.0 %collective-permute-start.2 = (bf16[16,32,128]{2,1,0:T(8,128)(2,1)}, bf16[16,32,128]{2,1,0:T(8,128)(2,1)S(1)}, u32[]{:S(2)}, u32[]{:S(2)}) collective-permute-start(bf16[16,32,128]{2,1,0:T(8,128)(2,1)} %param.9), channel_id=1, source_target_pairs={{4,0},{8,4},{12,8},{16,12},{20,16},{24,20},{28,24},{0,28},{5,1},{9... | collective-permute-start | bytes 393224 | tf_op jit(solution)/shard_map/ppermute | solution.py:22
  6.7 0.0 collective-permute-start.1
  6.7 0.0 collective-permute-start
  6.7 3.8 %collective-permute-start.3 = (bf16[16,32,128]{2,1,0:T(8,128)(2,1)}, bf16[16,32,128]{2,1,0:T(8,128)(2,1)S(1)}, u32[]{:S(2)}, u32[]{:S(2)}) collective-permute-start(bf16[16,32,128]{2,1,0:T(8,128)(2,1)} %param.9), channel_id=1, source_target_pairs={{8,0},{12,4},{16,8},{20,12},{24,16},{28,20},{0,24},{4,28},{9,1},{1... | collective-permute-start | bytes 393224 | tf_op jit(solution)/shard_map/ppermute | solution.py:22
  10.5 0.7 %convert_bitcast_fusion = bf16[1,32,128]{2,1,0:T(8,128)(2,1)S(1)} fusion(f32[32,128]{1,0:T(8,128)} %param.14), kind=kLoop, calls=%fused_computation.77 | loop fusion | flops 4096 | bytes 24576 | tf_op jit(solution)/shard_map/broadcast_in_dim | solution.py:124
  11.2 0.1 broadcast_in_dim.43
  11.3 1.0 %fusion.25 = (bf16[1,17,32,128]{3,2,1,0:T(8,128)(2,1)S(1)}, bf16[17,128,128]{2,1,0:T(8,128)(2,1)S(1)}) fusion(bf16[1,32,128]{2,1,0:T(8,128)(2,1)S(1)} %convert_bitcast_fusion, bf16[16,32,128]{2,1,0:T(8,128)(2,1)} %param.17, bf16[17,128,128]{2,1,0:T(8,128)(2,1)S(1)} %broadcast_in_dim.43, s32[]{:T(128)S(6)} %select_n.85), kind=kLoop, calls=%fused_computation.49 | loop fusion | flops 278528 | bytes 417796 | tf_op jit(solution)/shard_map/stack | solution.py:37
  12.3 1.6 %collective-permute-start.4 = (bf16[1,17,32,128]{3,2,1,0:T(8,128)(2,1)S(1)}, bf16[1,17,32,128]{3,2,1,0:T(8,128)(2,1)S(1)}, u32[]{:S(2)}, u32[]{:S(2)}) collective-permute-start(bf16[1,17,32,128]{3,2,1,0:T(8,128)(2,1)S(1)} %get-tuple-element.38), channel_id=1, source_target_pairs={{0,2},{1,3},{2,0},{3,1},{4,6},{5,7},{6,4},{7,5},{8,10},{9,11},{10,... | collective-permute-start | bytes 417800 | tf_op jit(solution)/shard_map/ppermute | solution.py:38
  14.5 0.7 %compare_and_fusion.1 = (pred[256]{0:T(512)(128)(4,1)S(1)}, s32[256]{0:T(256)S(1)}) fusion(s32[]{:T(128)S(6)} %axis_index.17, s32[256]{0:T(256)} %param.12), kind=kLoop, calls=%fused_computation.85 | loop fusion | flops 11264 | bytes 2308 | tf_op jit(solution)/shard_map/jit(_take)/and | solution.py:129
  15.2 1.2 %compare_and_fusion = (pred[256]{0:T(512)(128)(4,1)}, s32[256]{0:T(256)S(1)}) fusion(s32[256]{0:T(256)} %param.11, s32[]{:T(128)S(6)} %mul.87), kind=kLoop, calls=%fused_computation.83 | loop fusion | flops 2048 | bytes 2308 | tf_op jit(solution)/shard_map/jit(_take)/and | solution.py:149
  16.5 0.0 collective-permute-done
  16.5 0.0 collective-permute-done.1
  16.6 0.9 %constant_dynamic-update-slice_fusion.2 = bf16[80,32,128]{2,1,0:T(8,128)(2,1)S(1)} fusion(bf16[80,32,128]{2,1,0:T(8,128)(2,1)S(1)} %constant_dynamic-update-slice_fusion.3, bf16[16,32,128]{2,1,0:T(8,128)(2,1)} %param.9), kind=kLoop, calls=%fused_computation.70 | loop fusion | bytes 262144
  17.5 0.0 collective-permute-done.2
  17.5 0.0 collective-permute-done.4
  17.6 0.1 collective-permute-start.5
  17.7 0.0 collective-permute-done.3
  17.7 1.5 %collective-permute-done.5 = bf16[2,17,32,128]{3,2,1,0:T(8,128)(2,1)S(1)} collective-permute-done((bf16[2,17,32,128]{3,2,1,0:T(8,128)(2,1)S(1)}, bf16[2,17,32,128]{3,2,1,0:T(8,128)(2,1)S(1)}, u32[]{:S(2)}, u32[]{:S(2)}) %collective-permute-start.5) | collective-permute-done | bytes 278560 | tf_op jit(solution)/shard_map/ppermute | solution.py:38
  19.3 0.6 slice_bitcast_fusion.4
  19.9 0.8 %slice.59 = bf16[16,128,128]{2,1,0:T(8,128)(2,1)} slice(bf16[17,128,128]{2,1,0:T(8,128)(2,1)S(1)} %fusion.21), slice={[0:16], [0:128], [0:128]} | slice | bytes 1048576 | tf_op jit(solution)/shard_map/slice | solution.py:126
  20.7 1.0 %gather_fusion = bf16[256,32,128]{2,1,0:T(8,128)(2,1)S(1)} fusion(bf16[80,32,128]{2,1,0:T(8,128)(2,1)S(1)} %constant_dynamic-update-slice_fusion, s32[1024]{0:T(1024)S(1)} %pad_clamp_fusion.1), kind=kCustom, calls=%fused_computation | custom fusion | bytes 4195328 | tf_op jit(solution)/shard_map/jit(_take)/gather | solution.py:129
  21.7 7.9 %reduce-precision_convert_fusion.1 = (bf16[256,128,32]{1,2,0:T(8,128)(2,1)S(1)}, bf16[256,128,32]{1,2,0:T(8,128)(2,1)S(1)}) fusion(bf16[256,128,128]{2,1,0:T(8,128)(2,1)} %param.10, bf16[256,32,128]{2,1,0:T(8,128)(2,1)S(1)} %gather_fusion, pred[256]{0:T(512)(128)(4,1)S(1)} %get-tuple-element.26), kind=kOutput, calls=%fused_computation.5 | convolution fusion | flops 273678336 | bytes 14680320 | tf_op jit(solution)/shard_map/tjk,tfk->tjf/dot_general | solution.py:130
  29.6 0.4 pad_maximum_fusion
  30.0 1.2 %fusion.12 = bf16[128,32,16]{0,2,1:T(8,128)(2,1)S(1)} fusion(bf16[512,128,32]{1,2,0:T(8,128)(2,1)S(1)} %pad_maximum_fusion, bf16[256,16]{0,1:T(8,128)(2,1)S(1)} %select_convert_fusion.2), kind=kOutput, calls=%fused_computation.22 | convolution fusion | flops 67207168 | bytes 4333568 | tf_op jit(solution)/shard_map/tb,tjf->bfj/dot_general | solution.py:78
  31.2 1.4 %collective-permute-start.6 = (bf16[1,16,32,128]{3,1,2,0:T(8,128)(2,1)S(1)}, bf16[1,16,32,128]{3,1,2,0:T(8,128)(2,1)S(1)}, u32[]{:S(2)}, u32[]{:S(2)}) collective-permute-start(bf16[1,16,32,128]{3,1,2,0:T(8,128)(2,1)S(1)} %bitcast.61), channel_id=1, source_target_pairs={{0,2},{1,3},{2,0},{3,1},{4,6},{5,7},{6,4},{7,5},{8,10},{9,11},{10,... | collective-permute-start | bytes 393224 | tf_op jit(solution)/shard_map/ppermute | solution.py:38
  32.6 0.6 select_convert_fusion.1
  33.2 0.6 pad_clamp_fusion
  33.8 2.9 %collective-permute-done.6 = bf16[1,16,32,128]{3,1,2,0:T(8,128)(2,1)S(1)} collective-permute-done((bf16[1,16,32,128]{3,1,2,0:T(8,128)(2,1)S(1)}, bf16[1,16,32,128]{3,1,2,0:T(8,128)(2,1)S(1)}, u32[]{:S(2)}, u32[]{:S(2)}) %collective-permute-start.6) | collective-permute-done | bytes 131104 | tf_op jit(solution)/shard_map/ppermute | solution.py:38
  36.8 0.1 collective-permute-start.7
  36.9 0.1 broadcast_in_dim.45
  37.0 0.1 copy_dynamic-update-slice_fusion.3
  37.1 0.1 copy_dynamic-update-slice_fusion.2
  37.1 1.3 %collective-permute-done.7 = bf16[2,16,32,128]{3,1,2,0:T(8,128)(2,1)S(1)} collective-permute-done((bf16[2,16,32,128]{3,1,2,0:T(8,128)(2,1)S(1)}, bf16[2,16,32,128]{3,1,2,0:T(8,128)(2,1)S(1)}, u32[]{:S(2)}, u32[]{:S(2)}) %collective-permute-start.7) | collective-permute-done | bytes 262176 | tf_op jit(solution)/shard_map/ppermute | solution.py:38
  38.4 0.1 copy_dynamic-update-slice_fusion.1
  38.5 0.0 copy-start.3
  38.5 0.1 copy_dynamic-update-slice_fusion
  38.6 0.3 broadcast_compare_fusion
  38.9 1.0 %fusion.23 = f32[32,128,1]{1,0,2:T(8,128)} fusion(bf16[16,32,128]{2,0,1:T(8,128)(2,1)S(1)} %bitcast.64, f32[16,128,128]{2,1,0:T(8,128)S(1)} %get-tuple-element.41, bf16[16,128,128]{2,1,0:T(8,128)(2,1)S(1)} %copy-done), kind=kOutput, calls=%fused_computation.46 | convolution fusion | flops 18350080 | bytes 1720320 | tf_op jit(solution)/shard_map/bij,boj->io/dot_general | solution.py:144
  39.9 0.4 fusion.15
  40.3 0.1 collective-permute-start.13
  40.4 2.9 %collective-permute-start.12 = (f32[32,128]{1,0:T(8,128)}, f32[32,128]{1,0:T(8,128)}, u32[]{:S(2)}, u32[]{:S(2)}) collective-permute-start(f32[32,128]{1,0:T(8,128)} %bitcast.20), channel_id=1, source_target_pairs={{0,4},{4,0},{8,12},{12,8},{16,20},{20,16},{24,28},{28,24},{1,5},{5... | collective-permute-start | bytes 49160 | tf_op jit(solution)/shard_map/ppermute | solution.py:60
  43.3 1.4 %collective-permute-start.14 = (f32[32,128]{1,0:T(8,128)}, f32[32,128]{1,0:T(8,128)}, u32[]{:S(2)}, u32[]{:S(2)}) collective-permute-start(f32[32,128]{1,0:T(8,128)} %bitcast.20), channel_id=1, source_target_pairs={{0,12},{4,8},{8,4},{12,0},{16,28},{20,24},{24,20},{28,16},{1,13},{... | collective-permute-start | bytes 49160 | tf_op jit(solution)/shard_map/ppermute | solution.py:60
  44.7 1.1 %gather_fusion.1 = bf16[256,32,128]{2,1,0:T(8,128)(2,1)S(1)} fusion(bf16[16,32,128]{2,1,0:T(8,128)(2,1)S(1)} %fusion.15, s32[1024]{0:T(1024)} %pad_clamp_fusion), kind=kCustom, calls=%fused_computation.1 | custom fusion | bytes 4195328 | tf_op jit(solution)/shard_map/jit(_take)/gather | solution.py:149
  45.8 5.8 %reduce-precision_convert_fusion = (bf16[256,32,128]{2,1,0:T(8,128)(2,1)S(1)}, bf16[256,32,128]{2,1,0:T(8,128)(2,1)S(1)}) fusion(bf16[256,128,128]{2,1,0:T(8,128)(2,1)} %param.10, bf16[256,32,128]{2,1,0:T(8,128)(2,1)S(1)} %gather_fusion.1, pred[256]{0:T(512)(128)(4,1)} %get-tuple-element.24), kind=kOutput, calls=%fused_computation.3 | convolution fusion | flops 273678336 | bytes 14680320 | tf_op jit(solution)/shard_map/tfj,tjk->tfk/dot_general | solution.py:150
  51.6 0.0 copy-start.1
  51.6 0.4 pad_maximum_fusion.1
  52.0 0.4 copy-done.1
  52.4 1.5 %fusion.44 = (bf16[80,32,128]{2,0,1:T(8,128)(2,1)S(1)}, f32[80,32,128]{2,0,1:T(8,128)S(1)}) fusion(bf16[512,32,128]{2,1,0:T(8,128)(2,1)S(1)} %pad_maximum_fusion.1, bf16[256,80]{0,1:T(8,128)(2,1)S(1)} %copy-done.1), kind=kOutput, calls=%fused_computation.102 | convolution fusion | flops 336035840 | bytes 6201344 | tf_op jit(solution)/shard_map/ts,tfk->sfk/dot_general | solution.py:78
  53.9 0.0 collective-permute-done.13
  53.9 0.0 collective-permute-done.12
  54.0 0.8 %pad_maximum_fusion.5 = f32[4,32,128]{2,1,0:T(8,128)S(1)} fusion(f32[1,32,128]{2,1,0:T(8,128)} %bitcast.24, f32[1,32,128]{2,1,0:T(8,128)} %bitcast.23, f32[1,32,128]{2,1,0:T(8,128)} %bitcast.22, f32[1,32,128]{2,1,0:T(8,128)} %bitcast.21), kind=kLoop, calls=%fused_computation.56 | loop fusion | flops 49152 | bytes 131072 | tf_op jit(solution)/shard_map/stack | solution.py:61
  54.7 0.1 collective-permute-start.15
  54.8 0.8 %select_convert_fusion = bf16[16,32,128]{2,1,0:T(8,128)(2,1)} fusion(f32[16,128,128]{2,1,0:T(8,128)S(1)} %get-tuple-element.41, s32[]{:T(128)S(6)} %select_n.85, pred[16,128,128]{2,1,0:T(8,128)(4,1)S(1)} %get-tuple-element.40), kind=kLoop, calls=%fused_computation.34 | loop fusion | flops 196608 | bytes 458756 | tf_op jit(solution)/shard_map/convert_element_type | solution.py:141
  55.6 2.9 %collective-permute-start.8 = (bf16[16,32,128]{2,0,1:T(8,128)(2,1)S(1)}, bf16[16,32,128]{2,0,1:T(8,128)(2,1)S(1)}, u32[]{:S(2)}, u32[]{:S(2)}) collective-permute-start(bf16[16,32,128]{2,0,1:T(8,128)(2,1)S(1)} %get-tuple-element.32), channel_id=1, source_target_pairs={{8,0},{12,4},{16,8},{20,12},{24,16},{28,20},{0,24},{4,28},{9,1},{1... | collective-permute-start | bytes 393224 | tf_op jit(solution)/shard_map/ppermute | solution.py:22
  58.5 0.0 collective-permute-start.11
  58.5 1.5 %collective-permute-start.10 = (bf16[16,32,128]{2,0,1:T(8,128)(2,1)S(1)}, bf16[16,32,128]{2,0,1:T(8,128)(2,1)S(1)}, u32[]{:S(2)}, u32[]{:S(2)}) collective-permute-start(bf16[16,32,128]{2,0,1:T(8,128)(2,1)S(1)} %get-tuple-element.34), channel_id=1, source_target_pairs={{28,0},{0,4},{4,8},{8,12},{12,16},{16,20},{20,24},{24,28},{29,1},{... | collective-permute-start | bytes 393224 | tf_op jit(solution)/shard_map/ppermute | solution.py:22
  60.1 3.3 %collective-permute-start.9 = (bf16[16,32,128]{2,0,1:T(8,128)(2,1)S(1)}, bf16[16,32,128]{2,0,1:T(8,128)(2,1)S(1)}, u32[]{:S(2)}, u32[]{:S(2)}) collective-permute-start(bf16[16,32,128]{2,0,1:T(8,128)(2,1)S(1)} %get-tuple-element.35), channel_id=1, source_target_pairs={{4,0},{8,4},{12,8},{16,12},{20,16},{24,20},{28,24},{0,28},{5,1},{9... | collective-permute-start | bytes 393224 | tf_op jit(solution)/shard_map/ppermute | solution.py:22
  63.3 0.0 collective-permute-done.15
  63.3 0.6 divide_subtract_fusion
  64.0 2.8 %collective-permute-done.11 = bf16[16,32,128]{2,0,1:T(8,128)(2,1)S(1)} collective-permute-done((bf16[16,32,128]{2,0,1:T(8,128)(2,1)S(1)}, bf16[16,32,128]{2,0,1:T(8,128)(2,1)S(1)}, u32[]{:S(2)}, u32[]{:S(2)}) %collective-permute-start.11) | collective-permute-done | bytes 131104 | tf_op jit(solution)/shard_map/ppermute | solution.py:22
  66.8 3.1 %collective-permute-done.10 = bf16[16,32,128]{2,0,1:T(8,128)(2,1)S(1)} collective-permute-done((bf16[16,32,128]{2,0,1:T(8,128)(2,1)S(1)}, bf16[16,32,128]{2,0,1:T(8,128)(2,1)S(1)}, u32[]{:S(2)}, u32[]{:S(2)}) %collective-permute-start.10) | collective-permute-done | bytes 131104 | tf_op jit(solution)/shard_map/ppermute | solution.py:22
  69.9 0.0 collective-permute-done.9
  69.9 0.1 fusion.20
  70.0 0.8 %copy.31 = f32[16,32,128]{2,1,0:T(8,128)} copy(f32[16,32,128]{2,0,1:T(8,128)S(1)} %fusion.20) | data formatting | bytes 524288
  (27 shorter events, 0.3 us)
Async XLA Ops:
  0.6 16.9 %collective-permute-start.2 = (bf16[16,32,128]{2,1,0:T(8,128)(2,1)}, bf16[16,32,128]{2,1,0:T(8,128)(2,1)S(1)}, u32[]{:S(2)}, u32[]{:S(2)}) collective-permute-start(bf16[16,32,128]{2,1,0:T(8,128)(2,1)} %param.9), channel_id=1, source_target_pairs={{4,0},{8,4},{12,8},{16,12},{20,16},{24,20},{28,24},{0,28},{5,1},{9... | collective-permute-start | bytes 393224 | tf_op jit(solution)/shard_map/ppermute | solution.py:22
  6.7 9.9 %collective-permute-start.1 = (bf16[16,32,128]{2,1,0:T(8,128)(2,1)}, bf16[16,32,128]{2,1,0:T(8,128)(2,1)S(1)}, u32[]{:S(2)}, u32[]{:S(2)}) collective-permute-start(bf16[16,32,128]{2,1,0:T(8,128)(2,1)} %param.9), channel_id=1, source_target_pairs={{28,0},{0,4},{4,8},{8,12},{12,16},{16,20},{20,24},{24,28},{29,1},{... | collective-permute-start | bytes 393224 | tf_op jit(solution)/shard_map/ppermute | solution.py:22
  6.7 9.8 %collective-permute-start = (bf16[16,32,128]{2,1,0:T(8,128)(2,1)}, bf16[16,32,128]{2,1,0:T(8,128)(2,1)S(1)}, u32[]{:S(2)}, u32[]{:S(2)}) collective-permute-start(bf16[16,32,128]{2,1,0:T(8,128)(2,1)} %param.9), channel_id=1, source_target_pairs={{24,0},{28,4},{0,8},{4,12},{8,16},{12,20},{16,24},{20,28},{25,1},{... | collective-permute-start | bytes 393224 | tf_op jit(solution)/shard_map/ppermute | solution.py:22
  6.7 11.0 %collective-permute-start.3 = (bf16[16,32,128]{2,1,0:T(8,128)(2,1)}, bf16[16,32,128]{2,1,0:T(8,128)(2,1)S(1)}, u32[]{:S(2)}, u32[]{:S(2)}) collective-permute-start(bf16[16,32,128]{2,1,0:T(8,128)(2,1)} %param.9), channel_id=1, source_target_pairs={{8,0},{12,4},{16,8},{20,12},{24,16},{28,20},{0,24},{4,28},{9,1},{1... | collective-permute-start | bytes 393224 | tf_op jit(solution)/shard_map/ppermute | solution.py:22
  12.3 5.2 %collective-permute-start.4 = (bf16[1,17,32,128]{3,2,1,0:T(8,128)(2,1)S(1)}, bf16[1,17,32,128]{3,2,1,0:T(8,128)(2,1)S(1)}, u32[]{:S(2)}, u32[]{:S(2)}) collective-permute-start(bf16[1,17,32,128]{3,2,1,0:T(8,128)(2,1)S(1)} %get-tuple-element.38), channel_id=1, source_target_pairs={{0,2},{1,3},{2,0},{3,1},{4,6},{5,7},{6,4},{7,5},{8,10},{9,11},{10,... | collective-permute-start | bytes 417800 | tf_op jit(solution)/shard_map/ppermute | solution.py:38
  17.6 1.6 %collective-permute-start.5 = (bf16[2,17,32,128]{3,2,1,0:T(8,128)(2,1)S(1)}, bf16[2,17,32,128]{3,2,1,0:T(8,128)(2,1)S(1)}, u32[]{:S(2)}, u32[]{:S(2)}) collective-permute-start(bf16[2,17,32,128]{3,2,1,0:T(8,128)(2,1)S(1)} %pad_maximum_fusion.2), channel_id=1, source_target_pairs={{0,1},{1,0},{2,3},{3,2},{4,5},{5,4},{6,7},{7,6},{8,9},{9,8},{10,11... | collective-permute-start | bytes 835592 | tf_op jit(solution)/shard_map/ppermute | solution.py:38
  31.2 7.3 %copy-start.2 = (bf16[128,128]{1,0:T(8,128)(2,1)S(1)}, bf16[128,128]{1,0:T(8,128)(2,1)}, u32[]{:S(2)}) copy-start(bf16[128,128]{1,0:T(8,128)(2,1)} %slice_bitcast_fusion.4) | copy-start | bytes 98308
  31.2 5.6 %collective-permute-start.6 = (bf16[1,16,32,128]{3,1,2,0:T(8,128)(2,1)S(1)}, bf16[1,16,32,128]{3,1,2,0:T(8,128)(2,1)S(1)}, u32[]{:S(2)}, u32[]{:S(2)}) collective-permute-start(bf16[1,16,32,128]{3,1,2,0:T(8,128)(2,1)S(1)} %bitcast.61), channel_id=1, source_target_pairs={{0,2},{1,3},{2,0},{3,1},{4,6},{5,7},{6,4},{7,5},{8,10},{9,11},{10,... | collective-permute-start | bytes 393224 | tf_op jit(solution)/shard_map/ppermute | solution.py:38
  36.8 2.1 %copy-start = (bf16[16,128,128]{2,1,0:T(8,128)(2,1)S(1)}, bf16[16,128,128]{2,1,0:T(8,128)(2,1)}, u32[]{:S(2)}) copy-start(bf16[16,128,128]{2,1,0:T(8,128)(2,1)} %slice.59) | copy-start | bytes 1572868
  36.8 1.6 %collective-permute-start.7 = (bf16[2,16,32,128]{3,1,2,0:T(8,128)(2,1)S(1)}, bf16[2,16,32,128]{3,1,2,0:T(8,128)(2,1)S(1)}, u32[]{:S(2)}, u32[]{:S(2)}) collective-permute-start(bf16[2,16,32,128]{3,1,2,0:T(8,128)(2,1)S(1)} %pad_maximum_fusion.3), channel_id=1, source_target_pairs={{0,1},{1,0},{2,3},{3,2},{4,5},{5,4},{6,7},{7,6},{8,9},{9,8},{10,11... | collective-permute-start | bytes 786440 | tf_op jit(solution)/shard_map/ppermute | solution.py:38
  38.5 1.4 %copy-start.3 = (f32[32,128]{1,0:T(8,128)S(1)}, f32[32,128]{1,0:T(8,128)}, u32[]{:S(2)}) copy-start(f32[32,128]{1,0:T(8,128)} %param.14) | copy-start | bytes 49156
  40.3 13.6 %collective-permute-start.13 = (f32[32,128]{1,0:T(8,128)}, f32[32,128]{1,0:T(8,128)}, u32[]{:S(2)}, u32[]{:S(2)}) collective-permute-start(f32[32,128]{1,0:T(8,128)} %bitcast.20), channel_id=1, source_target_pairs={{0,8},{4,12},{8,0},{12,4},{16,24},{20,28},{24,16},{28,20},{1,9},{5... | collective-permute-start | bytes 49160 | tf_op jit(solution)/shard_map/ppermute | solution.py:60
  40.4 13.5 %collective-permute-start.12 = (f32[32,128]{1,0:T(8,128)}, f32[32,128]{1,0:T(8,128)}, u32[]{:S(2)}, u32[]{:S(2)}) collective-permute-start(f32[32,128]{1,0:T(8,128)} %bitcast.20), channel_id=1, source_target_pairs={{0,4},{4,0},{8,12},{12,8},{16,20},{20,16},{24,28},{28,24},{1,5},{5... | collective-permute-start | bytes 49160 | tf_op jit(solution)/shard_map/ppermute | solution.py:60
  43.3 10.7 %collective-permute-start.14 = (f32[32,128]{1,0:T(8,128)}, f32[32,128]{1,0:T(8,128)}, u32[]{:S(2)}, u32[]{:S(2)}) collective-permute-start(f32[32,128]{1,0:T(8,128)} %bitcast.20), channel_id=1, source_target_pairs={{0,12},{4,8},{8,4},{12,0},{16,28},{20,24},{24,20},{28,16},{1,13},{... | collective-permute-start | bytes 49160 | tf_op jit(solution)/shard_map/ppermute | solution.py:60
  51.6 0.8 %copy-start.1 = (bf16[256,80]{0,1:T(8,128)(2,1)S(1)}, bf16[256,80]{0,1:T(8,128)(2,1)}, u32[]{:S(2)}) copy-start(bf16[256,80]{0,1:T(8,128)(2,1)} %select_convert_fusion.1) | copy-start | bytes 122884
  52.4 10.9 %copy-start.4 = (f32[32,128]{1,0:T(8,128)S(1)}, f32[32,128]{1,0:T(8,128)}, u32[]{:S(2)}) copy-start(f32[32,128]{1,0:T(8,128)} %param.15) | copy-start | bytes 49156
  52.4 10.9 %copy-start.5 = (f32[32,128]{1,0:T(8,128)S(1)}, f32[32,128]{1,0:T(8,128)}, u32[]{:S(2)}) copy-start(f32[32,128]{1,0:T(8,128)} %param.16) | copy-start | bytes 49156
  54.7 8.6 %collective-permute-start.15 = (f32[32,128]{1,0:T(8,128)S(1)}, f32[32,128]{1,0:T(8,128)S(1)}, u32[]{:S(2)}, u32[]{:S(2)}) collective-permute-start(f32[32,128]{1,0:T(8,128)S(1)} %add_bitcast_fusion), channel_id=1, source_target_pairs={{0,16},{4,20},{8,24},{12,28},{16,0},{20,4},{24,8},{28,12},{1,17},{... | collective-permute-start | bytes 49160 | tf_op jit(solution)/shard_map/ppermute | solution.py:67
  55.6 8.4 %collective-permute-start.8 = (bf16[16,32,128]{2,0,1:T(8,128)(2,1)S(1)}, bf16[16,32,128]{2,0,1:T(8,128)(2,1)S(1)}, u32[]{:S(2)}, u32[]{:S(2)}) collective-permute-start(bf16[16,32,128]{2,0,1:T(8,128)(2,1)S(1)} %get-tuple-element.32), channel_id=1, source_target_pairs={{8,0},{12,4},{16,8},{20,12},{24,16},{28,20},{0,24},{4,28},{9,1},{1... | collective-permute-start | bytes 393224 | tf_op jit(solution)/shard_map/ppermute | solution.py:22
  58.5 8.3 %collective-permute-start.11 = (bf16[16,32,128]{2,0,1:T(8,128)(2,1)S(1)}, bf16[16,32,128]{2,0,1:T(8,128)(2,1)S(1)}, u32[]{:S(2)}, u32[]{:S(2)}) collective-permute-start(bf16[16,32,128]{2,0,1:T(8,128)(2,1)S(1)} %get-tuple-element.33), channel_id=1, source_target_pairs={{24,0},{28,4},{0,8},{4,12},{8,16},{12,20},{16,24},{20,28},{25,1},{... | collective-permute-start | bytes 393224 | tf_op jit(solution)/shard_map/ppermute | solution.py:22
  58.5 11.4 %collective-permute-start.10 = (bf16[16,32,128]{2,0,1:T(8,128)(2,1)S(1)}, bf16[16,32,128]{2,0,1:T(8,128)(2,1)S(1)}, u32[]{:S(2)}, u32[]{:S(2)}) collective-permute-start(bf16[16,32,128]{2,0,1:T(8,128)(2,1)S(1)} %get-tuple-element.34), channel_id=1, source_target_pairs={{28,0},{0,4},{4,8},{8,12},{12,16},{16,20},{20,24},{24,28},{29,1},{... | collective-permute-start | bytes 393224 | tf_op jit(solution)/shard_map/ppermute | solution.py:22
  60.1 9.9 %collective-permute-start.9 = (bf16[16,32,128]{2,0,1:T(8,128)(2,1)S(1)}, bf16[16,32,128]{2,0,1:T(8,128)(2,1)S(1)}, u32[]{:S(2)}, u32[]{:S(2)}) collective-permute-start(bf16[16,32,128]{2,0,1:T(8,128)(2,1)S(1)} %get-tuple-element.35), channel_id=1, source_target_pairs={{4,0},{8,4},{12,8},{16,12},{20,16},{24,20},{28,24},{0,28},{5,1},{9... | collective-permute-start | bytes 393224 | tf_op jit(solution)/shard_map/ppermute | solution.py:22

commit v16 on v8

--- a/solution.py
+++ b/solution.py
@@ -22,7 +22,7 @@
     return lax.ppermute(block, axis, route)
 
 
-def gathered_along(block, axis, dim):
+def gathered_along(block, axis, dim, beside=None):
     size = lax.axis_size(axis)
     own = lax.axis_index(axis)
     width = block.shape[dim]
@@ -30,12 +30,17 @@
         pieces = [(block, own)]
         for step in range(1, size):
             pieces.append((passed_along(block, axis, -step), (own + step) % size))
+        if beside is not None:
+            arrays, beside = lax.optimization_barrier(([piece for piece, _ in pieces], beside))
+            pieces = [(array, index) for array, (_, index) in zip(arrays, pieces)]
     else:
         pieces = [(block, own)]
         mask = size // 2
         while mask >= 1:
             held = jnp.stack([piece for piece, _ in pieces])
             got = lax.ppermute(held, axis, [(i, i ^ mask) for i in range(size)])
+            if beside is not None and mask == size // 2:
+                got, beside = lax.optimization_barrier((got, beside))
             pieces = pieces + [(got[k], index ^ mask) for k, (_, index) in enumerate(pieces)]
             mask //= 2
     shape = list(block.shape)
@@ -43,7 +48,9 @@
     whole = jnp.zeros(shape, block.dtype)
     for piece, index in pieces:
         whole = lax.dynamic_update_slice_in_dim(whole, piece, index * width, dim)
-    return whole
+    if beside is None:
+        return whole
+    return whole, beside
 
 
 def summed_over(block, axis):
@@ -112,10 +119,9 @@
     nearby = jnp.concatenate(pieces, axis=0)
     weight_half = weight.astype(jnp.bfloat16)
     packed = jnp.concatenate([cotangent, weight_half[None]], axis=0)
-    packed_all = gathered_along(packed, "feat", 1)
+    packed_all, nearby = gathered_along(packed, "feat", 1, beside=nearby)
     cotangent_all = packed_all[:blocks]
     weight_all = packed_all[blocks]
-    nearby, cotangent_all, weight_all = lax.optimization_barrier((nearby, cotangent_all, weight_all))
     sources = jnp.einsum(
         "ts,sfk->tfk", pick_source, nearby, preferred_element_type=jnp.float32
     ).astype(jnp.bfloat16)

time: 67.8 us -> 83 us (1.22)
  local copies, waits for them, and re-layouts: 2.61 us -> 26.2 us
  waiting for transfers between devices: 15.1 us -> 6.27 us
  starting transfers between devices: 23.3 us -> 24.3 us
    dynamic_update_slice x7 -> x8, local copies, waits for them, and re-layouts: 0.28 us -> 21.1 us  [gathered_along(): whole = lax.dynamic_update_slice_in_dim(whole, piece, index * width, dim)]
    ppermute x4, waiting for transfers between devices: 7.11 us -> 0.01 us  [gathered_along(): got = lax.ppermute(held, axis, [(i, i ^ mask) for i in range(size)])]
    ppermute x4, starting transfers between devices: 3.26 us -> 5.96 us  [gathered_along(): got = lax.ppermute(held, axis, [(i, i ^ mask) for i in range(size)])]
    ppermute x8, starting transfers between devices: 16.9 us -> 14.8 us  [passed_along(): return lax.ppermute(block, axis, route)]
    unnamed x11 -> x14, local copies, waits for them, and re-layouts: 1.78 us -> 3.27 us
    ppermute x3, waiting for transfers between devices: 3.69 us -> 2.37 us  [summed_over(): lax.ppermute(block, axis, [(i, i ^ mask) for i in range(size)])]
    another operation x3 -> x2, other arithmetic: 1.01 us -> 0.06 us  [gathered_along(): held = jnp.stack([piece for piece, _ in pieces])]
    concatenate x0 -> x1, other arithmetic: none -> 0.92 us  [per_device(): packed = jnp.concatenate([cotangent, weight_half[None]], axis=0)]
  transfers between devices with their start and end apart: 15 -> 15, of which waited for: 8 -> 4; matrix products, arithmetic and copies ran while one was open for 22% -> 37% of each run, Pallas kernels for 0% -> 0%
where the time goes in v16:
time: 83 us; the launch traced here: 82.7 us
  local copies, waits for them, and re-layouts  26.2 us (32%)
  starting transfers between devices  24.3 us (29%)
  matrix products  18.8 us (23%)
  waiting for transfers between devices  6.27 us (8%)
  other arithmetic  5.47 us (7%)
  between operations  1.65 us (2%)
    dynamic_update_slice x8, local copies, waits for them, and re-layouts, gathered_along(): whole = lax.dynamic_update_slice_in_dim(whole, piece, index * width, dim)  21.1 us
    ppermute x8, starting transfers between devices, passed_along(): return lax.ppermute(block, axis, route)  14.8 us
    dot_general x1, matrix products, per_device(): jnp.einsum('tfk,tjk->tfj', sources, tile_values, preferred_element_type=j...  7.91 us
    ppermute x4, starting transfers between devices, gathered_along(): got = lax.ppermute(held, axis, [(i, i ^ mask) for i in range(size)])  5.96 us
    dot_general x1, matrix products, per_device(): jnp.einsum('tfj,tjk->tfk', back_sources, tile_values, preferred_element_t...  5.8 us
    ppermute x8, waiting for transfers between devices, passed_along(): return lax.ppermute(block, axis, route)  3.88 us
    ppermute x3, starting transfers between devices, summed_over(): lax.ppermute(block, axis, [(i, i ^ mask) for i in range(size)])  3.49 us
    unnamed x14, local copies, waits for them, and re-layouts  3.27 us
  transfers between devices with their start and end apart: 15, of which 4 were waited for; matrix products, arithmetic and copies ran while one was open for 37% of the time, Pallas kernels for 0%

profile of v16, /device:TPU:0, one launch (start us, length us, event | category | flops | bytes accessed | tf_op | source)
XLA Modules:
  0.0 82.7 jit_solution(18238266736968809544)
XLA Ops:
  0.6 3.1 %collective-permute-start.1 = (bf16[16,32,128]{2,1,0:T(8,128)(2,1)}, bf16[16,32,128]{2,1,0:T(8,128)(2,1)S(1)}, u32[]{:S(2)}, u32[]{:S(2)}) collective-permute-start(bf16[16,32,128]{2,1,0:T(8,128)(2,1)} %param.9), channel_id=1, source_target_pairs={{24,0},{28,4},{0,8},{4,12},{8,16},{12,20},{16,24},{20,28},{25,1},{... | collective-permute-start | bytes 393224 | tf_op jit(solution)/shard_map/ppermute | solution.py:22
  3.7 1.5 %collective-permute-start.2 = (bf16[16,32,128]{2,1,0:T(8,128)(2,1)}, bf16[16,32,128]{2,1,0:T(8,128)(2,1)S(1)}, u32[]{:S(2)}, u32[]{:S(2)}) collective-permute-start(bf16[16,32,128]{2,1,0:T(8,128)(2,1)} %param.9), channel_id=1, source_target_pairs={{28,0},{0,4},{4,8},{8,12},{12,16},{16,20},{20,24},{24,28},{29,1},{... | collective-permute-start | bytes 393224 | tf_op jit(solution)/shard_map/ppermute | solution.py:22
  5.2 3.2 %collective-permute-start.3 = (bf16[16,32,128]{2,1,0:T(8,128)(2,1)}, bf16[16,32,128]{2,1,0:T(8,128)(2,1)S(1)}, u32[]{:S(2)}, u32[]{:S(2)}) collective-permute-start(bf16[16,32,128]{2,1,0:T(8,128)(2,1)} %param.9), channel_id=1, source_target_pairs={{4,0},{8,4},{12,8},{16,12},{20,16},{24,20},{28,24},{0,28},{5,1},{9... | collective-permute-start | bytes 393224 | tf_op jit(solution)/shard_map/ppermute | solution.py:22
  8.4 0.3 collective-permute-start.4
  8.7 0.7 convert_bitcast_fusion
  9.4 0.9 %pad_maximum_fusion.4 = (bf16[17,32,128]{2,1,0:T(8,128)(2,1)S(1)}, bf16[1,17,32,128]{3,2,1,0:T(8,128)(2,1)S(1)}) fusion(bf16[1,32,128]{2,1,0:T(8,128)(2,1)S(1)} %convert_bitcast_fusion, bf16[16,32,128]{2,1,0:T(8,128)(2,1)} %param.17), kind=kLoop, calls=%fused_computation.32 | loop fusion | flops 69632 | bytes 417792 | tf_op jit(solution)/shard_map/concatenate | solution.py:121
  10.4 1.7 %collective-permute-start = (bf16[1,17,32,128]{3,2,1,0:T(8,128)(2,1)S(1)}, bf16[1,17,32,128]{3,2,1,0:T(8,128)(2,1)S(1)}, u32[]{:S(2)}, u32[]{:S(2)}) collective-permute-start(bf16[1,17,32,128]{3,2,1,0:T(8,128)(2,1)S(1)} %get-tuple-element.35), channel_id=1, source_target_pairs={{0,2},{1,3},{2,0},{3,1},{4,6},{5,7},{6,4},{7,5},{8,10},{9,11},{10,... | collective-permute-start | bytes 417800 | tf_op jit(solution)/shard_map/ppermute | solution.py:41
  12.8 0.7 fusion.31
  13.5 0.7 broadcast_subtract_fusion
  14.2 0.3 copy.27
  14.6 0.1 broadcast_in_dim.11
  14.7 2.7 %dynamic_update_slice.24 = bf16[17,128,128]{1,2,0:T(8,128)(2,1)S(1)} dynamic-update-slice(bf16[17,128,128]{1,2,0:T(8,128)(2,1)S(1)} %broadcast_in_dim.11, bf16[17,32,128]{1,2,0:T(8,128)(2,1)S(1)} %copy.27, s32[]{:T(128)} %constant.72.clone.1, s32[]{:T(128)S(6)} %select_n.49, s32[]{:T(128)} %constant.72.clone.1) | dynamic-update-slice | bytes 278532 | tf_op jit(solution)/shard_map/dynamic_update_slice | solution.py:50
  17.4 0.0 collective-permute-done.1
  17.4 0.9 %constant_dynamic-update-slice_fusion.2 = bf16[80,32,128]{2,1,0:T(8,128)(2,1)S(1)} fusion(bf16[80,32,128]{2,1,0:T(8,128)(2,1)S(1)} %constant_dynamic-update-slice_fusion.3, bf16[16,32,128]{2,1,0:T(8,128)(2,1)} %param.9), kind=kLoop, calls=%fused_computation.60 | loop fusion | bytes 262144
  18.4 0.0 collective-permute-done.3
  18.4 0.0 collective-permute-done.4
  18.5 0.3 copy.28
  18.8 0.8 fusion.12
  19.6 7.9 %reduce-precision_convert_fusion.1 = (bf16[256,32,128]{2,1,0:T(8,128)(2,1)S(1)}, bf16[256,32,128]{2,1,0:T(8,128)(2,1)S(1)}) fusion(bf16[256,128,128]{2,1,0:T(8,128)(2,1)} %param.10, bf16[256,32,128]{2,0,1:T(8,128)(2,1)S(1)} %fusion.12), kind=kOutput, calls=%fused_computation.3 | convolution fusion | flops 272629760 | bytes 14680064 | tf_op jit(solution)/shard_map/tfk,tjk->tfj/dot_general | solution.py:128
  27.5 0.4 pad_maximum_fusion
  27.9 1.2 %fusion.9 = bf16[16,32,128]{2,0,1:T(8,128)(2,1)S(1)} fusion(bf16[512,32,128]{2,1,0:T(8,128)(2,1)S(1)} %pad_maximum_fusion, bf16[256,16]{0,1:T(8,128)(2,1)S(1)} %select_convert_fusion.2), kind=kOutput, calls=%fused_computation.19 | convolution fusion | flops 67207168 | bytes 4333568 | tf_op jit(solution)/shard_map/tb,tfj->bfj/dot_general | solution.py:73
  29.1 3.6 %collective-permute-start.6 = (bf16[1,16,32,128]{3,1,2,0:T(8,128)(2,1)S(1)}, bf16[1,16,32,128]{3,1,2,0:T(8,128)(2,1)S(1)}, u32[]{:S(2)}, u32[]{:S(2)}) collective-permute-start(bf16[1,16,32,128]{3,1,2,0:T(8,128)(2,1)S(1)} %bitcast.53), channel_id=1, source_target_pairs={{0,2},{1,3},{2,0},{3,1},{4,6},{5,7},{6,4},{7,5},{8,10},{9,11},{10,... | collective-permute-start | bytes 393224 | tf_op jit(solution)/shard_map/ppermute | solution.py:41
  32.8 6.0 %dynamic_update_slice.25 = bf16[17,128,128]{1,2,0:T(8,128)(2,1)S(1)} dynamic-update-slice(bf16[17,128,128]{1,2,0:T(8,128)(2,1)S(1)} %dynamic_update_slice.24, bf16[17,32,128]{1,2,0:T(8,128)(2,1)S(1)} %bitcast.50, s32[]{:T(128)} %constant.72.clone.1, s32[]{:T(128)S(6)} %select_n.50, s32[]{:T(128)} %constant.72.clone.1) | dynamic-update-slice | bytes 278532 | tf_op jit(solution)/shard_map/dynamic_update_slice | solution.py:50
  38.7 0.1 broadcast_in_dim.13
  38.8 0.1 copy_dynamic-update-slice_fusion.3
  38.9 0.6 collective-permute-start.7
  39.6 0.0 collective-permute-done.5
  39.6 0.3 copy.48
  39.9 0.3 copy.49
  40.3 6.0 %dynamic_update_slice.26 = bf16[17,128,128]{1,2,0:T(8,128)(2,1)S(1)} dynamic-update-slice(bf16[17,128,128]{1,2,0:T(8,128)(2,1)S(1)} %dynamic_update_slice.25, bf16[17,32,128]{1,2,0:T(8,128)(2,1)S(1)} %bitcast.51, s32[]{:T(128)} %constant.72.clone.1, s32[]{:T(128)S(6)} %select_n.51, s32[]{:T(128)} %constant.72.clone.1) | dynamic-update-slice | bytes 278532 | tf_op jit(solution)/shard_map/dynamic_update_slice | solution.py:50
  46.3 6.2 %dynamic_update_slice.27 = bf16[17,128,128]{1,2,0:T(8,128)(2,1)S(1)} dynamic-update-slice(bf16[17,128,128]{1,2,0:T(8,128)(2,1)S(1)} %dynamic_update_slice.26, bf16[17,32,128]{1,2,0:T(8,128)(2,1)S(1)} %bitcast.52, s32[]{:T(128)} %constant.72.clone.1, s32[]{:T(128)S(6)} %select_n.52, s32[]{:T(128)} %constant.72.clone.1) | dynamic-update-slice | bytes 278532 | tf_op jit(solution)/shard_map/dynamic_update_slice | solution.py:50
  52.5 0.1 copy_dynamic-update-slice_fusion.1
  52.6 0.1 copy_dynamic-update-slice_fusion
  52.6 0.4 broadcast_compare_fusion
  53.0 0.3 multiply_convert_fusion
  53.3 0.3 fusion.8
  53.5 0.2 convolution_bitcast_fusion.1
  53.8 0.2 copy.45
  54.0 0.7 fusion.26
  54.8 5.8 %reduce-precision_convert_fusion = (bf16[256,32,128]{2,1,0:T(8,128)(2,1)S(1)}, bf16[256,32,128]{2,1,0:T(8,128)(2,1)S(1)}) fusion(bf16[256,128,128]{2,1,0:T(8,128)(2,1)} %param.10, bf16[256,32,128]{2,0,1:T(8,128)(2,1)S(1)} %fusion.26), kind=kOutput, calls=%fused_computation.1 | convolution fusion | flops 272629760 | bytes 14680064 | tf_op jit(solution)/shard_map/tfj,tjk->tfk/dot_general | solution.py:150
  60.6 0.8 collective-permute-start.12
  61.4 0.4 pad_maximum_fusion.1
  61.7 0.0 copy-start.1
  61.7 0.0 copy-start.2
  61.8 1.5 %fusion.40 = (bf16[80,32,128]{2,0,1:T(8,128)(2,1)S(1)}, f32[80,32,128]{2,0,1:T(8,128)S(1)}) fusion(bf16[512,32,128]{2,1,0:T(8,128)(2,1)S(1)} %pad_maximum_fusion.1, bf16[256,80]{0,1:T(8,128)(2,1)S(1)} %select_convert_fusion.1), kind=kOutput, calls=%fused_computation.87 | convolution fusion | flops 336035840 | bytes 6201344 | tf_op jit(solution)/shard_map/ts,tfk->sfk/dot_general | solution.py:73
  63.3 1.1 %collective-permute-done.12 = f32[32,128]{1,0:T(8,128)S(1)} collective-permute-done((f32[32,128]{1,0:T(8,128)S(1)}, f32[32,128]{1,0:T(8,128)S(1)}, u32[]{:S(2)}, u32[]{:S(2)}) %collective-permute-start.12) | collective-permute-done | bytes 16416 | tf_op jit(solution)/shard_map/ppermute | solution.py:62
  64.4 1.7 %collective-permute-start.13 = (f32[32,128]{1,0:T(8,128)S(1)}, f32[32,128]{1,0:T(8,128)S(1)}, u32[]{:S(2)}, u32[]{:S(2)}) collective-permute-start(f32[32,128]{1,0:T(8,128)S(1)} %add.84), channel_id=1, source_target_pairs={{0,8},{4,12},{8,0},{12,4},{16,24},{20,28},{24,16},{28,20},{1,9},{5... | collective-permute-start | bytes 49160 | tf_op jit(solution)/shard_map/ppermute | solution.py:62
  66.1 0.7 fusion.38
  66.8 1.3 %collective-permute-done.13 = f32[32,128]{1,0:T(8,128)S(1)} collective-permute-done((f32[32,128]{1,0:T(8,128)S(1)}, f32[32,128]{1,0:T(8,128)S(1)}, u32[]{:S(2)}, u32[]{:S(2)}) %collective-permute-start.13) | collective-permute-done | bytes 16416 | tf_op jit(solution)/shard_map/ppermute | solution.py:62
  68.1 0.9 %collective-permute-start.14 = (f32[32,128]{1,0:T(8,128)S(1)}, f32[32,128]{1,0:T(8,128)S(1)}, u32[]{:S(2)}, u32[]{:S(2)}) collective-permute-start(f32[32,128]{1,0:T(8,128)S(1)} %add.85), channel_id=1, source_target_pairs={{0,16},{4,20},{8,24},{12,28},{16,0},{20,4},{24,8},{28,12},{1,17},{... | collective-permute-start | bytes 49160 | tf_op jit(solution)/shard_map/ppermute | solution.py:62
  69.1 0.6 select_convert_fusion
  69.7 0.8 %copy.40 = bf16[16,32,128]{2,1,0:T(8,128)(2,1)} copy(bf16[16,32,128]{1,2,0:T(8,128)(2,1)S(1)} %select_convert_fusion) | data formatting | bytes 262144
  70.5 1.6 %collective-permute-start.11 = (bf16[16,32,128]{2,0,1:T(8,128)(2,1)}, bf16[16,32,128]{2,0,1:T(8,128)(2,1)S(1)}, u32[]{:S(2)}, u32[]{:S(2)}) collective-permute-start(bf16[16,32,128]{2,0,1:T(8,128)(2,1)} %get-tuple-element.27), channel_id=1, source_target_pairs={{24,0},{28,4},{0,8},{4,12},{8,16},{12,20},{16,24},{20,28},{25,1},{... | collective-permute-start | bytes 393224 | tf_op jit(solution)/shard_map/ppermute | solution.py:22
  72.1 0.6 collective-permute-start.10
  72.7 4.1 %collective-permute-start.9 = (bf16[16,32,128]{2,0,1:T(8,128)(2,1)S(1)}, bf16[16,32,128]{2,0,1:T(8,128)(2,1)S(1)}, u32[]{:S(2)}, u32[]{:S(2)}) collective-permute-start(bf16[16,32,128]{2,0,1:T(8,128)(2,1)S(1)} %get-tuple-element.29), channel_id=1, source_target_pairs={{4,0},{8,4},{12,8},{16,12},{20,16},{24,20},{28,24},{0,28},{5,1},{9... | collective-permute-start | bytes 393224 | tf_op jit(solution)/shard_map/ppermute | solution.py:22
  76.8 0.4 collective-permute-start.8
  77.3 0.0 collective-permute-done.14
  77.3 0.6 divide_subtract_fusion
  77.9 0.0 collective-permute-done.11
  77.9 2.2 %collective-permute-done.10 = bf16[16,32,128]{2,0,1:T(8,128)(2,1)S(1)} collective-permute-done((bf16[16,32,128]{2,0,1:T(8,128)(2,1)}, bf16[16,32,128]{2,0,1:T(8,128)(2,1)S(1)}, u32[]{:S(2)}, u32[]{:S(2)}) %collective-permute-start.10) | collective-permute-done | bytes 131104 | tf_op jit(solution)/shard_map/ppermute | solution.py:22
  80.1 0.0 collective-permute-done.9
  80.2 1.7 %collective-permute-done.8 = bf16[16,32,128]{2,0,1:T(8,128)(2,1)S(1)} collective-permute-done((bf16[16,32,128]{2,0,1:T(8,128)(2,1)S(1)}, bf16[16,32,128]{2,0,1:T(8,128)(2,1)S(1)}, u32[]{:S(2)}, u32[]{:S(2)}) %collective-permute-start.8) | collective-permute-done | bytes 131104 | tf_op jit(solution)/shard_map/ppermute | solution.py:22
  81.8 0.1 fusion.16
  81.9 0.8 copy.41
  (23 shorter events, 0.3 us)
Async XLA Ops:
  0.6 16.8 %collective-permute-start.1 = (bf16[16,32,128]{2,1,0:T(8,128)(2,1)}, bf16[16,32,128]{2,1,0:T(8,128)(2,1)S(1)}, u32[]{:S(2)}, u32[]{:S(2)}) collective-permute-start(bf16[16,32,128]{2,1,0:T(8,128)(2,1)} %param.9), channel_id=1, source_target_pairs={{24,0},{28,4},{0,8},{4,12},{8,16},{12,20},{16,24},{20,28},{25,1},{... | collective-permute-start | bytes 393224 | tf_op jit(solution)/shard_map/ppermute | solution.py:22
  3.7 13.7 %collective-permute-start.2 = (bf16[16,32,128]{2,1,0:T(8,128)(2,1)}, bf16[16,32,128]{2,1,0:T(8,128)(2,1)S(1)}, u32[]{:S(2)}, u32[]{:S(2)}) collective-permute-start(bf16[16,32,128]{2,1,0:T(8,128)(2,1)} %param.9), channel_id=1, source_target_pairs={{28,0},{0,4},{4,8},{8,12},{12,16},{16,20},{20,24},{24,28},{29,1},{... | collective-permute-start | bytes 393224 | tf_op jit(solution)/shard_map/ppermute | solution.py:22
  5.2 13.2 %collective-permute-start.3 = (bf16[16,32,128]{2,1,0:T(8,128)(2,1)}, bf16[16,32,128]{2,1,0:T(8,128)(2,1)S(1)}, u32[]{:S(2)}, u32[]{:S(2)}) collective-permute-start(bf16[16,32,128]{2,1,0:T(8,128)(2,1)} %param.9), channel_id=1, source_target_pairs={{4,0},{8,4},{12,8},{16,12},{20,16},{24,20},{28,24},{0,28},{5,1},{9... | collective-permute-start | bytes 393224 | tf_op jit(solution)/shard_map/ppermute | solution.py:22
  8.4 10.0 %collective-permute-start.4 = (bf16[16,32,128]{2,1,0:T(8,128)(2,1)}, bf16[16,32,128]{2,1,0:T(8,128)(2,1)S(1)}, u32[]{:S(2)}, u32[]{:S(2)}) collective-permute-start(bf16[16,32,128]{2,1,0:T(8,128)(2,1)} %param.9), channel_id=1, source_target_pairs={{8,0},{12,4},{16,8},{20,12},{24,16},{28,20},{0,24},{4,28},{9,1},{1... | collective-permute-start | bytes 393224 | tf_op jit(solution)/shard_map/ppermute | solution.py:22
  10.4 8.1 %collective-permute-start = (bf16[1,17,32,128]{3,2,1,0:T(8,128)(2,1)S(1)}, bf16[1,17,32,128]{3,2,1,0:T(8,128)(2,1)S(1)}, u32[]{:S(2)}, u32[]{:S(2)}) collective-permute-start(bf16[1,17,32,128]{3,2,1,0:T(8,128)(2,1)S(1)} %get-tuple-element.35), channel_id=1, source_target_pairs={{0,2},{1,3},{2,0},{3,1},{4,6},{5,7},{6,4},{7,5},{8,10},{9,11},{10,... | collective-permute-start | bytes 417800 | tf_op jit(solution)/shard_map/ppermute | solution.py:41
  29.1 9.8 %collective-permute-start.6 = (bf16[1,16,32,128]{3,1,2,0:T(8,128)(2,1)S(1)}, bf16[1,16,32,128]{3,1,2,0:T(8,128)(2,1)S(1)}, u32[]{:S(2)}, u32[]{:S(2)}) collective-permute-start(bf16[1,16,32,128]{3,1,2,0:T(8,128)(2,1)S(1)} %bitcast.53), channel_id=1, source_target_pairs={{0,2},{1,3},{2,0},{3,1},{4,6},{5,7},{6,4},{7,5},{8,10},{9,11},{10,... | collective-permute-start | bytes 393224 | tf_op jit(solution)/shard_map/ppermute | solution.py:41
  32.8 6.8 %collective-permute-start.5 = (bf16[2,17,32,128]{3,2,1,0:T(8,128)(2,1)S(1)}, bf16[2,17,32,128]{3,2,1,0:T(8,128)(2,1)S(1)}, u32[]{:S(2)}, u32[]{:S(2)}) collective-permute-start(bf16[2,17,32,128]{3,2,1,0:T(8,128)(2,1)S(1)} %pad_maximum_fusion.2), channel_id=1, source_target_pairs={{0,1},{1,0},{2,3},{3,2},{4,5},{5,4},{6,7},{7,6},{8,9},{9,8},{10,11... | collective-permute-start | bytes 835592 | tf_op jit(solution)/shard_map/ppermute | solution.py:41
  38.9 13.5 %collective-permute-start.7 = (bf16[2,16,32,128]{3,1,2,0:T(8,128)(2,1)S(1)}, bf16[2,16,32,128]{3,1,2,0:T(8,128)(2,1)S(1)}, u32[]{:S(2)}, u32[]{:S(2)}) collective-permute-start(bf16[2,16,32,128]{3,1,2,0:T(8,128)(2,1)S(1)} %pad_maximum_fusion.3), channel_id=1, source_target_pairs={{0,1},{1,0},{2,3},{3,2},{4,5},{5,4},{6,7},{7,6},{8,9},{9,8},{10,11... | collective-permute-start | bytes 786440 | tf_op jit(solution)/shard_map/ppermute | solution.py:41
  39.9 13.3 %copy-start = (f32[32,128]{1,0:T(8,128)S(1)}, f32[32,128]{1,0:T(8,128)}, u32[]{:S(2)}) copy-start(f32[32,128]{1,0:T(8,128)} %param.14) | copy-start | bytes 49156
  60.6 3.8 %collective-permute-start.12 = (f32[32,128]{1,0:T(8,128)S(1)}, f32[32,128]{1,0:T(8,128)S(1)}, u32[]{:S(2)}, u32[]{:S(2)}) collective-permute-start(f32[32,128]{1,0:T(8,128)S(1)} %convolution_bitcast_fusion.1), channel_id=1, source_target_pairs={{0,4},{4,0},{8,12},{12,8},{16,20},{20,16},{24,28},{28,24},{1,5},{5... | collective-permute-start | bytes 49160 | tf_op jit(solution)/shard_map/ppermute | solution.py:62
  61.7 15.6 %copy-start.1 = (f32[32,128]{1,0:T(8,128)S(1)}, f32[32,128]{1,0:T(8,128)}, u32[]{:S(2)}) copy-start(f32[32,128]{1,0:T(8,128)} %param.15) | copy-start | bytes 49156
  61.7 15.6 %copy-start.2 = (f32[32,128]{1,0:T(8,128)S(1)}, f32[32,128]{1,0:T(8,128)}, u32[]{:S(2)}) copy-start(f32[32,128]{1,0:T(8,128)} %param.16) | copy-start | bytes 49156
  64.4 3.7 %collective-permute-start.13 = (f32[32,128]{1,0:T(8,128)S(1)}, f32[32,128]{1,0:T(8,128)S(1)}, u32[]{:S(2)}, u32[]{:S(2)}) collective-permute-start(f32[32,128]{1,0:T(8,128)S(1)} %add.84), channel_id=1, source_target_pairs={{0,8},{4,12},{8,0},{12,4},{16,24},{20,28},{24,16},{28,20},{1,9},{5... | collective-permute-start | bytes 49160 | tf_op jit(solution)/shard_map/ppermute | solution.py:62
  68.1 9.2 %collective-permute-start.14 = (f32[32,128]{1,0:T(8,128)S(1)}, f32[32,128]{1,0:T(8,128)S(1)}, u32[]{:S(2)}, u32[]{:S(2)}) collective-permute-start(f32[32,128]{1,0:T(8,128)S(1)} %add.85), channel_id=1, source_target_pairs={{0,16},{4,20},{8,24},{12,28},{16,0},{20,4},{24,8},{28,12},{1,17},{... | collective-permute-start | bytes 49160 | tf_op jit(solution)/shard_map/ppermute | solution.py:62
  70.5 7.4 %collective-permute-start.11 = (bf16[16,32,128]{2,0,1:T(8,128)(2,1)}, bf16[16,32,128]{2,0,1:T(8,128)(2,1)S(1)}, u32[]{:S(2)}, u32[]{:S(2)}) collective-permute-start(bf16[16,32,128]{2,0,1:T(8,128)(2,1)} %get-tuple-element.27), channel_id=1, source_target_pairs={{24,0},{28,4},{0,8},{4,12},{8,16},{12,20},{16,24},{20,28},{25,1},{... | collective-permute-start | bytes 393224 | tf_op jit(solution)/shard_map/ppermute | solution.py:22
  72.1 8.0 %collective-permute-start.10 = (bf16[16,32,128]{2,0,1:T(8,128)(2,1)}, bf16[16,32,128]{2,0,1:T(8,128)(2,1)S(1)}, u32[]{:S(2)}, u32[]{:S(2)}) collective-permute-start(bf16[16,32,128]{2,0,1:T(8,128)(2,1)} %get-tuple-element.28), channel_id=1, source_target_pairs={{28,0},{0,4},{4,8},{8,12},{12,16},{16,20},{20,24},{24,28},{29,1},{... | collective-permute-start | bytes 393224 | tf_op jit(solution)/shard_map/ppermute | solution.py:22
  72.7 7.4 %collective-permute-start.9 = (bf16[16,32,128]{2,0,1:T(8,128)(2,1)S(1)}, bf16[16,32,128]{2,0,1:T(8,128)(2,1)S(1)}, u32[]{:S(2)}, u32[]{:S(2)}) collective-permute-start(bf16[16,32,128]{2,0,1:T(8,128)(2,1)S(1)} %get-tuple-element.29), channel_id=1, source_target_pairs={{4,0},{8,4},{12,8},{16,12},{20,16},{24,20},{28,24},{0,28},{5,1},{9... | collective-permute-start | bytes 393224 | tf_op jit(solution)/shard_map/ppermute | solution.py:22
  76.8 5.0 %collective-permute-start.8 = (bf16[16,32,128]{2,0,1:T(8,128)(2,1)S(1)}, bf16[16,32,128]{2,0,1:T(8,128)(2,1)S(1)}, u32[]{:S(2)}, u32[]{:S(2)}) collective-permute-start(bf16[16,32,128]{2,0,1:T(8,128)(2,1)S(1)} %get-tuple-element.26), channel_id=1, source_target_pairs={{8,0},{12,4},{16,8},{20,12},{24,16},{28,20},{0,24},{4,28},{9,1},{1... | collective-permute-start | bytes 393224 | tf_op jit(solution)/shard_map/ppermute | solution.py:22

commit v17 on v8

--- a/solution.py
+++ b/solution.py
@@ -22,11 +22,16 @@
     return lax.ppermute(block, axis, route)
 
 
-def gathered_along(block, axis, dim):
+def gathered_along(block, axis, dim, direct=False):
     size = lax.axis_size(axis)
     own = lax.axis_index(axis)
     width = block.shape[dim]
-    if size & (size - 1):
+    if direct and not size & (size - 1):
+        pieces = [(block, own)]
+        for mask in range(1, size):
+            route = [(i, i ^ mask) for i in range(size)]
+            pieces.append((lax.ppermute(block, axis, route), own ^ mask))
+    elif size & (size - 1):
         pieces = [(block, own)]
         for step in range(1, size):
             pieces.append((passed_along(block, axis, -step), (own + step) % size))
@@ -112,7 +117,7 @@
     nearby = jnp.concatenate(pieces, axis=0)
     weight_half = weight.astype(jnp.bfloat16)
     packed = jnp.concatenate([cotangent, weight_half[None]], axis=0)
-    packed_all = gathered_along(packed, "feat", 1)
+    packed_all = gathered_along(packed, "feat", 1, direct=True)
     cotangent_all = packed_all[:blocks]
     weight_all = packed_all[blocks]
     nearby, cotangent_all, weight_all = lax.optimization_barrier((nearby, cotangent_all, weight_all))

time: 67.8 us -> 70.8 us (1.044)
  waiting for transfers between devices: 15.1 us -> 16.8 us
  starting transfers between devices: 23.3 us -> 24.7 us
    ppermute x0 -> x3, waiting for transfers between devices: none -> 3.57 us  [gathered_along(): pieces.append((lax.ppermute(block, axis, route), own ^ mask))]
    ppermute x0 -> x3, starting transfers between devices: none -> 2.37 us  [gathered_along(): pieces.append((lax.ppermute(block, axis, route), own ^ mask))]
    ppermute x4 -> x2, waiting for transfers between devices: 7.11 us -> 5.27 us  [gathered_along(): got = lax.ppermute(held, axis, [(i, i ^ mask) for i in range(size)])]
    ppermute x4 -> x2, starting transfers between devices: 3.26 us -> 1.95 us  [gathered_along(): got = lax.ppermute(held, axis, [(i, i ^ mask) for i in range(size)])]
    another operation x3 -> x1, other arithmetic: 1.01 us -> 0.03 us  [gathered_along(): held = jnp.stack([piece for piece, _ in pieces])]
    concatenate x0 -> x1, other arithmetic: none -> 0.96 us  [per_device(): packed = jnp.concatenate([cotangent, weight_half[None]], axis=0)]
  transfers between devices with their start and end apart: 15 -> 16, of which waited for: 8 -> 6; matrix products, arithmetic and copies ran while one was open for 22% -> 21% of each run, Pallas kernels for 0% -> 0%
where the time goes in v17:
time: 70.8 us; the launch traced here: 70.5 us
  starting transfers between devices  24.7 us (35%)
  matrix products  19.4 us (27%)
  waiting for transfers between devices  16.8 us (24%)
  other arithmetic  5.37 us (8%)
  local copies, waits for them, and re-layouts  2.61 us (4%)
  between operations  1.61 us (2%)
    ppermute x8, starting transfers between devices, passed_along(): return lax.ppermute(block, axis, route)  16.9 us
    dot_general x1, matrix products, per_device(): jnp.einsum('tfk,tjk->tfj', sources, tile_values, preferred_element_type=j...  7.92 us
    dot_general x1, matrix products, per_device(): jnp.einsum('tfj,tjk->tfk', back_sources, tile_values, preferred_element_t...  5.99 us
    ppermute x2, waiting for transfers between devices, gathered_along(): got = lax.ppermute(held, axis, [(i, i ^ mask) for i in range(size)])  5.27 us
    ppermute x8, waiting for transfers between devices, passed_along(): return lax.ppermute(block, axis, route)  4.24 us
    ppermute x3, waiting for transfers between devices, summed_over(): lax.ppermute(block, axis, [(i, i ^ mask) for i in range(size)])  3.69 us
    ppermute x3, waiting for transfers between devices, gathered_along(): pieces.append((lax.ppermute(block, axis, route), own ^ mask))  3.57 us
    ppermute x3, starting transfers between devices, summed_over(): lax.ppermute(block, axis, [(i, i ^ mask) for i in range(size)])  3.45 us
  transfers between devices with their start and end apart: 16, of which 6 were waited for; matrix products, arithmetic and copies ran while one was open for 21% of the time, Pallas kernels for 0%

profile of v17, /device:TPU:0, one launch (start us, length us, event | category | flops | bytes accessed | tf_op | source)
XLA Modules:
  0.0 70.5 jit_solution(10729515160236702029)
XLA Ops:
  0.6 6.0 %collective-permute-start.2 = (bf16[16,32,128]{2,1,0:T(8,128)(2,1)}, bf16[16,32,128]{2,1,0:T(8,128)(2,1)S(1)}, u32[]{:S(2)}, u32[]{:S(2)}) collective-permute-start(bf16[16,32,128]{2,1,0:T(8,128)(2,1)} %param.9), channel_id=1, source_target_pairs={{4,0},{8,4},{12,8},{16,12},{20,16},{24,20},{28,24},{0,28},{5,1},{9... | collective-permute-start | bytes 393224 | tf_op jit(solution)/shard_map/ppermute | solution.py:22
  6.7 0.0 collective-permute-start.1
  6.7 0.0 collective-permute-start
  6.7 3.8 %collective-permute-start.3 = (bf16[16,32,128]{2,1,0:T(8,128)(2,1)}, bf16[16,32,128]{2,1,0:T(8,128)(2,1)S(1)}, u32[]{:S(2)}, u32[]{:S(2)}) collective-permute-start(bf16[16,32,128]{2,1,0:T(8,128)(2,1)} %param.9), channel_id=1, source_target_pairs={{8,0},{12,4},{16,8},{20,12},{24,16},{28,20},{0,24},{4,28},{9,1},{1... | collective-permute-start | bytes 393224 | tf_op jit(solution)/shard_map/ppermute | solution.py:22
  10.5 0.7 %convert_bitcast_fusion = bf16[1,32,128]{2,1,0:T(8,128)(2,1)S(1)} fusion(f32[32,128]{1,0:T(8,128)} %param.14), kind=kLoop, calls=%fused_computation.66 | loop fusion | flops 4096 | bytes 24576 | tf_op jit(solution)/shard_map/broadcast_in_dim | solution.py:119
  11.2 0.1 broadcast_in_dim.11
  11.3 1.0 %pad_maximum_fusion.3 = (bf16[17,32,128]{2,1,0:T(8,128)(2,1)S(1)}, bf16[17,128,128]{2,1,0:T(8,128)(2,1)S(1)}) fusion(bf16[1,32,128]{2,1,0:T(8,128)(2,1)S(1)} %convert_bitcast_fusion, bf16[16,32,128]{2,1,0:T(8,128)(2,1)} %param.17, bf16[17,128,128]{2,1,0:T(8,128)(2,1)S(1)} %broadcast_in_dim.11, s32[]{:T(128)S(6)} %select_n.51), kind=kLoop, calls=%fused_computation.31 | loop fusion | flops 278528 | bytes 417796 | tf_op jit(solution)/shard_map/concatenate | solution.py:119
  12.3 1.6 %collective-permute-start.5 = (bf16[17,32,128]{2,1,0:T(8,128)(2,1)S(1)}, bf16[17,32,128]{2,1,0:T(8,128)(2,1)S(1)}, u32[]{:S(2)}, u32[]{:S(2)}) collective-permute-start(bf16[17,32,128]{2,1,0:T(8,128)(2,1)S(1)} %get-tuple-element.29), channel_id=1, source_target_pairs={{0,2},{1,3},{2,0},{3,1},{4,6},{5,7},{6,4},{7,5},{8,10},{9,11},{10,... | collective-permute-start | bytes 417800 | tf_op jit(solution)/shard_map/ppermute | solution.py:33
  14.5 0.7 broadcast_subtract_fusion
  15.2 0.7 fusion.32
  16.0 0.0 collective-permute-done
  16.0 0.1 collective-permute-start.4
  16.1 0.0 collective-permute-done.1
  16.1 0.7 %collective-permute-start.6 = (bf16[17,32,128]{2,1,0:T(8,128)(2,1)S(1)}, bf16[17,32,128]{2,1,0:T(8,128)(2,1)S(1)}, u32[]{:S(2)}, u32[]{:S(2)}) collective-permute-start(bf16[17,32,128]{2,1,0:T(8,128)(2,1)S(1)} %get-tuple-element.29), channel_id=1, source_target_pairs={{0,3},{1,2},{2,1},{3,0},{4,7},{5,6},{6,5},{7,4},{8,11},{9,10},{10,... | collective-permute-start | bytes 417800 | tf_op jit(solution)/shard_map/ppermute | solution.py:33
  16.8 0.9 %constant_dynamic-update-slice_fusion.2 = bf16[80,32,128]{2,1,0:T(8,128)(2,1)S(1)} fusion(bf16[80,32,128]{2,1,0:T(8,128)(2,1)S(1)} %constant_dynamic-update-slice_fusion.3, bf16[16,32,128]{2,1,0:T(8,128)(2,1)} %param.9), kind=kLoop, calls=%fused_computation.60 | loop fusion | bytes 262144
  17.8 0.0 collective-permute-done.2
  17.8 0.0 collective-permute-done.3
  17.8 0.0 collective-permute-done.4
  17.9 0.0 collective-permute-done.5
  17.9 3.6 %collective-permute-done.6 = bf16[17,32,128]{2,1,0:T(8,128)(2,1)S(1)} collective-permute-done((bf16[17,32,128]{2,1,0:T(8,128)(2,1)S(1)}, bf16[17,32,128]{2,1,0:T(8,128)(2,1)S(1)}, u32[]{:S(2)}, u32[]{:S(2)}) %collective-permute-start.6) | collective-permute-done | bytes 139296 | tf_op jit(solution)/shard_map/ppermute | solution.py:33
  21.6 0.8 %fusion.12 = bf16[256,32,128]{2,0,1:T(8,128)(2,1)S(1)} fusion(bf16[80,32,128]{2,1,0:T(8,128)(2,1)S(1)} %constant_dynamic-update-slice_fusion, s32[256]{0:T(256)S(1)} %fusion.32), kind=kOutput, calls=%fused_computation.22 | convolution fusion | flops 167792640 | bytes 2753536 | tf_op jit(solution)/shard_map/ts,sfk->tfk/dot_general | solution.py:124
  22.3 7.9 %reduce-precision_convert_fusion.1 = (bf16[256,32,128]{2,1,0:T(8,128)(2,1)S(1)}, bf16[256,32,128]{2,1,0:T(8,128)(2,1)S(1)}) fusion(bf16[256,128,128]{2,1,0:T(8,128)(2,1)} %param.10, bf16[256,32,128]{2,0,1:T(8,128)(2,1)S(1)} %fusion.12), kind=kOutput, calls=%fused_computation.3 | convolution fusion | flops 272629760 | bytes 14680064 | tf_op jit(solution)/shard_map/tfk,tjk->tfj/dot_general | solution.py:127
  30.3 0.4 pad_maximum_fusion
  30.6 1.2 %fusion.9 = bf16[16,32,128]{2,0,1:T(8,128)(2,1)S(1)} fusion(bf16[512,32,128]{2,1,0:T(8,128)(2,1)S(1)} %pad_maximum_fusion, bf16[256,16]{0,1:T(8,128)(2,1)S(1)} %select_convert_fusion.2), kind=kOutput, calls=%fused_computation.19 | convolution fusion | flops 67207168 | bytes 4333568 | tf_op jit(solution)/shard_map/tb,tfj->bfj/dot_general | solution.py:71
  31.9 1.9 %collective-permute-start.7 = (bf16[1,16,32,128]{3,1,2,0:T(8,128)(2,1)S(1)}, bf16[1,16,32,128]{3,1,2,0:T(8,128)(2,1)S(1)}, u32[]{:S(2)}, u32[]{:S(2)}) collective-permute-start(bf16[1,16,32,128]{3,1,2,0:T(8,128)(2,1)S(1)} %bitcast.44), channel_id=1, source_target_pairs={{0,2},{1,3},{2,0},{3,1},{4,6},{5,7},{6,4},{7,5},{8,10},{9,11},{10,... | collective-permute-start | bytes 393224 | tf_op jit(solution)/shard_map/ppermute | solution.py:43
  33.8 4.0 %collective-permute-done.7 = bf16[1,16,32,128]{3,1,2,0:T(8,128)(2,1)S(1)} collective-permute-done((bf16[1,16,32,128]{3,1,2,0:T(8,128)(2,1)S(1)}, bf16[1,16,32,128]{3,1,2,0:T(8,128)(2,1)S(1)}, u32[]{:S(2)}, u32[]{:S(2)}) %collective-permute-start.7) | collective-permute-done | bytes 131104 | tf_op jit(solution)/shard_map/ppermute | solution.py:43
  37.8 0.1 collective-permute-start.8
  37.8 0.1 broadcast_in_dim.13
  38.0 0.1 copy_dynamic-update-slice_fusion.3
  38.0 0.1 copy_dynamic-update-slice_fusion.2
  38.1 1.3 %collective-permute-done.8 = bf16[2,16,32,128]{3,1,2,0:T(8,128)(2,1)S(1)} collective-permute-done((bf16[2,16,32,128]{3,1,2,0:T(8,128)(2,1)S(1)}, bf16[2,16,32,128]{3,1,2,0:T(8,128)(2,1)S(1)}, u32[]{:S(2)}, u32[]{:S(2)}) %collective-permute-start.8) | collective-permute-done | bytes 262176 | tf_op jit(solution)/shard_map/ppermute | solution.py:43
  39.4 0.1 copy_dynamic-update-slice_fusion.1
  39.4 0.1 copy_dynamic-update-slice_fusion
  39.5 0.3 broadcast_compare_fusion
  39.8 0.4 convolution_bitcast_fusion.1
  40.2 0.0 copy-done
  40.3 0.5 fusion.8
  40.8 0.2 copy.26
  41.0 3.4 %collective-permute-start.13 = (f32[32,128]{1,0:T(8,128)S(1)}, f32[32,128]{1,0:T(8,128)S(1)}, u32[]{:S(2)}, u32[]{:S(2)}) collective-permute-start(f32[32,128]{1,0:T(8,128)S(1)} %convolution_bitcast_fusion.1), channel_id=1, source_target_pairs={{0,4},{4,0},{8,12},{12,8},{16,20},{20,16},{24,28},{28,24},{1,5},{5... | collective-permute-start | bytes 49160 | tf_op jit(solution)/shard_map/ppermute | solution.py:60
  44.4 0.7 %fusion.27 = bf16[256,32,128]{2,0,1:T(8,128)(2,1)S(1)} fusion(bf16[16,32,128]{2,0,1:T(8,128)(2,1)S(1)} %copy.26, s32[256]{0:T(256)S(1)} %broadcast_subtract_fusion), kind=kOutput, calls=%fused_computation.57 | convolution fusion | flops 33558528 | bytes 2229248 | tf_op jit(solution)/shard_map/tb,bfj->tfj/dot_general | solution.py:146
  45.1 6.0 %reduce-precision_convert_fusion = (bf16[256,32,128]{2,1,0:T(8,128)(2,1)S(1)}, bf16[256,32,128]{2,1,0:T(8,128)(2,1)S(1)}) fusion(bf16[256,128,128]{2,1,0:T(8,128)(2,1)} %param.10, bf16[256,32,128]{2,0,1:T(8,128)(2,1)S(1)} %fusion.27), kind=kOutput, calls=%fused_computation.1 | convolution fusion | flops 272629760 | bytes 14680064 | tf_op jit(solution)/shard_map/tfj,tjk->tfk/dot_general | solution.py:149
  51.1 0.4 pad_maximum_fusion.1
  51.5 0.0 copy-start.1
  51.5 0.0 copy-start.2
  51.5 1.5 %fusion.39 = (bf16[80,32,128]{2,0,1:T(8,128)(2,1)S(1)}, f32[80,32,128]{2,0,1:T(8,128)S(1)}) fusion(bf16[512,32,128]{2,1,0:T(8,128)(2,1)S(1)} %pad_maximum_fusion.1, bf16[256,80]{0,1:T(8,128)(2,1)S(1)} %select_convert_fusion.1), kind=kOutput, calls=%fused_computation.89 | convolution fusion | flops 336035840 | bytes 6201344 | tf_op jit(solution)/shard_map/ts,tfk->sfk/dot_general | solution.py:71
  53.0 0.0 collective-permute-done.13
  53.1 0.1 collective-permute-start.14
  53.2 3.7 %collective-permute-done.14 = f32[32,128]{1,0:T(8,128)S(1)} collective-permute-done((f32[32,128]{1,0:T(8,128)S(1)}, f32[32,128]{1,0:T(8,128)S(1)}, u32[]{:S(2)}, u32[]{:S(2)}) %collective-permute-start.14) | collective-permute-done | bytes 16416 | tf_op jit(solution)/shard_map/ppermute | solution.py:60
  56.9 0.0 collective-permute-start.15
  56.9 0.8 %select_convert_fusion = bf16[16,32,128]{2,1,0:T(8,128)(2,1)} fusion(f32[16,128,128]{2,1,0:T(8,128)S(1)} %get-tuple-element.32, s32[]{:T(128)S(6)} %select_n.51, pred[16,128,128]{2,1,0:T(8,128)(4,1)S(1)} %get-tuple-element.31), kind=kLoop, calls=%fused_computation.30 | loop fusion | flops 196608 | bytes 458756 | tf_op jit(solution)/shard_map/convert_element_type | solution.py:138
  57.7 2.4 %collective-permute-start.9 = (bf16[16,32,128]{2,0,1:T(8,128)(2,1)S(1)}, bf16[16,32,128]{2,0,1:T(8,128)(2,1)S(1)}, u32[]{:S(2)}, u32[]{:S(2)}) collective-permute-start(bf16[16,32,128]{2,0,1:T(8,128)(2,1)S(1)} %get-tuple-element.23), channel_id=1, source_target_pairs={{8,0},{12,4},{16,8},{20,12},{24,16},{28,20},{0,24},{4,28},{9,1},{1... | collective-permute-start | bytes 393224 | tf_op jit(solution)/shard_map/ppermute | solution.py:22
  60.0 0.0 collective-permute-start.12
  60.0 0.0 collective-permute-start.11
  60.0 4.7 %collective-permute-start.10 = (bf16[16,32,128]{2,0,1:T(8,128)(2,1)S(1)}, bf16[16,32,128]{2,0,1:T(8,128)(2,1)S(1)}, u32[]{:S(2)}, u32[]{:S(2)}) collective-permute-start(bf16[16,32,128]{2,0,1:T(8,128)(2,1)S(1)} %get-tuple-element.26), channel_id=1, source_target_pairs={{4,0},{8,4},{12,8},{16,12},{20,16},{24,20},{28,24},{0,28},{5,1},{9... | collective-permute-start | bytes 393224 | tf_op jit(solution)/shard_map/ppermute | solution.py:22
  64.7 0.0 collective-permute-done.15
  64.7 0.0 copy-done.1
  64.7 0.0 copy-done.2
  64.7 0.6 divide_subtract_fusion
  65.4 0.0 collective-permute-done.9
  65.4 3.2 %collective-permute-done.12 = bf16[16,32,128]{2,0,1:T(8,128)(2,1)S(1)} collective-permute-done((bf16[16,32,128]{2,0,1:T(8,128)(2,1)S(1)}, bf16[16,32,128]{2,0,1:T(8,128)(2,1)S(1)}, u32[]{:S(2)}, u32[]{:S(2)}) %collective-permute-start.12) | collective-permute-done | bytes 131104 | tf_op jit(solution)/shard_map/ppermute | solution.py:22
  68.5 1.0 %collective-permute-done.11 = bf16[16,32,128]{2,0,1:T(8,128)(2,1)S(1)} collective-permute-done((bf16[16,32,128]{2,0,1:T(8,128)(2,1)S(1)}, bf16[16,32,128]{2,0,1:T(8,128)(2,1)S(1)}, u32[]{:S(2)}, u32[]{:S(2)}) %collective-permute-start.11) | collective-permute-done | bytes 131104 | tf_op jit(solution)/shard_map/ppermute | solution.py:22
  69.6 0.0 collective-permute-done.10
  69.6 0.1 fusion.16
  69.7 0.8 %copy.22 = f32[16,32,128]{2,1,0:T(8,128)} copy(f32[16,32,128]{2,0,1:T(8,128)S(1)} %fusion.16) | data formatting | bytes 524288
  (18 shorter events, 0.3 us)
Async XLA Ops:
  0.6 17.1 %collective-permute-start.2 = (bf16[16,32,128]{2,1,0:T(8,128)(2,1)}, bf16[16,32,128]{2,1,0:T(8,128)(2,1)S(1)}, u32[]{:S(2)}, u32[]{:S(2)}) collective-permute-start(bf16[16,32,128]{2,1,0:T(8,128)(2,1)} %param.9), channel_id=1, source_target_pairs={{4,0},{8,4},{12,8},{16,12},{20,16},{24,20},{28,24},{0,28},{5,1},{9... | collective-permute-start | bytes 393224 | tf_op jit(solution)/shard_map/ppermute | solution.py:22
  6.7 9.4 %collective-permute-start.1 = (bf16[16,32,128]{2,1,0:T(8,128)(2,1)}, bf16[16,32,128]{2,1,0:T(8,128)(2,1)S(1)}, u32[]{:S(2)}, u32[]{:S(2)}) collective-permute-start(bf16[16,32,128]{2,1,0:T(8,128)(2,1)} %param.9), channel_id=1, source_target_pairs={{28,0},{0,4},{4,8},{8,12},{12,16},{16,20},{20,24},{24,28},{29,1},{... | collective-permute-start | bytes 393224 | tf_op jit(solution)/shard_map/ppermute | solution.py:22
  6.7 9.3 %collective-permute-start = (bf16[16,32,128]{2,1,0:T(8,128)(2,1)}, bf16[16,32,128]{2,1,0:T(8,128)(2,1)S(1)}, u32[]{:S(2)}, u32[]{:S(2)}) collective-permute-start(bf16[16,32,128]{2,1,0:T(8,128)(2,1)} %param.9), channel_id=1, source_target_pairs={{24,0},{28,4},{0,8},{4,12},{8,16},{12,20},{16,24},{20,28},{25,1},{... | collective-permute-start | bytes 393224 | tf_op jit(solution)/shard_map/ppermute | solution.py:22
  6.7 11.1 %collective-permute-start.3 = (bf16[16,32,128]{2,1,0:T(8,128)(2,1)}, bf16[16,32,128]{2,1,0:T(8,128)(2,1)S(1)}, u32[]{:S(2)}, u32[]{:S(2)}) collective-permute-start(bf16[16,32,128]{2,1,0:T(8,128)(2,1)} %param.9), channel_id=1, source_target_pairs={{8,0},{12,4},{16,8},{20,12},{24,16},{28,20},{0,24},{4,28},{9,1},{1... | collective-permute-start | bytes 393224 | tf_op jit(solution)/shard_map/ppermute | solution.py:22
  12.3 5.6 %collective-permute-start.5 = (bf16[17,32,128]{2,1,0:T(8,128)(2,1)S(1)}, bf16[17,32,128]{2,1,0:T(8,128)(2,1)S(1)}, u32[]{:S(2)}, u32[]{:S(2)}) collective-permute-start(bf16[17,32,128]{2,1,0:T(8,128)(2,1)S(1)} %get-tuple-element.29), channel_id=1, source_target_pairs={{0,2},{1,3},{2,0},{3,1},{4,6},{5,7},{6,4},{7,5},{8,10},{9,11},{10,... | collective-permute-start | bytes 417800 | tf_op jit(solution)/shard_map/ppermute | solution.py:33
  16.0 1.9 %collective-permute-start.4 = (bf16[17,32,128]{2,1,0:T(8,128)(2,1)S(1)}, bf16[17,32,128]{2,1,0:T(8,128)(2,1)S(1)}, u32[]{:S(2)}, u32[]{:S(2)}) collective-permute-start(bf16[17,32,128]{2,1,0:T(8,128)(2,1)S(1)} %get-tuple-element.29), channel_id=1, source_target_pairs={{0,1},{1,0},{2,3},{3,2},{4,5},{5,4},{6,7},{7,6},{8,9},{9,8},{10,11... | collective-permute-start | bytes 417800 | tf_op jit(solution)/shard_map/ppermute | solution.py:33
  16.1 5.4 %collective-permute-start.6 = (bf16[17,32,128]{2,1,0:T(8,128)(2,1)S(1)}, bf16[17,32,128]{2,1,0:T(8,128)(2,1)S(1)}, u32[]{:S(2)}, u32[]{:S(2)}) collective-permute-start(bf16[17,32,128]{2,1,0:T(8,128)(2,1)S(1)} %get-tuple-element.29), channel_id=1, source_target_pairs={{0,3},{1,2},{2,1},{3,0},{4,7},{5,6},{6,5},{7,4},{8,11},{9,10},{10,... | collective-permute-start | bytes 417800 | tf_op jit(solution)/shard_map/ppermute | solution.py:33
  31.9 8.4 %copy-start = (f32[32,128]{1,0:T(8,128)S(1)}, f32[32,128]{1,0:T(8,128)}, u32[]{:S(2)}) copy-start(f32[32,128]{1,0:T(8,128)} %param.14) | copy-start | bytes 49156
  31.9 5.9 %collective-permute-start.7 = (bf16[1,16,32,128]{3,1,2,0:T(8,128)(2,1)S(1)}, bf16[1,16,32,128]{3,1,2,0:T(8,128)(2,1)S(1)}, u32[]{:S(2)}, u32[]{:S(2)}) collective-permute-start(bf16[1,16,32,128]{3,1,2,0:T(8,128)(2,1)S(1)} %bitcast.44), channel_id=1, source_target_pairs={{0,2},{1,3},{2,0},{3,1},{4,6},{5,7},{6,4},{7,5},{8,10},{9,11},{10,... | collective-permute-start | bytes 393224 | tf_op jit(solution)/shard_map/ppermute | solution.py:43
  37.8 1.6 %collective-permute-start.8 = (bf16[2,16,32,128]{3,1,2,0:T(8,128)(2,1)S(1)}, bf16[2,16,32,128]{3,1,2,0:T(8,128)(2,1)S(1)}, u32[]{:S(2)}, u32[]{:S(2)}) collective-permute-start(bf16[2,16,32,128]{3,1,2,0:T(8,128)(2,1)S(1)} %pad_maximum_fusion.2), channel_id=1, source_target_pairs={{0,1},{1,0},{2,3},{3,2},{4,5},{5,4},{6,7},{7,6},{8,9},{9,8},{10,11... | collective-permute-start | bytes 786440 | tf_op jit(solution)/shard_map/ppermute | solution.py:43
  41.0 12.0 %collective-permute-start.13 = (f32[32,128]{1,0:T(8,128)S(1)}, f32[32,128]{1,0:T(8,128)S(1)}, u32[]{:S(2)}, u32[]{:S(2)}) collective-permute-start(f32[32,128]{1,0:T(8,128)S(1)} %convolution_bitcast_fusion.1), channel_id=1, source_target_pairs={{0,4},{4,0},{8,12},{12,8},{16,20},{20,16},{24,28},{28,24},{1,5},{5... | collective-permute-start | bytes 49160 | tf_op jit(solution)/shard_map/ppermute | solution.py:60
  51.5 13.2 %copy-start.1 = (f32[32,128]{1,0:T(8,128)S(1)}, f32[32,128]{1,0:T(8,128)}, u32[]{:S(2)}) copy-start(f32[32,128]{1,0:T(8,128)} %param.15) | copy-start | bytes 49156
  51.5 13.2 %copy-start.2 = (f32[32,128]{1,0:T(8,128)S(1)}, f32[32,128]{1,0:T(8,128)}, u32[]{:S(2)}) copy-start(f32[32,128]{1,0:T(8,128)} %param.16) | copy-start | bytes 49156
  53.1 3.8 %collective-permute-start.14 = (f32[32,128]{1,0:T(8,128)S(1)}, f32[32,128]{1,0:T(8,128)S(1)}, u32[]{:S(2)}, u32[]{:S(2)}) collective-permute-start(f32[32,128]{1,0:T(8,128)S(1)} %add.87), channel_id=1, source_target_pairs={{0,8},{4,12},{8,0},{12,4},{16,24},{20,28},{24,16},{28,20},{1,9},{5... | collective-permute-start | bytes 49160 | tf_op jit(solution)/shard_map/ppermute | solution.py:60
  56.9 7.9 %collective-permute-start.15 = (f32[32,128]{1,0:T(8,128)S(1)}, f32[32,128]{1,0:T(8,128)S(1)}, u32[]{:S(2)}, u32[]{:S(2)}) collective-permute-start(f32[32,128]{1,0:T(8,128)S(1)} %add.88), channel_id=1, source_target_pairs={{0,16},{4,20},{8,24},{12,28},{16,0},{20,4},{24,8},{28,12},{1,17},{... | collective-permute-start | bytes 49160 | tf_op jit(solution)/shard_map/ppermute | solution.py:60
  57.7 7.7 %collective-permute-start.9 = (bf16[16,32,128]{2,0,1:T(8,128)(2,1)S(1)}, bf16[16,32,128]{2,0,1:T(8,128)(2,1)S(1)}, u32[]{:S(2)}, u32[]{:S(2)}) collective-permute-start(bf16[16,32,128]{2,0,1:T(8,128)(2,1)S(1)} %get-tuple-element.23), channel_id=1, source_target_pairs={{8,0},{12,4},{16,8},{20,12},{24,16},{28,20},{0,24},{4,28},{9,1},{1... | collective-permute-start | bytes 393224 | tf_op jit(solution)/shard_map/ppermute | solution.py:22
  60.0 8.5 %collective-permute-start.12 = (bf16[16,32,128]{2,0,1:T(8,128)(2,1)S(1)}, bf16[16,32,128]{2,0,1:T(8,128)(2,1)S(1)}, u32[]{:S(2)}, u32[]{:S(2)}) collective-permute-start(bf16[16,32,128]{2,0,1:T(8,128)(2,1)S(1)} %get-tuple-element.24), channel_id=1, source_target_pairs={{24,0},{28,4},{0,8},{4,12},{8,16},{12,20},{16,24},{20,28},{25,1},{... | collective-permute-start | bytes 393224 | tf_op jit(solution)/shard_map/ppermute | solution.py:22
  60.0 9.6 %collective-permute-start.11 = (bf16[16,32,128]{2,0,1:T(8,128)(2,1)S(1)}, bf16[16,32,128]{2,0,1:T(8,128)(2,1)S(1)}, u32[]{:S(2)}, u32[]{:S(2)}) collective-permute-start(bf16[16,32,128]{2,0,1:T(8,128)(2,1)S(1)} %get-tuple-element.25), channel_id=1, source_target_pairs={{28,0},{0,4},{4,8},{8,12},{12,16},{16,20},{20,24},{24,28},{29,1},{... | collective-permute-start | bytes 393224 | tf_op jit(solution)/shard_map/ppermute | solution.py:22
  60.0 9.6 %collective-permute-start.10 = (bf16[16,32,128]{2,0,1:T(8,128)(2,1)S(1)}, bf16[16,32,128]{2,0,1:T(8,128)(2,1)S(1)}, u32[]{:S(2)}, u32[]{:S(2)}) collective-permute-start(bf16[16,32,128]{2,0,1:T(8,128)(2,1)S(1)} %get-tuple-element.26), channel_id=1, source_target_pairs={{4,0},{8,4},{12,8},{16,12},{20,16},{24,20},{28,24},{0,28},{5,1},{9... | collective-permute-start | bytes 393224 | tf_op jit(solution)/shard_map/ppermute | solution.py:22

commit v18 on v8

--- a/solution.py
+++ b/solution.py
@@ -46,15 +46,17 @@
     return whole
 
 
-def summed_over(block, axis):
+def summed_over(block, axis, beside=None):
     size = lax.axis_size(axis)
     if size & (size - 1):
-        return lax.psum(block, axis)
+        return lax.psum(block, axis), beside
     mask = 1
     while mask < size:
         block = block + lax.ppermute(block, axis, [(i, i ^ mask) for i in range(size)])
+        if mask == 1 and beside is not None:
+            block, beside = lax.optimization_barrier((block, beside))
         mask *= 2
-    return block
+    return block, beside
 
 
 def summed_by_table(table, terms, spec):
@@ -134,7 +136,8 @@
     slope_all = (cotangent_all.astype(jnp.float32) * elu_slope(preact)).astype(jnp.bfloat16)
     node_total = cycle_size * blocks * tile_size
     grad_local = jnp.einsum("bij,boj->io", aggregate, slope_all, preferred_element_type=jnp.float32)
-    grad = summed_over(grad_local, "node") * (1.0 / math.sqrt(node_total))
+    grad, activated = summed_over(grad_local, "node", beside=activated)
+    grad = grad * (1.0 / math.sqrt(node_total))
     back_rows = jnp.einsum(
         "io,boj->bij", weight_half, slope_all, preferred_element_type=jnp.float32
     ).astype(jnp.bfloat16)

time: 67.8 us -> 64.3 us (0.948)
  waiting for transfers between devices: 15.1 us -> 12.8 us
  starting transfers between devices: 23.3 us -> 22.2 us
    ppermute x3, waiting for transfers between devices: 3.69 us -> 1.24 us  [summed_over(): lax.ppermute(block, axis, [(i, i ^ mask) for i in range(size)])]
    ppermute x8, starting transfers between devices: 16.9 us -> 15.4 us  [passed_along(): return lax.ppermute(block, axis, route)]
  transfers between devices with their start and end apart: 15 -> 15, of which waited for: 8 -> 6; matrix products, arithmetic and copies ran while one was open for 22% -> 23% of each run, Pallas kernels for 0% -> 0%
where the time goes in v18:
time: 64.3 us; the launch traced here: 64 us
  starting transfers between devices  22.2 us (35%)
  matrix products  19.4 us (30%)
  waiting for transfers between devices  12.8 us (20%)
  other arithmetic  5.38 us (8%)
  local copies, waits for them, and re-layouts  2.6 us (4%)
  between operations  1.58 us (2%)
    ppermute x8, starting transfers between devices, passed_along(): return lax.ppermute(block, axis, route)  15.4 us
    dot_general x1, matrix products, per_device(): jnp.einsum('tfk,tjk->tfj', sources, tile_values, preferred_element_type=j...  7.92 us
    ppermute x4, waiting for transfers between devices, gathered_along(): got = lax.ppermute(held, axis, [(i, i ^ mask) for i in range(size)])  6.9 us
    dot_general x1, matrix products, per_device(): jnp.einsum('tfj,tjk->tfk', back_sources, tile_values, preferred_element_t...  5.99 us
    ppermute x8, waiting for transfers between devices, passed_along(): return lax.ppermute(block, axis, route)  4.65 us
    ppermute x4, starting transfers between devices, gathered_along(): got = lax.ppermute(held, axis, [(i, i ^ mask) for i in range(size)])  3.57 us
    ppermute x3, starting transfers between devices, summed_over(): lax.ppermute(block, axis, [(i, i ^ mask) for i in range(size)])  3.21 us
    dot_general x2, matrix products, summed_by_table(): return jnp.einsum(spec, doubled, both, preferred_element_type=jnp.float32)  2.73 us
  transfers between devices with their start and end apart: 15, of which 6 were waited for; matrix products, arithmetic and copies ran while one was open for 23% of the time, Pallas kernels for 0%

profile of v18, /device:TPU:0, one launch (start us, length us, event | category | flops | bytes accessed | tf_op | source)
XLA Modules:
  0.0 64.0 jit_solution(9903407288827155556)
XLA Ops:
  0.6 3.1 %collective-permute-start = (bf16[16,32,128]{2,1,0:T(8,128)(2,1)}, bf16[16,32,128]{2,1,0:T(8,128)(2,1)S(1)}, u32[]{:S(2)}, u32[]{:S(2)}) collective-permute-start(bf16[16,32,128]{2,1,0:T(8,128)(2,1)} %param.9), channel_id=1, source_target_pairs={{24,0},{28,4},{0,8},{4,12},{8,16},{12,20},{16,24},{20,28},{25,1},{... | collective-permute-start | bytes 393224 | tf_op jit(solution)/shard_map/ppermute | solution.py:22
  3.7 1.5 %collective-permute-start.1 = (bf16[16,32,128]{2,1,0:T(8,128)(2,1)}, bf16[16,32,128]{2,1,0:T(8,128)(2,1)S(1)}, u32[]{:S(2)}, u32[]{:S(2)}) collective-permute-start(bf16[16,32,128]{2,1,0:T(8,128)(2,1)} %param.9), channel_id=1, source_target_pairs={{28,0},{0,4},{4,8},{8,12},{12,16},{16,20},{20,24},{24,28},{29,1},{... | collective-permute-start | bytes 393224 | tf_op jit(solution)/shard_map/ppermute | solution.py:22
  5.2 3.2 %collective-permute-start.2 = (bf16[16,32,128]{2,1,0:T(8,128)(2,1)}, bf16[16,32,128]{2,1,0:T(8,128)(2,1)S(1)}, u32[]{:S(2)}, u32[]{:S(2)}) collective-permute-start(bf16[16,32,128]{2,1,0:T(8,128)(2,1)} %param.9), channel_id=1, source_target_pairs={{4,0},{8,4},{12,8},{16,12},{20,16},{24,20},{28,24},{0,28},{5,1},{9... | collective-permute-start | bytes 393224 | tf_op jit(solution)/shard_map/ppermute | solution.py:22
  8.4 0.3 collective-permute-start.3
  8.7 0.7 %convert_bitcast_fusion = bf16[1,32,128]{2,1,0:T(8,128)(2,1)S(1)} fusion(f32[32,128]{1,0:T(8,128)} %param.14), kind=kLoop, calls=%fused_computation.74 | loop fusion | flops 4096 | bytes 24576 | tf_op jit(solution)/shard_map/broadcast_in_dim | solution.py:116
  9.4 0.1 broadcast_in_dim.11
  9.6 1.0 %fusion.20 = (bf16[1,17,32,128]{3,2,1,0:T(8,128)(2,1)S(1)}, bf16[17,128,128]{2,1,0:T(8,128)(2,1)S(1)}) fusion(bf16[1,32,128]{2,1,0:T(8,128)(2,1)S(1)} %convert_bitcast_fusion, bf16[16,32,128]{2,1,0:T(8,128)(2,1)} %param.17, bf16[17,128,128]{2,1,0:T(8,128)(2,1)S(1)} %broadcast_in_dim.11, s32[]{:T(128)S(6)} %select_n.53), kind=kLoop, calls=%fused_computation.45 | loop fusion | flops 278528 | bytes 417796 | tf_op jit(solution)/shard_map/stack | solution.py:37
  10.5 1.7 %collective-permute-start.4 = (bf16[1,17,32,128]{3,2,1,0:T(8,128)(2,1)S(1)}, bf16[1,17,32,128]{3,2,1,0:T(8,128)(2,1)S(1)}, u32[]{:S(2)}, u32[]{:S(2)}) collective-permute-start(bf16[1,17,32,128]{3,2,1,0:T(8,128)(2,1)S(1)} %get-tuple-element.33), channel_id=1, source_target_pairs={{0,2},{1,3},{2,0},{3,1},{4,6},{5,7},{6,4},{7,5},{8,10},{9,11},{10,... | collective-permute-start | bytes 417800 | tf_op jit(solution)/shard_map/ppermute | solution.py:38
  12.9 0.7 %broadcast_subtract_fusion = s32[256]{0:T(256)S(1)} fusion(s32[256]{0:T(256)} %param.11, s32[]{:T(128)S(6)} %mul.82), kind=kLoop, calls=%fused_computation.89 | loop fusion | flops 256 | bytes 2052 | tf_op jit(solution)/shard_map/sub | solution.py:97
  13.6 0.7 %fusion.36 = s32[256]{0:T(256)S(1)} fusion(s32[256]{0:T(256)} %param.12, s32[]{:T(128)S(6)} %axis_index.15), kind=kLoop, calls=%fused_computation.85 | loop fusion | flops 9472 | bytes 2052 | tf_op jit(solution)/shard_map/add | solution.py:102
  14.3 0.0 collective-permute-done
  14.4 0.0 collective-permute-done.1
  14.4 0.9 %constant_dynamic-update-slice_fusion.2 = bf16[80,32,128]{2,1,0:T(8,128)(2,1)S(1)} fusion(bf16[80,32,128]{2,1,0:T(8,128)(2,1)S(1)} %constant_dynamic-update-slice_fusion.3, bf16[16,32,128]{2,1,0:T(8,128)(2,1)} %param.9), kind=kLoop, calls=%fused_computation.68 | loop fusion | bytes 262144
  15.3 0.0 collective-permute-done.2
  15.4 0.3 collective-permute-done.4
  15.7 0.1 collective-permute-start.5
  15.8 0.0 collective-permute-done.3
  15.8 1.5 %collective-permute-done.5 = bf16[2,17,32,128]{3,2,1,0:T(8,128)(2,1)S(1)} collective-permute-done((bf16[2,17,32,128]{3,2,1,0:T(8,128)(2,1)S(1)}, bf16[2,17,32,128]{3,2,1,0:T(8,128)(2,1)S(1)}, u32[]{:S(2)}, u32[]{:S(2)}) %collective-permute-start.5) | collective-permute-done | bytes 278560 | tf_op jit(solution)/shard_map/ppermute | solution.py:38
  17.4 0.8 %fusion.12 = bf16[256,32,128]{2,0,1:T(8,128)(2,1)S(1)} fusion(bf16[80,32,128]{2,1,0:T(8,128)(2,1)S(1)} %constant_dynamic-update-slice_fusion, s32[256]{0:T(256)S(1)} %fusion.36), kind=kOutput, calls=%fused_computation.22 | convolution fusion | flops 167792640 | bytes 2753536 | tf_op jit(solution)/shard_map/ts,sfk->tfk/dot_general | solution.py:121
  18.2 7.9 %reduce-precision_convert_fusion.1 = (bf16[256,32,128]{2,1,0:T(8,128)(2,1)S(1)}, bf16[256,32,128]{2,1,0:T(8,128)(2,1)S(1)}) fusion(bf16[256,128,128]{2,1,0:T(8,128)(2,1)} %param.10, bf16[256,32,128]{2,0,1:T(8,128)(2,1)S(1)} %fusion.12), kind=kOutput, calls=%fused_computation.3 | convolution fusion | flops 272629760 | bytes 14680064 | tf_op jit(solution)/shard_map/tfk,tjk->tfj/dot_general | solution.py:124
  26.1 0.4 pad_maximum_fusion
  26.5 1.2 %fusion.9 = bf16[16,32,128]{2,0,1:T(8,128)(2,1)S(1)} fusion(bf16[512,32,128]{2,1,0:T(8,128)(2,1)S(1)} %pad_maximum_fusion, bf16[256,16]{0,1:T(8,128)(2,1)S(1)} %select_convert_fusion.2), kind=kOutput, calls=%fused_computation.19 | convolution fusion | flops 67207168 | bytes 4333568 | tf_op jit(solution)/shard_map/tb,tfj->bfj/dot_general | solution.py:68
  27.7 0.0 copy-start
  27.7 1.7 %collective-permute-start.6 = (bf16[1,16,32,128]{3,1,2,0:T(8,128)(2,1)S(1)}, bf16[1,16,32,128]{3,1,2,0:T(8,128)(2,1)S(1)}, u32[]{:S(2)}, u32[]{:S(2)}) collective-permute-start(bf16[1,16,32,128]{3,1,2,0:T(8,128)(2,1)S(1)} %bitcast.56), channel_id=1, source_target_pairs={{0,2},{1,3},{2,0},{3,1},{4,6},{5,7},{6,4},{7,5},{8,10},{9,11},{10,... | collective-permute-start | bytes 393224 | tf_op jit(solution)/shard_map/ppermute | solution.py:38
  29.4 3.8 %collective-permute-done.6 = bf16[1,16,32,128]{3,1,2,0:T(8,128)(2,1)S(1)} collective-permute-done((bf16[1,16,32,128]{3,1,2,0:T(8,128)(2,1)S(1)}, bf16[1,16,32,128]{3,1,2,0:T(8,128)(2,1)S(1)}, u32[]{:S(2)}, u32[]{:S(2)}) %collective-permute-start.6) | collective-permute-done | bytes 131104 | tf_op jit(solution)/shard_map/ppermute | solution.py:38
  33.3 0.1 collective-permute-start.7
  33.4 0.1 broadcast_in_dim.13
  33.5 0.1 copy_dynamic-update-slice_fusion.3
  33.5 0.1 copy_dynamic-update-slice_fusion.2
  33.6 1.3 %collective-permute-done.7 = bf16[2,16,32,128]{3,1,2,0:T(8,128)(2,1)S(1)} collective-permute-done((bf16[2,16,32,128]{3,1,2,0:T(8,128)(2,1)S(1)}, bf16[2,16,32,128]{3,1,2,0:T(8,128)(2,1)S(1)}, u32[]{:S(2)}, u32[]{:S(2)}) %collective-permute-start.7) | collective-permute-done | bytes 262176 | tf_op jit(solution)/shard_map/ppermute | solution.py:38
  34.9 0.1 copy_dynamic-update-slice_fusion.1
  35.0 0.1 copy_dynamic-update-slice_fusion
  35.0 0.3 broadcast_compare_fusion
  35.4 0.4 convolution_bitcast_fusion.1
  35.8 0.0 copy-done
  35.8 0.5 fusion.8
  36.3 0.8 %collective-permute-start.8 = (f32[32,128]{1,0:T(8,128)S(1)}, f32[32,128]{1,0:T(8,128)S(1)}, u32[]{:S(2)}, u32[]{:S(2)}) collective-permute-start(f32[32,128]{1,0:T(8,128)S(1)} %convolution_bitcast_fusion.1), channel_id=1, source_target_pairs={{0,4},{4,0},{8,12},{12,8},{16,20},{20,16},{24,28},{28,24},{1,5},{5... | collective-permute-start | bytes 49160 | tf_op jit(solution)/shard_map/ppermute | solution.py:55
  37.1 0.2 copy.26
  37.4 0.7 %fusion.31 = bf16[256,32,128]{2,0,1:T(8,128)(2,1)S(1)} fusion(bf16[16,32,128]{2,0,1:T(8,128)(2,1)S(1)} %copy.26, s32[256]{0:T(256)S(1)} %broadcast_subtract_fusion), kind=kOutput, calls=%fused_computation.65 | convolution fusion | flops 33558528 | bytes 2229248 | tf_op jit(solution)/shard_map/tb,bfj->tfj/dot_general | solution.py:144
  38.1 6.0 %reduce-precision_convert_fusion = (bf16[256,32,128]{2,1,0:T(8,128)(2,1)S(1)}, bf16[256,32,128]{2,1,0:T(8,128)(2,1)S(1)}) fusion(bf16[256,128,128]{2,1,0:T(8,128)(2,1)} %param.10, bf16[256,32,128]{2,0,1:T(8,128)(2,1)S(1)} %fusion.31), kind=kOutput, calls=%fused_computation.1 | convolution fusion | flops 272629760 | bytes 14680064 | tf_op jit(solution)/shard_map/tfj,tjk->tfk/dot_general | solution.py:147
  44.1 0.4 pad_maximum_fusion.1
  44.5 0.0 copy-start.1
  44.5 0.0 copy-start.2
  44.5 0.8 %select_convert_fusion = bf16[16,32,128]{2,1,0:T(8,128)(2,1)} fusion(f32[16,128,128]{2,1,0:T(8,128)S(1)} %get-tuple-element.36, s32[]{:T(128)S(6)} %select_n.53, pred[16,128,128]{2,1,0:T(8,128)(4,1)S(1)} %get-tuple-element.35), kind=kLoop, calls=%fused_computation.31 | loop fusion | flops 196608 | bytes 458756 | tf_op jit(solution)/shard_map/convert_element_type | solution.py:135
  45.3 0.0 collective-permute-done.8
  45.3 1.1 %collective-permute-start.13 = (f32[32,128]{1,0:T(8,128)S(1)}, f32[32,128]{1,0:T(8,128)S(1)}, u32[]{:S(2)}, u32[]{:S(2)}) collective-permute-start(f32[32,128]{1,0:T(8,128)S(1)} %add.80), channel_id=1, source_target_pairs={{0,8},{4,12},{8,0},{12,4},{16,24},{20,28},{24,16},{28,20},{1,9},{5... | collective-permute-start | bytes 49160 | tf_op jit(solution)/shard_map/ppermute | solution.py:55
  46.3 1.5 %fusion.43 = (bf16[80,32,128]{2,0,1:T(8,128)(2,1)S(1)}, f32[80,32,128]{2,0,1:T(8,128)S(1)}) fusion(bf16[512,32,128]{2,1,0:T(8,128)(2,1)S(1)} %pad_maximum_fusion.1, bf16[256,80]{0,1:T(8,128)(2,1)S(1)} %select_convert_fusion.1), kind=kOutput, calls=%fused_computation.93 | convolution fusion | flops 336035840 | bytes 6201344 | tf_op jit(solution)/shard_map/ts,tfk->sfk/dot_general | solution.py:68
  47.9 1.2 %collective-permute-done.13 = f32[32,128]{1,0:T(8,128)S(1)} collective-permute-done((f32[32,128]{1,0:T(8,128)S(1)}, f32[32,128]{1,0:T(8,128)S(1)}, u32[]{:S(2)}, u32[]{:S(2)}) %collective-permute-start.13) | collective-permute-done | bytes 16416 | tf_op jit(solution)/shard_map/ppermute | solution.py:55
  49.1 1.3 %collective-permute-start.14 = (f32[32,128]{1,0:T(8,128)S(1)}, f32[32,128]{1,0:T(8,128)S(1)}, u32[]{:S(2)}, u32[]{:S(2)}) collective-permute-start(f32[32,128]{1,0:T(8,128)S(1)} %add.85), channel_id=1, source_target_pairs={{0,16},{4,20},{8,24},{12,28},{16,0},{20,4},{24,8},{28,12},{1,17},{... | collective-permute-start | bytes 49160 | tf_op jit(solution)/shard_map/ppermute | solution.py:55
  50.5 3.5 %collective-permute-start.10 = (bf16[16,32,128]{2,0,1:T(8,128)(2,1)S(1)}, bf16[16,32,128]{2,0,1:T(8,128)(2,1)S(1)}, u32[]{:S(2)}, u32[]{:S(2)}) collective-permute-start(bf16[16,32,128]{2,0,1:T(8,128)(2,1)S(1)} %get-tuple-element.30), channel_id=1, source_target_pairs={{4,0},{8,4},{12,8},{16,12},{20,16},{24,20},{28,24},{0,28},{5,1},{9... | collective-permute-start | bytes 393224 | tf_op jit(solution)/shard_map/ppermute | solution.py:22
  54.0 0.0 collective-permute-start.11
  54.0 0.2 collective-permute-start.12
  54.2 3.6 %collective-permute-start.9 = (bf16[16,32,128]{2,0,1:T(8,128)(2,1)S(1)}, bf16[16,32,128]{2,0,1:T(8,128)(2,1)S(1)}, u32[]{:S(2)}, u32[]{:S(2)}) collective-permute-start(bf16[16,32,128]{2,0,1:T(8,128)(2,1)S(1)} %get-tuple-element.27), channel_id=1, source_target_pairs={{8,0},{12,4},{16,8},{20,12},{24,16},{28,20},{0,24},{4,28},{9,1},{1... | collective-permute-start | bytes 393224 | tf_op jit(solution)/shard_map/ppermute | solution.py:22
  57.8 0.0 collective-permute-done.14
  57.8 0.0 copy-done.1
  57.8 0.0 copy-done.2
  57.8 0.6 divide_subtract_fusion
  58.5 0.0 collective-permute-done.10
  58.5 4.6 %collective-permute-done.11 = bf16[16,32,128]{2,0,1:T(8,128)(2,1)S(1)} collective-permute-done((bf16[16,32,128]{2,0,1:T(8,128)(2,1)S(1)}, bf16[16,32,128]{2,0,1:T(8,128)(2,1)S(1)}, u32[]{:S(2)}, u32[]{:S(2)}) %collective-permute-start.11) | collective-permute-done | bytes 131104 | tf_op jit(solution)/shard_map/ppermute | solution.py:22
  63.1 0.0 collective-permute-done.12
  63.1 0.0 collective-permute-done.9
  63.1 0.1 fusion.16
  63.2 0.8 %copy.22 = f32[16,32,128]{2,1,0:T(8,128)} copy(f32[16,32,128]{2,0,1:T(8,128)S(1)} %fusion.16) | data formatting | bytes 524288
  (18 shorter events, 0.3 us)
Async XLA Ops:
  0.6 13.7 %collective-permute-start = (bf16[16,32,128]{2,1,0:T(8,128)(2,1)}, bf16[16,32,128]{2,1,0:T(8,128)(2,1)S(1)}, u32[]{:S(2)}, u32[]{:S(2)}) collective-permute-start(bf16[16,32,128]{2,1,0:T(8,128)(2,1)} %param.9), channel_id=1, source_target_pairs={{24,0},{28,4},{0,8},{4,12},{8,16},{12,20},{16,24},{20,28},{25,1},{... | collective-permute-start | bytes 393224 | tf_op jit(solution)/shard_map/ppermute | solution.py:22
  3.7 10.7 %collective-permute-start.1 = (bf16[16,32,128]{2,1,0:T(8,128)(2,1)}, bf16[16,32,128]{2,1,0:T(8,128)(2,1)S(1)}, u32[]{:S(2)}, u32[]{:S(2)}) collective-permute-start(bf16[16,32,128]{2,1,0:T(8,128)(2,1)} %param.9), channel_id=1, source_target_pairs={{28,0},{0,4},{4,8},{8,12},{12,16},{16,20},{20,24},{24,28},{29,1},{... | collective-permute-start | bytes 393224 | tf_op jit(solution)/shard_map/ppermute | solution.py:22
  5.2 10.1 %collective-permute-start.2 = (bf16[16,32,128]{2,1,0:T(8,128)(2,1)}, bf16[16,32,128]{2,1,0:T(8,128)(2,1)S(1)}, u32[]{:S(2)}, u32[]{:S(2)}) collective-permute-start(bf16[16,32,128]{2,1,0:T(8,128)(2,1)} %param.9), channel_id=1, source_target_pairs={{4,0},{8,4},{12,8},{16,12},{20,16},{24,20},{28,24},{0,28},{5,1},{9... | collective-permute-start | bytes 393224 | tf_op jit(solution)/shard_map/ppermute | solution.py:22
  8.4 7.3 %collective-permute-start.3 = (bf16[16,32,128]{2,1,0:T(8,128)(2,1)}, bf16[16,32,128]{2,1,0:T(8,128)(2,1)S(1)}, u32[]{:S(2)}, u32[]{:S(2)}) collective-permute-start(bf16[16,32,128]{2,1,0:T(8,128)(2,1)} %param.9), channel_id=1, source_target_pairs={{8,0},{12,4},{16,8},{20,12},{24,16},{28,20},{0,24},{4,28},{9,1},{1... | collective-permute-start | bytes 393224 | tf_op jit(solution)/shard_map/ppermute | solution.py:22
  10.5 5.1 %collective-permute-start.4 = (bf16[1,17,32,128]{3,2,1,0:T(8,128)(2,1)S(1)}, bf16[1,17,32,128]{3,2,1,0:T(8,128)(2,1)S(1)}, u32[]{:S(2)}, u32[]{:S(2)}) collective-permute-start(bf16[1,17,32,128]{3,2,1,0:T(8,128)(2,1)S(1)} %get-tuple-element.33), channel_id=1, source_target_pairs={{0,2},{1,3},{2,0},{3,1},{4,6},{5,7},{6,4},{7,5},{8,10},{9,11},{10,... | collective-permute-start | bytes 417800 | tf_op jit(solution)/shard_map/ppermute | solution.py:38
  15.7 1.6 %collective-permute-start.5 = (bf16[2,17,32,128]{3,2,1,0:T(8,128)(2,1)S(1)}, bf16[2,17,32,128]{3,2,1,0:T(8,128)(2,1)S(1)}, u32[]{:S(2)}, u32[]{:S(2)}) collective-permute-start(bf16[2,17,32,128]{3,2,1,0:T(8,128)(2,1)S(1)} %pad_maximum_fusion.2), channel_id=1, source_target_pairs={{0,1},{1,0},{2,3},{3,2},{4,5},{5,4},{6,7},{7,6},{8,9},{9,8},{10,11... | collective-permute-start | bytes 835592 | tf_op jit(solution)/shard_map/ppermute | solution.py:38
  27.7 8.1 %copy-start = (f32[32,128]{1,0:T(8,128)S(1)}, f32[32,128]{1,0:T(8,128)}, u32[]{:S(2)}) copy-start(f32[32,128]{1,0:T(8,128)} %param.14) | copy-start | bytes 49156
  27.7 5.6 %collective-permute-start.6 = (bf16[1,16,32,128]{3,1,2,0:T(8,128)(2,1)S(1)}, bf16[1,16,32,128]{3,1,2,0:T(8,128)(2,1)S(1)}, u32[]{:S(2)}, u32[]{:S(2)}) collective-permute-start(bf16[1,16,32,128]{3,1,2,0:T(8,128)(2,1)S(1)} %bitcast.56), channel_id=1, source_target_pairs={{0,2},{1,3},{2,0},{3,1},{4,6},{5,7},{6,4},{7,5},{8,10},{9,11},{10,... | collective-permute-start | bytes 393224 | tf_op jit(solution)/shard_map/ppermute | solution.py:38
  33.3 1.6 %collective-permute-start.7 = (bf16[2,16,32,128]{3,1,2,0:T(8,128)(2,1)S(1)}, bf16[2,16,32,128]{3,1,2,0:T(8,128)(2,1)S(1)}, u32[]{:S(2)}, u32[]{:S(2)}) collective-permute-start(bf16[2,16,32,128]{3,1,2,0:T(8,128)(2,1)S(1)} %pad_maximum_fusion.3), channel_id=1, source_target_pairs={{0,1},{1,0},{2,3},{3,2},{4,5},{5,4},{6,7},{7,6},{8,9},{9,8},{10,11... | collective-permute-start | bytes 786440 | tf_op jit(solution)/shard_map/ppermute | solution.py:38
  36.3 9.0 %collective-permute-start.8 = (f32[32,128]{1,0:T(8,128)S(1)}, f32[32,128]{1,0:T(8,128)S(1)}, u32[]{:S(2)}, u32[]{:S(2)}) collective-permute-start(f32[32,128]{1,0:T(8,128)S(1)} %convolution_bitcast_fusion.1), channel_id=1, source_target_pairs={{0,4},{4,0},{8,12},{12,8},{16,20},{20,16},{24,28},{28,24},{1,5},{5... | collective-permute-start | bytes 49160 | tf_op jit(solution)/shard_map/ppermute | solution.py:55
  44.5 13.4 %copy-start.1 = (f32[32,128]{1,0:T(8,128)S(1)}, f32[32,128]{1,0:T(8,128)}, u32[]{:S(2)}) copy-start(f32[32,128]{1,0:T(8,128)} %param.15) | copy-start | bytes 49156
  44.5 13.3 %copy-start.2 = (f32[32,128]{1,0:T(8,128)S(1)}, f32[32,128]{1,0:T(8,128)}, u32[]{:S(2)}) copy-start(f32[32,128]{1,0:T(8,128)} %param.16) | copy-start | bytes 49156
  45.3 3.8 %collective-permute-start.13 = (f32[32,128]{1,0:T(8,128)S(1)}, f32[32,128]{1,0:T(8,128)S(1)}, u32[]{:S(2)}, u32[]{:S(2)}) collective-permute-start(f32[32,128]{1,0:T(8,128)S(1)} %add.80), channel_id=1, source_target_pairs={{0,8},{4,12},{8,0},{12,4},{16,24},{20,28},{24,16},{28,20},{1,9},{5... | collective-permute-start | bytes 49160 | tf_op jit(solution)/shard_map/ppermute | solution.py:55
  49.1 8.7 %collective-permute-start.14 = (f32[32,128]{1,0:T(8,128)S(1)}, f32[32,128]{1,0:T(8,128)S(1)}, u32[]{:S(2)}, u32[]{:S(2)}) collective-permute-start(f32[32,128]{1,0:T(8,128)S(1)} %add.85), channel_id=1, source_target_pairs={{0,16},{4,20},{8,24},{12,28},{16,0},{20,4},{24,8},{28,12},{1,17},{... | collective-permute-start | bytes 49160 | tf_op jit(solution)/shard_map/ppermute | solution.py:55
  50.5 8.0 %collective-permute-start.10 = (bf16[16,32,128]{2,0,1:T(8,128)(2,1)S(1)}, bf16[16,32,128]{2,0,1:T(8,128)(2,1)S(1)}, u32[]{:S(2)}, u32[]{:S(2)}) collective-permute-start(bf16[16,32,128]{2,0,1:T(8,128)(2,1)S(1)} %get-tuple-element.30), channel_id=1, source_target_pairs={{4,0},{8,4},{12,8},{16,12},{20,16},{24,20},{28,24},{0,28},{5,1},{9... | collective-permute-start | bytes 393224 | tf_op jit(solution)/shard_map/ppermute | solution.py:22
  54.0 9.1 %collective-permute-start.11 = (bf16[16,32,128]{2,0,1:T(8,128)(2,1)S(1)}, bf16[16,32,128]{2,0,1:T(8,128)(2,1)S(1)}, u32[]{:S(2)}, u32[]{:S(2)}) collective-permute-start(bf16[16,32,128]{2,0,1:T(8,128)(2,1)S(1)} %get-tuple-element.29), channel_id=1, source_target_pairs={{28,0},{0,4},{4,8},{8,12},{12,16},{16,20},{20,24},{24,28},{29,1},{... | collective-permute-start | bytes 393224 | tf_op jit(solution)/shard_map/ppermute | solution.py:22
  54.0 9.1 %collective-permute-start.12 = (bf16[16,32,128]{2,0,1:T(8,128)(2,1)S(1)}, bf16[16,32,128]{2,0,1:T(8,128)(2,1)S(1)}, u32[]{:S(2)}, u32[]{:S(2)}) collective-permute-start(bf16[16,32,128]{2,0,1:T(8,128)(2,1)S(1)} %get-tuple-element.28), channel_id=1, source_target_pairs={{24,0},{28,4},{0,8},{4,12},{8,16},{12,20},{16,24},{20,28},{25,1},{... | collective-permute-start | bytes 393224 | tf_op jit(solution)/shard_map/ppermute | solution.py:22
  54.2 8.9 %collective-permute-start.9 = (bf16[16,32,128]{2,0,1:T(8,128)(2,1)S(1)}, bf16[16,32,128]{2,0,1:T(8,128)(2,1)S(1)}, u32[]{:S(2)}, u32[]{:S(2)}) collective-permute-start(bf16[16,32,128]{2,0,1:T(8,128)(2,1)S(1)} %get-tuple-element.27), channel_id=1, source_target_pairs={{8,0},{12,4},{16,8},{20,12},{24,16},{28,20},{0,24},{4,28},{9,1},{1... | collective-permute-start | bytes 393224 | tf_op jit(solution)/shard_map/ppermute | solution.py:22

commit v19 on v11

--- a/solution.py
+++ b/solution.py
@@ -46,10 +46,10 @@
     return whole
 
 
-def summed_over(block, axis):
+def summed_over(block, axis, beside=None):
     size = lax.axis_size(axis)
     if size & (size - 1):
-        return lax.psum(block, axis)
+        return lax.psum(block, axis), beside
     own = lax.axis_index(axis)
     stride = 1
     while stride < size:
@@ -66,7 +66,9 @@
         else:
             block = block + lax.ppermute(block, axis, [(i, i ^ stride) for i in range(size)])
             stride *= 2
-    return block
+        if beside is not None and stride <= 4:
+            block, beside = lax.optimization_barrier((block, beside))
+    return block, beside
 
 
 def summed_by_table(table, terms, spec):
@@ -131,10 +133,8 @@
     sources = jnp.einsum(
         "ts,sfk->tfk", pick_source, nearby, preferred_element_type=jnp.float32
     ).astype(jnp.bfloat16)
-    tiles_turned = jnp.swapaxes(tile_values, 1, 2)
-    tiles_turned, nearby = lax.optimization_barrier((tiles_turned, nearby))
     forward_terms = jnp.einsum(
-        "tfk,tkj->tfj", sources, tiles_turned, preferred_element_type=jnp.float32
+        "tfk,tjk->tfj", sources, tile_values, preferred_element_type=jnp.float32
     )
     aggregate = summed_by_table(add_row, forward_terms, "tb,tfj->bfj")
     aggregate = aggregate.astype(jnp.bfloat16)
@@ -148,7 +148,8 @@
     slope_all = (cotangent_all.astype(jnp.float32) * elu_slope(preact)).astype(jnp.bfloat16)
     node_total = cycle_size * blocks * tile_size
     grad_local = jnp.einsum("bij,boj->io", aggregate, slope_all, preferred_element_type=jnp.float32)
-    grad = summed_over(grad_local, "node") * (1.0 / math.sqrt(node_total))
+    grad, activated = summed_over(grad_local, "node", beside=activated)
+    grad = grad * (1.0 / math.sqrt(node_total))
     back_rows = jnp.einsum(
         "io,boj->bij", weight_half, slope_all, preferred_element_type=jnp.float32
     ).astype(jnp.bfloat16)

time: 68 us -> 63.8 us (0.938)
  starting transfers between devices: 25.4 us -> 21.4 us
    ppermute x8, starting transfers between devices: 17.6 us -> 12.2 us  [passed_along(): return lax.ppermute(block, axis, route)]
    ppermute x1, starting transfers between devices: 0.07 us -> 2.14 us  [summed_over(): lax.ppermute(block, axis, [(i, i ^ stride) for i in range(size)])]
    ppermute x3, starting transfers between devices: 4.5 us -> 3.5 us  [summed_over(): held.append(lax.ppermute(block, axis, route))]
  transfers between devices with their start and end apart: 16 -> 16, of which waited for: 7 -> 8; matrix products, arithmetic and copies ran while one was open for 22% -> 24% of each run, Pallas kernels for 0% -> 0%
where the time goes in v19:
time: 63.8 us; the launch traced here: 63.4 us
  starting transfers between devices  21.4 us (34%)
  matrix products  19.4 us (30%)
  waiting for transfers between devices  13 us (20%)
  other arithmetic  5.39 us (8%)
  local copies, waits for them, and re-layouts  2.6 us (4%)
  between operations  1.62 us (3%)
    ppermute x8, starting transfers between devices, passed_along(): return lax.ppermute(block, axis, route)  12.2 us
    dot_general x1, matrix products, per_device(): jnp.einsum('tfk,tjk->tfj', sources, tile_values, preferred_element_type=j...  7.92 us
    ppermute x4, waiting for transfers between devices, gathered_along(): got = lax.ppermute(held, axis, [(i, i ^ mask) for i in range(size)])  6.87 us
    ppermute x8, waiting for transfers between devices, passed_along(): return lax.ppermute(block, axis, route)  6.12 us
    dot_general x1, matrix products, per_device(): jnp.einsum('tfj,tjk->tfk', back_sources, tile_values, preferred_element_t...  5.99 us
    ppermute x4, starting transfers between devices, gathered_along(): got = lax.ppermute(held, axis, [(i, i ^ mask) for i in range(size)])  3.57 us
    ppermute x3, starting transfers between devices, summed_over(): held.append(lax.ppermute(block, axis, route))  3.5 us
    dot_general x2, matrix products, summed_by_table(): return jnp.einsum(spec, doubled, both, preferred_element_type=jnp.float32)  2.74 us
  transfers between devices with their start and end apart: 16, of which 8 were waited for; matrix products, arithmetic and copies ran while one was open for 24% of the time, Pallas kernels for 0%

profile of v19, /device:TPU:0, one launch (start us, length us, event | category | flops | bytes accessed | tf_op | source)
XLA Modules:
  0.0 63.4 jit_solution(13202787809860817255)
XLA Ops:
  0.6 3.1 %collective-permute-start = (bf16[16,32,128]{2,1,0:T(8,128)(2,1)}, bf16[16,32,128]{2,1,0:T(8,128)(2,1)S(1)}, u32[]{:S(2)}, u32[]{:S(2)}) collective-permute-start(bf16[16,32,128]{2,1,0:T(8,128)(2,1)} %param.9), channel_id=1, source_target_pairs={{24,0},{28,4},{0,8},{4,12},{8,16},{12,20},{16,24},{20,28},{25,1},{... | collective-permute-start | bytes 393224 | tf_op jit(solution)/shard_map/ppermute | solution.py:22
  3.7 1.5 %collective-permute-start.1 = (bf16[16,32,128]{2,1,0:T(8,128)(2,1)}, bf16[16,32,128]{2,1,0:T(8,128)(2,1)S(1)}, u32[]{:S(2)}, u32[]{:S(2)}) collective-permute-start(bf16[16,32,128]{2,1,0:T(8,128)(2,1)} %param.9), channel_id=1, source_target_pairs={{28,0},{0,4},{4,8},{8,12},{12,16},{16,20},{20,24},{24,28},{29,1},{... | collective-permute-start | bytes 393224 | tf_op jit(solution)/shard_map/ppermute | solution.py:22
  5.2 3.2 %collective-permute-start.2 = (bf16[16,32,128]{2,1,0:T(8,128)(2,1)}, bf16[16,32,128]{2,1,0:T(8,128)(2,1)S(1)}, u32[]{:S(2)}, u32[]{:S(2)}) collective-permute-start(bf16[16,32,128]{2,1,0:T(8,128)(2,1)} %param.9), channel_id=1, source_target_pairs={{4,0},{8,4},{12,8},{16,12},{20,16},{24,20},{28,24},{0,28},{5,1},{9... | collective-permute-start | bytes 393224 | tf_op jit(solution)/shard_map/ppermute | solution.py:22
  8.4 0.3 collective-permute-start.3
  8.7 0.7 %convert_bitcast_fusion = bf16[1,32,128]{2,1,0:T(8,128)(2,1)S(1)} fusion(f32[32,128]{1,0:T(8,128)} %param.14), kind=kLoop, calls=%fused_computation.76 | loop fusion | flops 4096 | bytes 24576 | tf_op jit(solution)/shard_map/broadcast_in_dim | solution.py:128
  9.4 0.1 broadcast_in_dim.11
  9.6 1.0 %fusion.21 = (bf16[1,17,32,128]{3,2,1,0:T(8,128)(2,1)S(1)}, bf16[17,128,128]{2,1,0:T(8,128)(2,1)S(1)}) fusion(bf16[1,32,128]{2,1,0:T(8,128)(2,1)S(1)} %convert_bitcast_fusion, bf16[16,32,128]{2,1,0:T(8,128)(2,1)} %param.17, bf16[17,128,128]{2,1,0:T(8,128)(2,1)S(1)} %broadcast_in_dim.11, s32[]{:T(128)S(6)} %select_n.73), kind=kLoop, calls=%fused_computation.45 | loop fusion | flops 278528 | bytes 417796 | tf_op jit(solution)/shard_map/stack | solution.py:37
  10.5 1.7 %collective-permute-start.4 = (bf16[1,17,32,128]{3,2,1,0:T(8,128)(2,1)S(1)}, bf16[1,17,32,128]{3,2,1,0:T(8,128)(2,1)S(1)}, u32[]{:S(2)}, u32[]{:S(2)}) collective-permute-start(bf16[1,17,32,128]{3,2,1,0:T(8,128)(2,1)S(1)} %get-tuple-element.33), channel_id=1, source_target_pairs={{0,2},{1,3},{2,0},{3,1},{4,6},{5,7},{6,4},{7,5},{8,10},{9,11},{10,... | collective-permute-start | bytes 417800 | tf_op jit(solution)/shard_map/ppermute | solution.py:38
  12.9 0.7 %broadcast_subtract_fusion = s32[256]{0:T(256)S(1)} fusion(s32[256]{0:T(256)} %param.11, s32[]{:T(128)S(6)} %mul.82), kind=kLoop, calls=%fused_computation.91 | loop fusion | flops 256 | bytes 2052 | tf_op jit(solution)/shard_map/sub | solution.py:109
  13.6 0.7 %fusion.37 = s32[256]{0:T(256)S(1)} fusion(s32[256]{0:T(256)} %param.12, s32[]{:T(128)S(6)} %axis_index.15), kind=kLoop, calls=%fused_computation.87 | loop fusion | flops 9472 | bytes 2052 | tf_op jit(solution)/shard_map/add | solution.py:114
  14.4 0.0 collective-permute-done
  14.4 0.0 collective-permute-done.1
  14.4 0.9 %constant_dynamic-update-slice_fusion.2 = bf16[80,32,128]{2,1,0:T(8,128)(2,1)S(1)} fusion(bf16[80,32,128]{2,1,0:T(8,128)(2,1)S(1)} %constant_dynamic-update-slice_fusion.3, bf16[16,32,128]{2,1,0:T(8,128)(2,1)} %param.9), kind=kLoop, calls=%fused_computation.70 | loop fusion | bytes 262144
  15.4 0.0 collective-permute-done.2
  15.4 0.2 collective-permute-done.4
  15.7 0.1 collective-permute-start.5
  15.8 0.0 collective-permute-done.3
  15.8 1.5 %collective-permute-done.5 = bf16[2,17,32,128]{3,2,1,0:T(8,128)(2,1)S(1)} collective-permute-done((bf16[2,17,32,128]{3,2,1,0:T(8,128)(2,1)S(1)}, bf16[2,17,32,128]{3,2,1,0:T(8,128)(2,1)S(1)}, u32[]{:S(2)}, u32[]{:S(2)}) %collective-permute-start.5) | collective-permute-done | bytes 278560 | tf_op jit(solution)/shard_map/ppermute | solution.py:38
  17.4 0.8 %fusion.12 = bf16[256,32,128]{2,0,1:T(8,128)(2,1)S(1)} fusion(bf16[80,32,128]{2,1,0:T(8,128)(2,1)S(1)} %constant_dynamic-update-slice_fusion, s32[256]{0:T(256)S(1)} %fusion.37), kind=kOutput, calls=%fused_computation.21 | convolution fusion | flops 167792640 | bytes 2753536 | tf_op jit(solution)/shard_map/ts,sfk->tfk/dot_general | solution.py:133
  18.2 7.9 %reduce-precision_convert_fusion.1 = (bf16[256,32,128]{2,1,0:T(8,128)(2,1)S(1)}, bf16[256,32,128]{2,1,0:T(8,128)(2,1)S(1)}) fusion(bf16[256,128,128]{2,1,0:T(8,128)(2,1)} %param.10, bf16[256,32,128]{2,0,1:T(8,128)(2,1)S(1)} %fusion.12), kind=kOutput, calls=%fused_computation.3 | convolution fusion | flops 272629760 | bytes 14680064 | tf_op jit(solution)/shard_map/tfk,tjk->tfj/dot_general | solution.py:136
  26.1 0.4 pad_maximum_fusion
  26.5 1.2 %fusion.9 = bf16[16,32,128]{2,0,1:T(8,128)(2,1)S(1)} fusion(bf16[512,32,128]{2,1,0:T(8,128)(2,1)S(1)} %pad_maximum_fusion, bf16[256,16]{0,1:T(8,128)(2,1)S(1)} %select_convert_fusion.2), kind=kOutput, calls=%fused_computation.19 | convolution fusion | flops 67207168 | bytes 4333568 | tf_op jit(solution)/shard_map/tb,tfj->bfj/dot_general | solution.py:80
  27.7 1.7 %collective-permute-start.6 = (bf16[1,16,32,128]{3,1,2,0:T(8,128)(2,1)S(1)}, bf16[1,16,32,128]{3,1,2,0:T(8,128)(2,1)S(1)}, u32[]{:S(2)}, u32[]{:S(2)}) collective-permute-start(bf16[1,16,32,128]{3,1,2,0:T(8,128)(2,1)S(1)} %bitcast.61), channel_id=1, source_target_pairs={{0,2},{1,3},{2,0},{3,1},{4,6},{5,7},{6,4},{7,5},{8,10},{9,11},{10,... | collective-permute-start | bytes 393224 | tf_op jit(solution)/shard_map/ppermute | solution.py:38
  29.4 3.8 %collective-permute-done.6 = bf16[1,16,32,128]{3,1,2,0:T(8,128)(2,1)S(1)} collective-permute-done((bf16[1,16,32,128]{3,1,2,0:T(8,128)(2,1)S(1)}, bf16[1,16,32,128]{3,1,2,0:T(8,128)(2,1)S(1)}, u32[]{:S(2)}, u32[]{:S(2)}) %collective-permute-start.6) | collective-permute-done | bytes 131104 | tf_op jit(solution)/shard_map/ppermute | solution.py:38
  33.3 0.1 collective-permute-start.7
  33.4 0.1 broadcast_in_dim.13
  33.5 0.1 copy_dynamic-update-slice_fusion.3
  33.5 0.1 copy_dynamic-update-slice_fusion.2
  33.6 1.3 %collective-permute-done.7 = bf16[2,16,32,128]{3,1,2,0:T(8,128)(2,1)S(1)} collective-permute-done((bf16[2,16,32,128]{3,1,2,0:T(8,128)(2,1)S(1)}, bf16[2,16,32,128]{3,1,2,0:T(8,128)(2,1)S(1)}, u32[]{:S(2)}, u32[]{:S(2)}) %collective-permute-start.7) | collective-permute-done | bytes 262176 | tf_op jit(solution)/shard_map/ppermute | solution.py:38
  34.9 0.1 copy_dynamic-update-slice_fusion.1
  35.0 0.1 copy_dynamic-update-slice_fusion
  35.0 0.3 broadcast_compare_fusion
  35.4 0.4 fusion.19
  35.8 0.8 %collective-permute-start.8 = (f32[32,128]{1,0:T(8,128)S(1)}, f32[32,128]{1,0:T(8,128)S(1)}, u32[]{:S(2)}, u32[]{:S(2)}) collective-permute-start(f32[32,128]{1,0:T(8,128)S(1)} %bitcast.64), channel_id=1, source_target_pairs={{0,4},{4,0},{8,12},{12,8},{16,20},{20,16},{24,28},{28,24},{1,5},{5... | collective-permute-start | bytes 49160 | tf_op jit(solution)/shard_map/ppermute | solution.py:60
  36.5 1.1 %collective-permute-start.9 = (f32[32,128]{1,0:T(8,128)S(1)}, f32[32,128]{1,0:T(8,128)S(1)}, u32[]{:S(2)}, u32[]{:S(2)}) collective-permute-start(f32[32,128]{1,0:T(8,128)S(1)} %bitcast.65), channel_id=1, source_target_pairs={{0,8},{4,12},{8,0},{12,4},{16,24},{20,28},{24,16},{28,20},{1,9},{5... | collective-permute-start | bytes 49160 | tf_op jit(solution)/shard_map/ppermute | solution.py:60
  37.6 1.7 %collective-permute-start.10 = (f32[32,128]{1,0:T(8,128)S(1)}, f32[32,128]{1,0:T(8,128)S(1)}, u32[]{:S(2)}, u32[]{:S(2)}) collective-permute-start(f32[32,128]{1,0:T(8,128)S(1)} %bitcast.66), channel_id=1, source_target_pairs={{0,12},{4,8},{8,4},{12,0},{16,28},{20,24},{24,20},{28,16},{1,13},{... | collective-permute-start | bytes 49160 | tf_op jit(solution)/shard_map/ppermute | solution.py:60
  39.3 0.0 copy-done
  39.3 0.5 fusion.8
  39.8 0.2 copy.26
  40.0 0.7 %fusion.32 = bf16[256,32,128]{2,0,1:T(8,128)(2,1)S(1)} fusion(bf16[16,32,128]{2,0,1:T(8,128)(2,1)S(1)} %copy.26, s32[256]{0:T(256)S(1)} %broadcast_subtract_fusion), kind=kOutput, calls=%fused_computation.67 | convolution fusion | flops 33558528 | bytes 2229248 | tf_op jit(solution)/shard_map/tb,bfj->tfj/dot_general | solution.py:156
  40.8 6.0 %reduce-precision_convert_fusion = (bf16[256,32,128]{2,1,0:T(8,128)(2,1)S(1)}, bf16[256,32,128]{2,1,0:T(8,128)(2,1)S(1)}) fusion(bf16[256,128,128]{2,1,0:T(8,128)(2,1)} %param.10, bf16[256,32,128]{2,0,1:T(8,128)(2,1)S(1)} %fusion.32), kind=kOutput, calls=%fused_computation.1 | convolution fusion | flops 272629760 | bytes 14680064 | tf_op jit(solution)/shard_map/tfj,tjk->tfk/dot_general | solution.py:159
  46.8 0.4 pad_maximum_fusion.1
  47.2 0.0 copy-start.1
  47.2 0.0 copy-start.2
  47.2 1.5 %fusion.44 = (bf16[80,32,128]{2,0,1:T(8,128)(2,1)S(1)}, f32[80,32,128]{2,0,1:T(8,128)S(1)}) fusion(bf16[512,32,128]{2,1,0:T(8,128)(2,1)S(1)} %pad_maximum_fusion.1, bf16[256,80]{0,1:T(8,128)(2,1)S(1)} %select_convert_fusion.1), kind=kOutput, calls=%fused_computation.95 | convolution fusion | flops 336035840 | bytes 6201344 | tf_op jit(solution)/shard_map/ts,tfk->sfk/dot_general | solution.py:80
  48.7 0.8 %select_convert_fusion = bf16[16,32,128]{2,1,0:T(8,128)(2,1)} fusion(f32[16,128,128]{2,1,0:T(8,128)S(1)} %get-tuple-element.36, s32[]{:T(128)S(6)} %select_n.73, pred[16,128,128]{2,1,0:T(8,128)(4,1)S(1)} %get-tuple-element.35), kind=kLoop, calls=%fused_computation.30 | loop fusion | flops 196608 | bytes 458756 | tf_op jit(solution)/shard_map/convert_element_type | solution.py:147
  49.5 0.0 collective-permute-done.8
  49.5 0.0 collective-permute-done.9
  49.5 0.0 collective-permute-done.10
  49.5 2.1 %collective-permute-start.15 = (f32[32,128]{1,0:T(8,128)S(1)}, f32[32,128]{1,0:T(8,128)S(1)}, u32[]{:S(2)}, u32[]{:S(2)}) collective-permute-start(f32[32,128]{1,0:T(8,128)S(1)} %add_bitcast_fusion), channel_id=1, source_target_pairs={{0,16},{4,20},{8,24},{12,28},{16,0},{20,4},{24,8},{28,12},{1,17},{... | collective-permute-start | bytes 49160 | tf_op jit(solution)/shard_map/ppermute | solution.py:67
  51.7 2.1 %collective-permute-start.11 = (bf16[16,32,128]{2,0,1:T(8,128)(2,1)S(1)}, bf16[16,32,128]{2,0,1:T(8,128)(2,1)S(1)}, u32[]{:S(2)}, u32[]{:S(2)}) collective-permute-start(bf16[16,32,128]{2,0,1:T(8,128)(2,1)S(1)} %get-tuple-element.27), channel_id=1, source_target_pairs={{8,0},{12,4},{16,8},{20,12},{24,16},{28,20},{0,24},{4,28},{9,1},{1... | collective-permute-start | bytes 393224 | tf_op jit(solution)/shard_map/ppermute | solution.py:22
  53.8 0.5 collective-permute-start.12
  54.2 1.6 %collective-permute-start.13 = (bf16[16,32,128]{2,0,1:T(8,128)(2,1)S(1)}, bf16[16,32,128]{2,0,1:T(8,128)(2,1)S(1)}, u32[]{:S(2)}, u32[]{:S(2)}) collective-permute-start(bf16[16,32,128]{2,0,1:T(8,128)(2,1)S(1)} %get-tuple-element.29), channel_id=1, source_target_pairs={{28,0},{0,4},{4,8},{8,12},{12,16},{16,20},{20,24},{24,28},{29,1},{... | collective-permute-start | bytes 393224 | tf_op jit(solution)/shard_map/ppermute | solution.py:22
  55.8 0.0 collective-permute-start.14
  55.8 0.0 collective-permute-done.15
  55.8 0.0 copy-done.1
  55.8 0.0 copy-done.2
  55.8 0.6 divide_subtract_fusion
  56.5 1.3 %collective-permute-done.11 = bf16[16,32,128]{2,0,1:T(8,128)(2,1)S(1)} collective-permute-done((bf16[16,32,128]{2,0,1:T(8,128)(2,1)S(1)}, bf16[16,32,128]{2,0,1:T(8,128)(2,1)S(1)}, u32[]{:S(2)}, u32[]{:S(2)}) %collective-permute-start.11) | collective-permute-done | bytes 131104 | tf_op jit(solution)/shard_map/ppermute | solution.py:22
  57.8 2.4 %collective-permute-done.12 = bf16[16,32,128]{2,0,1:T(8,128)(2,1)S(1)} collective-permute-done((bf16[16,32,128]{2,0,1:T(8,128)(2,1)S(1)}, bf16[16,32,128]{2,0,1:T(8,128)(2,1)S(1)}, u32[]{:S(2)}, u32[]{:S(2)}) %collective-permute-start.12) | collective-permute-done | bytes 131104 | tf_op jit(solution)/shard_map/ppermute | solution.py:22
  60.1 2.1 %collective-permute-done.13 = bf16[16,32,128]{2,0,1:T(8,128)(2,1)S(1)} collective-permute-done((bf16[16,32,128]{2,0,1:T(8,128)(2,1)S(1)}, bf16[16,32,128]{2,0,1:T(8,128)(2,1)S(1)}, u32[]{:S(2)}, u32[]{:S(2)}) %collective-permute-start.13) | collective-permute-done | bytes 131104 | tf_op jit(solution)/shard_map/ppermute | solution.py:22
  62.3 0.3 collective-permute-done.14
  62.6 0.1 fusion.16
  62.6 0.8 %copy.22 = f32[16,32,128]{2,1,0:T(8,128)} copy(f32[16,32,128]{2,0,1:T(8,128)S(1)} %fusion.16) | data formatting | bytes 524288
  (19 shorter events, 0.3 us)
Async XLA Ops:
  0.6 13.7 %collective-permute-start = (bf16[16,32,128]{2,1,0:T(8,128)(2,1)}, bf16[16,32,128]{2,1,0:T(8,128)(2,1)S(1)}, u32[]{:S(2)}, u32[]{:S(2)}) collective-permute-start(bf16[16,32,128]{2,1,0:T(8,128)(2,1)} %param.9), channel_id=1, source_target_pairs={{24,0},{28,4},{0,8},{4,12},{8,16},{12,20},{16,24},{20,28},{25,1},{... | collective-permute-start | bytes 393224 | tf_op jit(solution)/shard_map/ppermute | solution.py:22
  3.7 10.7 %collective-permute-start.1 = (bf16[16,32,128]{2,1,0:T(8,128)(2,1)}, bf16[16,32,128]{2,1,0:T(8,128)(2,1)S(1)}, u32[]{:S(2)}, u32[]{:S(2)}) collective-permute-start(bf16[16,32,128]{2,1,0:T(8,128)(2,1)} %param.9), channel_id=1, source_target_pairs={{28,0},{0,4},{4,8},{8,12},{12,16},{16,20},{20,24},{24,28},{29,1},{... | collective-permute-start | bytes 393224 | tf_op jit(solution)/shard_map/ppermute | solution.py:22
  5.2 10.2 %collective-permute-start.2 = (bf16[16,32,128]{2,1,0:T(8,128)(2,1)}, bf16[16,32,128]{2,1,0:T(8,128)(2,1)S(1)}, u32[]{:S(2)}, u32[]{:S(2)}) collective-permute-start(bf16[16,32,128]{2,1,0:T(8,128)(2,1)} %param.9), channel_id=1, source_target_pairs={{4,0},{8,4},{12,8},{16,12},{20,16},{24,20},{28,24},{0,28},{5,1},{9... | collective-permute-start | bytes 393224 | tf_op jit(solution)/shard_map/ppermute | solution.py:22
  8.4 7.3 %collective-permute-start.3 = (bf16[16,32,128]{2,1,0:T(8,128)(2,1)}, bf16[16,32,128]{2,1,0:T(8,128)(2,1)S(1)}, u32[]{:S(2)}, u32[]{:S(2)}) collective-permute-start(bf16[16,32,128]{2,1,0:T(8,128)(2,1)} %param.9), channel_id=1, source_target_pairs={{8,0},{12,4},{16,8},{20,12},{24,16},{28,20},{0,24},{4,28},{9,1},{1... | collective-permute-start | bytes 393224 | tf_op jit(solution)/shard_map/ppermute | solution.py:22
  10.5 5.1 %collective-permute-start.4 = (bf16[1,17,32,128]{3,2,1,0:T(8,128)(2,1)S(1)}, bf16[1,17,32,128]{3,2,1,0:T(8,128)(2,1)S(1)}, u32[]{:S(2)}, u32[]{:S(2)}) collective-permute-start(bf16[1,17,32,128]{3,2,1,0:T(8,128)(2,1)S(1)} %get-tuple-element.33), channel_id=1, source_target_pairs={{0,2},{1,3},{2,0},{3,1},{4,6},{5,7},{6,4},{7,5},{8,10},{9,11},{10,... | collective-permute-start | bytes 417800 | tf_op jit(solution)/shard_map/ppermute | solution.py:38
  15.7 1.6 %collective-permute-start.5 = (bf16[2,17,32,128]{3,2,1,0:T(8,128)(2,1)S(1)}, bf16[2,17,32,128]{3,2,1,0:T(8,128)(2,1)S(1)}, u32[]{:S(2)}, u32[]{:S(2)}) collective-permute-start(bf16[2,17,32,128]{3,2,1,0:T(8,128)(2,1)S(1)} %pad_maximum_fusion.2), channel_id=1, source_target_pairs={{0,1},{1,0},{2,3},{3,2},{4,5},{5,4},{6,7},{7,6},{8,9},{9,8},{10,11... | collective-permute-start | bytes 835592 | tf_op jit(solution)/shard_map/ppermute | solution.py:38
  27.7 11.6 %copy-start = (f32[32,128]{1,0:T(8,128)S(1)}, f32[32,128]{1,0:T(8,128)}, u32[]{:S(2)}) copy-start(f32[32,128]{1,0:T(8,128)} %param.14) | copy-start | bytes 49156
  27.7 5.6 %collective-permute-start.6 = (bf16[1,16,32,128]{3,1,2,0:T(8,128)(2,1)S(1)}, bf16[1,16,32,128]{3,1,2,0:T(8,128)(2,1)S(1)}, u32[]{:S(2)}, u32[]{:S(2)}) collective-permute-start(bf16[1,16,32,128]{3,1,2,0:T(8,128)(2,1)S(1)} %bitcast.61), channel_id=1, source_target_pairs={{0,2},{1,3},{2,0},{3,1},{4,6},{5,7},{6,4},{7,5},{8,10},{9,11},{10,... | collective-permute-start | bytes 393224 | tf_op jit(solution)/shard_map/ppermute | solution.py:38
  33.3 1.6 %collective-permute-start.7 = (bf16[2,16,32,128]{3,1,2,0:T(8,128)(2,1)S(1)}, bf16[2,16,32,128]{3,1,2,0:T(8,128)(2,1)S(1)}, u32[]{:S(2)}, u32[]{:S(2)}) collective-permute-start(bf16[2,16,32,128]{3,1,2,0:T(8,128)(2,1)S(1)} %pad_maximum_fusion.3), channel_id=1, source_target_pairs={{0,1},{1,0},{2,3},{3,2},{4,5},{5,4},{6,7},{7,6},{8,9},{9,8},{10,11... | collective-permute-start | bytes 786440 | tf_op jit(solution)/shard_map/ppermute | solution.py:38
  35.8 13.7 %collective-permute-start.8 = (f32[32,128]{1,0:T(8,128)S(1)}, f32[32,128]{1,0:T(8,128)S(1)}, u32[]{:S(2)}, u32[]{:S(2)}) collective-permute-start(f32[32,128]{1,0:T(8,128)S(1)} %bitcast.64), channel_id=1, source_target_pairs={{0,4},{4,0},{8,12},{12,8},{16,20},{20,16},{24,28},{28,24},{1,5},{5... | collective-permute-start | bytes 49160 | tf_op jit(solution)/shard_map/ppermute | solution.py:60
  36.5 12.9 %collective-permute-start.9 = (f32[32,128]{1,0:T(8,128)S(1)}, f32[32,128]{1,0:T(8,128)S(1)}, u32[]{:S(2)}, u32[]{:S(2)}) collective-permute-start(f32[32,128]{1,0:T(8,128)S(1)} %bitcast.65), channel_id=1, source_target_pairs={{0,8},{4,12},{8,0},{12,4},{16,24},{20,28},{24,16},{28,20},{1,9},{5... | collective-permute-start | bytes 49160 | tf_op jit(solution)/shard_map/ppermute | solution.py:60
  37.6 11.9 %collective-permute-start.10 = (f32[32,128]{1,0:T(8,128)S(1)}, f32[32,128]{1,0:T(8,128)S(1)}, u32[]{:S(2)}, u32[]{:S(2)}) collective-permute-start(f32[32,128]{1,0:T(8,128)S(1)} %bitcast.66), channel_id=1, source_target_pairs={{0,12},{4,8},{8,4},{12,0},{16,28},{20,24},{24,20},{28,16},{1,13},{... | collective-permute-start | bytes 49160 | tf_op jit(solution)/shard_map/ppermute | solution.py:60
  47.2 8.6 %copy-start.1 = (f32[32,128]{1,0:T(8,128)S(1)}, f32[32,128]{1,0:T(8,128)}, u32[]{:S(2)}) copy-start(f32[32,128]{1,0:T(8,128)} %param.15) | copy-start | bytes 49156
  47.2 8.6 %copy-start.2 = (f32[32,128]{1,0:T(8,128)S(1)}, f32[32,128]{1,0:T(8,128)}, u32[]{:S(2)}) copy-start(f32[32,128]{1,0:T(8,128)} %param.16) | copy-start | bytes 49156
  49.5 6.3 %collective-permute-start.15 = (f32[32,128]{1,0:T(8,128)S(1)}, f32[32,128]{1,0:T(8,128)S(1)}, u32[]{:S(2)}, u32[]{:S(2)}) collective-permute-start(f32[32,128]{1,0:T(8,128)S(1)} %add_bitcast_fusion), channel_id=1, source_target_pairs={{0,16},{4,20},{8,24},{12,28},{16,0},{20,4},{24,8},{28,12},{1,17},{... | collective-permute-start | bytes 49160 | tf_op jit(solution)/shard_map/ppermute | solution.py:67
  51.7 6.1 %collective-permute-start.11 = (bf16[16,32,128]{2,0,1:T(8,128)(2,1)S(1)}, bf16[16,32,128]{2,0,1:T(8,128)(2,1)S(1)}, u32[]{:S(2)}, u32[]{:S(2)}) collective-permute-start(bf16[16,32,128]{2,0,1:T(8,128)(2,1)S(1)} %get-tuple-element.27), channel_id=1, source_target_pairs={{8,0},{12,4},{16,8},{20,12},{24,16},{28,20},{0,24},{4,28},{9,1},{1... | collective-permute-start | bytes 393224 | tf_op jit(solution)/shard_map/ppermute | solution.py:22
  53.8 6.4 %collective-permute-start.12 = (bf16[16,32,128]{2,0,1:T(8,128)(2,1)S(1)}, bf16[16,32,128]{2,0,1:T(8,128)(2,1)S(1)}, u32[]{:S(2)}, u32[]{:S(2)}) collective-permute-start(bf16[16,32,128]{2,0,1:T(8,128)(2,1)S(1)} %get-tuple-element.30), channel_id=1, source_target_pairs={{4,0},{8,4},{12,8},{16,12},{20,16},{24,20},{28,24},{0,28},{5,1},{9... | collective-permute-start | bytes 393224 | tf_op jit(solution)/shard_map/ppermute | solution.py:22
  54.2 8.0 %collective-permute-start.13 = (bf16[16,32,128]{2,0,1:T(8,128)(2,1)S(1)}, bf16[16,32,128]{2,0,1:T(8,128)(2,1)S(1)}, u32[]{:S(2)}, u32[]{:S(2)}) collective-permute-start(bf16[16,32,128]{2,0,1:T(8,128)(2,1)S(1)} %get-tuple-element.29), channel_id=1, source_target_pairs={{28,0},{0,4},{4,8},{8,12},{12,16},{16,20},{20,24},{24,28},{29,1},{... | collective-permute-start | bytes 393224 | tf_op jit(solution)/shard_map/ppermute | solution.py:22
  55.8 6.8 %collective-permute-start.14 = (bf16[16,32,128]{2,0,1:T(8,128)(2,1)S(1)}, bf16[16,32,128]{2,0,1:T(8,128)(2,1)S(1)}, u32[]{:S(2)}, u32[]{:S(2)}) collective-permute-start(bf16[16,32,128]{2,0,1:T(8,128)(2,1)S(1)} %get-tuple-element.28), channel_id=1, source_target_pairs={{24,0},{28,4},{0,8},{4,12},{8,16},{12,20},{16,24},{20,28},{25,1},{... | collective-permute-start | bytes 393224 | tf_op jit(solution)/shard_map/ppermute | solution.py:22

commit v20 on v11

--- a/solution.py
+++ b/solution.py
@@ -46,14 +46,15 @@
     return whole
 
 
-def summed_over(block, axis):
+def summed_over(block, axis, first=1, last=None):
     size = lax.axis_size(axis)
     if size & (size - 1):
-        return lax.psum(block, axis)
+        return lax.psum(block, axis) if first == 1 else block
+    last = size if last is None else min(last, size)
     own = lax.axis_index(axis)
-    stride = 1
-    while stride < size:
-        if stride * 4 <= size:
+    stride = first
+    while stride < last:
+        if stride * 4 <= last:
             held = [block]
             for k in (1, 2, 3):
                 route = [(i, i ^ (k * stride)) for i in range(size)]
@@ -131,10 +132,8 @@
     sources = jnp.einsum(
         "ts,sfk->tfk", pick_source, nearby, preferred_element_type=jnp.float32
     ).astype(jnp.bfloat16)
-    tiles_turned = jnp.swapaxes(tile_values, 1, 2)
-    tiles_turned, nearby = lax.optimization_barrier((tiles_turned, nearby))
     forward_terms = jnp.einsum(
-        "tfk,tkj->tfj", sources, tiles_turned, preferred_element_type=jnp.float32
+        "tfk,tjk->tfj", sources, tile_values, preferred_element_type=jnp.float32
     )
     aggregate = summed_by_table(add_row, forward_terms, "tb,tfj->bfj")
     aggregate = aggregate.astype(jnp.bfloat16)
@@ -148,7 +147,7 @@
     slope_all = (cotangent_all.astype(jnp.float32) * elu_slope(preact)).astype(jnp.bfloat16)
     node_total = cycle_size * blocks * tile_size
     grad_local = jnp.einsum("bij,boj->io", aggregate, slope_all, preferred_element_type=jnp.float32)
-    grad = summed_over(grad_local, "node") * (1.0 / math.sqrt(node_total))
+    grad_partial = summed_over(grad_local, "node", last=4)
     back_rows = jnp.einsum(
         "io,boj->bij", weight_half, slope_all, preferred_element_type=jnp.float32
     ).astype(jnp.bfloat16)
@@ -161,10 +160,17 @@
     outgoing = summed_by_table(add_source, back_terms, "ts,tfk->sfk")
     outgoing = outgoing.reshape(2 * REACH + 1, blocks, width_local, tile_size)
     feature_grad = outgoing[REACH]
+    received = []
     for distance in range(-REACH, REACH + 1):
         if distance != 0:
             sent = outgoing[distance + REACH].astype(jnp.bfloat16)
-            feature_grad = feature_grad + passed_along(sent, "node", distance).astype(jnp.float32)
+            received.append(passed_along(sent, "node", distance))
+    grad_partial, activated, received[0] = lax.optimization_barrier(
+        (grad_partial, activated, received[0])
+    )
+    grad = summed_over(grad_partial, "node", first=4) * (1.0 / math.sqrt(node_total))
+    for piece in received:
+        feature_grad = feature_grad + piece.astype(jnp.float32)
     new_first = first_decay * first_moment + (1.0 - first_decay) * grad
     new_second = second_decay * second_moment + (1.0 - second_decay) * grad * grad
     new_weight = weight - learn_rate * (new_first / first_fix) / (

time: 68 us -> 63.5 us (0.934)
  starting transfers between devices: 25.4 us -> 23 us
  waiting for transfers between devices: 13.2 us -> 11.1 us
    ppermute x8, waiting for transfers between devices: 6.03 us -> 4.18 us  [passed_along(): return lax.ppermute(block, axis, route)]
    ppermute x8, starting transfers between devices: 17.6 us -> 15.9 us  [passed_along(): return lax.ppermute(block, axis, route)]
    ppermute x3, starting transfers between devices: 4.5 us -> 3.49 us  [summed_over(): held.append(lax.ppermute(block, axis, route))]
  transfers between devices with their start and end apart: 16 -> 16, of which waited for: 7 -> 6; matrix products, arithmetic and copies ran while one was open for 22% -> 25% of each run, Pallas kernels for 0% -> 0%
where the time goes in v20:
time: 63.5 us; the launch traced here: 63.1 us
  starting transfers between devices  23 us (36%)
  matrix products  19.4 us (31%)
  waiting for transfers between devices  11.1 us (17%)
  other arithmetic  5.4 us (9%)
  local copies, waits for them, and re-layouts  2.6 us (4%)
  between operations  1.65 us (3%)
    ppermute x8, starting transfers between devices, passed_along(): return lax.ppermute(block, axis, route)  15.9 us
    dot_general x1, matrix products, per_device(): jnp.einsum('tfk,tjk->tfj', sources, tile_values, preferred_element_type=j...  7.92 us
    ppermute x4, waiting for transfers between devices, gathered_along(): got = lax.ppermute(held, axis, [(i, i ^ mask) for i in range(size)])  6.87 us
    dot_general x1, matrix products, per_device(): jnp.einsum('tfj,tjk->tfk', back_sources, tile_values, preferred_element_t...  5.99 us
    ppermute x8, waiting for transfers between devices, passed_along(): return lax.ppermute(block, axis, route)  4.18 us
    ppermute x4, starting transfers between devices, gathered_along(): got = lax.ppermute(held, axis, [(i, i ^ mask) for i in range(size)])  3.57 us
    ppermute x3, starting transfers between devices, summed_over(): held.append(lax.ppermute(block, axis, route))  3.49 us
    dot_general x2, matrix products, summed_by_table(): return jnp.einsum(spec, doubled, both, preferred_element_type=jnp.float32)  2.74 us
  transfers between devices with their start and end apart: 16, of which 6 were waited for; matrix products, arithmetic and copies ran while one was open for 25% of the time, Pallas kernels for 0%

profile of v20, /device:TPU:0, one launch (start us, length us, event | category | flops | bytes accessed | tf_op | source)
XLA Modules:
  0.0 63.1 jit_solution(14117550399007312487)
XLA Ops:
  0.6 3.1 %collective-permute-start = (bf16[16,32,128]{2,1,0:T(8,128)(2,1)}, bf16[16,32,128]{2,1,0:T(8,128)(2,1)S(1)}, u32[]{:S(2)}, u32[]{:S(2)}) collective-permute-start(bf16[16,32,128]{2,1,0:T(8,128)(2,1)} %param.9), channel_id=1, source_target_pairs={{24,0},{28,4},{0,8},{4,12},{8,16},{12,20},{16,24},{20,28},{25,1},{... | collective-permute-start | bytes 393224 | tf_op jit(solution)/shard_map/ppermute | solution.py:22
  3.7 1.5 %collective-permute-start.1 = (bf16[16,32,128]{2,1,0:T(8,128)(2,1)}, bf16[16,32,128]{2,1,0:T(8,128)(2,1)S(1)}, u32[]{:S(2)}, u32[]{:S(2)}) collective-permute-start(bf16[16,32,128]{2,1,0:T(8,128)(2,1)} %param.9), channel_id=1, source_target_pairs={{28,0},{0,4},{4,8},{8,12},{12,16},{16,20},{20,24},{24,28},{29,1},{... | collective-permute-start | bytes 393224 | tf_op jit(solution)/shard_map/ppermute | solution.py:22
  5.2 3.2 %collective-permute-start.2 = (bf16[16,32,128]{2,1,0:T(8,128)(2,1)}, bf16[16,32,128]{2,1,0:T(8,128)(2,1)S(1)}, u32[]{:S(2)}, u32[]{:S(2)}) collective-permute-start(bf16[16,32,128]{2,1,0:T(8,128)(2,1)} %param.9), channel_id=1, source_target_pairs={{4,0},{8,4},{12,8},{16,12},{20,16},{24,20},{28,24},{0,28},{5,1},{9... | collective-permute-start | bytes 393224 | tf_op jit(solution)/shard_map/ppermute | solution.py:22
  8.4 0.3 collective-permute-start.3
  8.7 0.7 %convert_bitcast_fusion = bf16[1,32,128]{2,1,0:T(8,128)(2,1)S(1)} fusion(f32[32,128]{1,0:T(8,128)} %param.14), kind=kLoop, calls=%fused_computation.76 | loop fusion | flops 4096 | bytes 24576 | tf_op jit(solution)/shard_map/broadcast_in_dim | solution.py:127
  9.4 0.1 broadcast_in_dim.11
  9.6 1.0 %fusion.21 = (bf16[1,17,32,128]{3,2,1,0:T(8,128)(2,1)S(1)}, bf16[17,128,128]{2,1,0:T(8,128)(2,1)S(1)}) fusion(bf16[1,32,128]{2,1,0:T(8,128)(2,1)S(1)} %convert_bitcast_fusion, bf16[16,32,128]{2,1,0:T(8,128)(2,1)} %param.17, bf16[17,128,128]{2,1,0:T(8,128)(2,1)S(1)} %broadcast_in_dim.11, s32[]{:T(128)S(6)} %select_n.73), kind=kLoop, calls=%fused_computation.45 | loop fusion | flops 278528 | bytes 417796 | tf_op jit(solution)/shard_map/stack | solution.py:37
  10.5 1.7 %collective-permute-start.4 = (bf16[1,17,32,128]{3,2,1,0:T(8,128)(2,1)S(1)}, bf16[1,17,32,128]{3,2,1,0:T(8,128)(2,1)S(1)}, u32[]{:S(2)}, u32[]{:S(2)}) collective-permute-start(bf16[1,17,32,128]{3,2,1,0:T(8,128)(2,1)S(1)} %get-tuple-element.35), channel_id=1, source_target_pairs={{0,2},{1,3},{2,0},{3,1},{4,6},{5,7},{6,4},{7,5},{8,10},{9,11},{10,... | collective-permute-start | bytes 417800 | tf_op jit(solution)/shard_map/ppermute | solution.py:38
  12.9 0.7 %broadcast_subtract_fusion = s32[256]{0:T(256)S(1)} fusion(s32[256]{0:T(256)} %param.11, s32[]{:T(128)S(6)} %mul.82), kind=kLoop, calls=%fused_computation.91 | loop fusion | flops 256 | bytes 2052 | tf_op jit(solution)/shard_map/sub | solution.py:108
  13.6 0.7 %fusion.37 = s32[256]{0:T(256)S(1)} fusion(s32[256]{0:T(256)} %param.12, s32[]{:T(128)S(6)} %axis_index.15), kind=kLoop, calls=%fused_computation.87 | loop fusion | flops 9472 | bytes 2052 | tf_op jit(solution)/shard_map/add | solution.py:113
  14.4 0.0 collective-permute-done
  14.4 0.0 collective-permute-done.1
  14.4 0.9 %constant_dynamic-update-slice_fusion.2 = bf16[80,32,128]{2,1,0:T(8,128)(2,1)S(1)} fusion(bf16[80,32,128]{2,1,0:T(8,128)(2,1)S(1)} %constant_dynamic-update-slice_fusion.3, bf16[16,32,128]{2,1,0:T(8,128)(2,1)} %param.9), kind=kLoop, calls=%fused_computation.70 | loop fusion | bytes 262144
  15.4 0.0 collective-permute-done.2
  15.4 0.2 collective-permute-done.4
  15.7 0.1 collective-permute-start.5
  15.8 0.0 collective-permute-done.3
  15.8 1.5 %collective-permute-done.5 = bf16[2,17,32,128]{3,2,1,0:T(8,128)(2,1)S(1)} collective-permute-done((bf16[2,17,32,128]{3,2,1,0:T(8,128)(2,1)S(1)}, bf16[2,17,32,128]{3,2,1,0:T(8,128)(2,1)S(1)}, u32[]{:S(2)}, u32[]{:S(2)}) %collective-permute-start.5) | collective-permute-done | bytes 278560 | tf_op jit(solution)/shard_map/ppermute | solution.py:38
  17.4 0.8 %fusion.12 = bf16[256,32,128]{2,0,1:T(8,128)(2,1)S(1)} fusion(bf16[80,32,128]{2,1,0:T(8,128)(2,1)S(1)} %constant_dynamic-update-slice_fusion, s32[256]{0:T(256)S(1)} %fusion.37), kind=kOutput, calls=%fused_computation.21 | convolution fusion | flops 167792640 | bytes 2753536 | tf_op jit(solution)/shard_map/ts,sfk->tfk/dot_general | solution.py:132
  18.2 7.9 %reduce-precision_convert_fusion.1 = (bf16[256,32,128]{2,1,0:T(8,128)(2,1)S(1)}, bf16[256,32,128]{2,1,0:T(8,128)(2,1)S(1)}) fusion(bf16[256,128,128]{2,1,0:T(8,128)(2,1)} %param.10, bf16[256,32,128]{2,0,1:T(8,128)(2,1)S(1)} %fusion.12), kind=kOutput, calls=%fused_computation.3 | convolution fusion | flops 272629760 | bytes 14680064 | tf_op jit(solution)/shard_map/tfk,tjk->tfj/dot_general | solution.py:135
  26.1 0.4 pad_maximum_fusion
  26.5 1.2 %fusion.9 = bf16[16,32,128]{2,0,1:T(8,128)(2,1)S(1)} fusion(bf16[512,32,128]{2,1,0:T(8,128)(2,1)S(1)} %pad_maximum_fusion, bf16[256,16]{0,1:T(8,128)(2,1)S(1)} %select_convert_fusion.2), kind=kOutput, calls=%fused_computation.19 | convolution fusion | flops 67207168 | bytes 4333568 | tf_op jit(solution)/shard_map/tb,tfj->bfj/dot_general | solution.py:79
  27.7 1.7 %collective-permute-start.6 = (bf16[1,16,32,128]{3,1,2,0:T(8,128)(2,1)S(1)}, bf16[1,16,32,128]{3,1,2,0:T(8,128)(2,1)S(1)}, u32[]{:S(2)}, u32[]{:S(2)}) collective-permute-start(bf16[1,16,32,128]{3,1,2,0:T(8,128)(2,1)S(1)} %bitcast.61), channel_id=1, source_target_pairs={{0,2},{1,3},{2,0},{3,1},{4,6},{5,7},{6,4},{7,5},{8,10},{9,11},{10,... | collective-permute-start | bytes 393224 | tf_op jit(solution)/shard_map/ppermute | solution.py:38
  29.4 3.8 %collective-permute-done.6 = bf16[1,16,32,128]{3,1,2,0:T(8,128)(2,1)S(1)} collective-permute-done((bf16[1,16,32,128]{3,1,2,0:T(8,128)(2,1)S(1)}, bf16[1,16,32,128]{3,1,2,0:T(8,128)(2,1)S(1)}, u32[]{:S(2)}, u32[]{:S(2)}) %collective-permute-start.6) | collective-permute-done | bytes 131104 | tf_op jit(solution)/shard_map/ppermute | solution.py:38
  33.3 0.1 collective-permute-start.7
  33.4 0.1 broadcast_in_dim.13
  33.5 0.1 copy_dynamic-update-slice_fusion.3
  33.5 0.1 copy_dynamic-update-slice_fusion.2
  33.6 1.3 %collective-permute-done.7 = bf16[2,16,32,128]{3,1,2,0:T(8,128)(2,1)S(1)} collective-permute-done((bf16[2,16,32,128]{3,1,2,0:T(8,128)(2,1)S(1)}, bf16[2,16,32,128]{3,1,2,0:T(8,128)(2,1)S(1)}, u32[]{:S(2)}, u32[]{:S(2)}) %collective-permute-start.7) | collective-permute-done | bytes 262176 | tf_op jit(solution)/shard_map/ppermute | solution.py:38
  34.9 0.1 copy_dynamic-update-slice_fusion.1
  35.0 0.1 copy_dynamic-update-slice_fusion
  35.0 0.3 broadcast_compare_fusion
  35.4 0.4 fusion.19
  35.8 0.0 collective-permute-start.10
  35.8 2.2 %collective-permute-start.9 = (f32[32,128]{1,0:T(8,128)S(1)}, f32[32,128]{1,0:T(8,128)S(1)}, u32[]{:S(2)}, u32[]{:S(2)}) collective-permute-start(f32[32,128]{1,0:T(8,128)S(1)} %bitcast.65), channel_id=1, source_target_pairs={{0,8},{4,12},{8,0},{12,4},{16,24},{20,28},{24,16},{28,20},{1,9},{5... | collective-permute-start | bytes 49160 | tf_op jit(solution)/shard_map/ppermute | solution.py:61
  38.0 1.3 %collective-permute-start.8 = (f32[32,128]{1,0:T(8,128)S(1)}, f32[32,128]{1,0:T(8,128)S(1)}, u32[]{:S(2)}, u32[]{:S(2)}) collective-permute-start(f32[32,128]{1,0:T(8,128)S(1)} %bitcast.66), channel_id=1, source_target_pairs={{0,4},{4,0},{8,12},{12,8},{16,20},{20,16},{24,28},{28,24},{1,5},{5... | collective-permute-start | bytes 49160 | tf_op jit(solution)/shard_map/ppermute | solution.py:61
  39.3 0.0 copy-done
  39.3 0.5 fusion.8
  39.8 0.2 copy.26
  40.0 0.7 %fusion.32 = bf16[256,32,128]{2,0,1:T(8,128)(2,1)S(1)} fusion(bf16[16,32,128]{2,0,1:T(8,128)(2,1)S(1)} %copy.26, s32[256]{0:T(256)S(1)} %broadcast_subtract_fusion), kind=kOutput, calls=%fused_computation.67 | convolution fusion | flops 33558528 | bytes 2229248 | tf_op jit(solution)/shard_map/tb,bfj->tfj/dot_general | solution.py:154
  40.8 6.0 %reduce-precision_convert_fusion = (bf16[256,32,128]{2,1,0:T(8,128)(2,1)S(1)}, bf16[256,32,128]{2,1,0:T(8,128)(2,1)S(1)}) fusion(bf16[256,128,128]{2,1,0:T(8,128)(2,1)} %param.10, bf16[256,32,128]{2,0,1:T(8,128)(2,1)S(1)} %fusion.32), kind=kOutput, calls=%fused_computation.1 | convolution fusion | flops 272629760 | bytes 14680064 | tf_op jit(solution)/shard_map/tfj,tjk->tfk/dot_general | solution.py:157
  46.8 0.4 pad_maximum_fusion.1
  47.2 0.0 copy-start.1
  47.2 0.0 copy-start.2
  47.2 1.5 %fusion.44 = (bf16[80,32,128]{2,0,1:T(8,128)(2,1)S(1)}, f32[80,32,128]{2,0,1:T(8,128)S(1)}) fusion(bf16[512,32,128]{2,1,0:T(8,128)(2,1)S(1)} %pad_maximum_fusion.1, bf16[256,80]{0,1:T(8,128)(2,1)S(1)} %select_convert_fusion.1), kind=kOutput, calls=%fused_computation.95 | convolution fusion | flops 336035840 | bytes 6201344 | tf_op jit(solution)/shard_map/ts,tfk->sfk/dot_general | solution.py:79
  48.7 0.8 %select_convert_fusion = bf16[16,32,128]{2,1,0:T(8,128)(2,1)} fusion(f32[16,128,128]{2,1,0:T(8,128)S(1)} %get-tuple-element.38, s32[]{:T(128)S(6)} %select_n.73, pred[16,128,128]{2,1,0:T(8,128)(4,1)S(1)} %get-tuple-element.37), kind=kLoop, calls=%fused_computation.30 | loop fusion | flops 196608 | bytes 458756 | tf_op jit(solution)/shard_map/convert_element_type | solution.py:146
  49.5 3.1 %collective-permute-start.11 = (bf16[16,32,128]{2,0,1:T(8,128)(2,1)S(1)}, bf16[16,32,128]{2,0,1:T(8,128)(2,1)S(1)}, u32[]{:S(2)}, u32[]{:S(2)}) collective-permute-start(bf16[16,32,128]{2,0,1:T(8,128)(2,1)S(1)} %get-tuple-element.32), channel_id=1, source_target_pairs={{8,0},{12,4},{16,8},{20,12},{24,16},{28,20},{0,24},{4,28},{9,1},{1... | collective-permute-start | bytes 393224 | tf_op jit(solution)/shard_map/ppermute | solution.py:22
  52.6 0.0 collective-permute-start.14
  52.6 0.0 collective-permute-done.10
  52.6 0.0 collective-permute-start.13
  52.6 0.0 collective-permute-done.9
  52.6 4.7 %collective-permute-start.12 = (bf16[16,32,128]{2,0,1:T(8,128)(2,1)S(1)}, bf16[16,32,128]{2,0,1:T(8,128)(2,1)S(1)}, u32[]{:S(2)}, u32[]{:S(2)}) collective-permute-start(bf16[16,32,128]{2,0,1:T(8,128)(2,1)S(1)} %get-tuple-element.29), channel_id=1, source_target_pairs={{4,0},{8,4},{12,8},{16,12},{20,16},{24,20},{28,24},{0,28},{5,1},{9... | collective-permute-start | bytes 393224 | tf_op jit(solution)/shard_map/ppermute | solution.py:22
  57.3 0.0 collective-permute-done.8
  57.4 0.0 collective-permute-done.11
  57.4 0.1 collective-permute-start.15
  57.5 3.0 %collective-permute-done.14 = bf16[16,32,128]{2,0,1:T(8,128)(2,1)S(1)} collective-permute-done((bf16[16,32,128]{2,0,1:T(8,128)(2,1)S(1)}, bf16[16,32,128]{2,0,1:T(8,128)(2,1)S(1)}, u32[]{:S(2)}, u32[]{:S(2)}) %collective-permute-start.14) | collective-permute-done | bytes 131104 | tf_op jit(solution)/shard_map/ppermute | solution.py:22
  60.4 1.2 %collective-permute-done.13 = bf16[16,32,128]{2,0,1:T(8,128)(2,1)S(1)} collective-permute-done((bf16[16,32,128]{2,0,1:T(8,128)(2,1)S(1)}, bf16[16,32,128]{2,0,1:T(8,128)(2,1)S(1)}, u32[]{:S(2)}, u32[]{:S(2)}) %collective-permute-start.13) | collective-permute-done | bytes 131104 | tf_op jit(solution)/shard_map/ppermute | solution.py:22
  61.6 0.0 collective-permute-done.12
  61.6 0.1 fusion.16
  61.7 0.8 %copy.22 = f32[16,32,128]{2,1,0:T(8,128)} copy(f32[16,32,128]{2,0,1:T(8,128)S(1)} %fusion.16) | data formatting | bytes 524288
  62.5 0.0 collective-permute-done.15
  62.5 0.0 copy-done.1
  62.5 0.0 copy-done.2
  62.5 0.6 %divide_subtract_fusion = (f32[32,128]{1,0:T(8,128)}, f32[32,128]{1,0:T(8,128)}, f32[32,128]{1,0:T(8,128)}) fusion(f32[32,128]{1,0:T(8,128)S(1)} %copy-done, f32[32,128]{1,0:T(8,128)S(1)} %add_bitcast_fusion, f32[32,128]{1,0:T(8,128)S(1)} %collective-permute-done.15, f32[32,128]{1,0:T(8,128)S(1)} %copy-done.1, f32[32,128]{1,0:T(8,128)S(1)} %copy-done.2), kind=kLoop, calls=%fused_computation.60 | loop fusion | flops 57344 | bytes 131072 | tf_op jit(solution)/shard_map/sub | solution.py:176
  (19 shorter events, 0.3 us)
Async XLA Ops:
  0.6 13.7 %collective-permute-start = (bf16[16,32,128]{2,1,0:T(8,128)(2,1)}, bf16[16,32,128]{2,1,0:T(8,128)(2,1)S(1)}, u32[]{:S(2)}, u32[]{:S(2)}) collective-permute-start(bf16[16,32,128]{2,1,0:T(8,128)(2,1)} %param.9), channel_id=1, source_target_pairs={{24,0},{28,4},{0,8},{4,12},{8,16},{12,20},{16,24},{20,28},{25,1},{... | collective-permute-start | bytes 393224 | tf_op jit(solution)/shard_map/ppermute | solution.py:22
  3.7 10.7 %collective-permute-start.1 = (bf16[16,32,128]{2,1,0:T(8,128)(2,1)}, bf16[16,32,128]{2,1,0:T(8,128)(2,1)S(1)}, u32[]{:S(2)}, u32[]{:S(2)}) collective-permute-start(bf16[16,32,128]{2,1,0:T(8,128)(2,1)} %param.9), channel_id=1, source_target_pairs={{28,0},{0,4},{4,8},{8,12},{12,16},{16,20},{20,24},{24,28},{29,1},{... | collective-permute-start | bytes 393224 | tf_op jit(solution)/shard_map/ppermute | solution.py:22
  5.2 10.2 %collective-permute-start.2 = (bf16[16,32,128]{2,1,0:T(8,128)(2,1)}, bf16[16,32,128]{2,1,0:T(8,128)(2,1)S(1)}, u32[]{:S(2)}, u32[]{:S(2)}) collective-permute-start(bf16[16,32,128]{2,1,0:T(8,128)(2,1)} %param.9), channel_id=1, source_target_pairs={{4,0},{8,4},{12,8},{16,12},{20,16},{24,20},{28,24},{0,28},{5,1},{9... | collective-permute-start | bytes 393224 | tf_op jit(solution)/shard_map/ppermute | solution.py:22
  8.4 7.3 %collective-permute-start.3 = (bf16[16,32,128]{2,1,0:T(8,128)(2,1)}, bf16[16,32,128]{2,1,0:T(8,128)(2,1)S(1)}, u32[]{:S(2)}, u32[]{:S(2)}) collective-permute-start(bf16[16,32,128]{2,1,0:T(8,128)(2,1)} %param.9), channel_id=1, source_target_pairs={{8,0},{12,4},{16,8},{20,12},{24,16},{28,20},{0,24},{4,28},{9,1},{1... | collective-permute-start | bytes 393224 | tf_op jit(solution)/shard_map/ppermute | solution.py:22
  10.5 5.1 %collective-permute-start.4 = (bf16[1,17,32,128]{3,2,1,0:T(8,128)(2,1)S(1)}, bf16[1,17,32,128]{3,2,1,0:T(8,128)(2,1)S(1)}, u32[]{:S(2)}, u32[]{:S(2)}) collective-permute-start(bf16[1,17,32,128]{3,2,1,0:T(8,128)(2,1)S(1)} %get-tuple-element.35), channel_id=1, source_target_pairs={{0,2},{1,3},{2,0},{3,1},{4,6},{5,7},{6,4},{7,5},{8,10},{9,11},{10,... | collective-permute-start | bytes 417800 | tf_op jit(solution)/shard_map/ppermute | solution.py:38
  15.7 1.6 %collective-permute-start.5 = (bf16[2,17,32,128]{3,2,1,0:T(8,128)(2,1)S(1)}, bf16[2,17,32,128]{3,2,1,0:T(8,128)(2,1)S(1)}, u32[]{:S(2)}, u32[]{:S(2)}) collective-permute-start(bf16[2,17,32,128]{3,2,1,0:T(8,128)(2,1)S(1)} %pad_maximum_fusion.2), channel_id=1, source_target_pairs={{0,1},{1,0},{2,3},{3,2},{4,5},{5,4},{6,7},{7,6},{8,9},{9,8},{10,11... | collective-permute-start | bytes 835592 | tf_op jit(solution)/shard_map/ppermute | solution.py:38
  27.7 11.6 %copy-start = (f32[32,128]{1,0:T(8,128)S(1)}, f32[32,128]{1,0:T(8,128)}, u32[]{:S(2)}) copy-start(f32[32,128]{1,0:T(8,128)} %param.14) | copy-start | bytes 49156
  27.7 5.6 %collective-permute-start.6 = (bf16[1,16,32,128]{3,1,2,0:T(8,128)(2,1)S(1)}, bf16[1,16,32,128]{3,1,2,0:T(8,128)(2,1)S(1)}, u32[]{:S(2)}, u32[]{:S(2)}) collective-permute-start(bf16[1,16,32,128]{3,1,2,0:T(8,128)(2,1)S(1)} %bitcast.61), channel_id=1, source_target_pairs={{0,2},{1,3},{2,0},{3,1},{4,6},{5,7},{6,4},{7,5},{8,10},{9,11},{10,... | collective-permute-start | bytes 393224 | tf_op jit(solution)/shard_map/ppermute | solution.py:38
  33.3 1.6 %collective-permute-start.7 = (bf16[2,16,32,128]{3,1,2,0:T(8,128)(2,1)S(1)}, bf16[2,16,32,128]{3,1,2,0:T(8,128)(2,1)S(1)}, u32[]{:S(2)}, u32[]{:S(2)}) collective-permute-start(bf16[2,16,32,128]{3,1,2,0:T(8,128)(2,1)S(1)} %pad_maximum_fusion.3), channel_id=1, source_target_pairs={{0,1},{1,0},{2,3},{3,2},{4,5},{5,4},{6,7},{7,6},{8,9},{9,8},{10,11... | collective-permute-start | bytes 786440 | tf_op jit(solution)/shard_map/ppermute | solution.py:38
  35.8 16.8 %collective-permute-start.10 = (f32[32,128]{1,0:T(8,128)S(1)}, f32[32,128]{1,0:T(8,128)S(1)}, u32[]{:S(2)}, u32[]{:S(2)}) collective-permute-start(f32[32,128]{1,0:T(8,128)S(1)} %bitcast.64), channel_id=1, source_target_pairs={{0,12},{4,8},{8,4},{12,0},{16,28},{20,24},{24,20},{28,16},{1,13},{... | collective-permute-start | bytes 49160 | tf_op jit(solution)/shard_map/ppermute | solution.py:61
  35.8 16.8 %collective-permute-start.9 = (f32[32,128]{1,0:T(8,128)S(1)}, f32[32,128]{1,0:T(8,128)S(1)}, u32[]{:S(2)}, u32[]{:S(2)}) collective-permute-start(f32[32,128]{1,0:T(8,128)S(1)} %bitcast.65), channel_id=1, source_target_pairs={{0,8},{4,12},{8,0},{12,4},{16,24},{20,28},{24,16},{28,20},{1,9},{5... | collective-permute-start | bytes 49160 | tf_op jit(solution)/shard_map/ppermute | solution.py:61
  38.0 19.3 %collective-permute-start.8 = (f32[32,128]{1,0:T(8,128)S(1)}, f32[32,128]{1,0:T(8,128)S(1)}, u32[]{:S(2)}, u32[]{:S(2)}) collective-permute-start(f32[32,128]{1,0:T(8,128)S(1)} %bitcast.66), channel_id=1, source_target_pairs={{0,4},{4,0},{8,12},{12,8},{16,20},{20,16},{24,28},{28,24},{1,5},{5... | collective-permute-start | bytes 49160 | tf_op jit(solution)/shard_map/ppermute | solution.py:61
  47.2 15.4 %copy-start.1 = (f32[32,128]{1,0:T(8,128)S(1)}, f32[32,128]{1,0:T(8,128)}, u32[]{:S(2)}) copy-start(f32[32,128]{1,0:T(8,128)} %param.15) | copy-start | bytes 49156
  47.2 15.3 %copy-start.2 = (f32[32,128]{1,0:T(8,128)S(1)}, f32[32,128]{1,0:T(8,128)}, u32[]{:S(2)}) copy-start(f32[32,128]{1,0:T(8,128)} %param.16) | copy-start | bytes 49156
  49.5 7.9 %collective-permute-start.11 = (bf16[16,32,128]{2,0,1:T(8,128)(2,1)S(1)}, bf16[16,32,128]{2,0,1:T(8,128)(2,1)S(1)}, u32[]{:S(2)}, u32[]{:S(2)}) collective-permute-start(bf16[16,32,128]{2,0,1:T(8,128)(2,1)S(1)} %get-tuple-element.32), channel_id=1, source_target_pairs={{8,0},{12,4},{16,8},{20,12},{24,16},{28,20},{0,24},{4,28},{9,1},{1... | collective-permute-start | bytes 393224 | tf_op jit(solution)/shard_map/ppermute | solution.py:22
  52.6 7.8 %collective-permute-start.14 = (bf16[16,32,128]{2,0,1:T(8,128)(2,1)S(1)}, bf16[16,32,128]{2,0,1:T(8,128)(2,1)S(1)}, u32[]{:S(2)}, u32[]{:S(2)}) collective-permute-start(bf16[16,32,128]{2,0,1:T(8,128)(2,1)S(1)} %get-tuple-element.30), channel_id=1, source_target_pairs={{24,0},{28,4},{0,8},{4,12},{8,16},{12,20},{16,24},{20,28},{25,1},{... | collective-permute-start | bytes 393224 | tf_op jit(solution)/shard_map/ppermute | solution.py:22
  52.6 9.0 %collective-permute-start.13 = (bf16[16,32,128]{2,0,1:T(8,128)(2,1)S(1)}, bf16[16,32,128]{2,0,1:T(8,128)(2,1)S(1)}, u32[]{:S(2)}, u32[]{:S(2)}) collective-permute-start(bf16[16,32,128]{2,0,1:T(8,128)(2,1)S(1)} %get-tuple-element.31), channel_id=1, source_target_pairs={{28,0},{0,4},{4,8},{8,12},{12,16},{16,20},{20,24},{24,28},{29,1},{... | collective-permute-start | bytes 393224 | tf_op jit(solution)/shard_map/ppermute | solution.py:22
  52.6 9.0 %collective-permute-start.12 = (bf16[16,32,128]{2,0,1:T(8,128)(2,1)S(1)}, bf16[16,32,128]{2,0,1:T(8,128)(2,1)S(1)}, u32[]{:S(2)}, u32[]{:S(2)}) collective-permute-start(bf16[16,32,128]{2,0,1:T(8,128)(2,1)S(1)} %get-tuple-element.29), channel_id=1, source_target_pairs={{4,0},{8,4},{12,8},{16,12},{20,16},{24,20},{28,24},{0,28},{5,1},{9... | collective-permute-start | bytes 393224 | tf_op jit(solution)/shard_map/ppermute | solution.py:22
  57.4 5.1 %collective-permute-start.15 = (f32[32,128]{1,0:T(8,128)S(1)}, f32[32,128]{1,0:T(8,128)S(1)}, u32[]{:S(2)}, u32[]{:S(2)}) collective-permute-start(f32[32,128]{1,0:T(8,128)S(1)} %add_bitcast_fusion), channel_id=1, source_target_pairs={{0,16},{4,20},{8,24},{12,28},{16,0},{20,4},{24,8},{28,12},{1,17},{... | collective-permute-start | bytes 49160 | tf_op jit(solution)/shard_map/ppermute | solution.py:68

commit v21 on v20

--- a/solution.py
+++ b/solution.py
@@ -142,8 +142,7 @@
     preact = jnp.einsum(
         "bij,io->boj", aggregate_all, weight_all, preferred_element_type=jnp.float32
     )
-    activated = lax.dynamic_slice_in_dim(jax.nn.elu(preact), column_start, width_local, 1)
-    activated = activated.astype(jnp.bfloat16)
+    preact_local = lax.dynamic_slice_in_dim(preact, column_start, width_local, 1)
     slope_all = (cotangent_all.astype(jnp.float32) * elu_slope(preact)).astype(jnp.bfloat16)
     node_total = cycle_size * blocks * tile_size
     grad_local = jnp.einsum("bij,boj->io", aggregate, slope_all, preferred_element_type=jnp.float32)
@@ -165,9 +164,10 @@
         if distance != 0:
             sent = outgoing[distance + REACH].astype(jnp.bfloat16)
             received.append(passed_along(sent, "node", distance))
-    grad_partial, activated, received[0] = lax.optimization_barrier(
-        (grad_partial, activated, received[0])
-    )
+    grad_partial, preact_local, received[0] = lax.optimization_barrier(
+        (grad_partial, preact_local, received[0])
+    )
+    activated = jax.nn.elu(preact_local).astype(jnp.bfloat16)
     grad = summed_over(grad_partial, "node", first=4) * (1.0 / math.sqrt(node_total))
     for piece in received:
         feature_grad = feature_grad + piece.astype(jnp.float32)

time: 63.5 us -> 63.5 us (level)
  no operation moved by 1% of the time
where the time goes in v21:
time: 63.5 us; the launch traced here: 63.2 us
  starting transfers between devices  23.1 us (36%)
  matrix products  19.4 us (31%)
  waiting for transfers between devices  11.1 us (17%)
  other arithmetic  5.39 us (8%)
  local copies, waits for them, and re-layouts  2.63 us (4%)
  between operations  1.65 us (3%)
    ppermute x8, starting transfers between devices, passed_along(): return lax.ppermute(block, axis, route)  15.9 us
    dot_general x1, matrix products, per_device(): jnp.einsum('tfk,tjk->tfj', sources, tile_values, preferred_element_type=j...  7.92 us
    ppermute x4, waiting for transfers between devices, gathered_along(): got = lax.ppermute(held, axis, [(i, i ^ mask) for i in range(size)])  6.87 us
    dot_general x1, matrix products, per_device(): jnp.einsum('tfj,tjk->tfk', back_sources, tile_values, preferred_element_t...  5.99 us
    ppermute x8, waiting for transfers between devices, passed_along(): return lax.ppermute(block, axis, route)  4.17 us
    ppermute x4, starting transfers between devices, gathered_along(): got = lax.ppermute(held, axis, [(i, i ^ mask) for i in range(size)])  3.57 us
    ppermute x3, starting transfers between devices, summed_over(): held.append(lax.ppermute(block, axis, route))  3.49 us
    dot_general x2, matrix products, summed_by_table(): return jnp.einsum(spec, doubled, both, preferred_element_type=jnp.float32)  2.74 us
  transfers between devices with their start and end apart: 16, of which 6 were waited for; matrix products, arithmetic and copies ran while one was open for 25% of the time, Pallas kernels for 0%

profile of v21, /device:TPU:0, one launch (start us, length us, event | category | flops | bytes accessed | tf_op | source)
XLA Modules:
  0.0 63.2 jit_solution(14338965627291310071)
XLA Ops:
  0.6 3.1 %collective-permute-start = (bf16[16,32,128]{2,1,0:T(8,128)(2,1)}, bf16[16,32,128]{2,1,0:T(8,128)(2,1)S(1)}, u32[]{:S(2)}, u32[]{:S(2)}) collective-permute-start(bf16[16,32,128]{2,1,0:T(8,128)(2,1)} %param.9), channel_id=1, source_target_pairs={{24,0},{28,4},{0,8},{4,12},{8,16},{12,20},{16,24},{20,28},{25,1},{... | collective-permute-start | bytes 393224 | tf_op jit(solution)/shard_map/ppermute | solution.py:22
  3.7 1.5 %collective-permute-start.1 = (bf16[16,32,128]{2,1,0:T(8,128)(2,1)}, bf16[16,32,128]{2,1,0:T(8,128)(2,1)S(1)}, u32[]{:S(2)}, u32[]{:S(2)}) collective-permute-start(bf16[16,32,128]{2,1,0:T(8,128)(2,1)} %param.9), channel_id=1, source_target_pairs={{28,0},{0,4},{4,8},{8,12},{12,16},{16,20},{20,24},{24,28},{29,1},{... | collective-permute-start | bytes 393224 | tf_op jit(solution)/shard_map/ppermute | solution.py:22
  5.2 3.2 %collective-permute-start.2 = (bf16[16,32,128]{2,1,0:T(8,128)(2,1)}, bf16[16,32,128]{2,1,0:T(8,128)(2,1)S(1)}, u32[]{:S(2)}, u32[]{:S(2)}) collective-permute-start(bf16[16,32,128]{2,1,0:T(8,128)(2,1)} %param.9), channel_id=1, source_target_pairs={{4,0},{8,4},{12,8},{16,12},{20,16},{24,20},{28,24},{0,28},{5,1},{9... | collective-permute-start | bytes 393224 | tf_op jit(solution)/shard_map/ppermute | solution.py:22
  8.4 0.3 collective-permute-start.3
  8.7 0.7 %convert_bitcast_fusion = bf16[1,32,128]{2,1,0:T(8,128)(2,1)S(1)} fusion(f32[32,128]{1,0:T(8,128)} %param.14), kind=kLoop, calls=%fused_computation.80 | loop fusion | flops 4096 | bytes 24576 | tf_op jit(solution)/shard_map/broadcast_in_dim | solution.py:127
  9.4 0.1 broadcast_in_dim.11
  9.6 1.0 %fusion.24 = (bf16[1,17,32,128]{3,2,1,0:T(8,128)(2,1)S(1)}, bf16[17,128,128]{2,1,0:T(8,128)(2,1)S(1)}) fusion(bf16[1,32,128]{2,1,0:T(8,128)(2,1)S(1)} %convert_bitcast_fusion, bf16[16,32,128]{2,1,0:T(8,128)(2,1)} %param.17, bf16[17,128,128]{2,1,0:T(8,128)(2,1)S(1)} %broadcast_in_dim.11, s32[]{:T(128)S(6)} %select_n.77), kind=kLoop, calls=%fused_computation.48 | loop fusion | flops 278528 | bytes 417796 | tf_op jit(solution)/shard_map/stack | solution.py:37
  10.5 1.7 %collective-permute-start.4 = (bf16[1,17,32,128]{3,2,1,0:T(8,128)(2,1)S(1)}, bf16[1,17,32,128]{3,2,1,0:T(8,128)(2,1)S(1)}, u32[]{:S(2)}, u32[]{:S(2)}) collective-permute-start(bf16[1,17,32,128]{3,2,1,0:T(8,128)(2,1)S(1)} %get-tuple-element.35), channel_id=1, source_target_pairs={{0,2},{1,3},{2,0},{3,1},{4,6},{5,7},{6,4},{7,5},{8,10},{9,11},{10,... | collective-permute-start | bytes 417800 | tf_op jit(solution)/shard_map/ppermute | solution.py:38
  12.9 0.7 %broadcast_subtract_fusion = s32[256]{0:T(256)S(1)} fusion(s32[256]{0:T(256)} %param.11, s32[]{:T(128)S(6)} %mul.82), kind=kLoop, calls=%fused_computation.95 | loop fusion | flops 256 | bytes 2052 | tf_op jit(solution)/shard_map/sub | solution.py:108
  13.6 0.7 %fusion.41 = s32[256]{0:T(256)S(1)} fusion(s32[256]{0:T(256)} %param.12, s32[]{:T(128)S(6)} %axis_index.15), kind=kLoop, calls=%fused_computation.91 | loop fusion | flops 9472 | bytes 2052 | tf_op jit(solution)/shard_map/add | solution.py:113
  14.4 0.0 collective-permute-done
  14.4 0.0 collective-permute-done.1
  14.4 0.9 %constant_dynamic-update-slice_fusion.2 = bf16[80,32,128]{2,1,0:T(8,128)(2,1)S(1)} fusion(bf16[80,32,128]{2,1,0:T(8,128)(2,1)S(1)} %constant_dynamic-update-slice_fusion.3, bf16[16,32,128]{2,1,0:T(8,128)(2,1)} %param.9), kind=kLoop, calls=%fused_computation.74 | loop fusion | bytes 262144
  15.4 0.0 collective-permute-done.2
  15.4 0.2 collective-permute-done.4
  15.7 0.1 collective-permute-start.5
  15.8 0.0 collective-permute-done.3
  15.8 1.5 %collective-permute-done.5 = bf16[2,17,32,128]{3,2,1,0:T(8,128)(2,1)S(1)} collective-permute-done((bf16[2,17,32,128]{3,2,1,0:T(8,128)(2,1)S(1)}, bf16[2,17,32,128]{3,2,1,0:T(8,128)(2,1)S(1)}, u32[]{:S(2)}, u32[]{:S(2)}) %collective-permute-start.5) | collective-permute-done | bytes 278560 | tf_op jit(solution)/shard_map/ppermute | solution.py:38
  17.4 0.8 %fusion.13 = bf16[256,32,128]{2,0,1:T(8,128)(2,1)S(1)} fusion(bf16[80,32,128]{2,1,0:T(8,128)(2,1)S(1)} %constant_dynamic-update-slice_fusion, s32[256]{0:T(256)S(1)} %fusion.41), kind=kOutput, calls=%fused_computation.23 | convolution fusion | flops 167792640 | bytes 2753536 | tf_op jit(solution)/shard_map/ts,sfk->tfk/dot_general | solution.py:132
  18.2 7.9 %reduce-precision_convert_fusion.1 = (bf16[256,32,128]{2,1,0:T(8,128)(2,1)S(1)}, bf16[256,32,128]{2,1,0:T(8,128)(2,1)S(1)}) fusion(bf16[256,128,128]{2,1,0:T(8,128)(2,1)} %param.10, bf16[256,32,128]{2,0,1:T(8,128)(2,1)S(1)} %fusion.13), kind=kOutput, calls=%fused_computation.3 | convolution fusion | flops 272629760 | bytes 14680064 | tf_op jit(solution)/shard_map/tfk,tjk->tfj/dot_general | solution.py:135
  26.1 0.4 pad_maximum_fusion
  26.5 1.2 %fusion.9 = bf16[16,32,128]{2,0,1:T(8,128)(2,1)S(1)} fusion(bf16[512,32,128]{2,1,0:T(8,128)(2,1)S(1)} %pad_maximum_fusion, bf16[256,16]{0,1:T(8,128)(2,1)S(1)} %select_convert_fusion.1), kind=kOutput, calls=%fused_computation.18 | convolution fusion | flops 67207168 | bytes 4333568 | tf_op jit(solution)/shard_map/tb,tfj->bfj/dot_general | solution.py:79
  27.7 1.7 %collective-permute-start.6 = (bf16[1,16,32,128]{3,1,2,0:T(8,128)(2,1)S(1)}, bf16[1,16,32,128]{3,1,2,0:T(8,128)(2,1)S(1)}, u32[]{:S(2)}, u32[]{:S(2)}) collective-permute-start(bf16[1,16,32,128]{3,1,2,0:T(8,128)(2,1)S(1)} %bitcast.65), channel_id=1, source_target_pairs={{0,2},{1,3},{2,0},{3,1},{4,6},{5,7},{6,4},{7,5},{8,10},{9,11},{10,... | collective-permute-start | bytes 393224 | tf_op jit(solution)/shard_map/ppermute | solution.py:38
  29.4 3.8 %collective-permute-done.6 = bf16[1,16,32,128]{3,1,2,0:T(8,128)(2,1)S(1)} collective-permute-done((bf16[1,16,32,128]{3,1,2,0:T(8,128)(2,1)S(1)}, bf16[1,16,32,128]{3,1,2,0:T(8,128)(2,1)S(1)}, u32[]{:S(2)}, u32[]{:S(2)}) %collective-permute-start.6) | collective-permute-done | bytes 131104 | tf_op jit(solution)/shard_map/ppermute | solution.py:38
  33.3 0.1 collective-permute-start.7
  33.4 0.1 broadcast_in_dim.13
  33.5 0.1 copy_dynamic-update-slice_fusion.3
  33.5 0.1 copy_dynamic-update-slice_fusion.2
  33.6 1.3 %collective-permute-done.7 = bf16[2,16,32,128]{3,1,2,0:T(8,128)(2,1)S(1)} collective-permute-done((bf16[2,16,32,128]{3,1,2,0:T(8,128)(2,1)S(1)}, bf16[2,16,32,128]{3,1,2,0:T(8,128)(2,1)S(1)}, u32[]{:S(2)}, u32[]{:S(2)}) %collective-permute-start.7) | collective-permute-done | bytes 262176 | tf_op jit(solution)/shard_map/ppermute | solution.py:38
  34.9 0.1 copy_dynamic-update-slice_fusion.1
  35.0 0.1 copy_dynamic-update-slice_fusion
  35.0 0.3 fusion.31
  35.4 0.4 fusion.22
  35.8 0.0 collective-permute-start.10
  35.8 2.2 %collective-permute-start.9 = (f32[32,128]{1,0:T(8,128)S(1)}, f32[32,128]{1,0:T(8,128)S(1)}, u32[]{:S(2)}, u32[]{:S(2)}) collective-permute-start(f32[32,128]{1,0:T(8,128)S(1)} %bitcast.69), channel_id=1, source_target_pairs={{0,8},{4,12},{8,0},{12,4},{16,24},{20,28},{24,16},{28,20},{1,9},{5... | collective-permute-start | bytes 49160 | tf_op jit(solution)/shard_map/ppermute | solution.py:61
  38.0 1.3 %collective-permute-start.8 = (f32[32,128]{1,0:T(8,128)S(1)}, f32[32,128]{1,0:T(8,128)S(1)}, u32[]{:S(2)}, u32[]{:S(2)}) collective-permute-start(f32[32,128]{1,0:T(8,128)S(1)} %bitcast.70), channel_id=1, source_target_pairs={{0,4},{4,0},{8,12},{12,8},{16,20},{20,16},{24,28},{28,24},{1,5},{5... | collective-permute-start | bytes 49160 | tf_op jit(solution)/shard_map/ppermute | solution.py:61
  39.3 0.0 copy-done
  39.3 0.5 fusion.8
  39.8 0.2 copy.26
  40.0 0.7 %fusion.36 = bf16[256,32,128]{2,0,1:T(8,128)(2,1)S(1)} fusion(bf16[16,32,128]{2,0,1:T(8,128)(2,1)S(1)} %copy.26, s32[256]{0:T(256)S(1)} %broadcast_subtract_fusion), kind=kOutput, calls=%fused_computation.71 | convolution fusion | flops 33558528 | bytes 2229248 | tf_op jit(solution)/shard_map/tb,bfj->tfj/dot_general | solution.py:153
  40.8 6.0 %reduce-precision_convert_fusion = (bf16[256,32,128]{2,1,0:T(8,128)(2,1)S(1)}, bf16[256,32,128]{2,1,0:T(8,128)(2,1)S(1)}) fusion(bf16[256,128,128]{2,1,0:T(8,128)(2,1)} %param.10, bf16[256,32,128]{2,0,1:T(8,128)(2,1)S(1)} %fusion.36), kind=kOutput, calls=%fused_computation.1 | convolution fusion | flops 272629760 | bytes 14680064 | tf_op jit(solution)/shard_map/tfj,tjk->tfk/dot_general | solution.py:156
  46.8 0.4 pad_maximum_fusion.1
  47.1 0.0 copy-start.1
  47.1 0.0 copy-start.2
  47.2 1.5 %fusion.50 = (bf16[80,32,128]{2,0,1:T(8,128)(2,1)S(1)}, f32[80,32,128]{2,0,1:T(8,128)S(1)}) fusion(bf16[512,32,128]{2,1,0:T(8,128)(2,1)S(1)} %pad_maximum_fusion.1, bf16[256,80]{0,1:T(8,128)(2,1)S(1)} %select_convert_fusion), kind=kOutput, calls=%fused_computation.99 | convolution fusion | flops 336035840 | bytes 6201344 | tf_op jit(solution)/shard_map/ts,tfk->sfk/dot_general | solution.py:79
  48.7 3.1 %collective-permute-start.11 = (bf16[16,32,128]{2,0,1:T(8,128)(2,1)S(1)}, bf16[16,32,128]{2,0,1:T(8,128)(2,1)S(1)}, u32[]{:S(2)}, u32[]{:S(2)}) collective-permute-start(bf16[16,32,128]{2,0,1:T(8,128)(2,1)S(1)} %get-tuple-element.32), channel_id=1, source_target_pairs={{8,0},{12,4},{16,8},{20,12},{24,16},{28,20},{0,24},{4,28},{9,1},{1... | collective-permute-start | bytes 393224 | tf_op jit(solution)/shard_map/ppermute | solution.py:22
  51.9 0.0 collective-permute-start.14
  51.9 0.0 collective-permute-done.10
  51.9 0.0 collective-permute-start.13
  51.9 0.0 collective-permute-done.9
  51.9 4.7 %collective-permute-start.12 = (bf16[16,32,128]{2,0,1:T(8,128)(2,1)S(1)}, bf16[16,32,128]{2,0,1:T(8,128)(2,1)S(1)}, u32[]{:S(2)}, u32[]{:S(2)}) collective-permute-start(bf16[16,32,128]{2,0,1:T(8,128)(2,1)S(1)} %get-tuple-element.29), channel_id=1, source_target_pairs={{4,0},{8,4},{12,8},{16,12},{20,16},{24,20},{28,24},{0,28},{5,1},{9... | collective-permute-start | bytes 393224 | tf_op jit(solution)/shard_map/ppermute | solution.py:22
  56.6 0.0 collective-permute-done.8
  56.7 0.0 collective-permute-done.11
  56.7 0.1 collective-permute-start.15
  56.7 3.0 %collective-permute-done.14 = bf16[16,32,128]{2,0,1:T(8,128)(2,1)S(1)} collective-permute-done((bf16[16,32,128]{2,0,1:T(8,128)(2,1)S(1)}, bf16[16,32,128]{2,0,1:T(8,128)(2,1)S(1)}, u32[]{:S(2)}, u32[]{:S(2)}) %collective-permute-start.14) | collective-permute-done | bytes 131104 | tf_op jit(solution)/shard_map/ppermute | solution.py:22
  59.7 1.2 %collective-permute-done.13 = bf16[16,32,128]{2,0,1:T(8,128)(2,1)S(1)} collective-permute-done((bf16[16,32,128]{2,0,1:T(8,128)(2,1)S(1)}, bf16[16,32,128]{2,0,1:T(8,128)(2,1)S(1)}, u32[]{:S(2)}, u32[]{:S(2)}) %collective-permute-start.13) | collective-permute-done | bytes 131104 | tf_op jit(solution)/shard_map/ppermute | solution.py:22
  60.9 0.0 collective-permute-done.12
  60.9 0.1 fusion.19
  61.0 0.8 %fusion.16 = bf16[16,32,128]{2,1,0:T(8,128)(2,1)} fusion(f32[16,32,128]{2,1,0:T(8,128)S(1)} %dynamic-slice_bitcast_fusion), kind=kLoop, calls=%fused_computation.27 | loop fusion | flops 262144 | bytes 393216 | tf_op jit(solution)/shard_map/convert_element_type | solution.py:170
  61.8 0.8 %copy.22 = f32[16,32,128]{2,1,0:T(8,128)} copy(f32[16,32,128]{2,0,1:T(8,128)S(1)} %fusion.19) | data formatting | bytes 524288
  62.6 0.0 collective-permute-done.15
  62.6 0.0 copy-done.1
  62.6 0.0 copy-done.2
  62.6 0.6 %divide_subtract_fusion = (f32[32,128]{1,0:T(8,128)}, f32[32,128]{1,0:T(8,128)}, f32[32,128]{1,0:T(8,128)}) fusion(f32[32,128]{1,0:T(8,128)S(1)} %copy-done, f32[32,128]{1,0:T(8,128)S(1)} %add_bitcast_fusion, f32[32,128]{1,0:T(8,128)S(1)} %collective-permute-done.15, f32[32,128]{1,0:T(8,128)S(1)} %copy-done.1, f32[32,128]{1,0:T(8,128)S(1)} %copy-done.2), kind=kLoop, calls=%fused_computation.64 | loop fusion | flops 57344 | bytes 131072 | tf_op jit(solution)/shard_map/sub | solution.py:176
  (20 shorter events, 0.4 us)
Async XLA Ops:
  0.6 13.7 %collective-permute-start = (bf16[16,32,128]{2,1,0:T(8,128)(2,1)}, bf16[16,32,128]{2,1,0:T(8,128)(2,1)S(1)}, u32[]{:S(2)}, u32[]{:S(2)}) collective-permute-start(bf16[16,32,128]{2,1,0:T(8,128)(2,1)} %param.9), channel_id=1, source_target_pairs={{24,0},{28,4},{0,8},{4,12},{8,16},{12,20},{16,24},{20,28},{25,1},{... | collective-permute-start | bytes 393224 | tf_op jit(solution)/shard_map/ppermute | solution.py:22
  3.7 10.7 %collective-permute-start.1 = (bf16[16,32,128]{2,1,0:T(8,128)(2,1)}, bf16[16,32,128]{2,1,0:T(8,128)(2,1)S(1)}, u32[]{:S(2)}, u32[]{:S(2)}) collective-permute-start(bf16[16,32,128]{2,1,0:T(8,128)(2,1)} %param.9), channel_id=1, source_target_pairs={{28,0},{0,4},{4,8},{8,12},{12,16},{16,20},{20,24},{24,28},{29,1},{... | collective-permute-start | bytes 393224 | tf_op jit(solution)/shard_map/ppermute | solution.py:22
  5.2 10.2 %collective-permute-start.2 = (bf16[16,32,128]{2,1,0:T(8,128)(2,1)}, bf16[16,32,128]{2,1,0:T(8,128)(2,1)S(1)}, u32[]{:S(2)}, u32[]{:S(2)}) collective-permute-start(bf16[16,32,128]{2,1,0:T(8,128)(2,1)} %param.9), channel_id=1, source_target_pairs={{4,0},{8,4},{12,8},{16,12},{20,16},{24,20},{28,24},{0,28},{5,1},{9... | collective-permute-start | bytes 393224 | tf_op jit(solution)/shard_map/ppermute | solution.py:22
  8.4 7.3 %collective-permute-start.3 = (bf16[16,32,128]{2,1,0:T(8,128)(2,1)}, bf16[16,32,128]{2,1,0:T(8,128)(2,1)S(1)}, u32[]{:S(2)}, u32[]{:S(2)}) collective-permute-start(bf16[16,32,128]{2,1,0:T(8,128)(2,1)} %param.9), channel_id=1, source_target_pairs={{8,0},{12,4},{16,8},{20,12},{24,16},{28,20},{0,24},{4,28},{9,1},{1... | collective-permute-start | bytes 393224 | tf_op jit(solution)/shard_map/ppermute | solution.py:22
  10.5 5.1 %collective-permute-start.4 = (bf16[1,17,32,128]{3,2,1,0:T(8,128)(2,1)S(1)}, bf16[1,17,32,128]{3,2,1,0:T(8,128)(2,1)S(1)}, u32[]{:S(2)}, u32[]{:S(2)}) collective-permute-start(bf16[1,17,32,128]{3,2,1,0:T(8,128)(2,1)S(1)} %get-tuple-element.35), channel_id=1, source_target_pairs={{0,2},{1,3},{2,0},{3,1},{4,6},{5,7},{6,4},{7,5},{8,10},{9,11},{10,... | collective-permute-start | bytes 417800 | tf_op jit(solution)/shard_map/ppermute | solution.py:38
  15.7 1.6 %collective-permute-start.5 = (bf16[2,17,32,128]{3,2,1,0:T(8,128)(2,1)S(1)}, bf16[2,17,32,128]{3,2,1,0:T(8,128)(2,1)S(1)}, u32[]{:S(2)}, u32[]{:S(2)}) collective-permute-start(bf16[2,17,32,128]{3,2,1,0:T(8,128)(2,1)S(1)} %pad_maximum_fusion.2), channel_id=1, source_target_pairs={{0,1},{1,0},{2,3},{3,2},{4,5},{5,4},{6,7},{7,6},{8,9},{9,8},{10,11... | collective-permute-start | bytes 835592 | tf_op jit(solution)/shard_map/ppermute | solution.py:38
  27.7 11.5 %copy-start = (f32[32,128]{1,0:T(8,128)S(1)}, f32[32,128]{1,0:T(8,128)}, u32[]{:S(2)}) copy-start(f32[32,128]{1,0:T(8,128)} %param.14) | copy-start | bytes 49156
  27.7 5.6 %collective-permute-start.6 = (bf16[1,16,32,128]{3,1,2,0:T(8,128)(2,1)S(1)}, bf16[1,16,32,128]{3,1,2,0:T(8,128)(2,1)S(1)}, u32[]{:S(2)}, u32[]{:S(2)}) collective-permute-start(bf16[1,16,32,128]{3,1,2,0:T(8,128)(2,1)S(1)} %bitcast.65), channel_id=1, source_target_pairs={{0,2},{1,3},{2,0},{3,1},{4,6},{5,7},{6,4},{7,5},{8,10},{9,11},{10,... | collective-permute-start | bytes 393224 | tf_op jit(solution)/shard_map/ppermute | solution.py:38
  33.3 1.6 %collective-permute-start.7 = (bf16[2,16,32,128]{3,1,2,0:T(8,128)(2,1)S(1)}, bf16[2,16,32,128]{3,1,2,0:T(8,128)(2,1)S(1)}, u32[]{:S(2)}, u32[]{:S(2)}) collective-permute-start(bf16[2,16,32,128]{3,1,2,0:T(8,128)(2,1)S(1)} %pad_maximum_fusion.3), channel_id=1, source_target_pairs={{0,1},{1,0},{2,3},{3,2},{4,5},{5,4},{6,7},{7,6},{8,9},{9,8},{10,11... | collective-permute-start | bytes 786440 | tf_op jit(solution)/shard_map/ppermute | solution.py:38
  35.8 16.1 %collective-permute-start.10 = (f32[32,128]{1,0:T(8,128)S(1)}, f32[32,128]{1,0:T(8,128)S(1)}, u32[]{:S(2)}, u32[]{:S(2)}) collective-permute-start(f32[32,128]{1,0:T(8,128)S(1)} %bitcast.68), channel_id=1, source_target_pairs={{0,12},{4,8},{8,4},{12,0},{16,28},{20,24},{24,20},{28,16},{1,13},{... | collective-permute-start | bytes 49160 | tf_op jit(solution)/shard_map/ppermute | solution.py:61
  35.8 16.1 %collective-permute-start.9 = (f32[32,128]{1,0:T(8,128)S(1)}, f32[32,128]{1,0:T(8,128)S(1)}, u32[]{:S(2)}, u32[]{:S(2)}) collective-permute-start(f32[32,128]{1,0:T(8,128)S(1)} %bitcast.69), channel_id=1, source_target_pairs={{0,8},{4,12},{8,0},{12,4},{16,24},{20,28},{24,16},{28,20},{1,9},{5... | collective-permute-start | bytes 49160 | tf_op jit(solution)/shard_map/ppermute | solution.py:61
  38.0 18.6 %collective-permute-start.8 = (f32[32,128]{1,0:T(8,128)S(1)}, f32[32,128]{1,0:T(8,128)S(1)}, u32[]{:S(2)}, u32[]{:S(2)}) collective-permute-start(f32[32,128]{1,0:T(8,128)S(1)} %bitcast.70), channel_id=1, source_target_pairs={{0,4},{4,0},{8,12},{12,8},{16,20},{20,16},{24,28},{28,24},{1,5},{5... | collective-permute-start | bytes 49160 | tf_op jit(solution)/shard_map/ppermute | solution.py:61
  47.1 15.4 %copy-start.1 = (f32[32,128]{1,0:T(8,128)S(1)}, f32[32,128]{1,0:T(8,128)}, u32[]{:S(2)}) copy-start(f32[32,128]{1,0:T(8,128)} %param.15) | copy-start | bytes 49156
  47.1 15.4 %copy-start.2 = (f32[32,128]{1,0:T(8,128)S(1)}, f32[32,128]{1,0:T(8,128)}, u32[]{:S(2)}) copy-start(f32[32,128]{1,0:T(8,128)} %param.16) | copy-start | bytes 49156
  48.7 7.9 %collective-permute-start.11 = (bf16[16,32,128]{2,0,1:T(8,128)(2,1)S(1)}, bf16[16,32,128]{2,0,1:T(8,128)(2,1)S(1)}, u32[]{:S(2)}, u32[]{:S(2)}) collective-permute-start(bf16[16,32,128]{2,0,1:T(8,128)(2,1)S(1)} %get-tuple-element.32), channel_id=1, source_target_pairs={{8,0},{12,4},{16,8},{20,12},{24,16},{28,20},{0,24},{4,28},{9,1},{1... | collective-permute-start | bytes 393224 | tf_op jit(solution)/shard_map/ppermute | solution.py:22
  51.9 7.8 %collective-permute-start.14 = (bf16[16,32,128]{2,0,1:T(8,128)(2,1)S(1)}, bf16[16,32,128]{2,0,1:T(8,128)(2,1)S(1)}, u32[]{:S(2)}, u32[]{:S(2)}) collective-permute-start(bf16[16,32,128]{2,0,1:T(8,128)(2,1)S(1)} %get-tuple-element.30), channel_id=1, source_target_pairs={{24,0},{28,4},{0,8},{4,12},{8,16},{12,20},{16,24},{20,28},{25,1},{... | collective-permute-start | bytes 393224 | tf_op jit(solution)/shard_map/ppermute | solution.py:22
  51.9 9.0 %collective-permute-start.13 = (bf16[16,32,128]{2,0,1:T(8,128)(2,1)S(1)}, bf16[16,32,128]{2,0,1:T(8,128)(2,1)S(1)}, u32[]{:S(2)}, u32[]{:S(2)}) collective-permute-start(bf16[16,32,128]{2,0,1:T(8,128)(2,1)S(1)} %get-tuple-element.31), channel_id=1, source_target_pairs={{28,0},{0,4},{4,8},{8,12},{12,16},{16,20},{20,24},{24,28},{29,1},{... | collective-permute-start | bytes 393224 | tf_op jit(solution)/shard_map/ppermute | solution.py:22
  51.9 9.0 %collective-permute-start.12 = (bf16[16,32,128]{2,0,1:T(8,128)(2,1)S(1)}, bf16[16,32,128]{2,0,1:T(8,128)(2,1)S(1)}, u32[]{:S(2)}, u32[]{:S(2)}) collective-permute-start(bf16[16,32,128]{2,0,1:T(8,128)(2,1)S(1)} %get-tuple-element.29), channel_id=1, source_target_pairs={{4,0},{8,4},{12,8},{16,12},{20,16},{24,20},{28,24},{0,28},{5,1},{9... | collective-permute-start | bytes 393224 | tf_op jit(solution)/shard_map/ppermute | solution.py:22
  56.7 5.9 %collective-permute-start.15 = (f32[32,128]{1,0:T(8,128)S(1)}, f32[32,128]{1,0:T(8,128)S(1)}, u32[]{:S(2)}, u32[]{:S(2)}) collective-permute-start(f32[32,128]{1,0:T(8,128)S(1)} %add_bitcast_fusion), channel_id=1, source_target_pairs={{0,16},{4,20},{8,24},{12,28},{16,0},{20,4},{24,8},{28,12},{1,17},{... | collective-permute-start | bytes 49160 | tf_op jit(solution)/shard_map/ppermute | solution.py:68

commit v22 on v20

--- a/solution.py
+++ b/solution.py
@@ -22,7 +22,7 @@
     return lax.ppermute(block, axis, route)
 
 
-def gathered_along(block, axis, dim):
+def gathered_along(block, axis, dim, beside=None):
     size = lax.axis_size(axis)
     own = lax.axis_index(axis)
     width = block.shape[dim]
@@ -36,6 +36,8 @@
         while mask >= 1:
             held = jnp.stack([piece for piece, _ in pieces])
             got = lax.ppermute(held, axis, [(i, i ^ mask) for i in range(size)])
+            if beside is not None and mask == size // 2:
+                got, beside = lax.optimization_barrier((got, beside))
             pieces = pieces + [(got[k], index ^ mask) for k, (_, index) in enumerate(pieces)]
             mask //= 2
     shape = list(block.shape)
@@ -43,7 +45,9 @@
     whole = jnp.zeros(shape, block.dtype)
     for piece, index in pieces:
         whole = lax.dynamic_update_slice_in_dim(whole, piece, index * width, dim)
-    return whole
+    if beside is None:
+        return whole
+    return whole, beside
 
 
 def summed_over(block, axis, first=1, last=None):
@@ -125,10 +129,9 @@
     nearby = jnp.concatenate(pieces, axis=0)
     weight_half = weight.astype(jnp.bfloat16)
     packed = jnp.concatenate([cotangent, weight_half[None]], axis=0)
-    packed_all = gathered_along(packed, "feat", 1)
+    packed_all, nearby = gathered_along(packed, "feat", 1, beside=nearby)
     cotangent_all = packed_all[:blocks]
     weight_all = packed_all[blocks]
-    nearby, cotangent_all, weight_all = lax.optimization_barrier((nearby, cotangent_all, weight_all))
     sources = jnp.einsum(
         "ts,sfk->tfk", pick_source, nearby, preferred_element_type=jnp.float32
     ).astype(jnp.bfloat16)

time: 63.5 us -> 80.6 us (1.27)
  local copies, waits for them, and re-layouts: 2.6 us -> 25.9 us
  waiting for transfers between devices: 11.1 us -> 3.32 us
  starting transfers between devices: 23 us -> 24.3 us
    dynamic_update_slice x7 -> x8, local copies, waits for them, and re-layouts: 0.28 us -> 21.1 us  [gathered_along(): whole = lax.dynamic_update_slice_in_dim(whole, piece, index * width, dim)]
    ppermute x4, waiting for transfers between devices: 6.87 us -> 0.01 us  [gathered_along(): got = lax.ppermute(held, axis, [(i, i ^ mask) for i in range(size)])]
    ppermute x4, starting transfers between devices: 3.57 us -> 5.75 us  [gathered_along(): got = lax.ppermute(held, axis, [(i, i ^ mask) for i in range(size)])]
    unnamed x11 -> x16, local copies, waits for them, and re-layouts: 1.78 us -> 3.68 us
    ppermute x8, starting transfers between devices: 15.9 us -> 14.9 us  [passed_along(): return lax.ppermute(block, axis, route)]
    another operation x3 -> x2, other arithmetic: 1.01 us -> 0.06 us  [gathered_along(): held = jnp.stack([piece for piece, _ in pieces])]
    concatenate x0 -> x1, other arithmetic: none -> 0.92 us  [per_device(): packed = jnp.concatenate([cotangent, weight_half[None]], axis=0)]
    ppermute x8, waiting for transfers between devices: 4.18 us -> 3.29 us  [passed_along(): return lax.ppermute(block, axis, route)]
  transfers between devices with their start and end apart: 16 -> 16, of which waited for: 6 -> 2; matrix products, arithmetic and copies ran while one was open for 25% -> 61% of each run, Pallas kernels for 0% -> 0%
where the time goes in v22:
time: 80.6 us; the launch traced here: 80.3 us
  local copies, waits for them, and re-layouts  25.9 us (32%)
  starting transfers between devices  24.3 us (30%)
  matrix products  19.1 us (24%)
  other arithmetic  5.99 us (7%)
  waiting for transfers between devices  3.32 us (4%)
  between operations  1.69 us (2%)
    dynamic_update_slice x8, local copies, waits for them, and re-layouts, gathered_along(): whole = lax.dynamic_update_slice_in_dim(whole, piece, index * width, dim)  21.1 us
    ppermute x8, starting transfers between devices, passed_along(): return lax.ppermute(block, axis, route)  14.9 us
    dot_general x1, matrix products, per_device(): jnp.einsum('tfk,tjk->tfj', sources, tile_values, preferred_element_type=j...  7.92 us
    dot_general x1, matrix products, per_device(): jnp.einsum('tfj,tjk->tfk', back_sources, tile_values, preferred_element_t...  5.99 us
    ppermute x4, starting transfers between devices, gathered_along(): got = lax.ppermute(held, axis, [(i, i ^ mask) for i in range(size)])  5.75 us
    unnamed x16, local copies, waits for them, and re-layouts  3.68 us
    ppermute x3, starting transfers between devices, summed_over(): held.append(lax.ppermute(block, axis, route))  3.55 us
    ppermute x8, waiting for transfers between devices, passed_along(): return lax.ppermute(block, axis, route)  3.29 us
  transfers between devices with their start and end apart: 16, of which 2 were waited for; matrix products, arithmetic and copies ran while one was open for 61% of the time, Pallas kernels for 0%

profile of v22, /device:TPU:0, one launch (start us, length us, event | category | flops | bytes accessed | tf_op | source)
XLA Modules:
  0.0 80.3 jit_solution(5262703390499506068)
XLA Ops:
  0.6 3.1 %collective-permute-start.1 = (bf16[16,32,128]{2,1,0:T(8,128)(2,1)}, bf16[16,32,128]{2,1,0:T(8,128)(2,1)S(1)}, u32[]{:S(2)}, u32[]{:S(2)}) collective-permute-start(bf16[16,32,128]{2,1,0:T(8,128)(2,1)} %param.9), channel_id=1, source_target_pairs={{24,0},{28,4},{0,8},{4,12},{8,16},{12,20},{16,24},{20,28},{25,1},{... | collective-permute-start | bytes 393224 | tf_op jit(solution)/shard_map/ppermute | solution.py:22
  3.7 1.5 %collective-permute-start.2 = (bf16[16,32,128]{2,1,0:T(8,128)(2,1)}, bf16[16,32,128]{2,1,0:T(8,128)(2,1)S(1)}, u32[]{:S(2)}, u32[]{:S(2)}) collective-permute-start(bf16[16,32,128]{2,1,0:T(8,128)(2,1)} %param.9), channel_id=1, source_target_pairs={{28,0},{0,4},{4,8},{8,12},{12,16},{16,20},{20,24},{24,28},{29,1},{... | collective-permute-start | bytes 393224 | tf_op jit(solution)/shard_map/ppermute | solution.py:22
  5.2 3.2 %collective-permute-start.3 = (bf16[16,32,128]{2,1,0:T(8,128)(2,1)}, bf16[16,32,128]{2,1,0:T(8,128)(2,1)S(1)}, u32[]{:S(2)}, u32[]{:S(2)}) collective-permute-start(bf16[16,32,128]{2,1,0:T(8,128)(2,1)} %param.9), channel_id=1, source_target_pairs={{4,0},{8,4},{12,8},{16,12},{20,16},{24,20},{28,24},{0,28},{5,1},{9... | collective-permute-start | bytes 393224 | tf_op jit(solution)/shard_map/ppermute | solution.py:22
  8.4 0.3 collective-permute-start.4
  8.7 0.7 convert_bitcast_fusion
  9.4 0.9 %pad_maximum_fusion.4 = (bf16[17,32,128]{2,1,0:T(8,128)(2,1)S(1)}, bf16[1,17,32,128]{3,2,1,0:T(8,128)(2,1)S(1)}) fusion(bf16[1,32,128]{2,1,0:T(8,128)(2,1)S(1)} %convert_bitcast_fusion, bf16[16,32,128]{2,1,0:T(8,128)(2,1)} %param.17), kind=kLoop, calls=%fused_computation.31 | loop fusion | flops 69632 | bytes 417792 | tf_op jit(solution)/shard_map/concatenate | solution.py:131
  10.4 1.7 %collective-permute-start = (bf16[1,17,32,128]{3,2,1,0:T(8,128)(2,1)S(1)}, bf16[1,17,32,128]{3,2,1,0:T(8,128)(2,1)S(1)}, u32[]{:S(2)}, u32[]{:S(2)}) collective-permute-start(bf16[1,17,32,128]{3,2,1,0:T(8,128)(2,1)S(1)} %get-tuple-element.41), channel_id=1, source_target_pairs={{0,2},{1,3},{2,0},{3,1},{4,6},{5,7},{6,4},{7,5},{8,10},{9,11},{10,... | collective-permute-start | bytes 417800 | tf_op jit(solution)/shard_map/ppermute | solution.py:38
  12.8 0.7 fusion.32
  13.5 0.7 broadcast_subtract_fusion
  14.2 0.6 select_convert_fusion.1
  14.8 0.3 copy.28
  15.2 0.1 broadcast_in_dim.12
  15.3 2.7 %dynamic_update_slice.24 = bf16[17,128,128]{1,2,0:T(8,128)(2,1)S(1)} dynamic-update-slice(bf16[17,128,128]{1,2,0:T(8,128)(2,1)S(1)} %broadcast_in_dim.12, bf16[17,32,128]{1,2,0:T(8,128)(2,1)S(1)} %copy.28, s32[]{:T(128)} %constant.97.clone.1, s32[]{:T(128)S(6)} %select_n.73, s32[]{:T(128)} %constant.97.clone.1) | dynamic-update-slice | bytes 278532 | tf_op jit(solution)/shard_map/dynamic_update_slice | solution.py:47
  18.0 0.0 collective-permute-done.2
  18.1 0.9 %constant_dynamic-update-slice_fusion.2 = bf16[80,32,128]{2,1,0:T(8,128)(2,1)S(1)} fusion(bf16[80,32,128]{2,1,0:T(8,128)(2,1)S(1)} %constant_dynamic-update-slice_fusion.3, bf16[16,32,128]{2,1,0:T(8,128)(2,1)} %param.9), kind=kLoop, calls=%fused_computation.62 | loop fusion | bytes 262144
  19.0 0.0 collective-permute-done.4
  19.1 0.0 collective-permute-done
  19.1 0.3 copy.29
  19.4 1.9 %collective-permute-start.5 = (bf16[2,17,32,128]{3,2,1,0:T(8,128)(2,1)S(1)}, bf16[2,17,32,128]{3,2,1,0:T(8,128)(2,1)S(1)}, u32[]{:S(2)}, u32[]{:S(2)}) collective-permute-start(bf16[2,17,32,128]{3,2,1,0:T(8,128)(2,1)S(1)} %pad_maximum_fusion.2), channel_id=1, source_target_pairs={{0,1},{1,0},{2,3},{3,2},{4,5},{5,4},{6,7},{7,6},{8,9},{9,8},{10,11... | collective-permute-start | bytes 835592 | tf_op jit(solution)/shard_map/ppermute | solution.py:38
  21.4 0.8 fusion.12
  22.1 7.9 %reduce-precision_convert_fusion.1 = (bf16[256,32,128]{2,1,0:T(8,128)(2,1)S(1)}, bf16[256,32,128]{2,1,0:T(8,128)(2,1)S(1)}) fusion(bf16[256,128,128]{2,1,0:T(8,128)(2,1)} %param.10, bf16[256,32,128]{2,0,1:T(8,128)(2,1)S(1)} %fusion.12), kind=kOutput, calls=%fused_computation.3 | convolution fusion | flops 272629760 | bytes 14680064 | tf_op jit(solution)/shard_map/tfk,tjk->tfj/dot_general | solution.py:138
  30.1 0.4 pad_maximum_fusion
  30.4 1.2 %fusion.9 = bf16[16,32,128]{2,0,1:T(8,128)(2,1)S(1)} fusion(bf16[512,32,128]{2,1,0:T(8,128)(2,1)S(1)} %pad_maximum_fusion, bf16[256,16]{0,1:T(8,128)(2,1)S(1)} %select_convert_fusion.2), kind=kOutput, calls=%fused_computation.19 | convolution fusion | flops 67207168 | bytes 4333568 | tf_op jit(solution)/shard_map/tb,tfj->bfj/dot_general | solution.py:83
  31.7 1.8 %collective-permute-start.6 = (bf16[1,16,32,128]{3,1,2,0:T(8,128)(2,1)S(1)}, bf16[1,16,32,128]{3,1,2,0:T(8,128)(2,1)S(1)}, u32[]{:S(2)}, u32[]{:S(2)}) collective-permute-start(bf16[1,16,32,128]{3,1,2,0:T(8,128)(2,1)S(1)} %bitcast.58), channel_id=1, source_target_pairs={{0,2},{1,3},{2,0},{3,1},{4,6},{5,7},{6,4},{7,5},{8,10},{9,11},{10,... | collective-permute-start | bytes 393224 | tf_op jit(solution)/shard_map/ppermute | solution.py:38
  33.5 6.0 %dynamic_update_slice.25 = bf16[17,128,128]{1,2,0:T(8,128)(2,1)S(1)} dynamic-update-slice(bf16[17,128,128]{1,2,0:T(8,128)(2,1)S(1)} %dynamic_update_slice.24, bf16[17,32,128]{1,2,0:T(8,128)(2,1)S(1)} %bitcast.55, s32[]{:T(128)} %constant.97.clone.1, s32[]{:T(128)S(6)} %select_n.74, s32[]{:T(128)} %constant.97.clone.1) | dynamic-update-slice | bytes 278532 | tf_op jit(solution)/shard_map/dynamic_update_slice | solution.py:47
  39.4 0.1 broadcast_in_dim.13
  39.5 0.1 copy_dynamic-update-slice_fusion.3
  39.6 0.0 copy-start.1
  39.7 0.3 collective-permute-start.7
  40.0 0.3 copy.48
  40.4 0.3 copy.49
  40.7 6.0 %dynamic_update_slice.26 = bf16[17,128,128]{1,2,0:T(8,128)(2,1)S(1)} dynamic-update-slice(bf16[17,128,128]{1,2,0:T(8,128)(2,1)S(1)} %dynamic_update_slice.25, bf16[17,32,128]{1,2,0:T(8,128)(2,1)S(1)} %bitcast.56, s32[]{:T(128)} %constant.97.clone.1, s32[]{:T(128)S(6)} %select_n.75, s32[]{:T(128)} %constant.97.clone.1) | dynamic-update-slice | bytes 278532 | tf_op jit(solution)/shard_map/dynamic_update_slice | solution.py:47
  46.7 6.2 %dynamic_update_slice.27 = bf16[17,128,128]{1,2,0:T(8,128)(2,1)S(1)} dynamic-update-slice(bf16[17,128,128]{1,2,0:T(8,128)(2,1)S(1)} %dynamic_update_slice.26, bf16[17,32,128]{1,2,0:T(8,128)(2,1)S(1)} %bitcast.57, s32[]{:T(128)} %constant.97.clone.1, s32[]{:T(128)S(6)} %select_n.76, s32[]{:T(128)} %constant.97.clone.1) | dynamic-update-slice | bytes 278532 | tf_op jit(solution)/shard_map/dynamic_update_slice | solution.py:47
  52.9 0.0 collective-permute-done.7
  52.9 0.1 copy_dynamic-update-slice_fusion.1
  53.0 0.1 copy_dynamic-update-slice_fusion
  53.0 0.5 multiply_convert_fusion
  53.5 0.2 fusion.17
  53.7 0.1 collective-permute-start.10
  53.8 2.2 %collective-permute-start.9 = (f32[32,128]{1,0:T(8,128)S(1)}, f32[32,128]{1,0:T(8,128)S(1)}, u32[]{:S(2)}, u32[]{:S(2)}) collective-permute-start(f32[32,128]{1,0:T(8,128)S(1)} %bitcast.62), channel_id=1, source_target_pairs={{0,8},{4,12},{8,0},{12,4},{16,24},{20,28},{24,16},{28,20},{1,9},{5... | collective-permute-start | bytes 49160 | tf_op jit(solution)/shard_map/ppermute | solution.py:65
  56.0 1.3 %collective-permute-start.8 = (f32[32,128]{1,0:T(8,128)S(1)}, f32[32,128]{1,0:T(8,128)S(1)}, u32[]{:S(2)}, u32[]{:S(2)}) collective-permute-start(f32[32,128]{1,0:T(8,128)S(1)} %bitcast.63), channel_id=1, source_target_pairs={{0,4},{4,0},{8,12},{12,8},{16,20},{20,16},{24,28},{28,24},{1,5},{5... | collective-permute-start | bytes 49160 | tf_op jit(solution)/shard_map/ppermute | solution.py:65
  57.3 0.3 fusion.8
  57.6 0.1 broadcast_compare_fusion
  57.7 0.2 copy.46
  57.9 0.7 fusion.27
  58.7 6.0 %reduce-precision_convert_fusion = (bf16[256,32,128]{2,1,0:T(8,128)(2,1)S(1)}, bf16[256,32,128]{2,1,0:T(8,128)(2,1)S(1)}) fusion(bf16[256,128,128]{2,1,0:T(8,128)(2,1)} %param.10, bf16[256,32,128]{2,0,1:T(8,128)(2,1)S(1)} %fusion.27), kind=kOutput, calls=%fused_computation.1 | convolution fusion | flops 272629760 | bytes 14680064 | tf_op jit(solution)/shard_map/tfj,tjk->tfk/dot_general | solution.py:160
  64.7 0.4 pad_maximum_fusion.1
  65.1 0.4 copy-done
  65.5 1.5 %fusion.41 = (bf16[80,32,128]{2,0,1:T(8,128)(2,1)S(1)}, f32[80,32,128]{2,0,1:T(8,128)S(1)}) fusion(bf16[512,32,128]{2,1,0:T(8,128)(2,1)S(1)} %pad_maximum_fusion.1, bf16[256,80]{0,1:T(8,128)(2,1)S(1)} %copy-done), kind=kOutput, calls=%fused_computation.89 | convolution fusion | flops 336035840 | bytes 6201344 | tf_op jit(solution)/shard_map/ts,tfk->sfk/dot_general | solution.py:83
  67.0 0.0 copy-start.3
  67.0 0.6 select_convert_fusion
  67.7 2.0 %collective-permute-start.11 = (bf16[16,32,128]{2,0,1:T(8,128)(2,1)S(1)}, bf16[16,32,128]{2,0,1:T(8,128)(2,1)S(1)}, u32[]{:S(2)}, u32[]{:S(2)}) collective-permute-start(bf16[16,32,128]{2,0,1:T(8,128)(2,1)S(1)} %get-tuple-element.35), channel_id=1, source_target_pairs={{8,0},{12,4},{16,8},{20,12},{24,16},{28,20},{0,24},{4,28},{9,1},{1... | collective-permute-start | bytes 393224 | tf_op jit(solution)/shard_map/ppermute | solution.py:22
  69.7 0.1 collective-permute-start.14
  69.8 0.0 collective-permute-done.10
  69.8 0.7 collective-permute-start.13
  70.5 0.0 collective-permute-done.9
  70.5 4.0 %collective-permute-start.12 = (bf16[16,32,128]{2,0,1:T(8,128)(2,1)S(1)}, bf16[16,32,128]{2,0,1:T(8,128)(2,1)S(1)}, u32[]{:S(2)}, u32[]{:S(2)}) collective-permute-start(bf16[16,32,128]{2,0,1:T(8,128)(2,1)S(1)} %get-tuple-element.32), channel_id=1, source_target_pairs={{4,0},{8,4},{12,8},{16,12},{20,16},{24,20},{28,24},{0,28},{5,1},{9... | collective-permute-start | bytes 393224 | tf_op jit(solution)/shard_map/ppermute | solution.py:22
  74.5 0.1 collective-permute-start.15
  74.6 2.0 %collective-permute-done.14 = bf16[16,32,128]{2,0,1:T(8,128)(2,1)S(1)} collective-permute-done((bf16[16,32,128]{2,0,1:T(8,128)(2,1)S(1)}, bf16[16,32,128]{2,0,1:T(8,128)(2,1)S(1)}, u32[]{:S(2)}, u32[]{:S(2)}) %collective-permute-start.14) | collective-permute-done | bytes 131104 | tf_op jit(solution)/shard_map/ppermute | solution.py:22
  76.6 1.3 %collective-permute-done.13 = bf16[16,32,128]{2,0,1:T(8,128)(2,1)S(1)} collective-permute-done((bf16[16,32,128]{2,0,1:T(8,128)(2,1)S(1)}, bf16[16,32,128]{2,0,1:T(8,128)(2,1)S(1)}, u32[]{:S(2)}, u32[]{:S(2)}) %collective-permute-start.13) | collective-permute-done | bytes 131104 | tf_op jit(solution)/shard_map/ppermute | solution.py:22
  77.9 0.1 fusion.16
  78.0 0.8 %copy.40 = bf16[16,32,128]{2,1,0:T(8,128)(2,1)} copy(bf16[16,32,128]{1,2,0:T(8,128)(2,1)S(1)} %select_convert_fusion) | data formatting | bytes 262144
  78.8 0.8 copy.41
  79.6 0.6 divide_subtract_fusion
  (27 shorter events, 0.3 us)
Async XLA Ops:
  0.6 17.4 %collective-permute-start.1 = (bf16[16,32,128]{2,1,0:T(8,128)(2,1)}, bf16[16,32,128]{2,1,0:T(8,128)(2,1)S(1)}, u32[]{:S(2)}, u32[]{:S(2)}) collective-permute-start(bf16[16,32,128]{2,1,0:T(8,128)(2,1)} %param.9), channel_id=1, source_target_pairs={{24,0},{28,4},{0,8},{4,12},{8,16},{12,20},{16,24},{20,28},{25,1},{... | collective-permute-start | bytes 393224 | tf_op jit(solution)/shard_map/ppermute | solution.py:22
  3.7 14.3 %collective-permute-start.2 = (bf16[16,32,128]{2,1,0:T(8,128)(2,1)}, bf16[16,32,128]{2,1,0:T(8,128)(2,1)S(1)}, u32[]{:S(2)}, u32[]{:S(2)}) collective-permute-start(bf16[16,32,128]{2,1,0:T(8,128)(2,1)} %param.9), channel_id=1, source_target_pairs={{28,0},{0,4},{4,8},{8,12},{12,16},{16,20},{20,24},{24,28},{29,1},{... | collective-permute-start | bytes 393224 | tf_op jit(solution)/shard_map/ppermute | solution.py:22
  5.2 13.8 %collective-permute-start.3 = (bf16[16,32,128]{2,1,0:T(8,128)(2,1)}, bf16[16,32,128]{2,1,0:T(8,128)(2,1)S(1)}, u32[]{:S(2)}, u32[]{:S(2)}) collective-permute-start(bf16[16,32,128]{2,1,0:T(8,128)(2,1)} %param.9), channel_id=1, source_target_pairs={{4,0},{8,4},{12,8},{16,12},{20,16},{24,20},{28,24},{0,28},{5,1},{9... | collective-permute-start | bytes 393224 | tf_op jit(solution)/shard_map/ppermute | solution.py:22
  8.4 10.6 %collective-permute-start.4 = (bf16[16,32,128]{2,1,0:T(8,128)(2,1)}, bf16[16,32,128]{2,1,0:T(8,128)(2,1)S(1)}, u32[]{:S(2)}, u32[]{:S(2)}) collective-permute-start(bf16[16,32,128]{2,1,0:T(8,128)(2,1)} %param.9), channel_id=1, source_target_pairs={{8,0},{12,4},{16,8},{20,12},{24,16},{28,20},{0,24},{4,28},{9,1},{1... | collective-permute-start | bytes 393224 | tf_op jit(solution)/shard_map/ppermute | solution.py:22
  10.4 8.7 %collective-permute-start = (bf16[1,17,32,128]{3,2,1,0:T(8,128)(2,1)S(1)}, bf16[1,17,32,128]{3,2,1,0:T(8,128)(2,1)S(1)}, u32[]{:S(2)}, u32[]{:S(2)}) collective-permute-start(bf16[1,17,32,128]{3,2,1,0:T(8,128)(2,1)S(1)} %get-tuple-element.41), channel_id=1, source_target_pairs={{0,2},{1,3},{2,0},{3,1},{4,6},{5,7},{6,4},{7,5},{8,10},{9,11},{10,... | collective-permute-start | bytes 417800 | tf_op jit(solution)/shard_map/ppermute | solution.py:38
  19.4 20.6 %collective-permute-start.5 = (bf16[2,17,32,128]{3,2,1,0:T(8,128)(2,1)S(1)}, bf16[2,17,32,128]{3,2,1,0:T(8,128)(2,1)S(1)}, u32[]{:S(2)}, u32[]{:S(2)}) collective-permute-start(bf16[2,17,32,128]{3,2,1,0:T(8,128)(2,1)S(1)} %pad_maximum_fusion.2), channel_id=1, source_target_pairs={{0,1},{1,0},{2,3},{3,2},{4,5},{5,4},{6,7},{7,6},{8,9},{9,8},{10,11... | collective-permute-start | bytes 835592 | tf_op jit(solution)/shard_map/ppermute | solution.py:38
  31.7 7.9 %collective-permute-start.6 = (bf16[1,16,32,128]{3,1,2,0:T(8,128)(2,1)S(1)}, bf16[1,16,32,128]{3,1,2,0:T(8,128)(2,1)S(1)}, u32[]{:S(2)}, u32[]{:S(2)}) collective-permute-start(bf16[1,16,32,128]{3,1,2,0:T(8,128)(2,1)S(1)} %bitcast.58), channel_id=1, source_target_pairs={{0,2},{1,3},{2,0},{3,1},{4,6},{5,7},{6,4},{7,5},{8,10},{9,11},{10,... | collective-permute-start | bytes 393224 | tf_op jit(solution)/shard_map/ppermute | solution.py:38
  39.6 17.6 %copy-start.1 = (f32[32,128]{1,0:T(8,128)S(1)}, f32[32,128]{1,0:T(8,128)}, u32[]{:S(2)}) copy-start(f32[32,128]{1,0:T(8,128)} %param.14) | copy-start | bytes 49156
  39.7 13.2 %collective-permute-start.7 = (bf16[2,16,32,128]{3,1,2,0:T(8,128)(2,1)S(1)}, bf16[2,16,32,128]{3,1,2,0:T(8,128)(2,1)S(1)}, u32[]{:S(2)}, u32[]{:S(2)}) collective-permute-start(bf16[2,16,32,128]{3,1,2,0:T(8,128)(2,1)S(1)} %pad_maximum_fusion.3), channel_id=1, source_target_pairs={{0,1},{1,0},{2,3},{3,2},{4,5},{5,4},{6,7},{7,6},{8,9},{9,8},{10,11... | collective-permute-start | bytes 786440 | tf_op jit(solution)/shard_map/ppermute | solution.py:38
  53.7 16.0 %collective-permute-start.10 = (f32[32,128]{1,0:T(8,128)S(1)}, f32[32,128]{1,0:T(8,128)S(1)}, u32[]{:S(2)}, u32[]{:S(2)}) collective-permute-start(f32[32,128]{1,0:T(8,128)S(1)} %bitcast.61), channel_id=1, source_target_pairs={{0,12},{4,8},{8,4},{12,0},{16,28},{20,24},{24,20},{28,16},{1,13},{... | collective-permute-start | bytes 49160 | tf_op jit(solution)/shard_map/ppermute | solution.py:65
  53.8 16.7 %collective-permute-start.9 = (f32[32,128]{1,0:T(8,128)S(1)}, f32[32,128]{1,0:T(8,128)S(1)}, u32[]{:S(2)}, u32[]{:S(2)}) collective-permute-start(f32[32,128]{1,0:T(8,128)S(1)} %bitcast.62), channel_id=1, source_target_pairs={{0,8},{4,12},{8,0},{12,4},{16,24},{20,28},{24,16},{28,20},{1,9},{5... | collective-permute-start | bytes 49160 | tf_op jit(solution)/shard_map/ppermute | solution.py:65
  56.0 18.5 %collective-permute-start.8 = (f32[32,128]{1,0:T(8,128)S(1)}, f32[32,128]{1,0:T(8,128)S(1)}, u32[]{:S(2)}, u32[]{:S(2)}) collective-permute-start(f32[32,128]{1,0:T(8,128)S(1)} %bitcast.63), channel_id=1, source_target_pairs={{0,4},{4,0},{8,12},{12,8},{16,20},{20,16},{24,28},{28,24},{1,5},{5... | collective-permute-start | bytes 49160 | tf_op jit(solution)/shard_map/ppermute | solution.py:65
  64.7 0.8 copy-start
  67.0 12.7 %copy-start.2 = (f32[32,128]{1,0:T(8,128)S(1)}, f32[32,128]{1,0:T(8,128)}, u32[]{:S(2)}) copy-start(f32[32,128]{1,0:T(8,128)} %param.15) | copy-start | bytes 49156
  67.0 12.6 %copy-start.3 = (f32[32,128]{1,0:T(8,128)S(1)}, f32[32,128]{1,0:T(8,128)}, u32[]{:S(2)}) copy-start(f32[32,128]{1,0:T(8,128)} %param.16) | copy-start | bytes 49156
  67.7 6.8 %collective-permute-start.11 = (bf16[16,32,128]{2,0,1:T(8,128)(2,1)S(1)}, bf16[16,32,128]{2,0,1:T(8,128)(2,1)S(1)}, u32[]{:S(2)}, u32[]{:S(2)}) collective-permute-start(bf16[16,32,128]{2,0,1:T(8,128)(2,1)S(1)} %get-tuple-element.35), channel_id=1, source_target_pairs={{8,0},{12,4},{16,8},{20,12},{24,16},{28,20},{0,24},{4,28},{9,1},{1... | collective-permute-start | bytes 393224 | tf_op jit(solution)/shard_map/ppermute | solution.py:22
  69.7 6.9 %collective-permute-start.14 = (bf16[16,32,128]{2,0,1:T(8,128)(2,1)S(1)}, bf16[16,32,128]{2,0,1:T(8,128)(2,1)S(1)}, u32[]{:S(2)}, u32[]{:S(2)}) collective-permute-start(bf16[16,32,128]{2,0,1:T(8,128)(2,1)S(1)} %get-tuple-element.33), channel_id=1, source_target_pairs={{24,0},{28,4},{0,8},{4,12},{8,16},{12,20},{16,24},{20,28},{25,1},{... | collective-permute-start | bytes 393224 | tf_op jit(solution)/shard_map/ppermute | solution.py:22
  69.8 8.1 %collective-permute-start.13 = (bf16[16,32,128]{2,0,1:T(8,128)(2,1)S(1)}, bf16[16,32,128]{2,0,1:T(8,128)(2,1)S(1)}, u32[]{:S(2)}, u32[]{:S(2)}) collective-permute-start(bf16[16,32,128]{2,0,1:T(8,128)(2,1)S(1)} %get-tuple-element.34), channel_id=1, source_target_pairs={{28,0},{0,4},{4,8},{8,12},{12,16},{16,20},{20,24},{24,28},{29,1},{... | collective-permute-start | bytes 393224 | tf_op jit(solution)/shard_map/ppermute | solution.py:22
  70.5 7.4 %collective-permute-start.12 = (bf16[16,32,128]{2,0,1:T(8,128)(2,1)S(1)}, bf16[16,32,128]{2,0,1:T(8,128)(2,1)S(1)}, u32[]{:S(2)}, u32[]{:S(2)}) collective-permute-start(bf16[16,32,128]{2,0,1:T(8,128)(2,1)S(1)} %get-tuple-element.32), channel_id=1, source_target_pairs={{4,0},{8,4},{12,8},{16,12},{20,16},{24,20},{28,24},{0,28},{5,1},{9... | collective-permute-start | bytes 393224 | tf_op jit(solution)/shard_map/ppermute | solution.py:22
  74.5 5.1 %collective-permute-start.15 = (f32[32,128]{1,0:T(8,128)S(1)}, f32[32,128]{1,0:T(8,128)S(1)}, u32[]{:S(2)}, u32[]{:S(2)}) collective-permute-start(f32[32,128]{1,0:T(8,128)S(1)} %add_bitcast_fusion), channel_id=1, source_target_pairs={{0,16},{4,20},{8,24},{12,28},{16,0},{20,4},{24,8},{28,12},{1,17},{... | collective-permute-start | bytes 49160 | tf_op jit(solution)/shard_map/ppermute | solution.py:72

commit v23 on v20

--- a/solution.py
+++ b/solution.py
@@ -22,11 +22,16 @@
     return lax.ppermute(block, axis, route)
 
 
-def gathered_along(block, axis, dim):
+def gathered_along(block, axis, dim, direct=False):
     size = lax.axis_size(axis)
     own = lax.axis_index(axis)
     width = block.shape[dim]
-    if size & (size - 1):
+    if direct and not size & (size - 1):
+        pieces = [(block, own)]
+        for mask in range(1, size):
+            route = [(i, i ^ mask) for i in range(size)]
+            pieces.append((lax.ppermute(block, axis, route), own ^ mask))
+    elif size & (size - 1):
         pieces = [(block, own)]
         for step in range(1, size):
             pieces.append((passed_along(block, axis, -step), (own + step) % size))
@@ -137,7 +142,7 @@
     )
     aggregate = summed_by_table(add_row, forward_terms, "tb,tfj->bfj")
     aggregate = aggregate.astype(jnp.bfloat16)
-    aggregate_all = gathered_along(aggregate, "feat", 1)
+    aggregate_all = gathered_along(aggregate, "feat", 1, direct=True)
     column_start = lax.axis_index("feat") * width_local
     preact = jnp.einsum(
         "bij,io->boj", aggregate_all, weight_all, preferred_element_type=jnp.float32

time: 63.5 us -> 64.6 us (1.017)
  waiting for transfers between devices: 11.1 us -> 12.1 us
    ppermute x0 -> x3, waiting for transfers between devices: none -> 6.03 us  [gathered_along(): pieces.append((lax.ppermute(block, axis, route), own ^ mask))]
    ppermute x4 -> x2, waiting for transfers between devices: 6.87 us -> 1.68 us  [gathered_along(): got = lax.ppermute(held, axis, [(i, i ^ mask) for i in range(size)])]
    ppermute x0 -> x3, starting transfers between devices: none -> 1.86 us  [gathered_along(): pieces.append((lax.ppermute(block, axis, route), own ^ mask))]
    ppermute x4 -> x2, starting transfers between devices: 3.57 us -> 1.81 us  [gathered_along(): got = lax.ppermute(held, axis, [(i, i ^ mask) for i in range(size)])]
  transfers between devices with their start and end apart: 16 -> 17, of which waited for: 6 -> 6; matrix products, arithmetic and copies ran while one was open for 25% -> 24% of each run, Pallas kernels for 0% -> 0%
where the time goes in v23:
time: 64.6 us; the launch traced here: 64.3 us
  starting transfers between devices  23.1 us (36%)
  matrix products  19.4 us (30%)
  waiting for transfers between devices  12.1 us (19%)
  other arithmetic  5.38 us (8%)
  local copies, waits for them, and re-layouts  2.57 us (4%)
  between operations  1.66 us (3%)
    ppermute x8, starting transfers between devices, passed_along(): return lax.ppermute(block, axis, route)  15.9 us
    dot_general x1, matrix products, per_device(): jnp.einsum('tfk,tjk->tfj', sources, tile_values, preferred_element_type=j...  7.92 us
    ppermute x3, waiting for transfers between devices, gathered_along(): pieces.append((lax.ppermute(block, axis, route), own ^ mask))  6.03 us
    dot_general x1, matrix products, per_device(): jnp.einsum('tfj,tjk->tfk', back_sources, tile_values, preferred_element_t...  5.99 us
    ppermute x8, waiting for transfers between devices, passed_along(): return lax.ppermute(block, axis, route)  4.4 us
    ppermute x3, starting transfers between devices, summed_over(): held.append(lax.ppermute(block, axis, route))  3.5 us
    dot_general x2, matrix products, summed_by_table(): return jnp.einsum(spec, doubled, both, preferred_element_type=jnp.float32)  2.74 us
    ppermute x3, starting transfers between devices, gathered_along(): pieces.append((lax.ppermute(block, axis, route), own ^ mask))  1.86 us
  transfers between devices with their start and end apart: 17, of which 6 were waited for; matrix products, arithmetic and copies ran while one was open for 24% of the time, Pallas kernels for 0%

profile of v23, /device:TPU:0, one launch (start us, length us, event | category | flops | bytes accessed | tf_op | source)
XLA Modules:
  0.0 64.3 jit_solution(520738761625819990)
XLA Ops:
  0.6 3.1 %collective-permute-start = (bf16[16,32,128]{2,1,0:T(8,128)(2,1)}, bf16[16,32,128]{2,1,0:T(8,128)(2,1)S(1)}, u32[]{:S(2)}, u32[]{:S(2)}) collective-permute-start(bf16[16,32,128]{2,1,0:T(8,128)(2,1)} %param.9), channel_id=1, source_target_pairs={{24,0},{28,4},{0,8},{4,12},{8,16},{12,20},{16,24},{20,28},{25,1},{... | collective-permute-start | bytes 393224 | tf_op jit(solution)/shard_map/ppermute | solution.py:22
  3.7 1.5 %collective-permute-start.1 = (bf16[16,32,128]{2,1,0:T(8,128)(2,1)}, bf16[16,32,128]{2,1,0:T(8,128)(2,1)S(1)}, u32[]{:S(2)}, u32[]{:S(2)}) collective-permute-start(bf16[16,32,128]{2,1,0:T(8,128)(2,1)} %param.9), channel_id=1, source_target_pairs={{28,0},{0,4},{4,8},{8,12},{12,16},{16,20},{20,24},{24,28},{29,1},{... | collective-permute-start | bytes 393224 | tf_op jit(solution)/shard_map/ppermute | solution.py:22
  5.2 3.2 %collective-permute-start.2 = (bf16[16,32,128]{2,1,0:T(8,128)(2,1)}, bf16[16,32,128]{2,1,0:T(8,128)(2,1)S(1)}, u32[]{:S(2)}, u32[]{:S(2)}) collective-permute-start(bf16[16,32,128]{2,1,0:T(8,128)(2,1)} %param.9), channel_id=1, source_target_pairs={{4,0},{8,4},{12,8},{16,12},{20,16},{24,20},{28,24},{0,28},{5,1},{9... | collective-permute-start | bytes 393224 | tf_op jit(solution)/shard_map/ppermute | solution.py:22
  8.4 0.3 collective-permute-start.3
  8.7 0.7 %convert_bitcast_fusion = bf16[1,32,128]{2,1,0:T(8,128)(2,1)S(1)} fusion(f32[32,128]{1,0:T(8,128)} %param.14), kind=kLoop, calls=%fused_computation.73 | loop fusion | flops 4096 | bytes 24576 | tf_op jit(solution)/shard_map/broadcast_in_dim | solution.py:132
  9.4 0.1 broadcast_in_dim.11
  9.6 1.0 %fusion.21 = (bf16[1,17,32,128]{3,2,1,0:T(8,128)(2,1)S(1)}, bf16[17,128,128]{2,1,0:T(8,128)(2,1)S(1)}) fusion(bf16[1,32,128]{2,1,0:T(8,128)(2,1)S(1)} %convert_bitcast_fusion, bf16[16,32,128]{2,1,0:T(8,128)(2,1)} %param.17, bf16[17,128,128]{2,1,0:T(8,128)(2,1)S(1)} %broadcast_in_dim.11, s32[]{:T(128)S(6)} %select_n.75), kind=kLoop, calls=%fused_computation.42 | loop fusion | flops 278528 | bytes 417796 | tf_op jit(solution)/shard_map/stack | solution.py:42
  10.5 1.7 %collective-permute-start.4 = (bf16[1,17,32,128]{3,2,1,0:T(8,128)(2,1)S(1)}, bf16[1,17,32,128]{3,2,1,0:T(8,128)(2,1)S(1)}, u32[]{:S(2)}, u32[]{:S(2)}) collective-permute-start(bf16[1,17,32,128]{3,2,1,0:T(8,128)(2,1)S(1)} %get-tuple-element.33), channel_id=1, source_target_pairs={{0,2},{1,3},{2,0},{3,1},{4,6},{5,7},{6,4},{7,5},{8,10},{9,11},{10,... | collective-permute-start | bytes 417800 | tf_op jit(solution)/shard_map/ppermute | solution.py:43
  12.9 0.7 %fusion.37 = s32[256]{0:T(256)S(1)} fusion(s32[256]{0:T(256)} %param.12, s32[]{:T(128)S(6)} %axis_index.15), kind=kLoop, calls=%fused_computation.84 | loop fusion | flops 9472 | bytes 2052 | tf_op jit(solution)/shard_map/add | solution.py:118
  13.6 0.7 %broadcast_subtract_fusion = s32[256]{0:T(256)S(1)} fusion(s32[256]{0:T(256)} %param.11, s32[]{:T(128)S(6)} %mul.84), kind=kLoop, calls=%fused_computation.88 | loop fusion | flops 256 | bytes 2052 | tf_op jit(solution)/shard_map/sub | solution.py:113
  14.4 0.0 collective-permute-done
  14.4 0.0 collective-permute-done.1
  14.5 0.9 %constant_dynamic-update-slice_fusion.2 = bf16[80,32,128]{2,1,0:T(8,128)(2,1)S(1)} fusion(bf16[80,32,128]{2,1,0:T(8,128)(2,1)S(1)} %constant_dynamic-update-slice_fusion.3, bf16[16,32,128]{2,1,0:T(8,128)(2,1)} %param.9), kind=kLoop, calls=%fused_computation.67 | loop fusion | bytes 262144
  15.4 0.0 collective-permute-done.2
  15.4 0.2 collective-permute-done.4
  15.7 0.1 collective-permute-start.5
  15.8 0.0 collective-permute-done.3
  15.8 1.5 %collective-permute-done.5 = bf16[2,17,32,128]{3,2,1,0:T(8,128)(2,1)S(1)} collective-permute-done((bf16[2,17,32,128]{3,2,1,0:T(8,128)(2,1)S(1)}, bf16[2,17,32,128]{3,2,1,0:T(8,128)(2,1)S(1)}, u32[]{:S(2)}, u32[]{:S(2)}) %collective-permute-start.5) | collective-permute-done | bytes 278560 | tf_op jit(solution)/shard_map/ppermute | solution.py:43
  17.4 0.8 %fusion.12 = bf16[256,32,128]{2,0,1:T(8,128)(2,1)S(1)} fusion(bf16[80,32,128]{2,1,0:T(8,128)(2,1)S(1)} %constant_dynamic-update-slice_fusion, s32[256]{0:T(256)S(1)} %fusion.37), kind=kOutput, calls=%fused_computation.21 | convolution fusion | flops 167792640 | bytes 2753536 | tf_op jit(solution)/shard_map/ts,sfk->tfk/dot_general | solution.py:137
  18.2 7.9 %reduce-precision_convert_fusion.1 = (bf16[256,32,128]{2,1,0:T(8,128)(2,1)S(1)}, bf16[256,32,128]{2,1,0:T(8,128)(2,1)S(1)}) fusion(bf16[256,128,128]{2,1,0:T(8,128)(2,1)} %param.10, bf16[256,32,128]{2,0,1:T(8,128)(2,1)S(1)} %fusion.12), kind=kOutput, calls=%fused_computation.3 | convolution fusion | flops 272629760 | bytes 14680064 | tf_op jit(solution)/shard_map/tfk,tjk->tfj/dot_general | solution.py:140
  26.1 0.4 pad_maximum_fusion
  26.5 0.0 copy-start
  26.5 1.2 %fusion.9 = bf16[16,32,128]{2,0,1:T(8,128)(2,1)S(1)} fusion(bf16[512,32,128]{2,1,0:T(8,128)(2,1)S(1)} %pad_maximum_fusion, bf16[256,16]{0,1:T(8,128)(2,1)S(1)} %select_convert_fusion.2), kind=kOutput, calls=%fused_computation.19 | convolution fusion | flops 67207168 | bytes 4333568 | tf_op jit(solution)/shard_map/tb,tfj->bfj/dot_general | solution.py:84
  27.7 0.1 collective-permute-start.6
  27.9 1.7 %collective-permute-start.7 = (bf16[16,32,128]{2,0,1:T(8,128)(2,1)S(1)}, bf16[16,32,128]{2,0,1:T(8,128)(2,1)S(1)}, u32[]{:S(2)}, u32[]{:S(2)}) collective-permute-start(bf16[16,32,128]{2,0,1:T(8,128)(2,1)S(1)} %fusion.9), channel_id=1, source_target_pairs={{0,2},{1,3},{2,0},{3,1},{4,6},{5,7},{6,4},{7,5},{8,10},{9,11},{10,... | collective-permute-start | bytes 393224 | tf_op jit(solution)/shard_map/ppermute | solution.py:33
  29.6 0.0 collective-permute-start.8
  29.6 0.1 broadcast_in_dim.13
  29.7 0.1 copy_dynamic-update-slice_fusion.3
  29.8 0.0 collective-permute-done.6
  29.8 0.1 copy_dynamic-update-slice_fusion.2
  29.8 4.4 %collective-permute-done.7 = bf16[16,32,128]{2,0,1:T(8,128)(2,1)S(1)} collective-permute-done((bf16[16,32,128]{2,0,1:T(8,128)(2,1)S(1)}, bf16[16,32,128]{2,0,1:T(8,128)(2,1)S(1)}, u32[]{:S(2)}, u32[]{:S(2)}) %collective-permute-start.7) | collective-permute-done | bytes 131104 | tf_op jit(solution)/shard_map/ppermute | solution.py:33
  34.3 1.6 %collective-permute-done.8 = bf16[16,32,128]{2,0,1:T(8,128)(2,1)S(1)} collective-permute-done((bf16[16,32,128]{2,0,1:T(8,128)(2,1)S(1)}, bf16[16,32,128]{2,0,1:T(8,128)(2,1)S(1)}, u32[]{:S(2)}, u32[]{:S(2)}) %collective-permute-start.8) | collective-permute-done | bytes 131104 | tf_op jit(solution)/shard_map/ppermute | solution.py:33
  35.9 0.3 broadcast_compare_fusion
  36.3 0.4 fusion.19
  36.7 0.0 collective-permute-start.11
  36.7 2.2 %collective-permute-start.10 = (f32[32,128]{1,0:T(8,128)S(1)}, f32[32,128]{1,0:T(8,128)S(1)}, u32[]{:S(2)}, u32[]{:S(2)}) collective-permute-start(f32[32,128]{1,0:T(8,128)S(1)} %bitcast.56), channel_id=1, source_target_pairs={{0,8},{4,12},{8,0},{12,4},{16,24},{20,28},{24,16},{28,20},{1,9},{5... | collective-permute-start | bytes 49160 | tf_op jit(solution)/shard_map/ppermute | solution.py:66
  38.9 1.3 %collective-permute-start.9 = (f32[32,128]{1,0:T(8,128)S(1)}, f32[32,128]{1,0:T(8,128)S(1)}, u32[]{:S(2)}, u32[]{:S(2)}) collective-permute-start(f32[32,128]{1,0:T(8,128)S(1)} %bitcast.57), channel_id=1, source_target_pairs={{0,4},{4,0},{8,12},{12,8},{16,20},{20,16},{24,28},{28,24},{1,5},{5... | collective-permute-start | bytes 49160 | tf_op jit(solution)/shard_map/ppermute | solution.py:66
  40.2 0.0 copy-done
  40.2 0.5 fusion.8
  40.7 0.2 copy.26
  41.0 0.7 %fusion.32 = bf16[256,32,128]{2,0,1:T(8,128)(2,1)S(1)} fusion(bf16[16,32,128]{2,0,1:T(8,128)(2,1)S(1)} %copy.26, s32[256]{0:T(256)S(1)} %broadcast_subtract_fusion), kind=kOutput, calls=%fused_computation.64 | convolution fusion | flops 33558528 | bytes 2229248 | tf_op jit(solution)/shard_map/tb,bfj->tfj/dot_general | solution.py:159
  41.7 6.0 %reduce-precision_convert_fusion = (bf16[256,32,128]{2,1,0:T(8,128)(2,1)S(1)}, bf16[256,32,128]{2,1,0:T(8,128)(2,1)S(1)}) fusion(bf16[256,128,128]{2,1,0:T(8,128)(2,1)} %param.10, bf16[256,32,128]{2,0,1:T(8,128)(2,1)S(1)} %fusion.32), kind=kOutput, calls=%fused_computation.1 | convolution fusion | flops 272629760 | bytes 14680064 | tf_op jit(solution)/shard_map/tfj,tjk->tfk/dot_general | solution.py:162
  47.7 0.4 pad_maximum_fusion.1
  48.1 0.0 copy-start.1
  48.1 0.0 copy-start.2
  48.1 1.5 %fusion.44 = (bf16[80,32,128]{2,0,1:T(8,128)(2,1)S(1)}, f32[80,32,128]{2,0,1:T(8,128)S(1)}) fusion(bf16[512,32,128]{2,1,0:T(8,128)(2,1)S(1)} %pad_maximum_fusion.1, bf16[256,80]{0,1:T(8,128)(2,1)S(1)} %select_convert_fusion.1), kind=kOutput, calls=%fused_computation.92 | convolution fusion | flops 336035840 | bytes 6201344 | tf_op jit(solution)/shard_map/ts,tfk->sfk/dot_general | solution.py:84
  49.6 0.8 %select_convert_fusion = bf16[16,32,128]{2,1,0:T(8,128)(2,1)} fusion(f32[16,128,128]{2,1,0:T(8,128)S(1)} %get-tuple-element.36, s32[]{:T(128)S(6)} %select_n.75, pred[16,128,128]{2,1,0:T(8,128)(4,1)S(1)} %get-tuple-element.35), kind=kLoop, calls=%fused_computation.29 | loop fusion | flops 196608 | bytes 458756 | tf_op jit(solution)/shard_map/convert_element_type | solution.py:151
  50.4 3.1 %collective-permute-start.12 = (bf16[16,32,128]{2,0,1:T(8,128)(2,1)S(1)}, bf16[16,32,128]{2,0,1:T(8,128)(2,1)S(1)}, u32[]{:S(2)}, u32[]{:S(2)}) collective-permute-start(bf16[16,32,128]{2,0,1:T(8,128)(2,1)S(1)} %get-tuple-element.32), channel_id=1, source_target_pairs={{8,0},{12,4},{16,8},{20,12},{24,16},{28,20},{0,24},{4,28},{9,1},{1... | collective-permute-start | bytes 393224 | tf_op jit(solution)/shard_map/ppermute | solution.py:22
  53.5 0.0 collective-permute-start.15
  53.5 0.0 collective-permute-done.11
  53.5 0.0 collective-permute-start.14
  53.5 0.0 collective-permute-done.10
  53.5 4.7 %collective-permute-start.13 = (bf16[16,32,128]{2,0,1:T(8,128)(2,1)S(1)}, bf16[16,32,128]{2,0,1:T(8,128)(2,1)S(1)}, u32[]{:S(2)}, u32[]{:S(2)}) collective-permute-start(bf16[16,32,128]{2,0,1:T(8,128)(2,1)S(1)} %get-tuple-element.29), channel_id=1, source_target_pairs={{4,0},{8,4},{12,8},{16,12},{20,16},{24,20},{28,24},{0,28},{5,1},{9... | collective-permute-start | bytes 393224 | tf_op jit(solution)/shard_map/ppermute | solution.py:22
  58.3 0.0 collective-permute-done.9
  58.3 0.0 collective-permute-done.12
  58.3 0.1 collective-permute-start.16
  58.4 2.7 %collective-permute-done.15 = bf16[16,32,128]{2,0,1:T(8,128)(2,1)S(1)} collective-permute-done((bf16[16,32,128]{2,0,1:T(8,128)(2,1)S(1)}, bf16[16,32,128]{2,0,1:T(8,128)(2,1)S(1)}, u32[]{:S(2)}, u32[]{:S(2)}) %collective-permute-start.15) | collective-permute-done | bytes 131104 | tf_op jit(solution)/shard_map/ppermute | solution.py:22
  61.1 1.7 %collective-permute-done.14 = bf16[16,32,128]{2,0,1:T(8,128)(2,1)S(1)} collective-permute-done((bf16[16,32,128]{2,0,1:T(8,128)(2,1)S(1)}, bf16[16,32,128]{2,0,1:T(8,128)(2,1)S(1)}, u32[]{:S(2)}, u32[]{:S(2)}) %collective-permute-start.14) | collective-permute-done | bytes 131104 | tf_op jit(solution)/shard_map/ppermute | solution.py:22
  62.8 0.0 collective-permute-done.13
  62.8 0.1 fusion.16
  62.9 0.8 %copy.22 = f32[16,32,128]{2,1,0:T(8,128)} copy(f32[16,32,128]{2,0,1:T(8,128)S(1)} %fusion.16) | data formatting | bytes 524288
  63.6 0.0 collective-permute-done.16
  63.7 0.0 copy-done.1
  63.7 0.6 divide_subtract_fusion
  (19 shorter events, 0.4 us)
Async XLA Ops:
  0.6 13.8 %collective-permute-start = (bf16[16,32,128]{2,1,0:T(8,128)(2,1)}, bf16[16,32,128]{2,1,0:T(8,128)(2,1)S(1)}, u32[]{:S(2)}, u32[]{:S(2)}) collective-permute-start(bf16[16,32,128]{2,1,0:T(8,128)(2,1)} %param.9), channel_id=1, source_target_pairs={{24,0},{28,4},{0,8},{4,12},{8,16},{12,20},{16,24},{20,28},{25,1},{... | collective-permute-start | bytes 393224 | tf_op jit(solution)/shard_map/ppermute | solution.py:22
  3.7 10.7 %collective-permute-start.1 = (bf16[16,32,128]{2,1,0:T(8,128)(2,1)}, bf16[16,32,128]{2,1,0:T(8,128)(2,1)S(1)}, u32[]{:S(2)}, u32[]{:S(2)}) collective-permute-start(bf16[16,32,128]{2,1,0:T(8,128)(2,1)} %param.9), channel_id=1, source_target_pairs={{28,0},{0,4},{4,8},{8,12},{12,16},{16,20},{20,24},{24,28},{29,1},{... | collective-permute-start | bytes 393224 | tf_op jit(solution)/shard_map/ppermute | solution.py:22
  5.2 10.2 %collective-permute-start.2 = (bf16[16,32,128]{2,1,0:T(8,128)(2,1)}, bf16[16,32,128]{2,1,0:T(8,128)(2,1)S(1)}, u32[]{:S(2)}, u32[]{:S(2)}) collective-permute-start(bf16[16,32,128]{2,1,0:T(8,128)(2,1)} %param.9), channel_id=1, source_target_pairs={{4,0},{8,4},{12,8},{16,12},{20,16},{24,20},{28,24},{0,28},{5,1},{9... | collective-permute-start | bytes 393224 | tf_op jit(solution)/shard_map/ppermute | solution.py:22
  8.4 7.3 %collective-permute-start.3 = (bf16[16,32,128]{2,1,0:T(8,128)(2,1)}, bf16[16,32,128]{2,1,0:T(8,128)(2,1)S(1)}, u32[]{:S(2)}, u32[]{:S(2)}) collective-permute-start(bf16[16,32,128]{2,1,0:T(8,128)(2,1)} %param.9), channel_id=1, source_target_pairs={{8,0},{12,4},{16,8},{20,12},{24,16},{28,20},{0,24},{4,28},{9,1},{1... | collective-permute-start | bytes 393224 | tf_op jit(solution)/shard_map/ppermute | solution.py:22
  10.5 5.1 %collective-permute-start.4 = (bf16[1,17,32,128]{3,2,1,0:T(8,128)(2,1)S(1)}, bf16[1,17,32,128]{3,2,1,0:T(8,128)(2,1)S(1)}, u32[]{:S(2)}, u32[]{:S(2)}) collective-permute-start(bf16[1,17,32,128]{3,2,1,0:T(8,128)(2,1)S(1)} %get-tuple-element.33), channel_id=1, source_target_pairs={{0,2},{1,3},{2,0},{3,1},{4,6},{5,7},{6,4},{7,5},{8,10},{9,11},{10,... | collective-permute-start | bytes 417800 | tf_op jit(solution)/shard_map/ppermute | solution.py:43
  15.7 1.6 %collective-permute-start.5 = (bf16[2,17,32,128]{3,2,1,0:T(8,128)(2,1)S(1)}, bf16[2,17,32,128]{3,2,1,0:T(8,128)(2,1)S(1)}, u32[]{:S(2)}, u32[]{:S(2)}) collective-permute-start(bf16[2,17,32,128]{3,2,1,0:T(8,128)(2,1)S(1)} %pad_maximum_fusion.2), channel_id=1, source_target_pairs={{0,1},{1,0},{2,3},{3,2},{4,5},{5,4},{6,7},{7,6},{8,9},{9,8},{10,11... | collective-permute-start | bytes 835592 | tf_op jit(solution)/shard_map/ppermute | solution.py:43
  26.5 13.7 %copy-start = (f32[32,128]{1,0:T(8,128)S(1)}, f32[32,128]{1,0:T(8,128)}, u32[]{:S(2)}) copy-start(f32[32,128]{1,0:T(8,128)} %param.14) | copy-start | bytes 49156
  27.7 2.0 %collective-permute-start.6 = (bf16[16,32,128]{2,0,1:T(8,128)(2,1)S(1)}, bf16[16,32,128]{2,0,1:T(8,128)(2,1)S(1)}, u32[]{:S(2)}, u32[]{:S(2)}) collective-permute-start(bf16[16,32,128]{2,0,1:T(8,128)(2,1)S(1)} %fusion.9), channel_id=1, source_target_pairs={{0,1},{1,0},{2,3},{3,2},{4,5},{5,4},{6,7},{7,6},{8,9},{9,8},{10,11... | collective-permute-start | bytes 393224 | tf_op jit(solution)/shard_map/ppermute | solution.py:33
  27.9 6.3 %collective-permute-start.7 = (bf16[16,32,128]{2,0,1:T(8,128)(2,1)S(1)}, bf16[16,32,128]{2,0,1:T(8,128)(2,1)S(1)}, u32[]{:S(2)}, u32[]{:S(2)}) collective-permute-start(bf16[16,32,128]{2,0,1:T(8,128)(2,1)S(1)} %fusion.9), channel_id=1, source_target_pairs={{0,2},{1,3},{2,0},{3,1},{4,6},{5,7},{6,4},{7,5},{8,10},{9,11},{10,... | collective-permute-start | bytes 393224 | tf_op jit(solution)/shard_map/ppermute | solution.py:33
  29.6 6.3 %collective-permute-start.8 = (bf16[16,32,128]{2,0,1:T(8,128)(2,1)S(1)}, bf16[16,32,128]{2,0,1:T(8,128)(2,1)S(1)}, u32[]{:S(2)}, u32[]{:S(2)}) collective-permute-start(bf16[16,32,128]{2,0,1:T(8,128)(2,1)S(1)} %fusion.9), channel_id=1, source_target_pairs={{0,3},{1,2},{2,1},{3,0},{4,7},{5,6},{6,5},{7,4},{8,11},{9,10},{10,... | collective-permute-start | bytes 393224 | tf_op jit(solution)/shard_map/ppermute | solution.py:33
  36.7 16.8 %collective-permute-start.11 = (f32[32,128]{1,0:T(8,128)S(1)}, f32[32,128]{1,0:T(8,128)S(1)}, u32[]{:S(2)}, u32[]{:S(2)}) collective-permute-start(f32[32,128]{1,0:T(8,128)S(1)} %bitcast.55), channel_id=1, source_target_pairs={{0,12},{4,8},{8,4},{12,0},{16,28},{20,24},{24,20},{28,16},{1,13},{... | collective-permute-start | bytes 49160 | tf_op jit(solution)/shard_map/ppermute | solution.py:66
  36.7 16.8 %collective-permute-start.10 = (f32[32,128]{1,0:T(8,128)S(1)}, f32[32,128]{1,0:T(8,128)S(1)}, u32[]{:S(2)}, u32[]{:S(2)}) collective-permute-start(f32[32,128]{1,0:T(8,128)S(1)} %bitcast.56), channel_id=1, source_target_pairs={{0,8},{4,12},{8,0},{12,4},{16,24},{20,28},{24,16},{28,20},{1,9},{5... | collective-permute-start | bytes 49160 | tf_op jit(solution)/shard_map/ppermute | solution.py:66
  38.9 19.3 %collective-permute-start.9 = (f32[32,128]{1,0:T(8,128)S(1)}, f32[32,128]{1,0:T(8,128)S(1)}, u32[]{:S(2)}, u32[]{:S(2)}) collective-permute-start(f32[32,128]{1,0:T(8,128)S(1)} %bitcast.57), channel_id=1, source_target_pairs={{0,4},{4,0},{8,12},{12,8},{16,20},{20,16},{24,28},{28,24},{1,5},{5... | collective-permute-start | bytes 49160 | tf_op jit(solution)/shard_map/ppermute | solution.py:66
  48.1 15.6 %copy-start.1 = (f32[32,128]{1,0:T(8,128)S(1)}, f32[32,128]{1,0:T(8,128)}, u32[]{:S(2)}) copy-start(f32[32,128]{1,0:T(8,128)} %param.15) | copy-start | bytes 49156
  48.1 15.6 %copy-start.2 = (f32[32,128]{1,0:T(8,128)S(1)}, f32[32,128]{1,0:T(8,128)}, u32[]{:S(2)}) copy-start(f32[32,128]{1,0:T(8,128)} %param.16) | copy-start | bytes 49156
  50.4 7.9 %collective-permute-start.12 = (bf16[16,32,128]{2,0,1:T(8,128)(2,1)S(1)}, bf16[16,32,128]{2,0,1:T(8,128)(2,1)S(1)}, u32[]{:S(2)}, u32[]{:S(2)}) collective-permute-start(bf16[16,32,128]{2,0,1:T(8,128)(2,1)S(1)} %get-tuple-element.32), channel_id=1, source_target_pairs={{8,0},{12,4},{16,8},{20,12},{24,16},{28,20},{0,24},{4,28},{9,1},{1... | collective-permute-start | bytes 393224 | tf_op jit(solution)/shard_map/ppermute | solution.py:22
  53.5 7.6 %collective-permute-start.15 = (bf16[16,32,128]{2,0,1:T(8,128)(2,1)S(1)}, bf16[16,32,128]{2,0,1:T(8,128)(2,1)S(1)}, u32[]{:S(2)}, u32[]{:S(2)}) collective-permute-start(bf16[16,32,128]{2,0,1:T(8,128)(2,1)S(1)} %get-tuple-element.30), channel_id=1, source_target_pairs={{24,0},{28,4},{0,8},{4,12},{8,16},{12,20},{16,24},{20,28},{25,1},{... | collective-permute-start | bytes 393224 | tf_op jit(solution)/shard_map/ppermute | solution.py:22
  53.5 9.2 %collective-permute-start.14 = (bf16[16,32,128]{2,0,1:T(8,128)(2,1)S(1)}, bf16[16,32,128]{2,0,1:T(8,128)(2,1)S(1)}, u32[]{:S(2)}, u32[]{:S(2)}) collective-permute-start(bf16[16,32,128]{2,0,1:T(8,128)(2,1)S(1)} %get-tuple-element.31), channel_id=1, source_target_pairs={{28,0},{0,4},{4,8},{8,12},{12,16},{16,20},{20,24},{24,28},{29,1},{... | collective-permute-start | bytes 393224 | tf_op jit(solution)/shard_map/ppermute | solution.py:22
  53.5 9.2 %collective-permute-start.13 = (bf16[16,32,128]{2,0,1:T(8,128)(2,1)S(1)}, bf16[16,32,128]{2,0,1:T(8,128)(2,1)S(1)}, u32[]{:S(2)}, u32[]{:S(2)}) collective-permute-start(bf16[16,32,128]{2,0,1:T(8,128)(2,1)S(1)} %get-tuple-element.29), channel_id=1, source_target_pairs={{4,0},{8,4},{12,8},{16,12},{20,16},{24,20},{28,24},{0,28},{5,1},{9... | collective-permute-start | bytes 393224 | tf_op jit(solution)/shard_map/ppermute | solution.py:22
  58.3 5.3 %collective-permute-start.16 = (f32[32,128]{1,0:T(8,128)S(1)}, f32[32,128]{1,0:T(8,128)S(1)}, u32[]{:S(2)}, u32[]{:S(2)}) collective-permute-start(f32[32,128]{1,0:T(8,128)S(1)} %add_bitcast_fusion), channel_id=1, source_target_pairs={{0,16},{4,20},{8,24},{12,28},{16,0},{20,4},{24,8},{28,12},{1,17},{... | collective-permute-start | bytes 49160 | tf_op jit(solution)/shard_map/ppermute | solution.py:73
